TPU v7x, 32 devices: a whole 2x2x4 slice. The times are simulated.
32 devices in a mesh: groups: 2 (over y), seq: 4 (over z), queue: 4 (over x, core).
Axes of the slice: x: 2, y: 2, z: 4, core: 2. Of those that a mesh axis runs over, the one named last changes fastest.
Arguments:
- query_rows: bfloat16 [8, 512, 4096], P(('groups', 'queue'), 'seq'), parts along dimension 0, may hold values from -8 to 8
- key_rows: bfloat16 [8, 512, 4096], P(('groups', 'queue'), 'seq'), parts along dimension 0, may hold values from -8 to 8
- value_rows: bfloat16 [8, 512, 4096], P(('groups', 'queue'), 'seq'), parts along dimension 0, may hold values from -6 to 6
- hidden_state: bfloat16 [8, 512, 5120], P(('groups', 'queue'), 'seq'), parts along dimension 0, may hold values from -6 to 6
- modulation: float32 [8, 2, 5120], P(('groups', 'queue')), parts along dimension 0, may hold values from -4 to 4
- head_weight: bfloat16 [5120, 64], replicated, may hold values from -0.078125 to 0.078125
- latents: float32 [8, 512, 64], P(('groups', 'queue'), 'seq'), parts along dimension 0, may hold values from -6 to 6
- time_index: int32 [8], P(('groups', 'queue')), parts along dimension 0, may hold values from 1 to 8, as said below
- live_counts: int32 [32, 4], replicated, may hold values from 1 to 4, as said below
- block_lists: int32 [32, 4, 4], replicated, may hold values from 0 to 3, as said below
Outputs:
- attention_out: bfloat16 [8, 512, 4096], P(('groups', 'queue'), 'seq'), parts along dimension 0
- queue_next: float32 [8, 512, 64], P(('groups', 'queue'), 'seq'), parts along dimension 0
There are 2 independent parts, one for each index of `groups`. A program takes and returns all parts, laid end to end along the dimension named above; an argument that names none is the same for every part. Nothing has to cross between parts.
Inputs may be any that keep to these rules, and one draw needn't show every extreme that they name: live_counts[h, b] leading entries of block_lists[h, b] are attended; 4 is reached in every draw. `block_lists`: for each head and query block the 4 entries are distinct block numbers, the first being the query block itself. `time_index`: strictly rising along the queue; the first position is at 1 and the last at 8.
All inputs are finite; a program needn't handle non-finite values.
Results may differ from a plain program's by a relative error of at most 0.0055.
Values may be sent and summed in bfloat16 or wider, within the bound.
No kernel may reach another device: no remote copies, remote signals or barrier semaphores. Data moves between devices by JAX's collectives and lax.ppermute only.
A program may use at most 64 MiB of HBM per device.

v0:
```python
import jax
import jax.numpy as jnp
from jax import lax
from jax.sharding import PartitionSpec as P

STEPS = 8


epsilon = 1e-06
plan_shift = 5.0


def passed_along(value, axis, steps):
    count = lax.axis_size(axis)
    pairs = [(source, (source + steps) % count) for source in range(count)]
    return lax.ppermute(value, axis, pairs)


def noise_level(step_value):
    fraction = step_value.astype(jnp.float32) / STEPS
    return plan_shift * fraction / (1.0 + (plan_shift - 1.0) * fraction)


def attend(query_head, key_head, value_head, live, blocks):
    block_total = live.shape[0]
    block_size = query_head.shape[0] // block_total
    head_depth = query_head.shape[1]
    slot_total = blocks.shape[1]
    query_blocks = query_head.reshape(block_total, block_size, head_depth)
    key_blocks = key_head.reshape(-1, block_size, head_depth)
    value_blocks = value_head.reshape(-1, block_size, head_depth)
    scale = head_depth ** (-0.5)

    def advance(slot_number, state_now):
        highest, totals, summed = state_now
        chosen = lax.dynamic_index_in_dim(blocks, slot_number, 1, keepdims=False)
        key_chosen = jnp.take(key_blocks, chosen, axis=0)
        value_chosen = jnp.take(value_blocks, chosen, axis=0)
        scores = (
            jnp.einsum("bid,bjd->bij", query_blocks, key_chosen, preferred_element_type=jnp.float32)
            * scale
        )
        active = (slot_number < live)[:, None]
        new_highest = jnp.where(active, jnp.maximum(highest, jnp.max(scores, axis=2)), highest)
        weights = jnp.exp(scores - new_highest[:, :, None])
        factor = jnp.exp(highest - new_highest)
        new_totals = jnp.where(active, totals * factor + jnp.sum(weights, axis=2), totals)
        mixed = jnp.einsum(
            "bij,bjd->bid",
            weights.astype(jnp.bfloat16),
            value_chosen,
            preferred_element_type=jnp.float32,
        )
        new_summed = jnp.where(active[:, :, None], summed * factor[:, :, None] + mixed, summed)
        return (new_highest, new_totals, new_summed)

    start_state = (
        jnp.full((block_total, block_size), -jnp.inf, jnp.float32),
        jnp.zeros((block_total, block_size), jnp.float32),
        jnp.zeros((block_total, block_size, head_depth), jnp.float32),
    )
    final_state = lax.fori_loop(0, slot_total, advance, start_state)
    result = (final_state[2] / final_state[1][:, :, None]).astype(jnp.bfloat16)
    return result.reshape(block_total * block_size, head_depth)


def attend_heads(query_cols, key_cols, value_cols, head_ids, live_counts, block_lists):
    head_total = head_ids.shape[0]
    head_depth = query_cols.shape[1] // head_total
    query_stack = jnp.transpose(
        query_cols.reshape(query_cols.shape[0], head_total, head_depth), (1, 0, 2)
    )
    key_stack = jnp.transpose(
        key_cols.reshape(key_cols.shape[0], head_total, head_depth), (1, 0, 2)
    )
    value_stack = jnp.transpose(
        value_cols.reshape(value_cols.shape[0], head_total, head_depth), (1, 0, 2)
    )
    live_heads = jnp.take(live_counts, head_ids, axis=0)
    list_heads = jnp.take(block_lists, head_ids, axis=0)
    results = jax.vmap(attend)(query_stack, key_stack, value_stack, live_heads, list_heads)
    return jnp.transpose(results, (1, 0, 2)).reshape(query_cols.shape[0], head_total * head_depth)


def local(
    query_rows,
    key_rows,
    value_rows,
    hidden_state,
    modulation,
    head_weight,
    latents,
    time_index,
    live_counts,
    block_lists,
):
    seq_count = lax.axis_size("seq")
    own_index = lax.axis_index("seq")
    head_count = live_counts.shape[0]
    per_device = head_count // seq_count
    order = jnp.arange(head_count, dtype=jnp.int32)
    query_send, key_send, value_send = (query_rows, key_rows, value_rows)
    query_heads, key_heads, value_heads = (
        lax.all_to_all(query_send, "seq", split_axis=2, concat_axis=1, tiled=True),
        lax.all_to_all(key_send, "seq", split_axis=2, concat_axis=1, tiled=True),
        lax.all_to_all(value_send, "seq", split_axis=2, concat_axis=1, tiled=True),
    )
    source = hidden_state[0].astype(jnp.float32)
    mean_row = jnp.mean(source, axis=1, keepdims=True)
    centred = source - mean_row
    spread = jnp.mean(centred * centred, axis=1, keepdims=True)
    normed = centred * lax.rsqrt(spread + epsilon)
    shaped = (normed * (1.0 + modulation[0, 1]) + modulation[0, 0]).astype(jnp.bfloat16)
    velocity = jnp.dot(shaped, head_weight, preferred_element_type=jnp.float32)
    change = noise_level(time_index[0] - 1) - noise_level(time_index[0])
    moved = latents[0] + change * velocity
    queue_next = passed_along(moved[None].astype(jnp.bfloat16), "queue", -1).astype(jnp.float32)
    query_cols = query_heads[0]
    key_cols = key_heads[0]
    value_cols = value_heads[0]
    own_ids = lax.dynamic_slice_in_dim(order, own_index * per_device, per_device, 0)
    attended = attend_heads(query_cols, key_cols, value_cols, own_ids, live_counts, block_lists)
    mixed_back = lax.all_to_all(attended[None], "seq", split_axis=1, concat_axis=2, tiled=True)
    return (mixed_back, queue_next)


def solution(mesh):
    placed = (
        P(("groups", "queue"), "seq", None),
        P(("groups", "queue"), "seq", None),
        P(("groups", "queue"), "seq", None),
        P(("groups", "queue"), "seq", None),
        P(("groups", "queue"), None, None),
        P(),
        P(("groups", "queue"), "seq", None),
        P(("groups", "queue")),
        P(),
        P(),
    )
    return jax.shard_map(
        local,
        mesh=mesh,
        in_specs=placed,
        out_specs=(P(("groups", "queue"), "seq", None), P(("groups", "queue"), "seq", None)),
        check_vma=False,
    )
```

profile of v0, /device:TPU:0, one launch (start us, length us, event | category | flops | bytes accessed | tf_op | source)
XLA Modules:
  0.0 262.5 jit_solution(8443359924427387490)
XLA Ops:
  0.6 5.1 %copy.80 = bf16[1,128,4096]{1,0,2:T(2,128)(2,1)S(1)} copy(bf16[1,128,4096]{2,1,0:T(8,128)(2,1)} %param.15) | data formatting | bytes 2097152 | tf_op args[1]
  6.3 23.3 %reduce.1 = bf16[4096,128]{1,0:T(8,128)(2,1)} reduce(bf16[4096,1,128]{2,1,0:T(2,128)(2,1)S(1)} %bitcast.140, bf16[]{:T(256)} %broadcast.180), dimensions={1}, to_apply=%bitcast.100.reduce_sub_computation | reduce | bytes 2097154
  29.6 3.5 %reshape.164 = bf16[4,2,65536]{2,1,0:T(2,128)(2,1)} reshape(bf16[4096,128]{1,0:T(8,128)(2,1)} %reduce.1) | data formatting | bytes 2097152
  33.0 6.3 %all-to-all-start = ((bf16[4,2,65536]{2,1,0:T(2,128)(2,1)}), bf16[4,2,65536]{2,1,0:T(2,128)(2,1)}, u32[]{:S(2)}, u32[]{:S(2)}) async-start(bf16[4,2,65536]{2,1,0:T(2,128)(2,1)} %reshape.164), calls=%async_computation | async-start | bytes 2097152 | tf_op jit(solution)/shard_map/all_to_all | solution.py:105
  39.4 5.0 %copy.82 = bf16[1,128,4096]{1,0,2:T(2,128)(2,1)S(1)} copy(bf16[1,128,4096]{2,1,0:T(8,128)(2,1)} %param.14) | data formatting | bytes 2097152 | tf_op args[0]
  44.4 23.3 %reduce.2 = bf16[4096,128]{1,0:T(8,128)(2,1)} reduce(bf16[4096,1,128]{2,1,0:T(2,128)(2,1)S(1)} %bitcast.142, bf16[]{:T(256)} %broadcast.180), dimensions={1}, to_apply=%bitcast.102.reduce_sub_computation | reduce | bytes 2097154
  67.7 3.5 %reshape.166 = bf16[4,2,65536]{2,1,0:T(2,128)(2,1)} reshape(bf16[4096,128]{1,0:T(8,128)(2,1)} %reduce.2) | data formatting | bytes 2097152
  71.2 5.1 %all-to-all-start.1 = ((bf16[4,2,65536]{2,1,0:T(2,128)(2,1)}), bf16[4,2,65536]{2,1,0:T(2,128)(2,1)}, u32[]{:S(2)}, u32[]{:S(2)}) async-start(bf16[4,2,65536]{2,1,0:T(2,128)(2,1)} %reshape.166), calls=%async_computation.1 | async-start | bytes 2097152 | tf_op jit(solution)/shard_map/all_to_all | solution.py:104
  76.3 5.0 %copy.84 = bf16[1,128,4096]{1,0,2:T(2,128)(2,1)S(1)} copy(bf16[1,128,4096]{2,1,0:T(8,128)(2,1)} %param.16) | data formatting | bytes 2097152 | tf_op args[2]
  81.3 23.3 %reduce.3 = bf16[4096,128]{1,0:T(8,128)(2,1)} reduce(bf16[4096,1,128]{2,1,0:T(2,128)(2,1)S(1)} %bitcast.143, bf16[]{:T(256)} %broadcast.180), dimensions={1}, to_apply=%bitcast.104.reduce_sub_computation | reduce | bytes 2097154
  104.6 3.6 %reshape.168 = bf16[4,2,65536]{2,1,0:T(2,128)(2,1)} reshape(bf16[4096,128]{1,0:T(8,128)(2,1)} %reduce.3) | data formatting | bytes 2097152
  108.2 5.1 %all-to-all-start.2 = ((bf16[4,2,65536]{2,1,0:T(2,128)(2,1)}), bf16[4,2,65536]{2,1,0:T(2,128)(2,1)}, u32[]{:S(2)}, u32[]{:S(2)}) async-start(bf16[4,2,65536]{2,1,0:T(2,128)(2,1)} %reshape.168), calls=%async_computation.2 | async-start | bytes 2097152 | tf_op jit(solution)/shard_map/all_to_all | solution.py:106
  130.1 7.9 %all-to-all-done.2 = bf16[4,2,65536]{2,1,0:T(2,128)(2,1)} async-done(((bf16[4,2,65536]{2,1,0:T(2,128)(2,1)}), bf16[4,2,65536]{2,1,0:T(2,128)(2,1)}, u32[]{:S(2)}, u32[]{:S(2)}) %all-to-all-start.2) | async-done | bytes 1048608 | tf_op jit(solution)/shard_map/all_to_all | solution.py:106
  144.8 61.4 %while.19 = (s32[]{:T(128)}, f32[8,4,128]{2,1,0:T(4,128)S(1)}, f32[8,4,128]{2,1,0:T(4,128)S(1)}, f32[8,4,128,128]{3,2,1,0:T(8,128)}, s32[8,4]{1,0:T(8,128)S(1)},...) while((s32[]{:T(128)}, f32[8,4,128]{2,1,0:T(4,128)S(1)}, ...), condition=%wide.region_3.5_spmd.clone, body=%wide.region_0.4_spmd.clone.sunk | while | flops 275804640 | bytes 18089924 | solution.py:62
  155.8 3.8 %add_select_fusion.5 = f32[8,4,128,128]{3,2,1,0:T(8,128)} fusion(f32[8,4,128,128]{3,2,1,0:T(8,128)} %get-tuple-element.347, f32[8,4,128,128]{3,2,1,0:T(8,128)S(1)} %get-tuple-element.329, bf16[8,4,128,128]{3,2,1,0:T(8,128)(2,1)} %bitcast.135, f32[8,4,128]{2,1,0:T(4,128)S(1)} %get-tuple-element.331, f32[8,4,128]{2,1,0:T(4,128)S(1)} %maximum_select_fusion.2, ...), kind=kOutput, calls=%fused_computation.7.clone.1 | convolution fusion | flops 138412032 | bytes 7372865 | tf_op jit(solution)/shard_map/vmap()/while/body/eval_jaxpr/bij,bjd->bid/dot_general | solution.py:48
  161.1 2.9 %gather_fusion = bf16[32,128,128]{2,1,0:T(8,128)(2,1)} fusion(bf16[8,4,128,128]{3,2,1,0:T(8,128)(2,1)} %get-tuple-element.362, s32[32]{0:T(128)S(1)} %reshape.181), kind=kCustom, calls=%fused_computation.clone.clone.1 | custom fusion | bytes 2097408 | tf_op jit(solution)/shard_map/vmap()/while/body/eval_jaxpr/jit(_take)/gather | solution.py:37
  170.7 4.5 %add_select_fusion.5 = f32[8,4,128,128]{3,2,1,0:T(8,128)} fusion(f32[8,4,128,128]{3,2,1,0:T(8,128)} %get-tuple-element.347, f32[8,4,128,128]{3,2,1,0:T(8,128)S(1)} %get-tuple-element.329, bf16[8,4,128,128]{3,2,1,0:T(8,128)(2,1)} %bitcast.135, f32[8,4,128]{2,1,0:T(4,128)S(1)} %get-tuple-element.331, f32[8,4,128]{2,1,0:T(4,128)S(1)} %maximum_select_fusion.2, ...), kind=kOutput, calls=%fused_computation.7.clone.1 | convolution fusion | flops 138412032 | bytes 7372865 | tf_op jit(solution)/shard_map/vmap()/while/body/eval_jaxpr/bij,bjd->bid/dot_general | solution.py:48
  186.2 4.5 %add_select_fusion.5 = f32[8,4,128,128]{3,2,1,0:T(8,128)} fusion(f32[8,4,128,128]{3,2,1,0:T(8,128)} %get-tuple-element.347, f32[8,4,128,128]{3,2,1,0:T(8,128)S(1)} %get-tuple-element.329, bf16[8,4,128,128]{3,2,1,0:T(8,128)(2,1)} %bitcast.135, f32[8,4,128]{2,1,0:T(4,128)S(1)} %get-tuple-element.331, f32[8,4,128]{2,1,0:T(4,128)S(1)} %maximum_select_fusion.2, ...), kind=kOutput, calls=%fused_computation.7.clone.1 | convolution fusion | flops 138412032 | bytes 7372865 | tf_op jit(solution)/shard_map/vmap()/while/body/eval_jaxpr/bij,bjd->bid/dot_general | solution.py:48
  201.7 4.5 %add_select_fusion.5 = f32[8,4,128,128]{3,2,1,0:T(8,128)} fusion(f32[8,4,128,128]{3,2,1,0:T(8,128)} %get-tuple-element.347, f32[8,4,128,128]{3,2,1,0:T(8,128)S(1)} %get-tuple-element.329, bf16[8,4,128,128]{3,2,1,0:T(8,128)(2,1)} %bitcast.135, f32[8,4,128]{2,1,0:T(4,128)S(1)} %get-tuple-element.331, f32[8,4,128]{2,1,0:T(4,128)S(1)} %maximum_select_fusion.2, ...), kind=kOutput, calls=%fused_computation.7.clone.1 | convolution fusion | flops 138412032 | bytes 7372865 | tf_op jit(solution)/shard_map/vmap()/while/body/eval_jaxpr/bij,bjd->bid/dot_general | solution.py:48
  209.5 5.0 %copy.91 = bf16[1,512,1024]{2,0,1:T(2,128)(2,1)S(1)} copy(bf16[1,512,1024]{1,2,0:T(8,128)(2,1)} %bitcast.148) | data formatting | bytes 2097152 | tf_op jit(solution)/shard_map/broadcast_in_dim;reshape | solution.py:123
  214.4 7.7 %reduce.4 = bf16[512,1024]{1,0:T(8,128)(2,1)} reduce(bf16[512,1,1024]{2,1,0:T(2,128)(2,1)S(1)} %bitcast.141, bf16[]{:T(256)} %broadcast.180), dimensions={1}, to_apply=%bitcast.106.reduce_sub_computation | reduce | bytes 2097154
  222.1 3.8 %reshape.170 = bf16[4,2,65536]{2,1,0:T(2,128)(2,1)} reshape(bf16[512,1024]{1,0:T(8,128)(2,1)} %reduce.4) | data formatting | bytes 2097152
  226.0 4.2 %all-to-all-start.3 = ((bf16[4,2,65536]{2,1,0:T(2,128)(2,1)}), bf16[4,2,65536]{2,1,0:T(2,128)(2,1)}, u32[]{:S(2)}, u32[]{:S(2)}) async-start(bf16[4,2,65536]{2,1,0:T(2,128)(2,1)} %reshape.170), calls=%async_computation.3 | async-start | bytes 2097152 | tf_op jit(solution)/shard_map/all_to_all | solution.py:123
  233.4 22.1 %all-to-all-done.3 = bf16[4,2,65536]{2,1,0:T(2,128)(2,1)} async-done(((bf16[4,2,65536]{2,1,0:T(2,128)(2,1)}), bf16[4,2,65536]{2,1,0:T(2,128)(2,1)}, u32[]{:S(2)}, u32[]{:S(2)}) %all-to-all-start.3) | async-done | bytes 1048608 | tf_op jit(solution)/shard_map/all_to_all | solution.py:123
  (119 shorter events, 77.8 us)
Async XLA Ops:
  0.6 229.7 %copy-start = (bf16[5120,64]{0,1:T(8,128)(2,1)S(1)}, bf16[5120,64]{0,1:T(8,128)(2,1)}, u32[]{:S(2)}) copy-start(bf16[5120,64]{0,1:T(8,128)(2,1)} %param.19) | copy-start | bytes 1966084
  33.0 38.1 %all-to-all-start = ((bf16[4,2,65536]{2,1,0:T(2,128)(2,1)}), bf16[4,2,65536]{2,1,0:T(2,128)(2,1)}, u32[]{:S(2)}, u32[]{:S(2)}) async-start(bf16[4,2,65536]{2,1,0:T(2,128)(2,1)} %reshape.164), calls=%async_computation | async-start | bytes 2097152 | tf_op jit(solution)/shard_map/all_to_all | solution.py:105
  71.2 37.0 %all-to-all-start.1 = ((bf16[4,2,65536]{2,1,0:T(2,128)(2,1)}), bf16[4,2,65536]{2,1,0:T(2,128)(2,1)}, u32[]{:S(2)}, u32[]{:S(2)}) async-start(bf16[4,2,65536]{2,1,0:T(2,128)(2,1)} %reshape.166), calls=%async_computation.1 | async-start | bytes 2097152 | tf_op jit(solution)/shard_map/all_to_all | solution.py:104
  104.6 9.4 %copy-start.4 = (s32[32,4,4]{0,2,1:T(4,128)S(1)}, s32[32,4,4]{0,2,1:T(4,128)}, u32[]{:S(2)}) copy-start(s32[32,4,4]{0,2,1:T(4,128)} %param.23) | copy-start | bytes 6148
  104.6 10.3 %copy-start.5 = (s32[32,4]{0,1:T(4,128)S(1)}, s32[32,4]{0,1:T(4,128)}, u32[]{:S(2)}) copy-start(s32[32,4]{0,1:T(4,128)} %param.22) | copy-start | bytes 1540
  104.6 11.1 %copy-start.1 = (bf16[1,128,5120]{2,1,0:T(8,128)(2,1)S(1)}, bf16[1,128,5120]{2,1,0:T(8,128)(2,1)}, u32[]{:S(2)}) copy-start(bf16[1,128,5120]{2,1,0:T(8,128)(2,1)} %param.17) | copy-start | bytes 3932164
  108.2 29.8 %all-to-all-start.2 = ((bf16[4,2,65536]{2,1,0:T(2,128)(2,1)}), bf16[4,2,65536]{2,1,0:T(2,128)(2,1)}, u32[]{:S(2)}, u32[]{:S(2)}) async-start(bf16[4,2,65536]{2,1,0:T(2,128)(2,1)} %reshape.168), calls=%async_computation.2 | async-start | bytes 2097152 | tf_op jit(solution)/shard_map/all_to_all | solution.py:106
  222.1 8.1 %copy-start.3 = (f32[1,2,5120]{2,1,0:T(2,128)S(1)}, f32[1,2,5120]{2,1,0:T(2,128)}, u32[]{:S(2)}) copy-start(f32[1,2,5120]{2,1,0:T(2,128)} %param.18) | copy-start | bytes 122884
  222.1 8.2 %copy-start.2 = (bf16[1,128,5120]{2,1,0:T(8,128)(2,1)S(1)}, bf16[1,128,5120]{2,1,0:T(8,128)(2,1)}, u32[]{:S(2)}) copy-start(bf16[1,128,5120]{2,1,0:T(8,128)(2,1)} %param.17) | copy-start | bytes 3932164
  222.1 8.2 %copy-start.6 = (f32[1,128,64]{1,2,0:T(8,128)S(1)}, f32[1,128,64]{1,2,0:T(8,128)}, u32[]{:S(2)}) copy-start(f32[1,128,64]{1,2,0:T(8,128)} %param.20) | copy-start | bytes 98308
  226.0 29.6 %all-to-all-start.3 = ((bf16[4,2,65536]{2,1,0:T(2,128)(2,1)}), bf16[4,2,65536]{2,1,0:T(2,128)(2,1)}, u32[]{:S(2)}, u32[]{:S(2)}) async-start(bf16[4,2,65536]{2,1,0:T(2,128)(2,1)} %reshape.170), calls=%async_computation.3 | async-start | bytes 2097152 | tf_op jit(solution)/shard_map/all_to_all | solution.py:123
  231.1 1.7 collective-permute-start
where the time goes:
time: 264 us; the launch traced here: 262 us
  local copies, waits for them, and re-layouts  91.5 us (35%)
  other arithmetic  89 us (34%)
  waiting for transfers between devices  31.5 us (12%)
  matrix products  27.7 us (10%)
  starting transfers between devices  21 us (8%)
    unnamed x7, other arithmetic  77.6 us
    unnamed x40, local copies, waits for them, and re-layouts  51.4 us
    all_to_all x1, waiting for transfers between devices, local(): lax.all_to_all(attended[None], 'seq', split_axis=1, concat_axis=2, tiled=...  22.1 us
    dot_general x4, matrix products, advance(): jnp.einsum('bij,bjd->bid', weights.astype(jnp.bfloat16), value_chosen, pr...  17.2 us
    gather x12, local copies, waits for them, and re-layouts, advance(): key_chosen = jnp.take(key_blocks, chosen, axis=0)  12.2 us
    gather x4, local copies, waits for them, and re-layouts, advance(): value_chosen = jnp.take(value_blocks, chosen, axis=0)  11.5 us
    dot_general x4, matrix products, advance(): jnp.einsum('bid,bjd->bij', query_blocks, key_chosen, preferred_element_ty...  9.79 us
    all_to_all x1, waiting for transfers between devices, local(): lax.all_to_all(value_send, 'seq', split_axis=2, concat_axis=1, tiled=True)  7.95 us
  transfers between devices with their start and end apart: 5, of which 3 were waited for; matrix products, arithmetic and copies ran while one was open for 31% of the time, Pallas kernels for 0%

commit v1 on v0

v1 whole, which is shorter than its diff:
```python
import functools

import jax
import jax.numpy as jnp
from jax import lax
from jax.experimental import pallas as pl
from jax.experimental.pallas import tpu as pltpu
from jax.sharding import PartitionSpec as P

STEPS = 8
CHUNKS = 2


epsilon = 1e-06
plan_shift = 5.0


def passed_along(value, axis, steps):
    count = lax.axis_size(axis)
    pairs = [(source, (source + steps) % count) for source in range(count)]
    return lax.ppermute(value, axis, pairs)


def noise_level(step_value):
    fraction = step_value.astype(jnp.float32) / STEPS
    return plan_shift * fraction / (1.0 + (plan_shift - 1.0) * fraction)


def attend_kernel(lists_ref, live_ref, q_ref, k_ref, v_ref, o_ref, *, block, slots, qblocks):
    head = pl.program_id(0)
    qblock = pl.program_id(1)
    total = k_ref.shape[0]
    scale = q_ref.shape[1] ** (-0.5)
    scores = (
        lax.dot_general(
            q_ref[...],
            k_ref[...],
            (((1,), (1,)), ((), ())),
            preferred_element_type=jnp.float32,
        )
        * scale
    )
    column = lax.broadcasted_iota(jnp.int32, (1, total), 1)
    live = live_ref[head * qblocks + qblock]
    active = column < 0
    for slot in range(slots):
        chosen = lists_ref[(head * qblocks + qblock) * slots + slot]
        low = chosen * block
        hit = (column >= low) & (column < low + block) & (slot < live)
        active = active | hit
    scores = jnp.where(active, scores, -jnp.inf)
    highest = jnp.max(scores, axis=1, keepdims=True)
    weights = jnp.exp(scores - highest)
    totals = jnp.sum(weights, axis=1, keepdims=True)
    mixed = jnp.dot(
        weights.astype(jnp.bfloat16), v_ref[...], preferred_element_type=jnp.float32
    )
    o_ref[...] = (mixed / totals).astype(o_ref.dtype)


def attend_heads(query_cols, key_cols, value_cols, lists, live):
    total, width = query_cols.shape
    head_total, qblocks = live.shape
    slots = lists.shape[2]
    depth = width // head_total
    block = total // qblocks
    kernel = functools.partial(attend_kernel, block=block, slots=slots, qblocks=qblocks)
    grid_spec = pltpu.PrefetchScalarGridSpec(
        num_scalar_prefetch=2,
        grid=(head_total, qblocks),
        in_specs=[
            pl.BlockSpec((block, depth), lambda h, b, *_: (b, h)),
            pl.BlockSpec((total, depth), lambda h, b, *_: (0, h)),
            pl.BlockSpec((total, depth), lambda h, b, *_: (0, h)),
        ],
        out_specs=pl.BlockSpec((block, depth), lambda h, b, *_: (b, h)),
    )
    return pl.pallas_call(
        kernel,
        grid_spec=grid_spec,
        out_shape=jax.ShapeDtypeStruct((total, width), jnp.bfloat16),
    )(lists.reshape(-1), live.reshape(-1), query_cols, key_cols, value_cols)


def local(
    query_rows,
    key_rows,
    value_rows,
    hidden_state,
    modulation,
    head_weight,
    latents,
    time_index,
    live_counts,
    block_lists,
):
    seq_count = lax.axis_size("seq")
    own_index = lax.axis_index("seq")
    head_count = live_counts.shape[0]
    per_device = head_count // seq_count
    chunks = CHUNKS if per_device % CHUNKS == 0 else 1
    per_chunk = per_device // chunks
    tokens = query_rows.shape[1]
    width = query_rows.shape[2]
    depth = width // head_count
    chunk_width = per_chunk * depth

    def split(rows):
        return rows[0].reshape(tokens, seq_count, chunks, chunk_width)

    query_split, key_split, value_split = split(query_rows), split(key_rows), split(value_rows)

    def gathered(parts, c):
        send = jnp.transpose(parts[:, :, c, :], (1, 0, 2))
        recv = lax.all_to_all(send, "seq", 0, 0, tiled=True)
        return recv.reshape(seq_count * tokens, chunk_width)

    backs = []
    for c in range(chunks):
        query_cols = gathered(query_split, c)
        key_cols = gathered(key_split, c)
        value_cols = gathered(value_split, c)
        first = own_index * per_device + c * per_chunk
        lists = lax.dynamic_slice_in_dim(block_lists, first, per_chunk, 0)
        live = lax.dynamic_slice_in_dim(live_counts, first, per_chunk, 0)
        attended = attend_heads(query_cols, key_cols, value_cols, lists, live)
        back = lax.all_to_all(
            attended.reshape(seq_count, tokens, chunk_width), "seq", 0, 0, tiled=True
        )
        backs.append(back)
    stacked = jnp.stack(backs)
    mixed_back = jnp.transpose(stacked, (2, 1, 0, 3)).reshape(1, tokens, width)

    source = hidden_state[0].astype(jnp.float32)
    mean_row = jnp.mean(source, axis=1, keepdims=True)
    centred = source - mean_row
    spread = jnp.mean(centred * centred, axis=1, keepdims=True)
    normed = centred * lax.rsqrt(spread + epsilon)
    shaped = (normed * (1.0 + modulation[0, 1]) + modulation[0, 0]).astype(jnp.bfloat16)
    velocity = jnp.dot(shaped, head_weight, preferred_element_type=jnp.float32)
    change = noise_level(time_index[0] - 1) - noise_level(time_index[0])
    moved = latents[0] + change * velocity
    queue_next = passed_along(moved[None], "queue", -1)
    return (mixed_back, queue_next)


def solution(mesh):
    placed = (
        P(("groups", "queue"), "seq", None),
        P(("groups", "queue"), "seq", None),
        P(("groups", "queue"), "seq", None),
        P(("groups", "queue"), "seq", None),
        P(("groups", "queue"), None, None),
        P(),
        P(("groups", "queue"), "seq", None),
        P(("groups", "queue")),
        P(),
        P(),
    )
    return jax.shard_map(
        local,
        mesh=mesh,
        in_specs=placed,
        out_specs=(P(("groups", "queue"), "seq", None), P(("groups", "queue"), "seq", None)),
        check_vma=False,
    )
```

time: 264 us -> 159 us (0.60)
  other arithmetic: 89 us -> 0.91 us
  local copies, waits for them, and re-layouts: 91.5 us -> 22.7 us
  waiting for transfers between devices: 31.5 us -> 72.9 us
  matrix products: 27.7 us -> 0.77 us
  Pallas kernels: 0 us -> 24.7 us
  starting transfers between devices: 21 us -> 33.6 us
    unnamed x7 -> x0, other arithmetic: 77.6 us -> none
    unnamed x40 -> x33, local copies, waits for them, and re-layouts: 51.4 us -> 8.85 us
    all_to_all x4 -> x8, waiting for transfers between devices: 30.1 us -> 71.3 us  [the longest x6 60.5 us: gathered(): recv = lax.all_to_all(send, 'seq', 0, 0, tiled=True)]
    dot_general x8 -> x0, matrix products: 27 us -> none  [the longest x4 17.2 us: advance(): jnp.einsum('bij,bjd->bid', weights.astype(jnp.bfloat16), value_chosen, pr...]
    gather x18 -> x0, local copies, waits for them, and re-layouts: 24.9 us -> none  [the longest x12 12.2 us: advance(): key_chosen = jnp.take(key_blocks, chosen, axis=0)]
    pallas_call x0 -> x2, Pallas kernels: none -> 24.7 us  [attend_heads(): pl.pallas_call(kernel, grid_spec=grid_spec, out_shape=jax.ShapeDtypeStruc...]
    all_to_all x4 -> x8, starting transfers between devices: 20.8 us -> 33.5 us  [the longest x6 24.4 us: gathered(): recv = lax.all_to_all(send, 'seq', 0, 0, tiled=True)]
    all_to_all x4 -> x0, local copies, waits for them, and re-layouts: 6.05 us -> none  [the longest x1 1.61 us: local(): lax.all_to_all(attended[None], 'seq', split_axis=1, concat_axis=2, tiled=...]
  transfers between devices with their start and end apart: 5 -> 9, of which waited for: 3 -> 8; matrix products, arithmetic and copies ran while one was open for 31% -> 9% of each run, Pallas kernels for 0% -> 16%
where the time goes in v1:
time: 159 us; the launch traced here: 157 us
  waiting for transfers between devices  72.9 us (46%)
  starting transfers between devices  33.6 us (21%)
  Pallas kernels  24.7 us (16%)
  local copies, waits for them, and re-layouts  22.7 us (14%)
  between operations  1.6 us (1%)
    all_to_all x6, waiting for transfers between devices, gathered(): recv = lax.all_to_all(send, 'seq', 0, 0, tiled=True)  60.5 us
    pallas_call x2, Pallas kernels, attend_heads(): pl.pallas_call(kernel, grid_spec=grid_spec, out_shape=jax.ShapeDtypeStruc...  24.7 us
    all_to_all x6, starting transfers between devices, gathered(): recv = lax.all_to_all(send, 'seq', 0, 0, tiled=True)  24.4 us
    all_to_all x2, waiting for transfers between devices, local(): lax.all_to_all(attended.reshape(seq_count, tokens, chunk_width), 'seq', 0...  10.8 us
    all_to_all x2, starting transfers between devices, local(): lax.all_to_all(attended.reshape(seq_count, tokens, chunk_width), 'seq', 0...  9.15 us
    unnamed x33, local copies, waits for them, and re-layouts  8.85 us
    slice x3, local copies, waits for them, and re-layouts, gathered(): send = jnp.transpose(parts[:, :, c, :], (1, 0, 2))  4.5 us
    another operation x3, local copies, waits for them, and re-layouts, split(): return rows[0].reshape(tokens, seq_count, chunks, chunk_width)  3.5 us
  transfers between devices with their start and end apart: 9, of which 8 were waited for; matrix products, arithmetic and copies ran while one was open for 9% of the time, Pallas kernels for 16%

profile of v1, /device:TPU:0, one launch (start us, length us, event | category | flops | bytes accessed | tf_op | source)
XLA Modules:
  0.0 157.2 jit_solution(11002751005712694361)
XLA Ops:
  0.6 1.9 %reshape_squeeze.11 = bf16[128,4,2,512]{3,2,1,0:T(2,128)(2,1)S(1)} reshape(bf16[1,128,4096]{2,1,0:T(8,128)(2,1)} %param.12) | data formatting | bytes 2097152 | tf_op jit(solution)/shard_map/reshape;squeeze | solution.py:109
  2.6 1.5 fusion.18
  4.1 1.1 copy.38
  5.2 6.3 %all-to-all-start.2 = ((bf16[4,128,512]{2,1,0:T(8,128)(2,1)}), bf16[4,128,512]{2,1,0:T(8,128)(2,1)S(1)}, u32[]{:S(2)}, u32[]{:S(2)}) async-start(bf16[4,128,512]{2,1,0:T(8,128)(2,1)} %bitcast.70), calls=%async_computation.2 | async-start | bytes 1048576 | tf_op jit(solution)/shard_map/all_to_all | solution.py:115
  12.6 13.4 %all-to-all-done.2 = bf16[4,128,512]{2,1,0:T(8,128)(2,1)S(1)} async-done(((bf16[4,128,512]{2,1,0:T(8,128)(2,1)}), bf16[4,128,512]{2,1,0:T(8,128)(2,1)S(1)}, u32[]{:S(2)}, u32[]{:S(2)}) %all-to-all-start.2) | async-done | bytes 524320 | tf_op jit(solution)/shard_map/all_to_all | solution.py:115
  26.8 3.5 %all-to-all-start.6 = ((bf16[4,128,512]{2,1,0:T(8,128)(2,1)}), bf16[4,128,512]{2,1,0:T(8,128)(2,1)S(1)}, u32[]{:S(2)}, u32[]{:S(2)}) async-start(bf16[4,128,512]{2,1,0:T(8,128)(2,1)} %bitcast.67), calls=%async_computation.6 | async-start | bytes 1048576 | tf_op jit(solution)/shard_map/all_to_all | solution.py:115
  31.1 1.5 fusion.19
  33.7 10.6 %all-to-all-done.6 = bf16[4,128,512]{2,1,0:T(8,128)(2,1)S(1)} async-done(((bf16[4,128,512]{2,1,0:T(8,128)(2,1)}), bf16[4,128,512]{2,1,0:T(8,128)(2,1)S(1)}, u32[]{:S(2)}, u32[]{:S(2)}) %all-to-all-start.6) | async-done | bytes 524320 | tf_op jit(solution)/shard_map/all_to_all | solution.py:115
  44.3 3.5 %all-to-all-start.1 = ((bf16[4,128,512]{2,1,0:T(8,128)(2,1)}), bf16[4,128,512]{2,1,0:T(8,128)(2,1)S(1)}, u32[]{:S(2)}, u32[]{:S(2)}) async-start(bf16[4,128,512]{2,1,0:T(8,128)(2,1)} %bitcast.71), calls=%async_computation.1 | async-start | bytes 1048576 | tf_op jit(solution)/shard_map/all_to_all | solution.py:115
  48.9 12.9 %all-to-all-done.1 = bf16[4,128,512]{2,1,0:T(8,128)(2,1)S(1)} async-done(((bf16[4,128,512]{2,1,0:T(8,128)(2,1)}), bf16[4,128,512]{2,1,0:T(8,128)(2,1)S(1)}, u32[]{:S(2)}, u32[]{:S(2)}) %all-to-all-start.1) | async-done | bytes 524320 | tf_op jit(solution)/shard_map/all_to_all | solution.py:115
  62.6 3.5 %all-to-all-start.5 = ((bf16[4,128,512]{2,1,0:T(8,128)(2,1)}), bf16[4,128,512]{2,1,0:T(8,128)(2,1)S(1)}, u32[]{:S(2)}, u32[]{:S(2)}) async-start(bf16[4,128,512]{2,1,0:T(8,128)(2,1)} %bitcast.68), calls=%async_computation.5 | async-start | bytes 1048576 | tf_op jit(solution)/shard_map/all_to_all | solution.py:115
  66.9 1.5 fusion.20
  69.5 10.6 %all-to-all-done.5 = bf16[4,128,512]{2,1,0:T(8,128)(2,1)S(1)} async-done(((bf16[4,128,512]{2,1,0:T(8,128)(2,1)}), bf16[4,128,512]{2,1,0:T(8,128)(2,1)S(1)}, u32[]{:S(2)}, u32[]{:S(2)}) %all-to-all-start.5) | async-done | bytes 524320 | tf_op jit(solution)/shard_map/all_to_all | solution.py:115
  80.1 4.1 %all-to-all-start = ((bf16[4,128,512]{2,1,0:T(8,128)(2,1)}), bf16[4,128,512]{2,1,0:T(8,128)(2,1)}, u32[]{:S(2)}, u32[]{:S(2)}) async-start(bf16[4,128,512]{2,1,0:T(8,128)(2,1)} %bitcast.72), calls=%async_computation | async-start | bytes 1048576 | tf_op jit(solution)/shard_map/all_to_all | solution.py:115
  85.4 13.0 %all-to-all-done = bf16[4,128,512]{2,1,0:T(8,128)(2,1)} async-done(((bf16[4,128,512]{2,1,0:T(8,128)(2,1)}), bf16[4,128,512]{2,1,0:T(8,128)(2,1)}, u32[]{:S(2)}, u32[]{:S(2)}) %all-to-all-start) | async-done | bytes 524320 | tf_op jit(solution)/shard_map/all_to_all | solution.py:115
  98.4 3.5 %all-to-all-start.4 = ((bf16[4,128,512]{2,1,0:T(8,128)(2,1)}), bf16[4,128,512]{2,1,0:T(8,128)(2,1)S(1)}, u32[]{:S(2)}, u32[]{:S(2)}) async-start(bf16[4,128,512]{2,1,0:T(8,128)(2,1)} %bitcast.69), calls=%async_computation.4 | async-start | bytes 1048576 | tf_op jit(solution)/shard_map/all_to_all | solution.py:115
  105.3 12.4 %shard_map.113 = bf16[512,512]{1,0:T(8,128)(2,1)} custom-call(s32[64]{0:T(128)} %reshape.81.lists_ref, s32[16]{0:T(128)} %reshape.82.live_ref, bf16[512,512]{1,0:T(8,128)(2,1)} %bitcast.2.q_ref, bf16[512,512]{1,0:T(8,128)(2,1)} %bitcast.76, bf16[512,512]{1,0:T(8,128)(2,1)} %bitcast.74), custom_call_target="tpu_custom_call" | custom-call | tf_op jit(solution)/shard_map/pallas_call | solution.py:78
  117.7 5.0 %all-to-all-start.3 = ((bf16[4,128,512]{2,1,0:T(8,128)(2,1)}), bf16[4,128,512]{2,1,0:T(8,128)(2,1)S(1)}, u32[]{:S(2)}, u32[]{:S(2)}) async-start(bf16[4,128,512]{2,1,0:T(8,128)(2,1)} %bitcast.81), calls=%async_computation.3 | async-start | bytes 1048576 | tf_op jit(solution)/shard_map/all_to_all | solution.py:127
  122.8 12.3 %shard_map.114 = bf16[512,512]{1,0:T(8,128)(2,1)} custom-call(s32[64]{0:T(128)} %reshape.87.lists_ref, s32[16]{0:T(128)} %reshape.88.live_ref, bf16[512,512]{1,0:T(8,128)(2,1)} %bitcast.77, bf16[512,512]{1,0:T(8,128)(2,1)} %bitcast.75, bf16[512,512]{1,0:T(8,128)(2,1)} %bitcast.73), custom_call_target="tpu_custom_call" | custom-call | tf_op jit(solution)/shard_map/pallas_call | solution.py:78
  135.1 1.1 all-to-all-done.3
  136.3 4.1 %all-to-all-start.7 = ((bf16[4,128,512]{2,1,0:T(8,128)(2,1)}), bf16[4,128,512]{2,1,0:T(8,128)(2,1)S(1)}, u32[]{:S(2)}, u32[]{:S(2)}) async-start(bf16[4,128,512]{2,1,0:T(8,128)(2,1)} %bitcast.79), calls=%async_computation.7 | async-start | bytes 1048576 | tf_op jit(solution)/shard_map/all_to_all | solution.py:127
  142.5 1.6 %collective-permute-done = f32[1,128,64]{1,2,0:T(8,128)S(1)} collective-permute-done((f32[1,128,64]{1,2,0:T(8,128)S(1)}, f32[1,128,64]{1,2,0:T(8,128)S(1)}, u32[]{:S(2)}, u32[]{:S(2)}) %collective-permute-start) | collective-permute-done | bytes 32800 | tf_op jit(solution)/shard_map/ppermute | solution.py:21
  144.1 9.7 %all-to-all-done.7 = bf16[4,128,512]{2,1,0:T(8,128)(2,1)S(1)} async-done(((bf16[4,128,512]{2,1,0:T(8,128)(2,1)}), bf16[4,128,512]{2,1,0:T(8,128)(2,1)S(1)}, u32[]{:S(2)}, u32[]{:S(2)}) %all-to-all-start.7) | async-done | bytes 524320 | tf_op jit(solution)/shard_map/all_to_all | solution.py:127
  154.9 1.6 %reshape.93 = bf16[1,128,4096]{2,1,0:T(8,128)(2,1)} reshape(bf16[128,4,2,512]{3,2,1,0:T(2,128)(2,1)S(1)} %copy.22) | data formatting | bytes 2097152 | tf_op jit(solution)/shard_map/reshape | solution.py:132
  (54 shorter events, 15.3 us)
Async XLA Ops:
  0.6 141.0 %copy-start = (bf16[5120,64]{0,1:T(8,128)(2,1)S(1)}, bf16[5120,64]{0,1:T(8,128)(2,1)}, u32[]{:S(2)}) copy-start(bf16[5120,64]{0,1:T(8,128)(2,1)} %param.15) | copy-start | bytes 1966084
  5.2 20.8 %all-to-all-start.2 = ((bf16[4,128,512]{2,1,0:T(8,128)(2,1)}), bf16[4,128,512]{2,1,0:T(8,128)(2,1)S(1)}, u32[]{:S(2)}, u32[]{:S(2)}) async-start(bf16[4,128,512]{2,1,0:T(8,128)(2,1)} %bitcast.70), calls=%async_computation.2 | async-start | bytes 1048576 | tf_op jit(solution)/shard_map/all_to_all | solution.py:115
  12.6 17.7 %copy-start.7 = (bf16[1,128,4096]{2,1,0:T(8,128)(2,1)S(1)}, bf16[1,128,4096]{2,1,0:T(8,128)(2,1)}, u32[]{:S(2)}) copy-start(bf16[1,128,4096]{2,1,0:T(8,128)(2,1)} %param.11) | copy-start | bytes 3145732
  26.0 0.8 copy-start.3
  26.8 17.5 %all-to-all-start.6 = ((bf16[4,128,512]{2,1,0:T(8,128)(2,1)}), bf16[4,128,512]{2,1,0:T(8,128)(2,1)S(1)}, u32[]{:S(2)}, u32[]{:S(2)}) async-start(bf16[4,128,512]{2,1,0:T(8,128)(2,1)} %bitcast.67), calls=%async_computation.6 | async-start | bytes 1048576 | tf_op jit(solution)/shard_map/all_to_all | solution.py:115
  44.3 4.6 %copy-start.2 = (bf16[4,128,512]{2,1,0:T(8,128)(2,1)}, bf16[4,128,512]{2,1,0:T(8,128)(2,1)S(1)}, u32[]{:S(2)}) copy-start(bf16[4,128,512]{2,1,0:T(8,128)(2,1)S(1)} %all-to-all-done.6) | copy-start | bytes 1572868
  44.3 17.5 %all-to-all-start.1 = ((bf16[4,128,512]{2,1,0:T(8,128)(2,1)}), bf16[4,128,512]{2,1,0:T(8,128)(2,1)S(1)}, u32[]{:S(2)}, u32[]{:S(2)}) async-start(bf16[4,128,512]{2,1,0:T(8,128)(2,1)} %bitcast.71), calls=%async_computation.1 | async-start | bytes 1048576 | tf_op jit(solution)/shard_map/all_to_all | solution.py:115
  48.9 17.2 %copy-start.8 = (bf16[1,128,4096]{2,1,0:T(8,128)(2,1)S(1)}, bf16[1,128,4096]{2,1,0:T(8,128)(2,1)}, u32[]{:S(2)}) copy-start(bf16[1,128,4096]{2,1,0:T(8,128)(2,1)} %param.10) | copy-start | bytes 3145732
  61.8 0.8 copy-start.5
  62.6 17.5 %all-to-all-start.5 = ((bf16[4,128,512]{2,1,0:T(8,128)(2,1)}), bf16[4,128,512]{2,1,0:T(8,128)(2,1)S(1)}, u32[]{:S(2)}, u32[]{:S(2)}) async-start(bf16[4,128,512]{2,1,0:T(8,128)(2,1)} %bitcast.68), calls=%async_computation.5 | async-start | bytes 1048576 | tf_op jit(solution)/shard_map/all_to_all | solution.py:115
  80.1 5.3 %copy-start.4 = (bf16[4,128,512]{2,1,0:T(8,128)(2,1)}, bf16[4,128,512]{2,1,0:T(8,128)(2,1)S(1)}, u32[]{:S(2)}) copy-start(bf16[4,128,512]{2,1,0:T(8,128)(2,1)S(1)} %all-to-all-done.5) | copy-start | bytes 1572868
  80.1 18.3 %all-to-all-start = ((bf16[4,128,512]{2,1,0:T(8,128)(2,1)}), bf16[4,128,512]{2,1,0:T(8,128)(2,1)}, u32[]{:S(2)}, u32[]{:S(2)}) async-start(bf16[4,128,512]{2,1,0:T(8,128)(2,1)} %bitcast.72), calls=%async_computation | async-start | bytes 1048576 | tf_op jit(solution)/shard_map/all_to_all | solution.py:115
  84.3 17.6 %copy-start.11 = (s32[32,4]{0,1:T(4,128)S(1)}, s32[32,4]{0,1:T(4,128)}, u32[]{:S(2)}) copy-start(s32[32,4]{0,1:T(4,128)} %param.18) | copy-start | bytes 1540
  84.3 19.1 %copy-start.10 = (s32[32,4,4]{0,2,1:T(4,128)S(1)}, s32[32,4,4]{0,2,1:T(4,128)}, u32[]{:S(2)}) copy-start(s32[32,4,4]{0,2,1:T(4,128)} %param.19) | copy-start | bytes 6148
  84.3 20.7 %copy-start.1 = (bf16[1,128,5120]{2,1,0:T(8,128)(2,1)S(1)}, bf16[1,128,5120]{2,1,0:T(8,128)(2,1)}, u32[]{:S(2)}) copy-start(bf16[1,128,5120]{2,1,0:T(8,128)(2,1)} %param.13) | copy-start | bytes 3932164
  98.4 19.4 %all-to-all-start.4 = ((bf16[4,128,512]{2,1,0:T(8,128)(2,1)}), bf16[4,128,512]{2,1,0:T(8,128)(2,1)S(1)}, u32[]{:S(2)}, u32[]{:S(2)}) async-start(bf16[4,128,512]{2,1,0:T(8,128)(2,1)} %bitcast.69), calls=%async_computation.4 | async-start | bytes 1048576 | tf_op jit(solution)/shard_map/all_to_all | solution.py:115
  105.3 17.5 %copy-start.9 = (f32[1,2,5120]{2,1,0:T(2,128)S(1)}, f32[1,2,5120]{2,1,0:T(2,128)}, u32[]{:S(2)}) copy-start(f32[1,2,5120]{2,1,0:T(2,128)} %param.14) | copy-start | bytes 122884
  117.7 5.1 %copy-start.6 = (bf16[4,128,512]{2,1,0:T(8,128)(2,1)}, bf16[4,128,512]{2,1,0:T(8,128)(2,1)S(1)}, u32[]{:S(2)}) copy-start(bf16[4,128,512]{2,1,0:T(8,128)(2,1)S(1)} %all-to-all-done.4) | copy-start | bytes 1572868
  117.7 18.5 %all-to-all-start.3 = ((bf16[4,128,512]{2,1,0:T(8,128)(2,1)}), bf16[4,128,512]{2,1,0:T(8,128)(2,1)S(1)}, u32[]{:S(2)}, u32[]{:S(2)}) async-start(bf16[4,128,512]{2,1,0:T(8,128)(2,1)} %bitcast.81), calls=%async_computation.3 | async-start | bytes 1048576 | tf_op jit(solution)/shard_map/all_to_all | solution.py:127
  135.1 6.5 %copy-start.12 = (f32[1,128,64]{1,2,0:T(8,128)S(1)}, f32[1,128,64]{1,2,0:T(8,128)}, u32[]{:S(2)}) copy-start(f32[1,128,64]{1,2,0:T(8,128)} %param.16) | copy-start | bytes 98308
  136.3 17.5 %all-to-all-start.7 = ((bf16[4,128,512]{2,1,0:T(8,128)(2,1)}), bf16[4,128,512]{2,1,0:T(8,128)(2,1)S(1)}, u32[]{:S(2)}, u32[]{:S(2)}) async-start(bf16[4,128,512]{2,1,0:T(8,128)(2,1)} %bitcast.79), calls=%async_computation.7 | async-start | bytes 1048576 | tf_op jit(solution)/shard_map/all_to_all | solution.py:127
  142.4 1.7 %collective-permute-start = (f32[1,128,64]{1,2,0:T(8,128)S(1)}, f32[1,128,64]{1,2,0:T(8,128)S(1)}, u32[]{:S(2)}, u32[]{:S(2)}) collective-permute-start(f32[1,128,64]{1,2,0:T(8,128)S(1)} %fusion.15), channel_id=1, source_target_pairs={{0,3},{1,0},{2,1},{3,2},{4,7},{5,4},{6,5},{7,6},{8,11},{9,8},{10,9... | collective-permute-start | bytes 98312 | tf_op jit(solution)/shard_map/ppermute | solution.py:21

commit v2 on v1

v2 whole, which is shorter than its diff:
```python
import functools

import jax
import jax.numpy as jnp
from jax import lax
from jax.experimental import pallas as pl
from jax.experimental.pallas import tpu as pltpu
from jax.sharding import PartitionSpec as P

STEPS = 8
CHUNKS = 2


epsilon = 1e-06
plan_shift = 5.0


def passed_along(value, axis, steps):
    count = lax.axis_size(axis)
    pairs = [(source, (source + steps) % count) for source in range(count)]
    return lax.ppermute(value, axis, pairs)


def noise_level(step_value):
    fraction = step_value.astype(jnp.float32) / STEPS
    return plan_shift * fraction / (1.0 + (plan_shift - 1.0) * fraction)


def attend_kernel(lists_ref, live_ref, x_ref, o_ref, *, block, slots, qblocks, heads, depth):
    sources, _, tokens, _ = x_ref.shape
    total = sources * tokens
    scale = depth ** (-0.5)
    column = lax.broadcasted_iota(jnp.int32, (1, total), 1)
    per_source = tokens // block
    for head in range(heads):
        cols = slice(head * depth, (head + 1) * depth)
        keys = x_ref[:, 1, :, cols].reshape(total, depth)
        values = x_ref[:, 2, :, cols].reshape(total, depth)

        def body(qblock, carry):
            source = qblock // per_source
            first = pl.multiple_of((qblock % per_source) * block, block)
            query = x_ref[source, 0, pl.ds(first, block), cols]
            scores = (
                lax.dot_general(
                    query, keys, (((1,), (1,)), ((), ())), preferred_element_type=jnp.float32
                )
                * scale
            )
            live = live_ref[head * qblocks + qblock]
            active = column < 0
            for slot in range(slots):
                low = lists_ref[(head * qblocks + qblock) * slots + slot] * block
                active = active | ((column >= low) & (column < low + block) & (slot < live))
            scores = jnp.where(active, scores, -jnp.inf)
            highest = jnp.max(scores, axis=1, keepdims=True)
            weights = jnp.exp(scores - highest)
            totals = jnp.sum(weights, axis=1, keepdims=True)
            mixed = jnp.dot(
                weights.astype(jnp.bfloat16), values, preferred_element_type=jnp.float32
            )
            o_ref[source, pl.ds(first, block), cols] = (mixed / totals).astype(o_ref.dtype)
            return carry

        lax.fori_loop(0, qblocks, body, 0)


def attend_heads(packed, lists, live):
    sources, _, tokens, width = packed.shape
    head_total, qblocks = live.shape
    slots = lists.shape[2]
    depth = width // head_total
    block = sources * tokens // qblocks
    kernel = functools.partial(
        attend_kernel, block=block, slots=slots, qblocks=qblocks, heads=head_total, depth=depth
    )
    smem = pltpu.SMEM
    return pl.pallas_call(
        kernel,
        in_specs=[
            pl.BlockSpec(memory_space=smem),
            pl.BlockSpec(memory_space=smem),
            pl.BlockSpec(memory_space=pltpu.VMEM),
        ],
        out_specs=pl.BlockSpec(memory_space=pltpu.VMEM),
        out_shape=jax.ShapeDtypeStruct((sources, tokens, width), jnp.bfloat16),
    )(lists.reshape(-1), live.reshape(-1), packed)


def pack_kernel(query_hbm, key_hbm, value_hbm, out_hbm, sems, *, seq, stride, offset, width):
    copies = []
    for group in range(seq):
        for kind, source in enumerate((query_hbm, key_hbm, value_hbm)):
            copy = pltpu.make_async_copy(
                source.at[0, :, pl.ds(group * stride + offset, width)],
                out_hbm.at[group, kind],
                sems.at[group * 3 + kind],
            )
            copy.start()
            copies.append(copy)
    for copy in copies:
        copy.wait()


def packed_chunk(query_rows, key_rows, value_rows, seq, stride, offset, width):
    tokens = query_rows.shape[1]
    kernel = functools.partial(pack_kernel, seq=seq, stride=stride, offset=offset, width=width)
    return pl.pallas_call(
        kernel,
        in_specs=[pl.BlockSpec(memory_space=pl.ANY)] * 3,
        out_specs=pl.BlockSpec(memory_space=pl.ANY),
        out_shape=jax.ShapeDtypeStruct((seq, 3, tokens, width), query_rows.dtype),
        scratch_shapes=[pltpu.SemaphoreType.DMA((seq * 3,))],
    )(query_rows, key_rows, value_rows)


def unpack_kernel(*refs, seq, stride, width):
    chunks = len(refs) - 2
    out_hbm, sems = refs[chunks], refs[chunks + 1]
    copies = []
    for c in range(chunks):
        for group in range(seq):
            copy = pltpu.make_async_copy(
                refs[c].at[group],
                out_hbm.at[0, :, pl.ds(group * stride + c * width, width)],
                sems.at[c * seq + group],
            )
            copy.start()
            copies.append(copy)
    for copy in copies:
        copy.wait()


def unpacked(backs, seq, stride, width):
    tokens = backs[0].shape[1]
    kernel = functools.partial(unpack_kernel, seq=seq, stride=stride, width=width)
    return pl.pallas_call(
        kernel,
        in_specs=[pl.BlockSpec(memory_space=pl.ANY)] * len(backs),
        out_specs=pl.BlockSpec(memory_space=pl.ANY),
        out_shape=jax.ShapeDtypeStruct((1, tokens, seq * stride), backs[0].dtype),
        scratch_shapes=[pltpu.SemaphoreType.DMA((seq * len(backs),))],
    )(*backs)


def local(
    query_rows,
    key_rows,
    value_rows,
    hidden_state,
    modulation,
    head_weight,
    latents,
    time_index,
    live_counts,
    block_lists,
):
    seq_count = lax.axis_size("seq")
    own_index = lax.axis_index("seq")
    head_count = live_counts.shape[0]
    per_device = head_count // seq_count
    chunks = CHUNKS if per_device % CHUNKS == 0 else 1
    per_chunk = per_device // chunks
    tokens = query_rows.shape[1]
    width = query_rows.shape[2]
    depth = width // head_count
    chunk_width = per_chunk * depth

    backs = []
    for c in range(chunks):
        send = packed_chunk(
            query_rows, key_rows, value_rows, seq_count, per_device * depth, c * chunk_width, chunk_width
        )
        packed = lax.all_to_all(send, "seq", 0, 0, tiled=True)
        first = own_index * per_device + c * per_chunk
        lists = lax.dynamic_slice_in_dim(block_lists, first, per_chunk, 0)
        live = lax.dynamic_slice_in_dim(live_counts, first, per_chunk, 0)
        attended = attend_heads(packed, lists, live)
        back = lax.all_to_all(attended, "seq", 0, 0, tiled=True)
        backs.append(back)
    mixed_back = unpacked(backs, seq_count, per_device * depth, chunk_width)

    source = hidden_state[0].astype(jnp.float32)
    mean_row = jnp.mean(source, axis=1, keepdims=True)
    centred = source - mean_row
    spread = jnp.mean(centred * centred, axis=1, keepdims=True)
    normed = centred * lax.rsqrt(spread + epsilon)
    shaped = (normed * (1.0 + modulation[0, 1]) + modulation[0, 0]).astype(jnp.bfloat16)
    velocity = jnp.dot(shaped, head_weight, preferred_element_type=jnp.float32)
    change = noise_level(time_index[0] - 1) - noise_level(time_index[0])
    moved = latents[0] + change * velocity
    queue_next = passed_along(moved[None], "queue", -1)
    return (mixed_back, queue_next)


def solution(mesh):
    placed = (
        P(("groups", "queue"), "seq", None),
        P(("groups", "queue"), "seq", None),
        P(("groups", "queue"), "seq", None),
        P(("groups", "queue"), "seq", None),
        P(("groups", "queue"), None, None),
        P(),
        P(("groups", "queue"), "seq", None),
        P(("groups", "queue")),
        P(),
        P(),
    )
    return jax.shard_map(
        local,
        mesh=mesh,
        in_specs=placed,
        out_specs=(P(("groups", "queue"), "seq", None), P(("groups", "queue"), "seq", None)),
        check_vma=False,
    )
```

time: 159 us -> 218 us (1.37)
  Pallas kernels: 24.7 us -> 149 us
  waiting for transfers between devices: 72.9 us -> 36.2 us
  starting transfers between devices: 33.6 us -> 19.3 us
  local copies, waits for them, and re-layouts: 22.7 us -> 8.9 us
    pallas_call x2 -> x5, Pallas kernels: 24.7 us -> 149 us  [the longest x2 97.7 us: packed_chunk(): pl.pallas_call(kernel, in_specs=[pl.BlockSpec(memory_space=pl.ANY)] * 3,...]
    all_to_all x8 -> x4, waiting for transfers between devices: 71.3 us -> 34.6 us  [the longest x2 20.9 us: local(): packed = lax.all_to_all(send, 'seq', 0, 0, tiled=True)]
    all_to_all x8 -> x4, starting transfers between devices: 33.5 us -> 19.1 us  [the longest x2 11.4 us: local(): packed = lax.all_to_all(send, 'seq', 0, 0, tiled=True)]
    unnamed x33 -> x19, local copies, waits for them, and re-layouts: 8.85 us -> 2.57 us
    slice x3 -> x0, local copies, waits for them, and re-layouts: 4.5 us -> none  [gathered(): send = jnp.transpose(parts[:, :, c, :], (1, 0, 2))]
    another operation x3 -> x0, local copies, waits for them, and re-layouts: 3.5 us -> none  [split(): return rows[0].reshape(tokens, seq_count, chunks, chunk_width)]
  transfers between devices with their start and end apart: 9 -> 5, of which waited for: 8 -> 4; matrix products, arithmetic and copies ran while one was open for 9% -> 4% of each run, Pallas kernels for 16% -> 31%
where the time goes in v2:
time: 218 us; the launch traced here: 217 us
  Pallas kernels  149 us (68%)
  waiting for transfers between devices  36.2 us (17%)
  starting transfers between devices  19.3 us (9%)
  local copies, waits for them, and re-layouts  8.9 us (4%)
  other arithmetic  2.29 us (1%)
    pallas_call x2, Pallas kernels, packed_chunk(): pl.pallas_call(kernel, in_specs=[pl.BlockSpec(memory_space=pl.ANY)] * 3,...  97.7 us
    pallas_call x1, Pallas kernels, unpacked(): pl.pallas_call(kernel, in_specs=[pl.BlockSpec(memory_space=pl.ANY)] * len...  32.9 us
    all_to_all x2, waiting for transfers between devices, local(): packed = lax.all_to_all(send, 'seq', 0, 0, tiled=True)  20.9 us
    pallas_call x2, Pallas kernels, attend_heads(): pl.pallas_call(kernel, in_specs=[pl.BlockSpec(memory_space=smem), pl.Bloc...  17.9 us
    all_to_all x2, waiting for transfers between devices, local(): back = lax.all_to_all(attended, 'seq', 0, 0, tiled=True)  13.8 us
    all_to_all x2, starting transfers between devices, local(): packed = lax.all_to_all(send, 'seq', 0, 0, tiled=True)  11.4 us
    all_to_all x2, starting transfers between devices, local(): back = lax.all_to_all(attended, 'seq', 0, 0, tiled=True)  7.6 us
  transfers between devices with their start and end apart: 5, of which 4 were waited for; matrix products, arithmetic and copies ran while one was open for 4% of the time, Pallas kernels for 31%

profile of v2, /device:TPU:0, one launch (start us, length us, event | category | flops | bytes accessed | tf_op | source)
XLA Modules:
  0.0 217.5 jit_solution(2918648829614016077)
XLA Ops:
  0.6 48.9 %shard_map.115 = bf16[4,3,128,512]{3,2,1,0:T(8,128)(2,1)} custom-call(bf16[1,128,4096]{2,1,0:T(8,128)(2,1)} %query_hbm.3, bf16[1,128,4096]{2,1,0:T(8,128)(2,1)} %key_hbm.3, bf16[1,128,4096]{2,1,0:T(8,128)(2,1)} %value_hbm.3), custom_call_target="tpu_custom_call" | custom-call | tf_op jit(solution)/shard_map/pallas_call | solution.py:108
  49.5 6.4 %all-to-all-start.2 = ((bf16[4,3,128,512]{3,2,1,0:T(8,128)(2,1)}), bf16[4,3,128,512]{3,2,1,0:T(8,128)(2,1)S(1)}, u32[]{:S(2)}, u32[]{:S(2)}) async-start(bf16[4,3,128,512]{3,2,1,0:T(8,128)(2,1)} %shard_map.115), calls=%async_computation.2 | async-start | bytes 3145728 | tf_op jit(solution)/shard_map/all_to_all | solution.py:174
  55.9 48.9 %shard_map.113 = bf16[4,3,128,512]{3,2,1,0:T(8,128)(2,1)} custom-call(bf16[1,128,4096]{2,1,0:T(8,128)(2,1)} %query_hbm.3, bf16[1,128,4096]{2,1,0:T(8,128)(2,1)} %key_hbm.3, bf16[1,128,4096]{2,1,0:T(8,128)(2,1)} %value_hbm.3), custom_call_target="tpu_custom_call" | custom-call | tf_op jit(solution)/shard_map/pallas_call | solution.py:108
  104.8 1.1 copy-done.2
  105.9 5.1 %all-to-all-start = ((bf16[4,3,128,512]{3,2,1,0:T(8,128)(2,1)}), bf16[4,3,128,512]{3,2,1,0:T(8,128)(2,1)S(1)}, u32[]{:S(2)}, u32[]{:S(2)}) async-start(bf16[4,3,128,512]{3,2,1,0:T(8,128)(2,1)} %shard_map.113), calls=%async_computation | async-start | bytes 3145728 | tf_op jit(solution)/shard_map/all_to_all | solution.py:174
  111.0 0.7 constant_dynamic-slice_fusion.1
  111.7 0.8 copy.14
  113.1 1.4 constant_dynamic-slice_fusion
  114.6 0.6 reshape.57.live_ref
  115.3 0.6 reshape.54.lists_ref
  115.9 0.8 copy.13
  116.7 0.6 reshape.55.live_ref
  117.6 8.9 %shard_map.116 = bf16[4,128,512]{2,1,0:T(8,128)(2,1)} custom-call(s32[64]{0:T(128)} %reshape.56.lists_ref, s32[16]{0:T(128)} %reshape.57.live_ref, bf16[4,3,128,512]{3,2,1,0:T(8,128)(2,1)} %copy-done.2), custom_call_target="tpu_custom_call" | custom-call | tf_op jit(solution)/shard_map/pallas_call | solution.py:78
  126.5 20.9 %all-to-all-done.x_ref = bf16[4,3,128,512]{3,2,1,0:T(8,128)(2,1)S(1)} async-done(((bf16[4,3,128,512]{3,2,1,0:T(8,128)(2,1)}), bf16[4,3,128,512]{3,2,1,0:T(8,128)(2,1)S(1)}, u32[]{:S(2)}, u32[]{:S(2)}) %all-to-all-start) | async-done | bytes 1572896 | tf_op jit(solution)/shard_map/all_to_all | solution.py:174
  147.4 4.1 %all-to-all-start.3 = ((bf16[4,128,512]{2,1,0:T(8,128)(2,1)}), bf16[4,128,512]{2,1,0:T(8,128)(2,1)}, u32[]{:S(2)}, u32[]{:S(2)}) async-start(bf16[4,128,512]{2,1,0:T(8,128)(2,1)} %shard_map.116), calls=%async_computation.3 | async-start | bytes 1048576 | tf_op jit(solution)/shard_map/all_to_all | solution.py:179
  151.5 1.5 slice_add_fusion
  153.0 8.9 %shard_map.114 = bf16[4,128,512]{2,1,0:T(8,128)(2,1)} custom-call(s32[64]{0:T(128)} %reshape.54.lists_ref, s32[16]{0:T(128)} %reshape.55.live_ref, bf16[4,3,128,512]{3,2,1,0:T(8,128)(2,1)} %copy-done.1), custom_call_target="tpu_custom_call" | custom-call | tf_op jit(solution)/shard_map/pallas_call | solution.py:78
  162.0 3.7 %all-to-all-done.3.refs_1_ = bf16[4,128,512]{2,1,0:T(8,128)(2,1)} async-done(((bf16[4,128,512]{2,1,0:T(8,128)(2,1)}), bf16[4,128,512]{2,1,0:T(8,128)(2,1)}, u32[]{:S(2)}, u32[]{:S(2)}) %all-to-all-start.3) | async-done | bytes 524320 | tf_op jit(solution)/shard_map/all_to_all | solution.py:179
  165.6 3.5 %all-to-all-start.1 = ((bf16[4,128,512]{2,1,0:T(8,128)(2,1)}), bf16[4,128,512]{2,1,0:T(8,128)(2,1)S(1)}, u32[]{:S(2)}, u32[]{:S(2)}) async-start(bf16[4,128,512]{2,1,0:T(8,128)(2,1)} %shard_map.114), calls=%async_computation.1 | async-start | bytes 1048576 | tf_op jit(solution)/shard_map/all_to_all | solution.py:179
  170.4 0.8 fusion.15
  171.4 1.6 collective-permute-done
  173.0 10.1 %all-to-all-done.1.refs_0_ = bf16[4,128,512]{2,1,0:T(8,128)(2,1)S(1)} async-done(((bf16[4,128,512]{2,1,0:T(8,128)(2,1)}), bf16[4,128,512]{2,1,0:T(8,128)(2,1)S(1)}, u32[]{:S(2)}, u32[]{:S(2)}) %all-to-all-start.1) | async-done | bytes 524320 | tf_op jit(solution)/shard_map/all_to_all | solution.py:179
  183.1 0.8 copy-done.4
  183.9 32.9 %shard_map.117 = bf16[1,128,4096]{2,1,0:T(8,128)(2,1)} custom-call(bf16[4,128,512]{2,1,0:T(8,128)(2,1)} %copy-done.4, bf16[4,128,512]{2,1,0:T(8,128)(2,1)} %all-to-all-done.3.refs_1_), custom_call_target="tpu_custom_call" | custom-call | tf_op jit(solution)/shard_map/pallas_call | solution.py:137
  (26 shorter events, 2.5 us)
Async XLA Ops:
  0.6 169.7 %copy-start = (bf16[5120,64]{0,1:T(8,128)(2,1)S(1)}, bf16[5120,64]{0,1:T(8,128)(2,1)}, u32[]{:S(2)}) copy-start(bf16[5120,64]{0,1:T(8,128)(2,1)} %param.15) | copy-start | bytes 1966084
  49.5 55.2 %all-to-all-start.2 = ((bf16[4,3,128,512]{3,2,1,0:T(8,128)(2,1)}), bf16[4,3,128,512]{3,2,1,0:T(8,128)(2,1)S(1)}, u32[]{:S(2)}, u32[]{:S(2)}) async-start(bf16[4,3,128,512]{3,2,1,0:T(8,128)(2,1)} %shard_map.115), calls=%async_computation.2 | async-start | bytes 3145728 | tf_op jit(solution)/shard_map/all_to_all | solution.py:174
  104.7 6.3 %copy-start.5 = (s32[32,4,4]{0,2,1:T(4,128)S(1)}, s32[32,4,4]{0,2,1:T(4,128)}, u32[]{:S(2)}) copy-start(s32[32,4,4]{0,2,1:T(4,128)} %param.19) | copy-start | bytes 6148
  104.7 12.6 %copy-start.3 = (bf16[1,128,5120]{2,1,0:T(8,128)(2,1)S(1)}, bf16[1,128,5120]{2,1,0:T(8,128)(2,1)}, u32[]{:S(2)}) copy-start(bf16[1,128,5120]{2,1,0:T(8,128)(2,1)} %param.13) | copy-start | bytes 3932164
  104.8 1.1 copy-start.2
  105.9 41.5 %all-to-all-start = ((bf16[4,3,128,512]{3,2,1,0:T(8,128)(2,1)}), bf16[4,3,128,512]{3,2,1,0:T(8,128)(2,1)S(1)}, u32[]{:S(2)}, u32[]{:S(2)}) async-start(bf16[4,3,128,512]{3,2,1,0:T(8,128)(2,1)} %shard_map.113), calls=%async_computation | async-start | bytes 3145728 | tf_op jit(solution)/shard_map/all_to_all | solution.py:174
  147.4 5.7 %copy-start.1 = (bf16[4,3,128,512]{3,2,1,0:T(8,128)(2,1)}, bf16[4,3,128,512]{3,2,1,0:T(8,128)(2,1)S(1)}, u32[]{:S(2)}) copy-start(bf16[4,3,128,512]{3,2,1,0:T(8,128)(2,1)S(1)} %all-to-all-done.x_ref) | copy-start | bytes 4718596
  147.4 18.2 %all-to-all-start.3 = ((bf16[4,128,512]{2,1,0:T(8,128)(2,1)}), bf16[4,128,512]{2,1,0:T(8,128)(2,1)}, u32[]{:S(2)}, u32[]{:S(2)}) async-start(bf16[4,128,512]{2,1,0:T(8,128)(2,1)} %shard_map.116), calls=%async_computation.3 | async-start | bytes 1048576 | tf_op jit(solution)/shard_map/all_to_all | solution.py:179
  162.0 8.4 %copy-start.6 = (f32[1,1,5120]{2,1,0:T(1,128)S(1)}, f32[1,1,5120]{2,1,0:T(1,128)}, u32[]{:S(2)}) copy-start(f32[1,1,5120]{2,1,0:T(1,128)} %get-tuple-element.2) | copy-start | bytes 61444
  162.0 8.4 %copy-start.7 = (f32[1,1,5120]{2,1,0:T(1,128)S(1)}, f32[1,1,5120]{2,1,0:T(1,128)}, u32[]{:S(2)}) copy-start(f32[1,1,5120]{2,1,0:T(1,128)} %get-tuple-element.3) | copy-start | bytes 61444
  162.0 8.4 %copy-start.8 = (f32[1,128,64]{1,2,0:T(8,128)S(1)}, f32[1,128,64]{1,2,0:T(8,128)}, u32[]{:S(2)}) copy-start(f32[1,128,64]{1,2,0:T(8,128)} %param.16) | copy-start | bytes 98308
  165.6 17.5 %all-to-all-start.1 = ((bf16[4,128,512]{2,1,0:T(8,128)(2,1)}), bf16[4,128,512]{2,1,0:T(8,128)(2,1)S(1)}, u32[]{:S(2)}, u32[]{:S(2)}) async-start(bf16[4,128,512]{2,1,0:T(8,128)(2,1)} %shard_map.114), calls=%async_computation.1 | async-start | bytes 1048576 | tf_op jit(solution)/shard_map/all_to_all | solution.py:179
  171.2 1.9 collective-permute-start
  183.1 0.8 copy-start.4

commit v3 on v2

--- a/solution.py
+++ b/solution.py
@@ -87,19 +87,11 @@
     )(lists.reshape(-1), live.reshape(-1), packed)
 
 
-def pack_kernel(query_hbm, key_hbm, value_hbm, out_hbm, sems, *, seq, stride, offset, width):
-    copies = []
+def pack_kernel(query_ref, key_ref, value_ref, out_ref, *, seq, stride, offset, width):
     for group in range(seq):
-        for kind, source in enumerate((query_hbm, key_hbm, value_hbm)):
-            copy = pltpu.make_async_copy(
-                source.at[0, :, pl.ds(group * stride + offset, width)],
-                out_hbm.at[group, kind],
-                sems.at[group * 3 + kind],
-            )
-            copy.start()
-            copies.append(copy)
-    for copy in copies:
-        copy.wait()
+        cols = slice(group * stride + offset, group * stride + offset + width)
+        for kind, source in enumerate((query_ref, key_ref, value_ref)):
+            out_ref[group, kind] = source[0, :, cols]
 
 
 def packed_chunk(query_rows, key_rows, value_rows, seq, stride, offset, width):
@@ -107,28 +99,19 @@
     kernel = functools.partial(pack_kernel, seq=seq, stride=stride, offset=offset, width=width)
     return pl.pallas_call(
         kernel,
-        in_specs=[pl.BlockSpec(memory_space=pl.ANY)] * 3,
-        out_specs=pl.BlockSpec(memory_space=pl.ANY),
+        in_specs=[pl.BlockSpec(memory_space=pltpu.VMEM)] * 3,
+        out_specs=pl.BlockSpec(memory_space=pltpu.VMEM),
         out_shape=jax.ShapeDtypeStruct((seq, 3, tokens, width), query_rows.dtype),
-        scratch_shapes=[pltpu.SemaphoreType.DMA((seq * 3,))],
     )(query_rows, key_rows, value_rows)
 
 
 def unpack_kernel(*refs, seq, stride, width):
-    chunks = len(refs) - 2
-    out_hbm, sems = refs[chunks], refs[chunks + 1]
-    copies = []
+    chunks = len(refs) - 1
+    out_ref = refs[chunks]
     for c in range(chunks):
         for group in range(seq):
-            copy = pltpu.make_async_copy(
-                refs[c].at[group],
-                out_hbm.at[0, :, pl.ds(group * stride + c * width, width)],
-                sems.at[c * seq + group],
-            )
-            copy.start()
-            copies.append(copy)
-    for copy in copies:
-        copy.wait()
+            low = group * stride + c * width
+            out_ref[0, :, low:low + width] = refs[c][group]
 
 
 def unpacked(backs, seq, stride, width):
@@ -136,10 +119,9 @@
     kernel = functools.partial(unpack_kernel, seq=seq, stride=stride, width=width)
     return pl.pallas_call(
         kernel,
-        in_specs=[pl.BlockSpec(memory_space=pl.ANY)] * len(backs),
-        out_specs=pl.BlockSpec(memory_space=pl.ANY),
+        in_specs=[pl.BlockSpec(memory_space=pltpu.VMEM)] * len(backs),
+        out_specs=pl.BlockSpec(memory_space=pltpu.VMEM),
         out_shape=jax.ShapeDtypeStruct((1, tokens, seq * stride), backs[0].dtype),
-        scratch_shapes=[pltpu.SemaphoreType.DMA((seq * len(backs),))],
     )(*backs)
 
 

time: 218 us -> 128 us (0.59)
  Pallas kernels: 149 us -> 26.4 us
  waiting for transfers between devices: 36.2 us -> 70.1 us
    pallas_call x3, Pallas kernels: 131 us -> 8.57 us  [the longest x2 6.32 us: packed_chunk(): pl.pallas_call(kernel, in_specs=[pl.BlockSpec(memory_space=pltpu.VMEM)] *...]
    all_to_all x2, waiting for transfers between devices: 20.9 us -> 54.7 us  [local(): packed = lax.all_to_all(send, 'seq', 0, 0, tiled=True)]
  transfers between devices with their start and end apart: 5 -> 5, of which waited for: 4 -> 5; matrix products, arithmetic and copies ran while one was open for 4% -> 7% of each run, Pallas kernels for 31% -> 16%
where the time goes in v3:
time: 128 us
  waiting for transfers between devices  70.1 us (55%)
  Pallas kernels  26.4 us (21%)
  starting transfers between devices  17.8 us (14%)
  local copies, waits for them, and re-layouts  8.9 us (7%)
  other arithmetic  2.29 us (2%)
  between operations  1.47 us (1%)
    all_to_all x2, waiting for transfers between devices, local(): packed = lax.all_to_all(send, 'seq', 0, 0, tiled=True)  54.7 us
    pallas_call x2, Pallas kernels, attend_heads(): pl.pallas_call(kernel, in_specs=[pl.BlockSpec(memory_space=smem), pl.Bloc...  17.9 us
    all_to_all x2, waiting for transfers between devices, local(): back = lax.all_to_all(attended, 'seq', 0, 0, tiled=True)  13.7 us
    all_to_all x2, starting transfers between devices, local(): packed = lax.all_to_all(send, 'seq', 0, 0, tiled=True)  9.91 us
    all_to_all x2, starting transfers between devices, local(): back = lax.all_to_all(attended, 'seq', 0, 0, tiled=True)  7.6 us
    pallas_call x2, Pallas kernels, packed_chunk(): pl.pallas_call(kernel, in_specs=[pl.BlockSpec(memory_space=pltpu.VMEM)] *...  6.32 us
    unnamed x19, local copies, waits for them, and re-layouts  2.57 us
  transfers between devices with their start and end apart: 5, of which 5 were waited for; matrix products, arithmetic and copies ran while one was open for 7% of the time, Pallas kernels for 16%

profile of v3, /device:TPU:0, one launch (start us, length us, event | category | flops | bytes accessed | tf_op | source)
XLA Modules:
  0.0 127.7 jit_solution(17211635856504013307)
XLA Ops:
  0.6 3.2 %shard_map.115 = bf16[4,3,128,512]{3,2,1,0:T(8,128)(2,1)} custom-call(bf16[1,128,4096]{2,1,0:T(8,128)(2,1)} %query_ref.3, bf16[1,128,4096]{2,1,0:T(8,128)(2,1)} %key_ref.3, bf16[1,128,4096]{2,1,0:T(8,128)(2,1)} %value_ref.3), custom_call_target="tpu_custom_call" | custom-call | tf_op jit(solution)/shard_map/pallas_call | solution.py:100
  3.8 6.3 %all-to-all-start.2 = ((bf16[4,3,128,512]{3,2,1,0:T(8,128)(2,1)}), bf16[4,3,128,512]{3,2,1,0:T(8,128)(2,1)S(1)}, u32[]{:S(2)}, u32[]{:S(2)}) async-start(bf16[4,3,128,512]{3,2,1,0:T(8,128)(2,1)} %shard_map.115), calls=%async_computation.2 | async-start | bytes 3145728 | tf_op jit(solution)/shard_map/all_to_all | solution.py:156
  10.2 3.1 %shard_map.113 = bf16[4,3,128,512]{3,2,1,0:T(8,128)(2,1)} custom-call(bf16[1,128,4096]{2,1,0:T(8,128)(2,1)} %query_ref.3, bf16[1,128,4096]{2,1,0:T(8,128)(2,1)} %key_ref.3, bf16[1,128,4096]{2,1,0:T(8,128)(2,1)} %value_ref.3), custom_call_target="tpu_custom_call" | custom-call | tf_op jit(solution)/shard_map/pallas_call | solution.py:100
  13.3 33.8 %all-to-all-done.2.x_ref = bf16[4,3,128,512]{3,2,1,0:T(8,128)(2,1)S(1)} async-done(((bf16[4,3,128,512]{3,2,1,0:T(8,128)(2,1)}), bf16[4,3,128,512]{3,2,1,0:T(8,128)(2,1)S(1)}, u32[]{:S(2)}, u32[]{:S(2)}) %all-to-all-start.2) | async-done | bytes 1572896 | tf_op jit(solution)/shard_map/all_to_all | solution.py:156
  47.1 1.1 copy-done.2
  48.3 3.6 %all-to-all-start = ((bf16[4,3,128,512]{3,2,1,0:T(8,128)(2,1)}), bf16[4,3,128,512]{3,2,1,0:T(8,128)(2,1)S(1)}, u32[]{:S(2)}, u32[]{:S(2)}) async-start(bf16[4,3,128,512]{3,2,1,0:T(8,128)(2,1)} %shard_map.113), calls=%async_computation | async-start | bytes 3145728 | tf_op jit(solution)/shard_map/all_to_all | solution.py:156
  51.9 0.7 constant_dynamic-slice_fusion.1
  52.5 0.8 copy.14
  53.9 1.4 %constant_dynamic-slice_fusion = (s32[4,4]{0,1:T(4,128)S(1)}, s32[4,4]{0,1:T(4,128)}) fusion(s32[32,4]{0,1:T(4,128)} %param.18, s32[]{:T(128)S(6)} %select_n.9, s32[]{:T(128)S(6)} %select_n.8), kind=kLoop, calls=%fused_computation.14 | loop fusion | bytes 264 | tf_op jit(solution)/shard_map/dynamic_slice | solution.py:159
  56.2 0.6 reshape.54.lists_ref
  56.8 0.8 copy.13
  57.6 0.6 reshape.55.live_ref
  58.5 8.9 %shard_map.116 = bf16[4,128,512]{2,1,0:T(8,128)(2,1)} custom-call(s32[64]{0:T(128)} %reshape.56.lists_ref, s32[16]{0:T(128)} %reshape.57.live_ref, bf16[4,3,128,512]{3,2,1,0:T(8,128)(2,1)} %copy-done.2), custom_call_target="tpu_custom_call" | custom-call | tf_op jit(solution)/shard_map/pallas_call | solution.py:78
  67.4 20.9 %all-to-all-done.x_ref = bf16[4,3,128,512]{3,2,1,0:T(8,128)(2,1)S(1)} async-done(((bf16[4,3,128,512]{3,2,1,0:T(8,128)(2,1)}), bf16[4,3,128,512]{3,2,1,0:T(8,128)(2,1)S(1)}, u32[]{:S(2)}, u32[]{:S(2)}) %all-to-all-start) | async-done | bytes 1572896 | tf_op jit(solution)/shard_map/all_to_all | solution.py:156
  88.3 4.1 %all-to-all-start.3 = ((bf16[4,128,512]{2,1,0:T(8,128)(2,1)}), bf16[4,128,512]{2,1,0:T(8,128)(2,1)}, u32[]{:S(2)}, u32[]{:S(2)}) async-start(bf16[4,128,512]{2,1,0:T(8,128)(2,1)} %shard_map.116), calls=%async_computation.3 | async-start | bytes 1048576 | tf_op jit(solution)/shard_map/all_to_all | solution.py:161
  92.5 1.5 %slice_add_fusion = (f32[1,1,5120]{2,1,0:T(1,128)}, f32[1,1,5120]{2,1,0:T(1,128)}) fusion(f32[1,2,5120]{2,1,0:T(2,128)} %param.14), kind=kLoop, calls=%fused_computation.13 | loop fusion | flops 5120 | bytes 81920 | tf_op jit(solution)/shard_map/add | solution.py:170
  94.0 8.9 %shard_map.114 = bf16[4,128,512]{2,1,0:T(8,128)(2,1)} custom-call(s32[64]{0:T(128)} %reshape.54.lists_ref, s32[16]{0:T(128)} %reshape.55.live_ref, bf16[4,3,128,512]{3,2,1,0:T(8,128)(2,1)} %copy-done.1), custom_call_target="tpu_custom_call" | custom-call | tf_op jit(solution)/shard_map/pallas_call | solution.py:78
  102.9 3.7 %all-to-all-done.3.refs_1_ = bf16[4,128,512]{2,1,0:T(8,128)(2,1)} async-done(((bf16[4,128,512]{2,1,0:T(8,128)(2,1)}), bf16[4,128,512]{2,1,0:T(8,128)(2,1)}, u32[]{:S(2)}, u32[]{:S(2)}) %all-to-all-start.3) | async-done | bytes 524320 | tf_op jit(solution)/shard_map/all_to_all | solution.py:161
  106.6 3.5 %all-to-all-start.1 = ((bf16[4,128,512]{2,1,0:T(8,128)(2,1)}), bf16[4,128,512]{2,1,0:T(8,128)(2,1)S(1)}, u32[]{:S(2)}, u32[]{:S(2)}) async-start(bf16[4,128,512]{2,1,0:T(8,128)(2,1)} %shard_map.114), calls=%async_computation.1 | async-start | bytes 1048576 | tf_op jit(solution)/shard_map/all_to_all | solution.py:161
  111.3 0.8 fusion.15
  112.4 1.6 %collective-permute-done = f32[1,128,64]{1,2,0:T(8,128)S(1)} collective-permute-done((f32[1,128,64]{1,2,0:T(8,128)S(1)}, f32[1,128,64]{1,2,0:T(8,128)S(1)}, u32[]{:S(2)}, u32[]{:S(2)}) %collective-permute-start) | collective-permute-done | bytes 32800 | tf_op jit(solution)/shard_map/ppermute | solution.py:21
  114.0 10.1 %all-to-all-done.1.refs_0_ = bf16[4,128,512]{2,1,0:T(8,128)(2,1)S(1)} async-done(((bf16[4,128,512]{2,1,0:T(8,128)(2,1)}), bf16[4,128,512]{2,1,0:T(8,128)(2,1)S(1)}, u32[]{:S(2)}, u32[]{:S(2)}) %all-to-all-start.1) | async-done | bytes 524320 | tf_op jit(solution)/shard_map/all_to_all | solution.py:161
  124.1 0.8 copy-done.4
  124.9 2.2 %shard_map.117 = bf16[1,128,4096]{2,1,0:T(8,128)(2,1)} custom-call(bf16[4,128,512]{2,1,0:T(8,128)(2,1)} %copy-done.4, bf16[4,128,512]{2,1,0:T(8,128)(2,1)} %all-to-all-done.3.refs_1_), custom_call_target="tpu_custom_call" | custom-call | tf_op jit(solution)/shard_map/pallas_call | solution.py:120
  (26 shorter events, 3.1 us)
Async XLA Ops:
  0.6 110.7 %copy-start = (bf16[5120,64]{0,1:T(8,128)(2,1)S(1)}, bf16[5120,64]{0,1:T(8,128)(2,1)}, u32[]{:S(2)}) copy-start(bf16[5120,64]{0,1:T(8,128)(2,1)} %param.15) | copy-start | bytes 1966084
  3.8 43.3 %all-to-all-start.2 = ((bf16[4,3,128,512]{3,2,1,0:T(8,128)(2,1)}), bf16[4,3,128,512]{3,2,1,0:T(8,128)(2,1)S(1)}, u32[]{:S(2)}, u32[]{:S(2)}) async-start(bf16[4,3,128,512]{3,2,1,0:T(8,128)(2,1)} %shard_map.115), calls=%async_computation.2 | async-start | bytes 3145728 | tf_op jit(solution)/shard_map/all_to_all | solution.py:156
  13.3 38.5 %copy-start.5 = (s32[32,4,4]{0,2,1:T(4,128)S(1)}, s32[32,4,4]{0,2,1:T(4,128)}, u32[]{:S(2)}) copy-start(s32[32,4,4]{0,2,1:T(4,128)} %param.19) | copy-start | bytes 6148
  13.3 44.9 %copy-start.3 = (bf16[1,128,5120]{2,1,0:T(8,128)(2,1)S(1)}, bf16[1,128,5120]{2,1,0:T(8,128)(2,1)}, u32[]{:S(2)}) copy-start(bf16[1,128,5120]{2,1,0:T(8,128)(2,1)} %param.13) | copy-start | bytes 3932164
  47.1 1.1 copy-start.2
  48.3 40.1 %all-to-all-start = ((bf16[4,3,128,512]{3,2,1,0:T(8,128)(2,1)}), bf16[4,3,128,512]{3,2,1,0:T(8,128)(2,1)S(1)}, u32[]{:S(2)}, u32[]{:S(2)}) async-start(bf16[4,3,128,512]{3,2,1,0:T(8,128)(2,1)} %shard_map.113), calls=%async_computation | async-start | bytes 3145728 | tf_op jit(solution)/shard_map/all_to_all | solution.py:156
  88.3 5.7 %copy-start.1 = (bf16[4,3,128,512]{3,2,1,0:T(8,128)(2,1)}, bf16[4,3,128,512]{3,2,1,0:T(8,128)(2,1)S(1)}, u32[]{:S(2)}) copy-start(bf16[4,3,128,512]{3,2,1,0:T(8,128)(2,1)S(1)} %all-to-all-done.x_ref) | copy-start | bytes 4718596
  88.3 18.2 %all-to-all-start.3 = ((bf16[4,128,512]{2,1,0:T(8,128)(2,1)}), bf16[4,128,512]{2,1,0:T(8,128)(2,1)}, u32[]{:S(2)}, u32[]{:S(2)}) async-start(bf16[4,128,512]{2,1,0:T(8,128)(2,1)} %shard_map.116), calls=%async_computation.3 | async-start | bytes 1048576 | tf_op jit(solution)/shard_map/all_to_all | solution.py:161
  102.9 8.4 %copy-start.6 = (f32[1,1,5120]{2,1,0:T(1,128)S(1)}, f32[1,1,5120]{2,1,0:T(1,128)}, u32[]{:S(2)}) copy-start(f32[1,1,5120]{2,1,0:T(1,128)} %get-tuple-element.2) | copy-start | bytes 61444
  102.9 8.4 %copy-start.7 = (f32[1,1,5120]{2,1,0:T(1,128)S(1)}, f32[1,1,5120]{2,1,0:T(1,128)}, u32[]{:S(2)}) copy-start(f32[1,1,5120]{2,1,0:T(1,128)} %get-tuple-element.3) | copy-start | bytes 61444
  102.9 8.4 %copy-start.8 = (f32[1,128,64]{1,2,0:T(8,128)S(1)}, f32[1,128,64]{1,2,0:T(8,128)}, u32[]{:S(2)}) copy-start(f32[1,128,64]{1,2,0:T(8,128)} %param.16) | copy-start | bytes 98308
  106.6 17.5 %all-to-all-start.1 = ((bf16[4,128,512]{2,1,0:T(8,128)(2,1)}), bf16[4,128,512]{2,1,0:T(8,128)(2,1)S(1)}, u32[]{:S(2)}, u32[]{:S(2)}) async-start(bf16[4,128,512]{2,1,0:T(8,128)(2,1)} %shard_map.114), calls=%async_computation.1 | async-start | bytes 1048576 | tf_op jit(solution)/shard_map/all_to_all | solution.py:161
  112.1 1.9 %collective-permute-start = (f32[1,128,64]{1,2,0:T(8,128)S(1)}, f32[1,128,64]{1,2,0:T(8,128)S(1)}, u32[]{:S(2)}, u32[]{:S(2)}) collective-permute-start(f32[1,128,64]{1,2,0:T(8,128)S(1)} %fusion.15), channel_id=1, source_target_pairs={{0,3},{1,0},{2,1},{3,2},{4,7},{5,4},{6,5},{7,6},{8,11},{9,8},{10,9... | collective-permute-start | bytes 98312 | tf_op jit(solution)/shard_map/ppermute | solution.py:21
  124.1 0.8 copy-start.4

commit v4 on v3

--- a/solution.py
+++ b/solution.py
@@ -26,8 +26,17 @@
     return plan_shift * fraction / (1.0 + (plan_shift - 1.0) * fraction)
 
 
-def attend_kernel(lists_ref, live_ref, x_ref, o_ref, *, block, slots, qblocks, heads, depth):
+def attend_kernel(
+    lists_ref, live_ref, me_ref, x_ref, o_ref, *, block, slots, qblocks, heads, depth, shifted
+):
     sources, _, tokens, _ = x_ref.shape
+    me = me_ref[0]
+
+    def slot_of(device):
+        if shifted:
+            return (me - device + sources) % sources
+        return device
+
     total = sources * tokens
     scale = depth ** (-0.5)
     column = lax.broadcasted_iota(jnp.int32, (1, total), 1)
@@ -38,7 +47,7 @@
         values = x_ref[:, 2, :, cols].reshape(total, depth)
 
         def body(qblock, carry):
-            source = qblock // per_source
+            source = slot_of(qblock // per_source)
             first = pl.multiple_of((qblock % per_source) * block, block)
             query = x_ref[source, 0, pl.ds(first, block), cols]
             scores = (
@@ -50,7 +59,9 @@
             live = live_ref[head * qblocks + qblock]
             active = column < 0
             for slot in range(slots):
-                low = lists_ref[(head * qblocks + qblock) * slots + slot] * block
+                chosen = lists_ref[(head * qblocks + qblock) * slots + slot]
+                place = slot_of(chosen // per_source)
+                low = place * tokens + (chosen % per_source) * block
                 active = active | ((column >= low) & (column < low + block) & (slot < live))
             scores = jnp.where(active, scores, -jnp.inf)
             highest = jnp.max(scores, axis=1, keepdims=True)
@@ -65,14 +76,20 @@
         lax.fori_loop(0, qblocks, body, 0)
 
 
-def attend_heads(packed, lists, live):
+def attend_heads(packed, lists, live, me, shifted):
     sources, _, tokens, width = packed.shape
     head_total, qblocks = live.shape
     slots = lists.shape[2]
     depth = width // head_total
     block = sources * tokens // qblocks
     kernel = functools.partial(
-        attend_kernel, block=block, slots=slots, qblocks=qblocks, heads=head_total, depth=depth
+        attend_kernel,
+        block=block,
+        slots=slots,
+        qblocks=qblocks,
+        heads=head_total,
+        depth=depth,
+        shifted=shifted,
     )
     smem = pltpu.SMEM
     return pl.pallas_call(
@@ -80,11 +97,12 @@
         in_specs=[
             pl.BlockSpec(memory_space=smem),
             pl.BlockSpec(memory_space=smem),
+            pl.BlockSpec(memory_space=smem),
             pl.BlockSpec(memory_space=pltpu.VMEM),
         ],
         out_specs=pl.BlockSpec(memory_space=pltpu.VMEM),
         out_shape=jax.ShapeDtypeStruct((sources, tokens, width), jnp.bfloat16),
-    )(lists.reshape(-1), live.reshape(-1), packed)
+    )(lists.reshape(-1), live.reshape(-1), me.reshape(1), packed)
 
 
 def pack_kernel(query_ref, key_ref, value_ref, out_ref, *, seq, stride, offset, width):
@@ -147,18 +165,35 @@
     width = query_rows.shape[2]
     depth = width // head_count
     chunk_width = per_chunk * depth
+    permuted = seq_count <= 8
 
     backs = []
     for c in range(chunks):
         send = packed_chunk(
             query_rows, key_rows, value_rows, seq_count, per_device * depth, c * chunk_width, chunk_width
         )
-        packed = lax.all_to_all(send, "seq", 0, 0, tiled=True)
+        if permuted:
+            pieces = [lax.dynamic_index_in_dim(send, own_index, 0, keepdims=False)]
+            for step in range(1, seq_count):
+                target = (own_index + step) % seq_count
+                piece = lax.dynamic_index_in_dim(send, target, 0, keepdims=False)
+                pieces.append(passed_along(piece, "seq", step))
+            packed = jnp.stack(pieces)
+            place = own_index
+        else:
+            packed = lax.all_to_all(send, "seq", 0, 0, tiled=True)
+            place = jnp.zeros((), jnp.int32)
         first = own_index * per_device + c * per_chunk
         lists = lax.dynamic_slice_in_dim(block_lists, first, per_chunk, 0)
         live = lax.dynamic_slice_in_dim(live_counts, first, per_chunk, 0)
-        attended = attend_heads(packed, lists, live)
-        back = lax.all_to_all(attended, "seq", 0, 0, tiled=True)
+        attended = attend_heads(packed, lists, live, place.astype(jnp.int32), permuted)
+        if permuted:
+            outs = [attended[0]]
+            for step in range(1, seq_count):
+                outs.append(passed_along(attended[step], "seq", -step))
+            back = jnp.roll(jnp.stack(outs), own_index, axis=0)
+        else:
+            back = lax.all_to_all(attended, "seq", 0, 0, tiled=True)
         backs.append(back)
     mixed_back = unpacked(backs, seq_count, per_device * depth, chunk_width)
 

time: 128 us -> 116 us (0.906)
  waiting for transfers between devices: 70.1 us -> 18.2 us
  starting transfers between devices: 17.8 us -> 50.2 us
  other arithmetic: 2.29 us -> 7.39 us
  local copies, waits for them, and re-layouts: 8.9 us -> 10.9 us
    all_to_all x4 -> x0, waiting for transfers between devices: 68.5 us -> none  [the longest x2 54.7 us: local(): packed = lax.all_to_all(send, 'seq', 0, 0, tiled=True)]
    ppermute x1 -> x13, starting transfers between devices: 0.26 us -> 50.2 us  [passed_along(): return lax.ppermute(value, axis, pairs)]
    all_to_all x4 -> x0, starting transfers between devices: 17.5 us -> none  [the longest x2 9.91 us: local(): packed = lax.all_to_all(send, 'seq', 0, 0, tiled=True)]
    ppermute x1 -> x13, waiting for transfers between devices: 1.6 us -> 18.2 us  [passed_along(): return lax.ppermute(value, axis, pairs)]
    dynamic_slice x0 -> x2, local copies, waits for them, and re-layouts: none -> 4.93 us  [local(): pieces = [lax.dynamic_index_in_dim(send, own_index, 0, keepdims=False)]]
    another operation x0 -> x2, other arithmetic: none -> 3.74 us  [local(): packed = jnp.stack(pieces)]
    concatenate x0 -> x2, other arithmetic: none -> 2.84 us  [local(): back = jnp.roll(jnp.stack(outs), own_index, axis=0)]
    squeeze x0 -> x2, local copies, waits for them, and re-layouts: none -> 2.26 us  [local(): outs.append(passed_along(attended[step], 'seq', -step))]
  transfers between devices with their start and end apart: 5 -> 13, of which waited for: 5 -> 4; matrix products, arithmetic and copies ran while one was open for 7% -> 13% of each run, Pallas kernels for 16% -> 18%
where the time goes in v4:
time: 116 us
  starting transfers between devices  50.2 us (43%)
  Pallas kernels  26.5 us (23%)
  waiting for transfers between devices  18.2 us (16%)
  local copies, waits for them, and re-layouts  10.9 us (9%)
  other arithmetic  7.39 us (6%)
  between operations  1.53 us (1%)
    ppermute x13, starting transfers between devices, passed_along(): return lax.ppermute(value, axis, pairs)  50.2 us
    ppermute x13, waiting for transfers between devices, passed_along(): return lax.ppermute(value, axis, pairs)  18.2 us
    pallas_call x2, Pallas kernels, attend_heads(): pl.pallas_call(kernel, in_specs=[pl.BlockSpec(memory_space=smem), pl.Bloc...  17.9 us
    pallas_call x2, Pallas kernels, packed_chunk(): pl.pallas_call(kernel, in_specs=[pl.BlockSpec(memory_space=pltpu.VMEM)] *...  6.36 us
    dynamic_slice x2, local copies, waits for them, and re-layouts, local(): pieces = [lax.dynamic_index_in_dim(send, own_index, 0, keepdims=False)]  4.93 us
    another operation x2, other arithmetic, local(): packed = jnp.stack(pieces)  3.74 us
    concatenate x2, other arithmetic, local(): back = jnp.roll(jnp.stack(outs), own_index, axis=0)  2.84 us
  transfers between devices with their start and end apart: 13, of which 4 were waited for; matrix products, arithmetic and copies ran while one was open for 13% of the time, Pallas kernels for 18%

profile of v4, /device:TPU:0, one launch (start us, length us, event | category | flops | bytes accessed | tf_op | source)
XLA Modules:
  0.0 115.6 jit_solution(14346645125048078924)
XLA Ops:
  0.7 3.2 %shard_map.113 = bf16[4,3,128,512]{3,2,1,0:T(8,128)(2,1)} custom-call(bf16[1,128,4096]{2,1,0:T(8,128)(2,1)} %query_ref.3, bf16[1,128,4096]{2,1,0:T(8,128)(2,1)} %key_ref.3, bf16[1,128,4096]{2,1,0:T(8,128)(2,1)} %value_ref.3), custom_call_target="tpu_custom_call" | custom-call | tf_op jit(solution)/shard_map/pallas_call | solution.py:118
  3.9 2.4 %constant_dynamic-slice_fusion.3 = (bf16[1,3,128,512]{3,2,1,0:T(8,128)(2,1)S(1)}, bf16[3,128,512]{2,1,0:T(8,128)(2,1)}, bf16[3,128,512]{2,1,0:T(8,128)(2,1)}, bf16[3,128,512]{2,1,0:T(8,128)(2,1)}) fusion(bf16[4,3,128,512]{3,2,1,0:T(8,128)(2,1)} %shard_map.113, s32[]{:T(128)S(6)} %select_n.56, s32[]{:T(128)S(6)} %select_n.62, s32[]{:T(128)S(6)} %select_n.60, ...), kind=kLoop, calls=%fused_computation.61 | loop fusion | bytes 3145744 | tf_op jit(solution)/shard_map/jit(dynamic_index_in_dim)/dynamic_slice | solution.py:176
  6.3 5.1 %collective-permute-start.2 = (bf16[3,128,512]{2,1,0:T(8,128)(2,1)}, bf16[3,128,512]{2,1,0:T(8,128)(2,1)S(1)}, u32[]{:S(2)}, u32[]{:S(2)}) collective-permute-start(bf16[3,128,512]{2,1,0:T(8,128)(2,1)} %get-tuple-element.8), channel_id=1, source_target_pairs={{0,12},{4,0},{8,4},{12,8},{1,13},{5,1},{9,5},{13,9},{2,14},{6,2},{... | collective-permute-start | bytes 1179656 | tf_op jit(solution)/shard_map/ppermute | solution.py:21
  12.4 3.2 %shard_map.115 = bf16[4,3,128,512]{3,2,1,0:T(8,128)(2,1)} custom-call(bf16[1,128,4096]{2,1,0:T(8,128)(2,1)} %query_ref.3, bf16[1,128,4096]{2,1,0:T(8,128)(2,1)} %key_ref.3, bf16[1,128,4096]{2,1,0:T(8,128)(2,1)} %value_ref.3), custom_call_target="tpu_custom_call" | custom-call | tf_op jit(solution)/shard_map/pallas_call | solution.py:118
  15.6 2.5 %constant_dynamic-slice_fusion = (bf16[1,3,128,512]{3,2,1,0:T(8,128)(2,1)S(1)}, bf16[3,128,512]{2,1,0:T(8,128)(2,1)}, bf16[3,128,512]{2,1,0:T(8,128)(2,1)}, bf16[3,128,512]{2,1,0:T(8,128)(2,1)}) fusion(bf16[4,3,128,512]{3,2,1,0:T(8,128)(2,1)} %shard_map.115, s32[]{:T(128)S(6)} %select_n.56, s32[]{:T(128)S(6)} %select_n.62, s32[]{:T(128)S(6)} %select_n.60, ...), kind=kLoop, calls=%fused_computation.58 | loop fusion | bytes 3145744 | tf_op jit(solution)/shard_map/jit(dynamic_index_in_dim)/dynamic_slice | solution.py:176
  18.1 2.8 %collective-permute-start.8 = (bf16[3,128,512]{2,1,0:T(8,128)(2,1)}, bf16[3,128,512]{2,1,0:T(8,128)(2,1)S(1)}, u32[]{:S(2)}, u32[]{:S(2)}) collective-permute-start(bf16[3,128,512]{2,1,0:T(8,128)(2,1)} %get-tuple-element.4), channel_id=1, source_target_pairs={{0,12},{4,0},{8,4},{12,8},{1,13},{5,1},{9,5},{13,9},{2,14},{6,2},{... | collective-permute-start | bytes 1179656 | tf_op jit(solution)/shard_map/ppermute | solution.py:21
  23.5 1.5 %collective-permute-done.12 = f32[1,128,64]{1,2,0:T(8,128)S(1)} collective-permute-done((f32[1,128,64]{1,2,0:T(8,128)S(1)}, f32[1,128,64]{1,2,0:T(8,128)S(1)}, u32[]{:S(2)}, u32[]{:S(2)}) %collective-permute-start.12) | collective-permute-done | bytes 32800 | tf_op jit(solution)/shard_map/ppermute | solution.py:21
  26.1 11.3 %collective-permute-start.6 = (bf16[3,128,512]{2,1,0:T(8,128)(2,1)}, bf16[3,128,512]{2,1,0:T(8,128)(2,1)}, u32[]{:S(2)}, u32[]{:S(2)}) collective-permute-start(bf16[3,128,512]{2,1,0:T(8,128)(2,1)} %get-tuple-element.6), channel_id=1, source_target_pairs={{0,4},{4,8},{8,12},{12,0},{1,5},{5,9},{9,13},{13,1},{2,6},{6,10},{... | collective-permute-start | bytes 1179656 | tf_op jit(solution)/shard_map/ppermute | solution.py:21
  40.4 7.0 %collective-permute-done.1 = bf16[3,128,512]{2,1,0:T(8,128)(2,1)S(1)} collective-permute-done((bf16[3,128,512]{2,1,0:T(8,128)(2,1)}, bf16[3,128,512]{2,1,0:T(8,128)(2,1)S(1)}, u32[]{:S(2)}, u32[]{:S(2)}) %collective-permute-start.1) | collective-permute-done | bytes 393248 | tf_op jit(solution)/shard_map/ppermute | solution.py:21
  47.4 1.4 %pad_maximum_fusion.x_ref = bf16[4,3,128,512]{3,2,1,0:T(8,128)(2,1)} fusion(bf16[1,3,128,512]{3,2,1,0:T(8,128)(2,1)S(1)} %bitcast.69, bf16[1,3,128,512]{3,2,1,0:T(8,128)(2,1)S(1)} %bitcast.70, bf16[1,3,128,512]{3,2,1,0:T(8,128)(2,1)S(1)} %bitcast.71, bf16[1,3,128,512]{3,2,1,0:T(8,128)(2,1)S(1)} %get-tuple-element.7), kind=kLoop, calls=%fused_computation.9 | loop fusion | flops 2359296 | bytes 3145728 | tf_op jit(solution)/shard_map/stack | solution.py:181
  48.8 8.9 %shard_map.114 = bf16[4,128,512]{2,1,0:T(8,128)(2,1)} custom-call(s32[64]{0:T(128)} %reshape.58.lists_ref, s32[16]{0:T(128)} %reshape.59.live_ref, s32[1]{0:T(128)} %bitcast.me_ref, bf16[4,3,128,512]{3,2,1,0:T(8,128)(2,1)} %pad_maximum_fusion.x_ref), custom_call_target="tpu_custom_call" | custom-call | tf_op jit(solution)/shard_map/pallas_call | solution.py:95
  57.7 1.1 slice_bitcast_fusion.3
  58.9 19.4 %collective-permute-start.4 = (bf16[128,512]{1,0:T(8,128)(2,1)S(1)}, bf16[128,512]{1,0:T(8,128)(2,1)S(1)}, u32[]{:S(2)}, u32[]{:S(2)}) collective-permute-start(bf16[128,512]{1,0:T(8,128)(2,1)S(1)} %get-tuple-element.16), channel_id=1, source_target_pairs={{0,8},{4,12},{8,0},{12,4},{1,9},{5,13},{9,1},{13,5},{2,10},{6,14},... | collective-permute-start | bytes 393224 | tf_op jit(solution)/shard_map/ppermute | solution.py:21
  78.3 1.9 %collective-permute-start.5 = (bf16[128,512]{1,0:T(8,128)(2,1)S(1)}, bf16[128,512]{1,0:T(8,128)(2,1)S(1)}, u32[]{:S(2)}, u32[]{:S(2)}) collective-permute-start(bf16[128,512]{1,0:T(8,128)(2,1)S(1)} %get-tuple-element.15), channel_id=1, source_target_pairs={{0,4},{4,8},{8,12},{12,0},{1,5},{5,9},{9,13},{13,1},{2,6},{6,10},{... | collective-permute-start | bytes 393224 | tf_op jit(solution)/shard_map/ppermute | solution.py:21
  80.3 2.6 %collective-permute-done.7 = bf16[3,128,512]{2,1,0:T(8,128)(2,1)S(1)} collective-permute-done((bf16[3,128,512]{2,1,0:T(8,128)(2,1)}, bf16[3,128,512]{2,1,0:T(8,128)(2,1)S(1)}, u32[]{:S(2)}, u32[]{:S(2)}) %collective-permute-start.7) | collective-permute-done | bytes 393248 | tf_op jit(solution)/shard_map/ppermute | solution.py:21
  82.8 2.4 %pad_maximum_fusion.1.x_ref = bf16[4,3,128,512]{3,2,1,0:T(8,128)(2,1)} fusion(bf16[1,3,128,512]{3,2,1,0:T(8,128)(2,1)S(1)} %bitcast.68, bf16[1,3,128,512]{3,2,1,0:T(8,128)(2,1)S(1)} %bitcast.72, bf16[1,3,128,512]{3,2,1,0:T(8,128)(2,1)} %bitcast.14, bf16[1,3,128,512]{3,2,1,0:T(8,128)(2,1)S(1)} %get-tuple-element.3), kind=kLoop, calls=%fused_computation.10 | loop fusion | flops 2359296 | bytes 3145728 | tf_op jit(solution)/shard_map/stack | solution.py:181
  85.2 8.9 %shard_map.116 = bf16[4,128,512]{2,1,0:T(8,128)(2,1)} custom-call(s32[64]{0:T(128)} %reshape.61.lists_ref, s32[16]{0:T(128)} %reshape.62.live_ref, s32[1]{0:T(128)} %bitcast.me_ref, bf16[4,3,128,512]{3,2,1,0:T(8,128)(2,1)} %pad_maximum_fusion.1.x_ref), custom_call_target="tpu_custom_call" | custom-call | tf_op jit(solution)/shard_map/pallas_call | solution.py:95
  94.1 1.1 slice_bitcast_fusion
  95.3 5.5 %collective-permute-start.10 = (bf16[128,512]{1,0:T(8,128)(2,1)S(1)}, bf16[128,512]{1,0:T(8,128)(2,1)S(1)}, u32[]{:S(2)}, u32[]{:S(2)}) collective-permute-start(bf16[128,512]{1,0:T(8,128)(2,1)S(1)} %get-tuple-element.12), channel_id=1, source_target_pairs={{0,8},{4,12},{8,0},{12,4},{1,9},{5,13},{9,1},{13,5},{2,10},{6,14},... | collective-permute-start | bytes 393224 | tf_op jit(solution)/shard_map/ppermute | solution.py:21
  100.8 1.9 %collective-permute-start.11 = (bf16[128,512]{1,0:T(8,128)(2,1)S(1)}, bf16[128,512]{1,0:T(8,128)(2,1)S(1)}, u32[]{:S(2)}, u32[]{:S(2)}) collective-permute-start(bf16[128,512]{1,0:T(8,128)(2,1)S(1)} %get-tuple-element.11), channel_id=1, source_target_pairs={{0,4},{4,8},{8,12},{12,0},{1,5},{5,9},{9,13},{13,1},{2,6},{6,10},{... | collective-permute-start | bytes 393224 | tf_op jit(solution)/shard_map/ppermute | solution.py:21
  102.8 1.4 %fusion.28.refs_0_ = bf16[4,128,512]{2,1,0:T(8,128)(2,1)} fusion(s32[]{:T(128)S(6)} %select_n.67, bf16[1,128,512]{2,1,0:T(8,128)(2,1)S(1)} %get-tuple-element.18, bf16[1,128,512]{2,1,0:T(8,128)(2,1)S(1)} %bitcast.73, bf16[1,128,512]{2,1,0:T(8,128)(2,1)S(1)} %bitcast.74, bf16[1,128,512]{2,1,0:T(8,128)(2,1)S(1)} %bitcast.75), kind=kLoop, calls=%fused_computation.41 | loop fusion | flops 1835008 | bytes 1048580 | tf_op jit(solution)/shard_map/jit(_roll_dynamic)/concatenate | solution.py:194
  104.2 7.1 %collective-permute-done.10 = bf16[128,512]{1,0:T(8,128)(2,1)S(1)} collective-permute-done((bf16[128,512]{1,0:T(8,128)(2,1)S(1)}, bf16[128,512]{1,0:T(8,128)(2,1)S(1)}, u32[]{:S(2)}, u32[]{:S(2)}) %collective-permute-start.10) | collective-permute-done | bytes 131104 | tf_op jit(solution)/shard_map/ppermute | solution.py:21
  111.3 1.4 %fusion.21.refs_1_ = bf16[4,128,512]{2,1,0:T(8,128)(2,1)} fusion(s32[]{:T(128)S(6)} %select_n.67, bf16[1,128,512]{2,1,0:T(8,128)(2,1)S(1)} %get-tuple-element.14, bf16[1,128,512]{2,1,0:T(8,128)(2,1)S(1)} %bitcast.76, bf16[1,128,512]{2,1,0:T(8,128)(2,1)S(1)} %bitcast.77, bf16[1,128,512]{2,1,0:T(8,128)(2,1)S(1)} %bitcast.78), kind=kLoop, calls=%fused_computation.34 | loop fusion | flops 1835008 | bytes 1048580 | tf_op jit(solution)/shard_map/jit(_roll_dynamic)/concatenate | solution.py:194
  112.7 2.2 %shard_map.117 = bf16[1,128,4096]{2,1,0:T(8,128)(2,1)} custom-call(bf16[4,128,512]{2,1,0:T(8,128)(2,1)} %fusion.28.refs_0_, bf16[4,128,512]{2,1,0:T(8,128)(2,1)} %fusion.21.refs_1_), custom_call_target="tpu_custom_call" | custom-call | tf_op jit(solution)/shard_map/pallas_call | solution.py:138
  (44 shorter events, 7.7 us)
Async XLA Ops:
  0.6 21.9 %copy-start = (bf16[5120,64]{0,1:T(8,128)(2,1)S(1)}, bf16[5120,64]{0,1:T(8,128)(2,1)}, u32[]{:S(2)}) copy-start(bf16[5120,64]{0,1:T(8,128)(2,1)} %param.17) | copy-start | bytes 1966084
  6.3 19.8 %collective-permute-start.2 = (bf16[3,128,512]{2,1,0:T(8,128)(2,1)}, bf16[3,128,512]{2,1,0:T(8,128)(2,1)S(1)}, u32[]{:S(2)}, u32[]{:S(2)}) collective-permute-start(bf16[3,128,512]{2,1,0:T(8,128)(2,1)} %get-tuple-element.8), channel_id=1, source_target_pairs={{0,12},{4,0},{8,4},{12,8},{1,13},{5,1},{9,5},{13,9},{2,14},{6,2},{... | collective-permute-start | bytes 1179656 | tf_op jit(solution)/shard_map/ppermute | solution.py:21
  11.4 36.0 %collective-permute-start.1 = (bf16[3,128,512]{2,1,0:T(8,128)(2,1)}, bf16[3,128,512]{2,1,0:T(8,128)(2,1)S(1)}, u32[]{:S(2)}, u32[]{:S(2)}) collective-permute-start(bf16[3,128,512]{2,1,0:T(8,128)(2,1)} %get-tuple-element.9), channel_id=1, source_target_pairs={{0,8},{4,12},{8,0},{12,4},{1,9},{5,13},{9,1},{13,5},{2,10},{6,14},... | collective-permute-start | bytes 1179656 | tf_op jit(solution)/shard_map/ppermute | solution.py:21
  11.4 36.0 %collective-permute-start = (bf16[3,128,512]{2,1,0:T(8,128)(2,1)}, bf16[3,128,512]{2,1,0:T(8,128)(2,1)S(1)}, u32[]{:S(2)}, u32[]{:S(2)}) collective-permute-start(bf16[3,128,512]{2,1,0:T(8,128)(2,1)} %get-tuple-element.10), channel_id=1, source_target_pairs={{0,4},{4,8},{8,12},{12,0},{1,5},{5,9},{9,13},{13,1},{2,6},{6,10},{... | collective-permute-start | bytes 1179656 | tf_op jit(solution)/shard_map/ppermute | solution.py:21
  15.6 5.3 %copy-start.2 = (f32[1,2,5120]{2,1,0:T(2,128)S(1)}, f32[1,2,5120]{2,1,0:T(2,128)}, u32[]{:S(2)}) copy-start(f32[1,2,5120]{2,1,0:T(2,128)} %param.16) | copy-start | bytes 122884
  15.6 5.4 %copy-start.1 = (bf16[1,128,5120]{2,1,0:T(8,128)(2,1)S(1)}, bf16[1,128,5120]{2,1,0:T(8,128)(2,1)}, u32[]{:S(2)}) copy-start(bf16[1,128,5120]{2,1,0:T(8,128)(2,1)} %param.15) | copy-start | bytes 3932164
  18.1 4.4 %copy-start.5 = (f32[1,128,64]{1,2,0:T(8,128)S(1)}, f32[1,128,64]{1,2,0:T(8,128)}, u32[]{:S(2)}) copy-start(f32[1,128,64]{1,2,0:T(8,128)} %param.18) | copy-start | bytes 98308
  18.1 60.2 %collective-permute-start.8 = (bf16[3,128,512]{2,1,0:T(8,128)(2,1)}, bf16[3,128,512]{2,1,0:T(8,128)(2,1)S(1)}, u32[]{:S(2)}, u32[]{:S(2)}) collective-permute-start(bf16[3,128,512]{2,1,0:T(8,128)(2,1)} %get-tuple-element.4), channel_id=1, source_target_pairs={{0,12},{4,0},{8,4},{12,8},{1,13},{5,1},{9,5},{13,9},{2,14},{6,2},{... | collective-permute-start | bytes 1179656 | tf_op jit(solution)/shard_map/ppermute | solution.py:21
  22.5 0.9 copy-start.3
  22.5 14.8 %copy-start.4 = (s32[32,4]{0,1:T(4,128)S(1)}, s32[32,4]{0,1:T(4,128)}, u32[]{:S(2)}) copy-start(s32[32,4]{0,1:T(4,128)} %param.20) | copy-start | bytes 1540
  23.3 1.7 %collective-permute-start.12 = (f32[1,128,64]{1,2,0:T(8,128)S(1)}, f32[1,128,64]{1,2,0:T(8,128)S(1)}, u32[]{:S(2)}, u32[]{:S(2)}) collective-permute-start(f32[1,128,64]{1,2,0:T(8,128)S(1)} %fusion.15), channel_id=1, source_target_pairs={{0,3},{1,0},{2,1},{3,2},{4,7},{5,4},{6,5},{7,6},{8,11},{9,8},{10,9... | collective-permute-start | bytes 98312 | tf_op jit(solution)/shard_map/ppermute | solution.py:21
  25.0 57.8 %collective-permute-start.7 = (bf16[3,128,512]{2,1,0:T(8,128)(2,1)}, bf16[3,128,512]{2,1,0:T(8,128)(2,1)S(1)}, u32[]{:S(2)}, u32[]{:S(2)}) collective-permute-start(bf16[3,128,512]{2,1,0:T(8,128)(2,1)} %get-tuple-element.5), channel_id=1, source_target_pairs={{0,8},{4,12},{8,0},{12,4},{1,9},{5,13},{9,1},{13,5},{2,10},{6,14},... | collective-permute-start | bytes 1179656 | tf_op jit(solution)/shard_map/ppermute | solution.py:21
  26.1 56.7 %collective-permute-start.6 = (bf16[3,128,512]{2,1,0:T(8,128)(2,1)}, bf16[3,128,512]{2,1,0:T(8,128)(2,1)}, u32[]{:S(2)}, u32[]{:S(2)}) collective-permute-start(bf16[3,128,512]{2,1,0:T(8,128)(2,1)} %get-tuple-element.6), channel_id=1, source_target_pairs={{0,4},{4,8},{8,12},{12,0},{1,5},{5,9},{9,13},{13,1},{2,6},{6,10},{... | collective-permute-start | bytes 1179656 | tf_op jit(solution)/shard_map/ppermute | solution.py:21
  58.9 41.9 %collective-permute-start.3 = (bf16[128,512]{1,0:T(8,128)(2,1)S(1)}, bf16[128,512]{1,0:T(8,128)(2,1)S(1)}, u32[]{:S(2)}, u32[]{:S(2)}) collective-permute-start(bf16[128,512]{1,0:T(8,128)(2,1)S(1)} %get-tuple-element.17), channel_id=1, source_target_pairs={{0,12},{4,0},{8,4},{12,8},{1,13},{5,1},{9,5},{13,9},{2,14},{6,2},{... | collective-permute-start | bytes 393224 | tf_op jit(solution)/shard_map/ppermute | solution.py:21
  58.9 43.8 %collective-permute-start.4 = (bf16[128,512]{1,0:T(8,128)(2,1)S(1)}, bf16[128,512]{1,0:T(8,128)(2,1)S(1)}, u32[]{:S(2)}, u32[]{:S(2)}) collective-permute-start(bf16[128,512]{1,0:T(8,128)(2,1)S(1)} %get-tuple-element.16), channel_id=1, source_target_pairs={{0,8},{4,12},{8,0},{12,4},{1,9},{5,13},{9,1},{13,5},{2,10},{6,14},... | collective-permute-start | bytes 393224 | tf_op jit(solution)/shard_map/ppermute | solution.py:21
  78.3 24.4 %collective-permute-start.5 = (bf16[128,512]{1,0:T(8,128)(2,1)S(1)}, bf16[128,512]{1,0:T(8,128)(2,1)S(1)}, u32[]{:S(2)}, u32[]{:S(2)}) collective-permute-start(bf16[128,512]{1,0:T(8,128)(2,1)S(1)} %get-tuple-element.15), channel_id=1, source_target_pairs={{0,4},{4,8},{8,12},{12,0},{1,5},{5,9},{9,13},{13,1},{2,6},{6,10},{... | collective-permute-start | bytes 393224 | tf_op jit(solution)/shard_map/ppermute | solution.py:21
  95.3 8.9 %collective-permute-start.9 = (bf16[128,512]{1,0:T(8,128)(2,1)S(1)}, bf16[128,512]{1,0:T(8,128)(2,1)S(1)}, u32[]{:S(2)}, u32[]{:S(2)}) collective-permute-start(bf16[128,512]{1,0:T(8,128)(2,1)S(1)} %get-tuple-element.13), channel_id=1, source_target_pairs={{0,12},{4,0},{8,4},{12,8},{1,13},{5,1},{9,5},{13,9},{2,14},{6,2},{... | collective-permute-start | bytes 393224 | tf_op jit(solution)/shard_map/ppermute | solution.py:21
  95.3 16.0 %collective-permute-start.10 = (bf16[128,512]{1,0:T(8,128)(2,1)S(1)}, bf16[128,512]{1,0:T(8,128)(2,1)S(1)}, u32[]{:S(2)}, u32[]{:S(2)}) collective-permute-start(bf16[128,512]{1,0:T(8,128)(2,1)S(1)} %get-tuple-element.12), channel_id=1, source_target_pairs={{0,8},{4,12},{8,0},{12,4},{1,9},{5,13},{9,1},{13,5},{2,10},{6,14},... | collective-permute-start | bytes 393224 | tf_op jit(solution)/shard_map/ppermute | solution.py:21
  100.8 10.5 %collective-permute-start.11 = (bf16[128,512]{1,0:T(8,128)(2,1)S(1)}, bf16[128,512]{1,0:T(8,128)(2,1)S(1)}, u32[]{:S(2)}, u32[]{:S(2)}) collective-permute-start(bf16[128,512]{1,0:T(8,128)(2,1)S(1)} %get-tuple-element.11), channel_id=1, source_target_pairs={{0,4},{4,8},{8,12},{12,0},{1,5},{5,9},{9,13},{13,1},{2,6},{6,10},{... | collective-permute-start | bytes 393224 | tf_op jit(solution)/shard_map/ppermute | solution.py:21

commit v5 on v4

--- a/solution.py
+++ b/solution.py
@@ -8,7 +8,7 @@
 from jax.sharding import PartitionSpec as P
 
 STEPS = 8
-CHUNKS = 2
+CHUNKS = 4
 
 
 epsilon = 1e-06

time: 116 us -> 119 us (1.026)
  starting transfers between devices: 50.2 us -> 40.2 us
  Pallas kernels: 26.5 us -> 34.7 us
  waiting for transfers between devices: 18.2 us -> 11.7 us
  local copies, waits for them, and re-layouts: 10.9 us -> 17.4 us
  other arithmetic: 7.39 us -> 11.9 us
    ppermute x13 -> x25, starting transfers between devices: 50.2 us -> 40.2 us  [passed_along(): return lax.ppermute(value, axis, pairs)]
    ppermute x13 -> x25, waiting for transfers between devices: 18.2 us -> 11.7 us  [passed_along(): return lax.ppermute(value, axis, pairs)]
    pallas_call x2 -> x4, Pallas kernels: 6.36 us -> 11.5 us  [packed_chunk(): pl.pallas_call(kernel, in_specs=[pl.BlockSpec(memory_space=pltpu.VMEM)] *...]
    another operation x2 -> x4, other arithmetic: 3.74 us -> 7.05 us  [local(): packed = jnp.stack(pieces)]
    pallas_call x2 -> x4, Pallas kernels: 17.9 us -> 20.8 us  [attend_heads(): pl.pallas_call(kernel, in_specs=[pl.BlockSpec(memory_space=smem), pl.Bloc...]
    squeeze x2 -> x4, local copies, waits for them, and re-layouts: 2.26 us -> 4.42 us  [local(): outs.append(passed_along(attended[step], 'seq', -step))]
    reshape x2 -> x4, local copies, waits for them, and re-layouts: 1.25 us -> 2.58 us  [attend_heads(): live.reshape(-1)]
    reshape x2 -> x4, local copies, waits for them, and re-layouts: 1.29 us -> 2.57 us  [attend_heads(): lists.reshape(-1)]
  transfers between devices with their start and end apart: 13 -> 25, of which waited for: 4 -> 5; matrix products, arithmetic and copies ran while one was open for 13% -> 21% of each run, Pallas kernels for 18% -> 25%
where the time goes in v5:
time: 119 us; the launch traced here: 118 us
  starting transfers between devices  40.2 us (34%)
  Pallas kernels  34.7 us (29%)
  local copies, waits for them, and re-layouts  17.4 us (15%)
  other arithmetic  11.9 us (10%)
  waiting for transfers between devices  11.7 us (10%)
  between operations  1.64 us (1%)
    ppermute x25, starting transfers between devices, passed_along(): return lax.ppermute(value, axis, pairs)  40.2 us
    pallas_call x4, Pallas kernels, attend_heads(): pl.pallas_call(kernel, in_specs=[pl.BlockSpec(memory_space=smem), pl.Bloc...  20.8 us
    ppermute x25, waiting for transfers between devices, passed_along(): return lax.ppermute(value, axis, pairs)  11.7 us
    pallas_call x4, Pallas kernels, packed_chunk(): pl.pallas_call(kernel, in_specs=[pl.BlockSpec(memory_space=pltpu.VMEM)] *...  11.5 us
    another operation x4, other arithmetic, local(): packed = jnp.stack(pieces)  7.05 us
    dynamic_slice x4, local copies, waits for them, and re-layouts, local(): pieces = [lax.dynamic_index_in_dim(send, own_index, 0, keepdims=False)]  4.98 us
    squeeze x4, local copies, waits for them, and re-layouts, local(): outs.append(passed_along(attended[step], 'seq', -step))  4.42 us
    concatenate x4, other arithmetic, local(): back = jnp.roll(jnp.stack(outs), own_index, axis=0)  4.06 us
  transfers between devices with their start and end apart: 25, of which 5 were waited for; matrix products, arithmetic and copies ran while one was open for 21% of the time, Pallas kernels for 25%

profile of v5, /device:TPU:0, one launch (start us, length us, event | category | flops | bytes accessed | tf_op | source)
XLA Modules:
  0.0 118.3 jit_solution(12356956777066633103)
XLA Ops:
  0.7 2.9 %shard_map.113 = bf16[4,3,128,256]{3,2,1,0:T(8,128)(2,1)} custom-call(bf16[1,128,4096]{2,1,0:T(8,128)(2,1)} %query_ref.7, bf16[1,128,4096]{2,1,0:T(8,128)(2,1)} %key_ref.7, bf16[1,128,4096]{2,1,0:T(8,128)(2,1)} %value_ref.7), custom_call_target="tpu_custom_call" | custom-call | tf_op jit(solution)/shard_map/pallas_call | solution.py:118
  3.6 2.0 %constant_dynamic-slice_fusion.9 = (bf16[1,3,128,256]{3,2,1,0:T(8,128)(2,1)S(1)}, bf16[3,128,256]{2,1,0:T(8,128)(2,1)}, bf16[3,128,256]{2,1,0:T(8,128)(2,1)}, bf16[3,128,256]{2,1,0:T(8,128)(2,1)}) fusion(bf16[4,3,128,256]{3,2,1,0:T(8,128)(2,1)} %shard_map.113, s32[]{:T(128)S(6)} %select_n.84, s32[]{:T(128)S(6)} %select_n.90, s32[]{:T(128)S(6)} %select_n.88, ...), kind=kLoop, calls=%fused_computation.111 | loop fusion | bytes 1572880 | tf_op jit(solution)/shard_map/jit(dynamic_index_in_dim)/dynamic_slice | solution.py:176
  5.6 5.1 %collective-permute-start.2 = (bf16[3,128,256]{2,1,0:T(8,128)(2,1)}, bf16[3,128,256]{2,1,0:T(8,128)(2,1)}, u32[]{:S(2)}, u32[]{:S(2)}) collective-permute-start(bf16[3,128,256]{2,1,0:T(8,128)(2,1)} %get-tuple-element.16), channel_id=1, source_target_pairs={{0,12},{4,0},{8,4},{12,8},{1,13},{5,1},{9,5},{13,9},{2,14},{6,2},{... | collective-permute-start | bytes 589832 | tf_op jit(solution)/shard_map/ppermute | solution.py:21
  11.7 2.8 %shard_map.115 = bf16[4,3,128,256]{3,2,1,0:T(8,128)(2,1)} custom-call(bf16[1,128,4096]{2,1,0:T(8,128)(2,1)} %query_ref.7, bf16[1,128,4096]{2,1,0:T(8,128)(2,1)} %key_ref.7, bf16[1,128,4096]{2,1,0:T(8,128)(2,1)} %value_ref.7), custom_call_target="tpu_custom_call" | custom-call | tf_op jit(solution)/shard_map/pallas_call | solution.py:118
  14.6 2.1 %constant_dynamic-slice_fusion.6 = (bf16[1,3,128,256]{3,2,1,0:T(8,128)(2,1)S(1)}, bf16[3,128,256]{2,1,0:T(8,128)(2,1)}, bf16[3,128,256]{2,1,0:T(8,128)(2,1)S(1)}, bf16[3,128,256]{2,1,0:T(8,128)(2,1)S(1)}) fusion(bf16[4,3,128,256]{3,2,1,0:T(8,128)(2,1)} %shard_map.115, s32[]{:T(128)S(6)} %select_n.84, s32[]{:T(128)S(6)} %select_n.90, s32[]{:T(128)S(6)} %select_n.88, ...), kind=kLoop, calls=%fused_computation.108 | loop fusion | bytes 1572880 | tf_op jit(solution)/shard_map/jit(dynamic_index_in_dim)/dynamic_slice | solution.py:176
  16.6 2.8 %collective-permute-start.8 = (bf16[3,128,256]{2,1,0:T(8,128)(2,1)}, bf16[3,128,256]{2,1,0:T(8,128)(2,1)S(1)}, u32[]{:S(2)}, u32[]{:S(2)}) collective-permute-start(bf16[3,128,256]{2,1,0:T(8,128)(2,1)} %get-tuple-element.12), channel_id=1, source_target_pairs={{0,12},{4,0},{8,4},{12,8},{1,13},{5,1},{9,5},{13,9},{2,14},{6,2},{... | collective-permute-start | bytes 589832 | tf_op jit(solution)/shard_map/ppermute | solution.py:21
  22.0 2.8 %shard_map.117 = bf16[4,3,128,256]{3,2,1,0:T(8,128)(2,1)} custom-call(bf16[1,128,4096]{2,1,0:T(8,128)(2,1)} %query_ref.7, bf16[1,128,4096]{2,1,0:T(8,128)(2,1)} %key_ref.7, bf16[1,128,4096]{2,1,0:T(8,128)(2,1)} %value_ref.7), custom_call_target="tpu_custom_call" | custom-call | tf_op jit(solution)/shard_map/pallas_call | solution.py:118
  24.8 2.9 %shard_map.119 = bf16[4,3,128,256]{3,2,1,0:T(8,128)(2,1)} custom-call(bf16[1,128,4096]{2,1,0:T(8,128)(2,1)} %query_ref.7, bf16[1,128,4096]{2,1,0:T(8,128)(2,1)} %key_ref.7, bf16[1,128,4096]{2,1,0:T(8,128)(2,1)} %value_ref.7), custom_call_target="tpu_custom_call" | custom-call | tf_op jit(solution)/shard_map/pallas_call | solution.py:118
  36.5 3.8 %collective-permute-start.14 = (bf16[3,128,256]{2,1,0:T(8,128)(2,1)}, bf16[3,128,256]{2,1,0:T(8,128)(2,1)S(1)}, u32[]{:S(2)}, u32[]{:S(2)}) collective-permute-start(bf16[3,128,256]{2,1,0:T(8,128)(2,1)} %get-tuple-element.8), channel_id=1, source_target_pairs={{0,12},{4,0},{8,4},{12,8},{1,13},{5,1},{9,5},{13,9},{2,14},{6,2},{... | collective-permute-start | bytes 589832 | tf_op jit(solution)/shard_map/ppermute | solution.py:21
  40.3 2.1 %pad_maximum_fusion.x_ref = bf16[4,3,128,256]{3,2,1,0:T(8,128)(2,1)} fusion(bf16[1,3,128,256]{3,2,1,0:T(8,128)(2,1)} %bitcast.6, bf16[1,3,128,256]{3,2,1,0:T(8,128)(2,1)} %bitcast.4, bf16[1,3,128,256]{3,2,1,0:T(8,128)(2,1)} %bitcast.2, bf16[1,3,128,256]{3,2,1,0:T(8,128)(2,1)S(1)} %get-tuple-element.15), kind=kLoop, calls=%fused_computation.13 | loop fusion | flops 1179648 | bytes 1572864 | tf_op jit(solution)/shard_map/stack | solution.py:181
  42.5 5.2 %shard_map.114 = bf16[4,128,256]{2,1,0:T(8,128)(2,1)} custom-call(s32[32]{0:T(128)} %reshape.72.lists_ref, s32[8]{0:T(128)} %reshape.73.live_ref, s32[1]{0:T(128)} %bitcast.me_ref, bf16[4,3,128,256]{3,2,1,0:T(8,128)(2,1)} %pad_maximum_fusion.x_ref), custom_call_target="tpu_custom_call" | custom-call | tf_op jit(solution)/shard_map/pallas_call | solution.py:95
  53.8 6.9 %collective-permute-start.19 = (bf16[3,128,256]{2,1,0:T(8,128)(2,1)S(1)}, bf16[3,128,256]{2,1,0:T(8,128)(2,1)S(1)}, u32[]{:S(2)}, u32[]{:S(2)}) collective-permute-start(bf16[3,128,256]{2,1,0:T(8,128)(2,1)S(1)} %get-tuple-element.5), channel_id=1, source_target_pairs={{0,8},{4,12},{8,0},{12,4},{1,9},{5,13},{9,1},{13,5},{2,10},{6,14},... | collective-permute-start | bytes 589832 | tf_op jit(solution)/shard_map/ppermute | solution.py:21
  60.7 2.0 %pad_maximum_fusion.1.x_ref = bf16[4,3,128,256]{3,2,1,0:T(8,128)(2,1)} fusion(bf16[1,3,128,256]{3,2,1,0:T(8,128)(2,1)S(1)} %bitcast.104, bf16[1,3,128,256]{3,2,1,0:T(8,128)(2,1)} %bitcast.109, bf16[1,3,128,256]{3,2,1,0:T(8,128)(2,1)} %bitcast.14, bf16[1,3,128,256]{3,2,1,0:T(8,128)(2,1)S(1)} %get-tuple-element.11), kind=kLoop, calls=%fused_computation.14 | loop fusion | flops 1179648 | bytes 1572864 | tf_op jit(solution)/shard_map/stack | solution.py:181
  62.7 5.2 %shard_map.116 = bf16[4,128,256]{2,1,0:T(8,128)(2,1)} custom-call(s32[32]{0:T(128)} %reshape.75.lists_ref, s32[8]{0:T(128)} %reshape.76.live_ref, s32[1]{0:T(128)} %bitcast.me_ref, bf16[4,3,128,256]{3,2,1,0:T(8,128)(2,1)} %pad_maximum_fusion.1.x_ref), custom_call_target="tpu_custom_call" | custom-call | tf_op jit(solution)/shard_map/pallas_call | solution.py:95
  68.9 5.3 %collective-permute-done.13 = bf16[3,128,256]{2,1,0:T(8,128)(2,1)S(1)} collective-permute-done((bf16[3,128,256]{2,1,0:T(8,128)(2,1)}, bf16[3,128,256]{2,1,0:T(8,128)(2,1)S(1)}, u32[]{:S(2)}, u32[]{:S(2)}) %collective-permute-start.13) | collective-permute-done | bytes 196640 | tf_op jit(solution)/shard_map/ppermute | solution.py:21
  74.3 4.0 %collective-permute-start.4 = (bf16[128,256]{1,0:T(8,128)(2,1)S(1)}, bf16[128,256]{1,0:T(8,128)(2,1)S(1)}, u32[]{:S(2)}, u32[]{:S(2)}) collective-permute-start(bf16[128,256]{1,0:T(8,128)(2,1)S(1)} %get-tuple-element.32), channel_id=1, source_target_pairs={{0,8},{4,12},{8,0},{12,4},{1,9},{5,13},{9,1},{13,5},{2,10},{6,14},... | collective-permute-start | bytes 196616 | tf_op jit(solution)/shard_map/ppermute | solution.py:21
  78.3 1.9 %pad_maximum_fusion.2.x_ref = bf16[4,3,128,256]{3,2,1,0:T(8,128)(2,1)} fusion(bf16[1,3,128,256]{3,2,1,0:T(8,128)(2,1)S(1)} %bitcast.105, bf16[1,3,128,256]{3,2,1,0:T(8,128)(2,1)S(1)} %bitcast.107, bf16[1,3,128,256]{3,2,1,0:T(8,128)(2,1)} %bitcast.26, bf16[1,3,128,256]{3,2,1,0:T(8,128)(2,1)S(1)} %get-tuple-element.7), kind=kLoop, calls=%fused_computation.15 | loop fusion | flops 1179648 | bytes 1572864 | tf_op jit(solution)/shard_map/stack | solution.py:181
  80.2 5.2 %shard_map.118 = bf16[4,128,256]{2,1,0:T(8,128)(2,1)} custom-call(s32[32]{0:T(128)} %reshape.77.lists_ref, s32[8]{0:T(128)} %reshape.78.live_ref, s32[1]{0:T(128)} %bitcast.me_ref, bf16[4,3,128,256]{3,2,1,0:T(8,128)(2,1)} %pad_maximum_fusion.2.x_ref), custom_call_target="tpu_custom_call" | custom-call | tf_op jit(solution)/shard_map/pallas_call | solution.py:95
  86.4 3.8 %collective-permute-start.9 = (bf16[128,256]{1,0:T(8,128)(2,1)S(1)}, bf16[128,256]{1,0:T(8,128)(2,1)S(1)}, u32[]{:S(2)}, u32[]{:S(2)}) collective-permute-start(bf16[128,256]{1,0:T(8,128)(2,1)S(1)} %get-tuple-element.29), channel_id=1, source_target_pairs={{0,12},{4,0},{8,4},{12,8},{1,13},{5,1},{9,5},{13,9},{2,14},{6,2},{... | collective-permute-start | bytes 196616 | tf_op jit(solution)/shard_map/ppermute | solution.py:21
  91.2 5.2 %shard_map.120 = bf16[4,128,256]{2,1,0:T(8,128)(2,1)} custom-call(s32[32]{0:T(128)} %reshape.79.lists_ref, s32[8]{0:T(128)} %reshape.80.live_ref, s32[1]{0:T(128)} %bitcast.me_ref, bf16[4,3,128,256]{3,2,1,0:T(8,128)(2,1)} %pad_maximum_fusion.3.x_ref), custom_call_target="tpu_custom_call" | custom-call | tf_op jit(solution)/shard_map/pallas_call | solution.py:95
  98.1 3.2 %collective-permute-start.15 = (bf16[128,256]{1,0:T(8,128)(2,1)S(1)}, bf16[128,256]{1,0:T(8,128)(2,1)S(1)}, u32[]{:S(2)}, u32[]{:S(2)}) collective-permute-start(bf16[128,256]{1,0:T(8,128)(2,1)S(1)} %get-tuple-element.25), channel_id=1, source_target_pairs={{0,12},{4,0},{8,4},{12,8},{1,13},{5,1},{9,5},{13,9},{2,14},{6,2},{... | collective-permute-start | bytes 196616 | tf_op jit(solution)/shard_map/ppermute | solution.py:21
  103.5 3.8 %collective-permute-start.21 = (bf16[128,256]{1,0:T(8,128)(2,1)S(1)}, bf16[128,256]{1,0:T(8,128)(2,1)S(1)}, u32[]{:S(2)}, u32[]{:S(2)}) collective-permute-start(bf16[128,256]{1,0:T(8,128)(2,1)S(1)} %get-tuple-element.21), channel_id=1, source_target_pairs={{0,12},{4,0},{8,4},{12,8},{1,13},{5,1},{9,5},{13,9},{2,14},{6,2},{... | collective-permute-start | bytes 196616 | tf_op jit(solution)/shard_map/ppermute | solution.py:21
  112.4 1.9 %collective-permute-done.23 = bf16[128,256]{1,0:T(8,128)(2,1)S(1)} collective-permute-done((bf16[128,256]{1,0:T(8,128)(2,1)S(1)}, bf16[128,256]{1,0:T(8,128)(2,1)S(1)}, u32[]{:S(2)}, u32[]{:S(2)}) %collective-permute-start.23) | collective-permute-done | bytes 65568 | tf_op jit(solution)/shard_map/ppermute | solution.py:21
  115.3 2.3 %shard_map.121 = bf16[1,128,4096]{2,1,0:T(8,128)(2,1)} custom-call(bf16[4,128,256]{2,1,0:T(8,128)(2,1)} %fusion.42.refs_0_, bf16[4,128,256]{2,1,0:T(8,128)(2,1)} %fusion.35.refs_1_, bf16[4,128,256]{2,1,0:T(8,128)(2,1)} %fusion.28.refs_2_, bf16[4,128,256]{2,1,0:T(8,128)(2,1)} %fusion.21.refs_3_), custom_call_target="tpu_custom_call" | custom-call | tf_op jit(solution)/shard_map/pallas_call | solution.py:138
  (102 shorter events, 31.3 us)
Async XLA Ops:
  5.6 30.8 %collective-permute-start.2 = (bf16[3,128,256]{2,1,0:T(8,128)(2,1)}, bf16[3,128,256]{2,1,0:T(8,128)(2,1)}, u32[]{:S(2)}, u32[]{:S(2)}) collective-permute-start(bf16[3,128,256]{2,1,0:T(8,128)(2,1)} %get-tuple-element.16), channel_id=1, source_target_pairs={{0,12},{4,0},{8,4},{12,8},{1,13},{5,1},{9,5},{13,9},{2,14},{6,2},{... | collective-permute-start | bytes 589832 | tf_op jit(solution)/shard_map/ppermute | solution.py:21
  10.7 25.8 %collective-permute-start.1 = (bf16[3,128,256]{2,1,0:T(8,128)(2,1)}, bf16[3,128,256]{2,1,0:T(8,128)(2,1)}, u32[]{:S(2)}, u32[]{:S(2)}) collective-permute-start(bf16[3,128,256]{2,1,0:T(8,128)(2,1)} %get-tuple-element.17), channel_id=1, source_target_pairs={{0,8},{4,12},{8,0},{12,4},{1,9},{5,13},{9,1},{13,5},{2,10},{6,14},... | collective-permute-start | bytes 589832 | tf_op jit(solution)/shard_map/ppermute | solution.py:21
  10.7 29.5 %collective-permute-start = (bf16[3,128,256]{2,1,0:T(8,128)(2,1)}, bf16[3,128,256]{2,1,0:T(8,128)(2,1)}, u32[]{:S(2)}, u32[]{:S(2)}) collective-permute-start(bf16[3,128,256]{2,1,0:T(8,128)(2,1)} %get-tuple-element.18), channel_id=1, source_target_pairs={{0,4},{4,8},{8,12},{12,0},{1,5},{5,9},{9,13},{13,1},{2,6},{6,10},{... | collective-permute-start | bytes 589832 | tf_op jit(solution)/shard_map/ppermute | solution.py:21
  16.6 32.6 %collective-permute-start.8 = (bf16[3,128,256]{2,1,0:T(8,128)(2,1)}, bf16[3,128,256]{2,1,0:T(8,128)(2,1)S(1)}, u32[]{:S(2)}, u32[]{:S(2)}) collective-permute-start(bf16[3,128,256]{2,1,0:T(8,128)(2,1)} %get-tuple-element.12), channel_id=1, source_target_pairs={{0,12},{4,0},{8,4},{12,8},{1,13},{5,1},{9,5},{13,9},{2,14},{6,2},{... | collective-permute-start | bytes 589832 | tf_op jit(solution)/shard_map/ppermute | solution.py:21
  21.9 13.5 %collective-permute-start.24 = (f32[1,128,64]{1,2,0:T(8,128)S(1)}, f32[1,128,64]{1,2,0:T(8,128)S(1)}, u32[]{:S(2)}, u32[]{:S(2)}) collective-permute-start(f32[1,128,64]{1,2,0:T(8,128)S(1)} %fusion.15), channel_id=1, source_target_pairs={{0,3},{1,0},{2,1},{3,2},{4,7},{5,4},{6,5},{7,6},{8,11},{9,8},{10,9... | collective-permute-start | bytes 98312 | tf_op jit(solution)/shard_map/ppermute | solution.py:21
  35.4 16.3 %collective-permute-start.7 = (bf16[3,128,256]{2,1,0:T(8,128)(2,1)S(1)}, bf16[3,128,256]{2,1,0:T(8,128)(2,1)S(1)}, u32[]{:S(2)}, u32[]{:S(2)}) collective-permute-start(bf16[3,128,256]{2,1,0:T(8,128)(2,1)S(1)} %get-tuple-element.13), channel_id=1, source_target_pairs={{0,8},{4,12},{8,0},{12,4},{1,9},{5,13},{9,1},{13,5},{2,10},{6,14},... | collective-permute-start | bytes 589832 | tf_op jit(solution)/shard_map/ppermute | solution.py:21
  36.4 17.3 %collective-permute-start.6 = (bf16[3,128,256]{2,1,0:T(8,128)(2,1)S(1)}, bf16[3,128,256]{2,1,0:T(8,128)(2,1)}, u32[]{:S(2)}, u32[]{:S(2)}) collective-permute-start(bf16[3,128,256]{2,1,0:T(8,128)(2,1)S(1)} %get-tuple-element.14), channel_id=1, source_target_pairs={{0,4},{4,8},{8,12},{12,0},{1,5},{5,9},{9,13},{13,1},{2,6},{6,10},{... | collective-permute-start | bytes 589832 | tf_op jit(solution)/shard_map/ppermute | solution.py:21
  36.5 32.4 %collective-permute-start.14 = (bf16[3,128,256]{2,1,0:T(8,128)(2,1)}, bf16[3,128,256]{2,1,0:T(8,128)(2,1)S(1)}, u32[]{:S(2)}, u32[]{:S(2)}) collective-permute-start(bf16[3,128,256]{2,1,0:T(8,128)(2,1)} %get-tuple-element.8), channel_id=1, source_target_pairs={{0,12},{4,0},{8,4},{12,8},{1,13},{5,1},{9,5},{13,9},{2,14},{6,2},{... | collective-permute-start | bytes 589832 | tf_op jit(solution)/shard_map/ppermute | solution.py:21
  40.3 34.0 %collective-permute-start.13 = (bf16[3,128,256]{2,1,0:T(8,128)(2,1)}, bf16[3,128,256]{2,1,0:T(8,128)(2,1)S(1)}, u32[]{:S(2)}, u32[]{:S(2)}) collective-permute-start(bf16[3,128,256]{2,1,0:T(8,128)(2,1)} %get-tuple-element.9), channel_id=1, source_target_pairs={{0,8},{4,12},{8,0},{12,4},{1,9},{5,13},{9,1},{13,5},{2,10},{6,14},... | collective-permute-start | bytes 589832 | tf_op jit(solution)/shard_map/ppermute | solution.py:21
  49.3 25.0 %collective-permute-start.12 = (bf16[3,128,256]{2,1,0:T(8,128)(2,1)S(1)}, bf16[3,128,256]{2,1,0:T(8,128)(2,1)}, u32[]{:S(2)}, u32[]{:S(2)}) collective-permute-start(bf16[3,128,256]{2,1,0:T(8,128)(2,1)S(1)} %copy-done.4), channel_id=1, source_target_pairs={{0,4},{4,8},{8,12},{12,0},{1,5},{5,9},{9,13},{13,1},{2,6},{6,10},{... | collective-permute-start | bytes 589832 | tf_op jit(solution)/shard_map/ppermute | solution.py:21
  52.3 34.0 %collective-permute-start.20 = (bf16[3,128,256]{2,1,0:T(8,128)(2,1)S(1)}, bf16[3,128,256]{2,1,0:T(8,128)(2,1)S(1)}, u32[]{:S(2)}, u32[]{:S(2)}) collective-permute-start(bf16[3,128,256]{2,1,0:T(8,128)(2,1)S(1)} %get-tuple-element.4), channel_id=1, source_target_pairs={{0,12},{4,0},{8,4},{12,8},{1,13},{5,1},{9,5},{13,9},{2,14},{6,2},{... | collective-permute-start | bytes 589832 | tf_op jit(solution)/shard_map/ppermute | solution.py:21
  53.8 32.7 %collective-permute-start.19 = (bf16[3,128,256]{2,1,0:T(8,128)(2,1)S(1)}, bf16[3,128,256]{2,1,0:T(8,128)(2,1)S(1)}, u32[]{:S(2)}, u32[]{:S(2)}) collective-permute-start(bf16[3,128,256]{2,1,0:T(8,128)(2,1)S(1)} %get-tuple-element.5), channel_id=1, source_target_pairs={{0,8},{4,12},{8,0},{12,4},{1,9},{5,13},{9,1},{13,5},{2,10},{6,14},... | collective-permute-start | bytes 589832 | tf_op jit(solution)/shard_map/ppermute | solution.py:21
  68.9 21.4 %collective-permute-start.18 = (bf16[3,128,256]{2,1,0:T(8,128)(2,1)S(1)}, bf16[3,128,256]{2,1,0:T(8,128)(2,1)S(1)}, u32[]{:S(2)}, u32[]{:S(2)}) collective-permute-start(bf16[3,128,256]{2,1,0:T(8,128)(2,1)S(1)} %get-tuple-element.6), channel_id=1, source_target_pairs={{0,4},{4,8},{8,12},{12,0},{1,5},{5,9},{9,13},{13,1},{2,6},{6,10},{... | collective-permute-start | bytes 589832 | tf_op jit(solution)/shard_map/ppermute | solution.py:21
  74.3 23.1 %collective-permute-start.3 = (bf16[128,256]{1,0:T(8,128)(2,1)S(1)}, bf16[128,256]{1,0:T(8,128)(2,1)S(1)}, u32[]{:S(2)}, u32[]{:S(2)}) collective-permute-start(bf16[128,256]{1,0:T(8,128)(2,1)S(1)} %copy-done.7), channel_id=1, source_target_pairs={{0,12},{4,0},{8,4},{12,8},{1,13},{5,1},{9,5},{13,9},{2,14},{6,2},{... | collective-permute-start | bytes 196616 | tf_op jit(solution)/shard_map/ppermute | solution.py:21
  74.3 23.8 %collective-permute-start.4 = (bf16[128,256]{1,0:T(8,128)(2,1)S(1)}, bf16[128,256]{1,0:T(8,128)(2,1)S(1)}, u32[]{:S(2)}, u32[]{:S(2)}) collective-permute-start(bf16[128,256]{1,0:T(8,128)(2,1)S(1)} %get-tuple-element.32), channel_id=1, source_target_pairs={{0,8},{4,12},{8,0},{12,4},{1,9},{5,13},{9,1},{13,5},{2,10},{6,14},... | collective-permute-start | bytes 196616 | tf_op jit(solution)/shard_map/ppermute | solution.py:21
  86.3 14.9 %collective-permute-start.5 = (bf16[128,256]{1,0:T(8,128)(2,1)S(1)}, bf16[128,256]{1,0:T(8,128)(2,1)S(1)}, u32[]{:S(2)}, u32[]{:S(2)}) collective-permute-start(bf16[128,256]{1,0:T(8,128)(2,1)S(1)} %get-tuple-element.31), channel_id=1, source_target_pairs={{0,4},{4,8},{8,12},{12,0},{1,5},{5,9},{9,13},{13,1},{2,6},{6,10},{... | collective-permute-start | bytes 196616 | tf_op jit(solution)/shard_map/ppermute | solution.py:21
  86.4 17.0 %collective-permute-start.9 = (bf16[128,256]{1,0:T(8,128)(2,1)S(1)}, bf16[128,256]{1,0:T(8,128)(2,1)S(1)}, u32[]{:S(2)}, u32[]{:S(2)}) collective-permute-start(bf16[128,256]{1,0:T(8,128)(2,1)S(1)} %get-tuple-element.29), channel_id=1, source_target_pairs={{0,12},{4,0},{8,4},{12,8},{1,13},{5,1},{9,5},{13,9},{2,14},{6,2},{... | collective-permute-start | bytes 196616 | tf_op jit(solution)/shard_map/ppermute | solution.py:21
  90.2 13.3 %collective-permute-start.10 = (bf16[128,256]{1,0:T(8,128)(2,1)S(1)}, bf16[128,256]{1,0:T(8,128)(2,1)S(1)}, u32[]{:S(2)}, u32[]{:S(2)}) collective-permute-start(bf16[128,256]{1,0:T(8,128)(2,1)S(1)} %get-tuple-element.28), channel_id=1, source_target_pairs={{0,8},{4,12},{8,0},{12,4},{1,9},{5,13},{9,1},{13,5},{2,10},{6,14},... | collective-permute-start | bytes 196616 | tf_op jit(solution)/shard_map/ppermute | solution.py:21
  97.4 9.9 %collective-permute-start.11 = (bf16[128,256]{1,0:T(8,128)(2,1)S(1)}, bf16[128,256]{1,0:T(8,128)(2,1)S(1)}, u32[]{:S(2)}, u32[]{:S(2)}) collective-permute-start(bf16[128,256]{1,0:T(8,128)(2,1)S(1)} %get-tuple-element.27), channel_id=1, source_target_pairs={{0,4},{4,8},{8,12},{12,0},{1,5},{5,9},{9,13},{13,1},{2,6},{6,10},{... | collective-permute-start | bytes 196616 | tf_op jit(solution)/shard_map/ppermute | solution.py:21
  98.1 10.2 %collective-permute-start.15 = (bf16[128,256]{1,0:T(8,128)(2,1)S(1)}, bf16[128,256]{1,0:T(8,128)(2,1)S(1)}, u32[]{:S(2)}, u32[]{:S(2)}) collective-permute-start(bf16[128,256]{1,0:T(8,128)(2,1)S(1)} %get-tuple-element.25), channel_id=1, source_target_pairs={{0,12},{4,0},{8,4},{12,8},{1,13},{5,1},{9,5},{13,9},{2,14},{6,2},{... | collective-permute-start | bytes 196616 | tf_op jit(solution)/shard_map/ppermute | solution.py:21
  101.3 8.8 %collective-permute-start.16 = (bf16[128,256]{1,0:T(8,128)(2,1)S(1)}, bf16[128,256]{1,0:T(8,128)(2,1)S(1)}, u32[]{:S(2)}, u32[]{:S(2)}) collective-permute-start(bf16[128,256]{1,0:T(8,128)(2,1)S(1)} %get-tuple-element.24), channel_id=1, source_target_pairs={{0,8},{4,12},{8,0},{12,4},{1,9},{5,13},{9,1},{13,5},{2,10},{6,14},... | collective-permute-start | bytes 196616 | tf_op jit(solution)/shard_map/ppermute | solution.py:21
  103.4 6.7 %collective-permute-start.17 = (bf16[128,256]{1,0:T(8,128)(2,1)S(1)}, bf16[128,256]{1,0:T(8,128)(2,1)S(1)}, u32[]{:S(2)}, u32[]{:S(2)}) collective-permute-start(bf16[128,256]{1,0:T(8,128)(2,1)S(1)} %get-tuple-element.23), channel_id=1, source_target_pairs={{0,4},{4,8},{8,12},{12,0},{1,5},{5,9},{9,13},{13,1},{2,6},{6,10},{... | collective-permute-start | bytes 196616 | tf_op jit(solution)/shard_map/ppermute | solution.py:21
  103.5 7.6 %collective-permute-start.21 = (bf16[128,256]{1,0:T(8,128)(2,1)S(1)}, bf16[128,256]{1,0:T(8,128)(2,1)S(1)}, u32[]{:S(2)}, u32[]{:S(2)}) collective-permute-start(bf16[128,256]{1,0:T(8,128)(2,1)S(1)} %get-tuple-element.21), channel_id=1, source_target_pairs={{0,12},{4,0},{8,4},{12,8},{1,13},{5,1},{9,5},{13,9},{2,14},{6,2},{... | collective-permute-start | bytes 196616 | tf_op jit(solution)/shard_map/ppermute | solution.py:21
  108.3 6.1 %collective-permute-start.23 = (bf16[128,256]{1,0:T(8,128)(2,1)S(1)}, bf16[128,256]{1,0:T(8,128)(2,1)S(1)}, u32[]{:S(2)}, u32[]{:S(2)}) collective-permute-start(bf16[128,256]{1,0:T(8,128)(2,1)S(1)} %get-tuple-element.19), channel_id=1, source_target_pairs={{0,4},{4,8},{8,12},{12,0},{1,5},{5,9},{9,13},{13,1},{2,6},{6,10},{... | collective-permute-start | bytes 196616 | tf_op jit(solution)/shard_map/ppermute | solution.py:21
  (14 other events, 78.4 us)

commit v6 on v4

--- a/solution.py
+++ b/solution.py
@@ -27,50 +27,88 @@
 
 
 def attend_kernel(
-    lists_ref, live_ref, me_ref, x_ref, o_ref, *, block, slots, qblocks, heads, depth, shifted
+    lists_ref,
+    live_ref,
+    me_ref,
+    x_ref,
+    o_ref,
+    scores_ref,
+    highest_ref,
+    totals_ref,
+    mixed_ref,
+    *,
+    block,
+    slots,
+    qblocks,
+    heads,
+    depth,
+    shifted,
 ):
     sources, _, tokens, _ = x_ref.shape
     me = me_ref[0]
+    scale = depth ** (-0.5)
+    per_source = tokens // block
 
     def slot_of(device):
         if shifted:
             return (me - device + sources) % sources
         return device
 
-    total = sources * tokens
-    scale = depth ** (-0.5)
-    column = lax.broadcasted_iota(jnp.int32, (1, total), 1)
-    per_source = tokens // block
     for head in range(heads):
         cols = slice(head * depth, (head + 1) * depth)
-        keys = x_ref[:, 1, :, cols].reshape(total, depth)
-        values = x_ref[:, 2, :, cols].reshape(total, depth)
 
         def body(qblock, carry):
             source = slot_of(qblock // per_source)
             first = pl.multiple_of((qblock % per_source) * block, block)
             query = x_ref[source, 0, pl.ds(first, block), cols]
-            scores = (
-                lax.dot_general(
-                    query, keys, (((1,), (1,)), ((), ())), preferred_element_type=jnp.float32
+            entry = head * qblocks + qblock
+            live = live_ref[entry]
+
+            def rows_of(slot):
+                chosen = lists_ref[entry * slots + slot]
+                low = pl.multiple_of((chosen % per_source) * block, block)
+                return slot_of(chosen // per_source), low
+
+            def score(slot):
+                place, low = rows_of(slot)
+                keys = x_ref[place, 1, pl.ds(low, block), cols]
+                scores = (
+                    lax.dot_general(
+                        query, keys, (((1,), (1,)), ((), ())), preferred_element_type=jnp.float32
+                    )
+                    * scale
                 )
-                * scale
-            )
-            live = live_ref[head * qblocks + qblock]
-            active = column < 0
-            for slot in range(slots):
-                chosen = lists_ref[(head * qblocks + qblock) * slots + slot]
-                place = slot_of(chosen // per_source)
-                low = place * tokens + (chosen % per_source) * block
-                active = active | ((column >= low) & (column < low + block) & (slot < live))
-            scores = jnp.where(active, scores, -jnp.inf)
-            highest = jnp.max(scores, axis=1, keepdims=True)
-            weights = jnp.exp(scores - highest)
-            totals = jnp.sum(weights, axis=1, keepdims=True)
-            mixed = jnp.dot(
-                weights.astype(jnp.bfloat16), values, preferred_element_type=jnp.float32
-            )
-            o_ref[source, pl.ds(first, block), cols] = (mixed / totals).astype(o_ref.dtype)
+                scores_ref[slot] = scores
+                return jnp.max(scores, axis=1, keepdims=True)
+
+            highest_ref[...] = score(0)
+            for slot in range(1, slots):
+
+                @pl.when(slot < live)
+                def _():
+                    highest_ref[...] = jnp.maximum(highest_ref[...], score(slot))
+
+            def mix(slot):
+                place, low = rows_of(slot)
+                weights = jnp.exp(scores_ref[slot] - highest_ref[...])
+                values = x_ref[place, 2, pl.ds(low, block), cols]
+                mixed = jnp.dot(
+                    weights.astype(jnp.bfloat16), values, preferred_element_type=jnp.float32
+                )
+                return jnp.sum(weights, axis=1, keepdims=True), mixed
+
+            totals_ref[...], mixed_ref[...] = mix(0)
+            for slot in range(1, slots):
+
+                @pl.when(slot < live)
+                def _():
+                    totals, mixed = mix(slot)
+                    totals_ref[...] += totals
+                    mixed_ref[...] += mixed
+
+            o_ref[source, pl.ds(first, block), cols] = (
+                mixed_ref[...] / totals_ref[...]
+            ).astype(o_ref.dtype)
             return carry
 
         lax.fori_loop(0, qblocks, body, 0)
@@ -102,6 +140,12 @@
         ],
         out_specs=pl.BlockSpec(memory_space=pltpu.VMEM),
         out_shape=jax.ShapeDtypeStruct((sources, tokens, width), jnp.bfloat16),
+        scratch_shapes=[
+            pltpu.VMEM((slots, block, block), jnp.float32),
+            pltpu.VMEM((block, 1), jnp.float32),
+            pltpu.VMEM((block, 1), jnp.float32),
+            pltpu.VMEM((block, depth), jnp.float32),
+        ],
     )(lists.reshape(-1), live.reshape(-1), me.reshape(1), packed)
 
 

time: 116 us -> 132 us (1.14)
  Pallas kernels: 26.5 us -> 49.1 us
  starting transfers between devices: 50.2 us -> 46.7 us
  waiting for transfers between devices: 18.2 us -> 15.8 us
    pallas_call x2, Pallas kernels: 17.9 us -> 40.5 us  [attend_heads(): pl.pallas_call(kernel, in_specs=[pl.BlockSpec(memory_space=smem), pl.Bloc...]
    ppermute x13, starting transfers between devices: 50.2 us -> 46.7 us  [passed_along(): return lax.ppermute(value, axis, pairs)]
    ppermute x13, waiting for transfers between devices: 18.2 us -> 15.8 us  [passed_along(): return lax.ppermute(value, axis, pairs)]
  transfers between devices with their start and end apart: 13 -> 13, of which waited for: 4 -> 4; matrix products, arithmetic and copies ran while one was open for 13% -> 11% of each run, Pallas kernels for 18% -> 33%
where the time goes in v6:
time: 132 us
  Pallas kernels  49.1 us (37%)
  starting transfers between devices  46.7 us (35%)
  waiting for transfers between devices  15.8 us (12%)
  local copies, waits for them, and re-layouts  10.9 us (8%)
  other arithmetic  7.39 us (6%)
  between operations  1.53 us (1%)
    ppermute x13, starting transfers between devices, passed_along(): return lax.ppermute(value, axis, pairs)  46.7 us
    pallas_call x2, Pallas kernels, attend_heads(): pl.pallas_call(kernel, in_specs=[pl.BlockSpec(memory_space=smem), pl.Bloc...  40.5 us
    ppermute x13, waiting for transfers between devices, passed_along(): return lax.ppermute(value, axis, pairs)  15.8 us
    pallas_call x2, Pallas kernels, packed_chunk(): pl.pallas_call(kernel, in_specs=[pl.BlockSpec(memory_space=pltpu.VMEM)] *...  6.36 us
    dynamic_slice x2, local copies, waits for them, and re-layouts, local(): pieces = [lax.dynamic_index_in_dim(send, own_index, 0, keepdims=False)]  4.93 us
    another operation x2, other arithmetic, local(): packed = jnp.stack(pieces)  3.74 us
    concatenate x2, other arithmetic, local(): back = jnp.roll(jnp.stack(outs), own_index, axis=0)  2.84 us
  transfers between devices with their start and end apart: 13, of which 4 were waited for; matrix products, arithmetic and copies ran while one was open for 11% of the time, Pallas kernels for 33%

profile of v6, /device:TPU:0, one launch (start us, length us, event | category | flops | bytes accessed | tf_op | source)
XLA Modules:
  0.0 132.3 jit_solution(6443481747266325908)
XLA Ops:
  0.7 3.2 %shard_map.113 = bf16[4,3,128,512]{3,2,1,0:T(8,128)(2,1)} custom-call(bf16[1,128,4096]{2,1,0:T(8,128)(2,1)} %query_ref.3, bf16[1,128,4096]{2,1,0:T(8,128)(2,1)} %key_ref.3, bf16[1,128,4096]{2,1,0:T(8,128)(2,1)} %value_ref.3), custom_call_target="tpu_custom_call" | custom-call | tf_op jit(solution)/shard_map/pallas_call | solution.py:162
  3.9 2.4 %constant_dynamic-slice_fusion.3 = (bf16[1,3,128,512]{3,2,1,0:T(8,128)(2,1)S(1)}, bf16[3,128,512]{2,1,0:T(8,128)(2,1)}, bf16[3,128,512]{2,1,0:T(8,128)(2,1)}, bf16[3,128,512]{2,1,0:T(8,128)(2,1)}) fusion(bf16[4,3,128,512]{3,2,1,0:T(8,128)(2,1)} %shard_map.113, s32[]{:T(128)S(6)} %select_n.56, s32[]{:T(128)S(6)} %select_n.62, s32[]{:T(128)S(6)} %select_n.60, ...), kind=kLoop, calls=%fused_computation.61 | loop fusion | bytes 3145744 | tf_op jit(solution)/shard_map/jit(dynamic_index_in_dim)/dynamic_slice | solution.py:220
  6.3 5.1 %collective-permute-start.2 = (bf16[3,128,512]{2,1,0:T(8,128)(2,1)}, bf16[3,128,512]{2,1,0:T(8,128)(2,1)S(1)}, u32[]{:S(2)}, u32[]{:S(2)}) collective-permute-start(bf16[3,128,512]{2,1,0:T(8,128)(2,1)} %get-tuple-element.8), channel_id=1, source_target_pairs={{0,12},{4,0},{8,4},{12,8},{1,13},{5,1},{9,5},{13,9},{2,14},{6,2},{... | collective-permute-start | bytes 1179656 | tf_op jit(solution)/shard_map/ppermute | solution.py:21
  11.4 1.0 collective-permute-start
  12.4 3.2 %shard_map.115 = bf16[4,3,128,512]{3,2,1,0:T(8,128)(2,1)} custom-call(bf16[1,128,4096]{2,1,0:T(8,128)(2,1)} %query_ref.3, bf16[1,128,4096]{2,1,0:T(8,128)(2,1)} %key_ref.3, bf16[1,128,4096]{2,1,0:T(8,128)(2,1)} %value_ref.3), custom_call_target="tpu_custom_call" | custom-call | tf_op jit(solution)/shard_map/pallas_call | solution.py:162
  15.6 2.5 %constant_dynamic-slice_fusion = (bf16[1,3,128,512]{3,2,1,0:T(8,128)(2,1)S(1)}, bf16[3,128,512]{2,1,0:T(8,128)(2,1)}, bf16[3,128,512]{2,1,0:T(8,128)(2,1)}, bf16[3,128,512]{2,1,0:T(8,128)(2,1)}) fusion(bf16[4,3,128,512]{3,2,1,0:T(8,128)(2,1)} %shard_map.115, s32[]{:T(128)S(6)} %select_n.56, s32[]{:T(128)S(6)} %select_n.62, s32[]{:T(128)S(6)} %select_n.60, ...), kind=kLoop, calls=%fused_computation.58 | loop fusion | bytes 3145744 | tf_op jit(solution)/shard_map/jit(dynamic_index_in_dim)/dynamic_slice | solution.py:220
  18.1 2.8 %collective-permute-start.8 = (bf16[3,128,512]{2,1,0:T(8,128)(2,1)}, bf16[3,128,512]{2,1,0:T(8,128)(2,1)S(1)}, u32[]{:S(2)}, u32[]{:S(2)}) collective-permute-start(bf16[3,128,512]{2,1,0:T(8,128)(2,1)} %get-tuple-element.4), channel_id=1, source_target_pairs={{0,12},{4,0},{8,4},{12,8},{1,13},{5,1},{9,5},{13,9},{2,14},{6,2},{... | collective-permute-start | bytes 1179656 | tf_op jit(solution)/shard_map/ppermute | solution.py:21
  23.5 1.5 %collective-permute-done.12 = f32[1,128,64]{1,2,0:T(8,128)S(1)} collective-permute-done((f32[1,128,64]{1,2,0:T(8,128)S(1)}, f32[1,128,64]{1,2,0:T(8,128)S(1)}, u32[]{:S(2)}, u32[]{:S(2)}) %collective-permute-start.12) | collective-permute-done | bytes 32800 | tf_op jit(solution)/shard_map/ppermute | solution.py:21
  25.0 1.0 collective-permute-start.7
  26.1 11.3 %collective-permute-start.6 = (bf16[3,128,512]{2,1,0:T(8,128)(2,1)}, bf16[3,128,512]{2,1,0:T(8,128)(2,1)}, u32[]{:S(2)}, u32[]{:S(2)}) collective-permute-start(bf16[3,128,512]{2,1,0:T(8,128)(2,1)} %get-tuple-element.6), channel_id=1, source_target_pairs={{0,4},{4,8},{8,12},{12,0},{1,5},{5,9},{9,13},{13,1},{2,6},{6,10},{... | collective-permute-start | bytes 1179656 | tf_op jit(solution)/shard_map/ppermute | solution.py:21
  40.4 7.0 %collective-permute-done.1 = bf16[3,128,512]{2,1,0:T(8,128)(2,1)S(1)} collective-permute-done((bf16[3,128,512]{2,1,0:T(8,128)(2,1)}, bf16[3,128,512]{2,1,0:T(8,128)(2,1)S(1)}, u32[]{:S(2)}, u32[]{:S(2)}) %collective-permute-start.1) | collective-permute-done | bytes 393248 | tf_op jit(solution)/shard_map/ppermute | solution.py:21
  47.4 1.4 %pad_maximum_fusion.x_ref = bf16[4,3,128,512]{3,2,1,0:T(8,128)(2,1)} fusion(bf16[1,3,128,512]{3,2,1,0:T(8,128)(2,1)S(1)} %bitcast.69, bf16[1,3,128,512]{3,2,1,0:T(8,128)(2,1)S(1)} %bitcast.70, bf16[1,3,128,512]{3,2,1,0:T(8,128)(2,1)S(1)} %bitcast.71, bf16[1,3,128,512]{3,2,1,0:T(8,128)(2,1)S(1)} %get-tuple-element.7), kind=kLoop, calls=%fused_computation.9 | loop fusion | flops 2359296 | bytes 3145728 | tf_op jit(solution)/shard_map/stack | solution.py:225
  48.8 18.2 %shard_map.114 = bf16[4,128,512]{2,1,0:T(8,128)(2,1)} custom-call(s32[64]{0:T(128)} %reshape.58.lists_ref, s32[16]{0:T(128)} %reshape.59.live_ref, s32[1]{0:T(128)} %bitcast.me_ref, bf16[4,3,128,512]{3,2,1,0:T(8,128)(2,1)} %pad_maximum_fusion.x_ref), custom_call_target="tpu_custom_call" | custom-call | tf_op jit(solution)/shard_map/pallas_call | solution.py:133
  67.0 1.1 slice_bitcast_fusion.3
  68.2 23.2 %collective-permute-start.4 = (bf16[128,512]{1,0:T(8,128)(2,1)S(1)}, bf16[128,512]{1,0:T(8,128)(2,1)S(1)}, u32[]{:S(2)}, u32[]{:S(2)}) collective-permute-start(bf16[128,512]{1,0:T(8,128)(2,1)S(1)} %get-tuple-element.16), channel_id=1, source_target_pairs={{0,8},{4,12},{8,0},{12,4},{1,9},{5,13},{9,1},{13,5},{2,10},{6,14},... | collective-permute-start | bytes 393224 | tf_op jit(solution)/shard_map/ppermute | solution.py:21
  91.5 2.4 %pad_maximum_fusion.1.x_ref = bf16[4,3,128,512]{3,2,1,0:T(8,128)(2,1)} fusion(bf16[1,3,128,512]{3,2,1,0:T(8,128)(2,1)S(1)} %bitcast.68, bf16[1,3,128,512]{3,2,1,0:T(8,128)(2,1)S(1)} %bitcast.72, bf16[1,3,128,512]{3,2,1,0:T(8,128)(2,1)} %bitcast.14, bf16[1,3,128,512]{3,2,1,0:T(8,128)(2,1)S(1)} %get-tuple-element.3), kind=kLoop, calls=%fused_computation.10 | loop fusion | flops 2359296 | bytes 3145728 | tf_op jit(solution)/shard_map/stack | solution.py:225
  93.8 22.3 %shard_map.116 = bf16[4,128,512]{2,1,0:T(8,128)(2,1)} custom-call(s32[64]{0:T(128)} %reshape.61.lists_ref, s32[16]{0:T(128)} %reshape.62.live_ref, s32[1]{0:T(128)} %bitcast.me_ref, bf16[4,3,128,512]{3,2,1,0:T(8,128)(2,1)} %pad_maximum_fusion.1.x_ref), custom_call_target="tpu_custom_call" | custom-call | tf_op jit(solution)/shard_map/pallas_call | solution.py:133
  116.1 1.1 slice_bitcast_fusion
  118.0 1.3 collective-permute-start.11
  119.3 1.4 %fusion.28.refs_0_ = bf16[4,128,512]{2,1,0:T(8,128)(2,1)} fusion(s32[]{:T(128)S(6)} %select_n.67, bf16[1,128,512]{2,1,0:T(8,128)(2,1)S(1)} %get-tuple-element.18, bf16[1,128,512]{2,1,0:T(8,128)(2,1)S(1)} %bitcast.73, bf16[1,128,512]{2,1,0:T(8,128)(2,1)S(1)} %bitcast.74, bf16[1,128,512]{2,1,0:T(8,128)(2,1)S(1)} %bitcast.75), kind=kLoop, calls=%fused_computation.41 | loop fusion | flops 1835008 | bytes 1048580 | tf_op jit(solution)/shard_map/jit(_roll_dynamic)/concatenate | solution.py:238
  120.7 1.5 %collective-permute-done.9 = bf16[128,512]{1,0:T(8,128)(2,1)S(1)} collective-permute-done((bf16[128,512]{1,0:T(8,128)(2,1)S(1)}, bf16[128,512]{1,0:T(8,128)(2,1)S(1)}, u32[]{:S(2)}, u32[]{:S(2)}) %collective-permute-start.9) | collective-permute-done | bytes 131104 | tf_op jit(solution)/shard_map/ppermute | solution.py:21
  122.2 5.7 %collective-permute-done.10 = bf16[128,512]{1,0:T(8,128)(2,1)S(1)} collective-permute-done((bf16[128,512]{1,0:T(8,128)(2,1)S(1)}, bf16[128,512]{1,0:T(8,128)(2,1)S(1)}, u32[]{:S(2)}, u32[]{:S(2)}) %collective-permute-start.10) | collective-permute-done | bytes 131104 | tf_op jit(solution)/shard_map/ppermute | solution.py:21
  128.0 1.4 %fusion.21.refs_1_ = bf16[4,128,512]{2,1,0:T(8,128)(2,1)} fusion(s32[]{:T(128)S(6)} %select_n.67, bf16[1,128,512]{2,1,0:T(8,128)(2,1)S(1)} %get-tuple-element.14, bf16[1,128,512]{2,1,0:T(8,128)(2,1)S(1)} %bitcast.76, bf16[1,128,512]{2,1,0:T(8,128)(2,1)S(1)} %bitcast.77, bf16[1,128,512]{2,1,0:T(8,128)(2,1)S(1)} %bitcast.78), kind=kLoop, calls=%fused_computation.34 | loop fusion | flops 1835008 | bytes 1048580 | tf_op jit(solution)/shard_map/jit(_roll_dynamic)/concatenate | solution.py:238
  129.4 2.2 %shard_map.117 = bf16[1,128,4096]{2,1,0:T(8,128)(2,1)} custom-call(bf16[4,128,512]{2,1,0:T(8,128)(2,1)} %fusion.28.refs_0_, bf16[4,128,512]{2,1,0:T(8,128)(2,1)} %fusion.21.refs_1_), custom_call_target="tpu_custom_call" | custom-call | tf_op jit(solution)/shard_map/pallas_call | solution.py:182
  (44 shorter events, 6.3 us)
Async XLA Ops:
  0.6 21.9 %copy-start = (bf16[5120,64]{0,1:T(8,128)(2,1)S(1)}, bf16[5120,64]{0,1:T(8,128)(2,1)}, u32[]{:S(2)}) copy-start(bf16[5120,64]{0,1:T(8,128)(2,1)} %param.17) | copy-start | bytes 1966084
  6.3 19.8 %collective-permute-start.2 = (bf16[3,128,512]{2,1,0:T(8,128)(2,1)}, bf16[3,128,512]{2,1,0:T(8,128)(2,1)S(1)}, u32[]{:S(2)}, u32[]{:S(2)}) collective-permute-start(bf16[3,128,512]{2,1,0:T(8,128)(2,1)} %get-tuple-element.8), channel_id=1, source_target_pairs={{0,12},{4,0},{8,4},{12,8},{1,13},{5,1},{9,5},{13,9},{2,14},{6,2},{... | collective-permute-start | bytes 1179656 | tf_op jit(solution)/shard_map/ppermute | solution.py:21
  11.4 36.0 %collective-permute-start.1 = (bf16[3,128,512]{2,1,0:T(8,128)(2,1)}, bf16[3,128,512]{2,1,0:T(8,128)(2,1)S(1)}, u32[]{:S(2)}, u32[]{:S(2)}) collective-permute-start(bf16[3,128,512]{2,1,0:T(8,128)(2,1)} %get-tuple-element.9), channel_id=1, source_target_pairs={{0,8},{4,12},{8,0},{12,4},{1,9},{5,13},{9,1},{13,5},{2,10},{6,14},... | collective-permute-start | bytes 1179656 | tf_op jit(solution)/shard_map/ppermute | solution.py:21
  11.4 36.0 %collective-permute-start = (bf16[3,128,512]{2,1,0:T(8,128)(2,1)}, bf16[3,128,512]{2,1,0:T(8,128)(2,1)S(1)}, u32[]{:S(2)}, u32[]{:S(2)}) collective-permute-start(bf16[3,128,512]{2,1,0:T(8,128)(2,1)} %get-tuple-element.10), channel_id=1, source_target_pairs={{0,4},{4,8},{8,12},{12,0},{1,5},{5,9},{9,13},{13,1},{2,6},{6,10},{... | collective-permute-start | bytes 1179656 | tf_op jit(solution)/shard_map/ppermute | solution.py:21
  15.6 5.3 %copy-start.2 = (f32[1,2,5120]{2,1,0:T(2,128)S(1)}, f32[1,2,5120]{2,1,0:T(2,128)}, u32[]{:S(2)}) copy-start(f32[1,2,5120]{2,1,0:T(2,128)} %param.16) | copy-start | bytes 122884
  15.6 5.4 %copy-start.1 = (bf16[1,128,5120]{2,1,0:T(8,128)(2,1)S(1)}, bf16[1,128,5120]{2,1,0:T(8,128)(2,1)}, u32[]{:S(2)}) copy-start(bf16[1,128,5120]{2,1,0:T(8,128)(2,1)} %param.15) | copy-start | bytes 3932164
  18.1 4.4 %copy-start.5 = (f32[1,128,64]{1,2,0:T(8,128)S(1)}, f32[1,128,64]{1,2,0:T(8,128)}, u32[]{:S(2)}) copy-start(f32[1,128,64]{1,2,0:T(8,128)} %param.18) | copy-start | bytes 98308
  18.1 73.4 %collective-permute-start.8 = (bf16[3,128,512]{2,1,0:T(8,128)(2,1)}, bf16[3,128,512]{2,1,0:T(8,128)(2,1)S(1)}, u32[]{:S(2)}, u32[]{:S(2)}) collective-permute-start(bf16[3,128,512]{2,1,0:T(8,128)(2,1)} %get-tuple-element.4), channel_id=1, source_target_pairs={{0,12},{4,0},{8,4},{12,8},{1,13},{5,1},{9,5},{13,9},{2,14},{6,2},{... | collective-permute-start | bytes 1179656 | tf_op jit(solution)/shard_map/ppermute | solution.py:21
  22.5 0.9 copy-start.3
  22.5 14.8 %copy-start.4 = (s32[32,4]{0,1:T(4,128)S(1)}, s32[32,4]{0,1:T(4,128)}, u32[]{:S(2)}) copy-start(s32[32,4]{0,1:T(4,128)} %param.20) | copy-start | bytes 1540
  23.3 1.7 %collective-permute-start.12 = (f32[1,128,64]{1,2,0:T(8,128)S(1)}, f32[1,128,64]{1,2,0:T(8,128)S(1)}, u32[]{:S(2)}, u32[]{:S(2)}) collective-permute-start(f32[1,128,64]{1,2,0:T(8,128)S(1)} %fusion.15), channel_id=1, source_target_pairs={{0,3},{1,0},{2,1},{3,2},{4,7},{5,4},{6,5},{7,6},{8,11},{9,8},{10,9... | collective-permute-start | bytes 98312 | tf_op jit(solution)/shard_map/ppermute | solution.py:21
  25.0 66.4 %collective-permute-start.7 = (bf16[3,128,512]{2,1,0:T(8,128)(2,1)}, bf16[3,128,512]{2,1,0:T(8,128)(2,1)S(1)}, u32[]{:S(2)}, u32[]{:S(2)}) collective-permute-start(bf16[3,128,512]{2,1,0:T(8,128)(2,1)} %get-tuple-element.5), channel_id=1, source_target_pairs={{0,8},{4,12},{8,0},{12,4},{1,9},{5,13},{9,1},{13,5},{2,10},{6,14},... | collective-permute-start | bytes 1179656 | tf_op jit(solution)/shard_map/ppermute | solution.py:21
  26.1 65.4 %collective-permute-start.6 = (bf16[3,128,512]{2,1,0:T(8,128)(2,1)}, bf16[3,128,512]{2,1,0:T(8,128)(2,1)}, u32[]{:S(2)}, u32[]{:S(2)}) collective-permute-start(bf16[3,128,512]{2,1,0:T(8,128)(2,1)} %get-tuple-element.6), channel_id=1, source_target_pairs={{0,4},{4,8},{8,12},{12,0},{1,5},{5,9},{9,13},{13,1},{2,6},{6,10},{... | collective-permute-start | bytes 1179656 | tf_op jit(solution)/shard_map/ppermute | solution.py:21
  68.2 49.9 %collective-permute-start.3 = (bf16[128,512]{1,0:T(8,128)(2,1)S(1)}, bf16[128,512]{1,0:T(8,128)(2,1)S(1)}, u32[]{:S(2)}, u32[]{:S(2)}) collective-permute-start(bf16[128,512]{1,0:T(8,128)(2,1)S(1)} %get-tuple-element.17), channel_id=1, source_target_pairs={{0,12},{4,0},{8,4},{12,8},{1,13},{5,1},{9,5},{13,9},{2,14},{6,2},{... | collective-permute-start | bytes 393224 | tf_op jit(solution)/shard_map/ppermute | solution.py:21
  68.2 51.1 %collective-permute-start.4 = (bf16[128,512]{1,0:T(8,128)(2,1)S(1)}, bf16[128,512]{1,0:T(8,128)(2,1)S(1)}, u32[]{:S(2)}, u32[]{:S(2)}) collective-permute-start(bf16[128,512]{1,0:T(8,128)(2,1)S(1)} %get-tuple-element.16), channel_id=1, source_target_pairs={{0,8},{4,12},{8,0},{12,4},{1,9},{5,13},{9,1},{13,5},{2,10},{6,14},... | collective-permute-start | bytes 393224 | tf_op jit(solution)/shard_map/ppermute | solution.py:21
  91.4 27.9 %collective-permute-start.5 = (bf16[128,512]{1,0:T(8,128)(2,1)S(1)}, bf16[128,512]{1,0:T(8,128)(2,1)S(1)}, u32[]{:S(2)}, u32[]{:S(2)}) collective-permute-start(bf16[128,512]{1,0:T(8,128)(2,1)S(1)} %get-tuple-element.15), channel_id=1, source_target_pairs={{0,4},{4,8},{8,12},{12,0},{1,5},{5,9},{9,13},{13,1},{2,6},{6,10},{... | collective-permute-start | bytes 393224 | tf_op jit(solution)/shard_map/ppermute | solution.py:21
  117.2 5.0 %collective-permute-start.9 = (bf16[128,512]{1,0:T(8,128)(2,1)S(1)}, bf16[128,512]{1,0:T(8,128)(2,1)S(1)}, u32[]{:S(2)}, u32[]{:S(2)}) collective-permute-start(bf16[128,512]{1,0:T(8,128)(2,1)S(1)} %get-tuple-element.13), channel_id=1, source_target_pairs={{0,12},{4,0},{8,4},{12,8},{1,13},{5,1},{9,5},{13,9},{2,14},{6,2},{... | collective-permute-start | bytes 393224 | tf_op jit(solution)/shard_map/ppermute | solution.py:21
  118.0 10.0 %collective-permute-start.10 = (bf16[128,512]{1,0:T(8,128)(2,1)S(1)}, bf16[128,512]{1,0:T(8,128)(2,1)S(1)}, u32[]{:S(2)}, u32[]{:S(2)}) collective-permute-start(bf16[128,512]{1,0:T(8,128)(2,1)S(1)} %get-tuple-element.12), channel_id=1, source_target_pairs={{0,8},{4,12},{8,0},{12,4},{1,9},{5,13},{9,1},{13,5},{2,10},{6,14},... | collective-permute-start | bytes 393224 | tf_op jit(solution)/shard_map/ppermute | solution.py:21
  118.0 10.0 %collective-permute-start.11 = (bf16[128,512]{1,0:T(8,128)(2,1)S(1)}, bf16[128,512]{1,0:T(8,128)(2,1)S(1)}, u32[]{:S(2)}, u32[]{:S(2)}) collective-permute-start(bf16[128,512]{1,0:T(8,128)(2,1)S(1)} %get-tuple-element.11), channel_id=1, source_target_pairs={{0,4},{4,8},{8,12},{12,0},{1,5},{5,9},{9,13},{13,1},{2,6},{6,10},{... | collective-permute-start | bytes 393224 | tf_op jit(solution)/shard_map/ppermute | solution.py:21

commit v7 on v5

--- a/solution.py
+++ b/solution.py
@@ -8,7 +8,6 @@
 from jax.sharding import PartitionSpec as P
 
 STEPS = 8
-CHUNKS = 4
 
 
 epsilon = 1e-06
@@ -123,18 +122,19 @@
     )(query_rows, key_rows, value_rows)
 
 
-def unpack_kernel(*refs, seq, stride, width):
+def unpack_kernel(*refs, seq, stride, offsets):
     chunks = len(refs) - 1
     out_ref = refs[chunks]
     for c in range(chunks):
+        width = refs[c].shape[2]
         for group in range(seq):
-            low = group * stride + c * width
+            low = group * stride + offsets[c]
             out_ref[0, :, low:low + width] = refs[c][group]
 
 
-def unpacked(backs, seq, stride, width):
+def unpacked(backs, seq, stride, offsets):
     tokens = backs[0].shape[1]
-    kernel = functools.partial(unpack_kernel, seq=seq, stride=stride, width=width)
+    kernel = functools.partial(unpack_kernel, seq=seq, stride=stride, offsets=tuple(offsets))
     return pl.pallas_call(
         kernel,
         in_specs=[pl.BlockSpec(memory_space=pltpu.VMEM)] * len(backs),
@@ -159,19 +159,25 @@
     own_index = lax.axis_index("seq")
     head_count = live_counts.shape[0]
     per_device = head_count // seq_count
-    chunks = CHUNKS if per_device % CHUNKS == 0 else 1
-    per_chunk = per_device // chunks
+    if per_device % 4 == 0:
+        sizes = [per_device * 3 // 4, per_device // 4]
+    else:
+        sizes = [per_device]
+    starts = [sum(sizes[:c]) for c in range(len(sizes))]
     tokens = query_rows.shape[1]
     width = query_rows.shape[2]
     depth = width // head_count
-    chunk_width = per_chunk * depth
     permuted = seq_count <= 8
 
     backs = []
-    for c in range(chunks):
+    previous = None
+    for per_chunk, start in zip(sizes, starts):
+        chunk_width = per_chunk * depth
         send = packed_chunk(
-            query_rows, key_rows, value_rows, seq_count, per_device * depth, c * chunk_width, chunk_width
+            query_rows, key_rows, value_rows, seq_count, per_device * depth, start * depth, chunk_width
         )
+        if previous is not None:
+            send, _ = lax.optimization_barrier((send, previous))
         if permuted:
             pieces = [lax.dynamic_index_in_dim(send, own_index, 0, keepdims=False)]
             for step in range(1, seq_count):
@@ -183,9 +189,10 @@
         else:
             packed = lax.all_to_all(send, "seq", 0, 0, tiled=True)
             place = jnp.zeros((), jnp.int32)
-        first = own_index * per_device + c * per_chunk
+        first = own_index * per_device + start
         lists = lax.dynamic_slice_in_dim(block_lists, first, per_chunk, 0)
         live = lax.dynamic_slice_in_dim(live_counts, first, per_chunk, 0)
+        previous = packed
         attended = attend_heads(packed, lists, live, place.astype(jnp.int32), permuted)
         if permuted:
             outs = [attended[0]]
@@ -195,7 +202,7 @@
         else:
             back = lax.all_to_all(attended, "seq", 0, 0, tiled=True)
         backs.append(back)
-    mixed_back = unpacked(backs, seq_count, per_device * depth, chunk_width)
+    mixed_back = unpacked(backs, seq_count, per_device * depth, [s * depth for s in starts])
 
     source = hidden_state[0].astype(jnp.float32)
     mean_row = jnp.mean(source, axis=1, keepdims=True)

time: 119 us -> 114 us (0.958)
  waiting for transfers between devices: 11.7 us -> 33.4 us
  Pallas kernels: 34.7 us -> 26.4 us
  starting transfers between devices: 40.2 us -> 32 us
  other arithmetic: 11.9 us -> 4.63 us
  local copies, waits for them, and re-layouts: 17.4 us -> 14.9 us
    ppermute x25 -> x13, waiting for transfers between devices: 11.7 us -> 33.4 us  [passed_along(): return lax.ppermute(value, axis, pairs)]
    ppermute x25 -> x13, starting transfers between devices: 40.2 us -> 32 us  [passed_along(): return lax.ppermute(value, axis, pairs)]
    pallas_call x4 -> x2, Pallas kernels: 11.5 us -> 6.33 us  [packed_chunk(): pl.pallas_call(kernel, in_specs=[pl.BlockSpec(memory_space=pltpu.VMEM)] *...]
    concatenate x4 -> x0, other arithmetic: 4.06 us -> none  [local(): back = jnp.roll(jnp.stack(outs), own_index, axis=0)]
    another operation x4 -> x2, other arithmetic: 7.05 us -> 3.81 us  [local(): packed = jnp.stack(pieces)]
    pallas_call x4 -> x2, Pallas kernels: 20.8 us -> 17.8 us  [attend_heads(): pl.pallas_call(kernel, in_specs=[pl.BlockSpec(memory_space=smem), pl.Bloc...]
    dynamic_slice x0 -> x2, local copies, waits for them, and re-layouts: none -> 1.67 us  [local(): back = jnp.roll(jnp.stack(outs), own_index, axis=0)]
    squeeze x4 -> x2, local copies, waits for them, and re-layouts: 4.42 us -> 2.92 us  [local(): outs.append(passed_along(attended[step], 'seq', -step))]
  transfers between devices with their start and end apart: 25 -> 13, of which waited for: 5 -> 3; matrix products, arithmetic and copies ran while one was open for 21% -> 10% of each run, Pallas kernels for 25% -> 18%
where the time goes in v7:
time: 114 us
  waiting for transfers between devices  33.4 us (29%)
  starting transfers between devices  32 us (28%)
  Pallas kernels  26.4 us (23%)
  local copies, waits for them, and re-layouts  14.9 us (13%)
  other arithmetic  4.63 us (4%)
  between operations  1.65 us (1%)
    ppermute x13, waiting for transfers between devices, passed_along(): return lax.ppermute(value, axis, pairs)  33.4 us
    ppermute x13, starting transfers between devices, passed_along(): return lax.ppermute(value, axis, pairs)  32 us
    pallas_call x2, Pallas kernels, attend_heads(): pl.pallas_call(kernel, in_specs=[pl.BlockSpec(memory_space=smem), pl.Bloc...  17.8 us
    pallas_call x2, Pallas kernels, packed_chunk(): pl.pallas_call(kernel, in_specs=[pl.BlockSpec(memory_space=pltpu.VMEM)] *...  6.33 us
    another operation x2, other arithmetic, local(): packed = jnp.stack(pieces)  3.81 us
    dynamic_slice x2, local copies, waits for them, and re-layouts, local(): pieces = [lax.dynamic_index_in_dim(send, own_index, 0, keepdims=False)]  3.79 us
    unnamed x29, local copies, waits for them, and re-layouts  3.22 us
    squeeze x2, local copies, waits for them, and re-layouts, local(): outs.append(passed_along(attended[step], 'seq', -step))  2.92 us
  transfers between devices with their start and end apart: 13, of which 3 were waited for; matrix products, arithmetic and copies ran while one was open for 10% of the time, Pallas kernels for 18%

profile of v7, /device:TPU:0, one launch (start us, length us, event | category | flops | bytes accessed | tf_op | source)
XLA Modules:
  0.0 113.7 jit_solution(13898263639248221638)
XLA Ops:
  0.7 3.5 %shard_map.113 = bf16[4,3,128,768]{3,2,1,0:T(8,128)(2,1)} custom-call(bf16[1,128,4096]{2,1,0:T(8,128)(2,1)} %query_ref.3, bf16[1,128,4096]{2,1,0:T(8,128)(2,1)} %key_ref.3, bf16[1,128,4096]{2,1,0:T(8,128)(2,1)} %value_ref.3), custom_call_target="tpu_custom_call" | custom-call | tf_op jit(solution)/shard_map/pallas_call | solution.py:117
  4.2 2.9 %constant_dynamic-slice_fusion.5 = (bf16[1,3,128,768]{3,2,1,0:T(8,128)(2,1)S(1)}, bf16[3,128,768]{2,1,0:T(8,128)(2,1)}, bf16[3,128,768]{2,1,0:T(8,128)(2,1)}, bf16[3,128,768]{2,1,0:T(8,128)(2,1)}) fusion(bf16[4,3,128,768]{3,2,1,0:T(8,128)(2,1)} %shard_map.113, s32[]{:T(128)S(6)} %select_n.66, s32[]{:T(128)S(6)} %select_n.72, s32[]{:T(128)S(6)} %select_n.70, ...), kind=kLoop, calls=%fused_computation.49 | loop fusion | bytes 4718608 | tf_op jit(solution)/shard_map/jit(dynamic_index_in_dim)/dynamic_slice | solution.py:182
  7.1 3.1 %collective-permute-start = (bf16[3,128,768]{2,1,0:T(8,128)(2,1)}, bf16[3,128,768]{2,1,0:T(8,128)(2,1)S(1)}, u32[]{:S(2)}, u32[]{:S(2)}) collective-permute-start(bf16[3,128,768]{2,1,0:T(8,128)(2,1)} %get-tuple-element.7), channel_id=1, source_target_pairs={{0,4},{4,8},{8,12},{12,0},{1,5},{5,9},{9,13},{13,1},{2,6},{6,10},{... | collective-permute-start | bytes 1769480 | tf_op jit(solution)/shard_map/ppermute | solution.py:20
  10.2 2.6 %collective-permute-start.1 = (bf16[3,128,768]{2,1,0:T(8,128)(2,1)}, bf16[3,128,768]{2,1,0:T(8,128)(2,1)S(1)}, u32[]{:S(2)}, u32[]{:S(2)}) collective-permute-start(bf16[3,128,768]{2,1,0:T(8,128)(2,1)} %get-tuple-element.6), channel_id=1, source_target_pairs={{0,8},{4,12},{8,0},{12,4},{1,9},{5,13},{9,1},{13,5},{2,10},{6,14},... | collective-permute-start | bytes 1769480 | tf_op jit(solution)/shard_map/ppermute | solution.py:20
  12.8 1.3 %collective-permute-start.2 = (bf16[3,128,768]{2,1,0:T(8,128)(2,1)}, bf16[3,128,768]{2,1,0:T(8,128)(2,1)S(1)}, u32[]{:S(2)}, u32[]{:S(2)}) collective-permute-start(bf16[3,128,768]{2,1,0:T(8,128)(2,1)} %get-tuple-element.5), channel_id=1, source_target_pairs={{0,12},{4,0},{8,4},{12,8},{1,13},{5,1},{9,5},{13,9},{2,14},{6,2},{... | collective-permute-start | bytes 1769480 | tf_op jit(solution)/shard_map/ppermute | solution.py:20
  17.0 2.8 %shard_map.115 = bf16[4,3,128,256]{3,2,1,0:T(8,128)(2,1)} custom-call(bf16[1,128,4096]{2,1,0:T(8,128)(2,1)} %query_ref.3, bf16[1,128,4096]{2,1,0:T(8,128)(2,1)} %key_ref.3, bf16[1,128,4096]{2,1,0:T(8,128)(2,1)} %value_ref.3), custom_call_target="tpu_custom_call" | custom-call | tf_op jit(solution)/shard_map/pallas_call | solution.py:117
  22.8 3.9 %collective-permute-done = bf16[3,128,768]{2,1,0:T(8,128)(2,1)S(1)} collective-permute-done((bf16[3,128,768]{2,1,0:T(8,128)(2,1)}, bf16[3,128,768]{2,1,0:T(8,128)(2,1)S(1)}, u32[]{:S(2)}, u32[]{:S(2)}) %collective-permute-start) | collective-permute-done | bytes 589856 | tf_op jit(solution)/shard_map/ppermute | solution.py:20
  26.7 24.4 %collective-permute-done.1 = bf16[3,128,768]{2,1,0:T(8,128)(2,1)S(1)} collective-permute-done((bf16[3,128,768]{2,1,0:T(8,128)(2,1)}, bf16[3,128,768]{2,1,0:T(8,128)(2,1)S(1)}, u32[]{:S(2)}, u32[]{:S(2)}) %collective-permute-start.1) | collective-permute-done | bytes 589856 | tf_op jit(solution)/shard_map/ppermute | solution.py:20
  51.2 1.7 %pad_maximum_fusion.x_ref = bf16[4,3,128,768]{3,2,1,0:T(8,128)(2,1)} fusion(bf16[1,3,128,768]{3,2,1,0:T(8,128)(2,1)S(1)} %bitcast.82, bf16[1,3,128,768]{3,2,1,0:T(8,128)(2,1)S(1)} %bitcast.81, bf16[1,3,128,768]{3,2,1,0:T(8,128)(2,1)S(1)} %bitcast.80, bf16[1,3,128,768]{3,2,1,0:T(8,128)(2,1)S(1)} %get-tuple-element.4), kind=kLoop, calls=%fused_computation.9 | loop fusion | flops 3538944 | bytes 4718592 | tf_op jit(solution)/shard_map/stack | solution.py:187
  53.7 13.1 %collective-permute-start.6 = (bf16[3,128,256]{2,1,0:T(8,128)(2,1)}, bf16[3,128,256]{2,1,0:T(8,128)(2,1)S(1)}, u32[]{:S(2)}, u32[]{:S(2)}) collective-permute-start(bf16[3,128,256]{2,1,0:T(8,128)(2,1)} %get-tuple-element.11), channel_id=1, source_target_pairs={{0,4},{4,8},{8,12},{12,0},{1,5},{5,9},{9,13},{13,1},{2,6},{6,10},{... | collective-permute-start | bytes 589832 | tf_op jit(solution)/shard_map/ppermute | solution.py:20
  66.8 1.6 %collective-permute-start.7 = (bf16[3,128,256]{2,1,0:T(8,128)(2,1)}, bf16[3,128,256]{2,1,0:T(8,128)(2,1)}, u32[]{:S(2)}, u32[]{:S(2)}) collective-permute-start(bf16[3,128,256]{2,1,0:T(8,128)(2,1)} %get-tuple-element.10), channel_id=1, source_target_pairs={{0,8},{4,12},{8,0},{12,4},{1,9},{5,13},{9,1},{13,5},{2,10},{6,14},... | collective-permute-start | bytes 589832 | tf_op jit(solution)/shard_map/ppermute | solution.py:20
  69.2 12.6 %shard_map.114 = bf16[4,128,768]{2,1,0:T(8,128)(2,1)} custom-call(s32[96]{0:T(128)} %reshape.58.lists_ref, s32[24]{0:T(128)} %reshape.59.live_ref, s32[1]{0:T(128)} %bitcast.me_ref, bf16[4,3,128,768]{3,2,1,0:T(8,128)(2,1)} %pad_maximum_fusion.x_ref), custom_call_target="tpu_custom_call" | custom-call | tf_op jit(solution)/shard_map/pallas_call | solution.py:94
  81.8 2.0 %slice_bitcast_fusion = (bf16[128,768]{1,0:T(8,128)(2,1)S(1)}, bf16[8,128,768]{2,1,0:T(8,128)(2,1)S(1)}, bf16[128,768]{1,0:T(8,128)(2,1)S(1)}, bf16[128,768]{1,0:T(8,128)(2,1)}) fusion(bf16[4,128,768]{2,1,0:T(8,128)(2,1)} %shard_map.114), kind=kLoop, calls=%fused_computation.18 | loop fusion | bytes 1572864 | tf_op jit(solution)/shard_map/squeeze | solution.py:200
  83.8 2.0 %collective-permute-start.3 = (bf16[128,768]{1,0:T(8,128)(2,1)}, bf16[128,768]{1,0:T(8,128)(2,1)S(1)}, u32[]{:S(2)}, u32[]{:S(2)}) collective-permute-start(bf16[128,768]{1,0:T(8,128)(2,1)} %get-tuple-element.15), channel_id=1, source_target_pairs={{0,12},{4,0},{8,4},{12,8},{1,13},{5,1},{9,5},{13,9},{2,14},{6,2},{... | collective-permute-start | bytes 589832 | tf_op jit(solution)/shard_map/ppermute | solution.py:20
  87.2 2.1 %pad_maximum_fusion.1.x_ref = bf16[4,3,128,256]{3,2,1,0:T(8,128)(2,1)} fusion(bf16[1,3,128,256]{3,2,1,0:T(8,128)(2,1)} %bitcast.18, bf16[1,3,128,256]{3,2,1,0:T(8,128)(2,1)} %bitcast.16, bf16[1,3,128,256]{3,2,1,0:T(8,128)(2,1)} %bitcast.83, bf16[1,3,128,256]{3,2,1,0:T(8,128)(2,1)S(1)} %get-tuple-element.8), kind=kLoop, calls=%fused_computation.14 | loop fusion | flops 1179648 | bytes 1572864 | tf_op jit(solution)/shard_map/stack | solution.py:187
  89.3 5.2 %shard_map.116 = bf16[4,128,256]{2,1,0:T(8,128)(2,1)} custom-call(s32[32]{0:T(128)} %reshape.61.lists_ref, s32[8]{0:T(128)} %reshape.62.live_ref, s32[1]{0:T(128)} %bitcast.me_ref, bf16[4,3,128,256]{3,2,1,0:T(8,128)(2,1)} %pad_maximum_fusion.1.x_ref), custom_call_target="tpu_custom_call" | custom-call | tf_op jit(solution)/shard_map/pallas_call | solution.py:94
  94.5 1.0 slice_bitcast_fusion.3
  95.5 3.9 %collective-permute-start.9 = (bf16[128,256]{1,0:T(8,128)(2,1)S(1)}, bf16[128,256]{1,0:T(8,128)(2,1)S(1)}, u32[]{:S(2)}, u32[]{:S(2)}) collective-permute-start(bf16[128,256]{1,0:T(8,128)(2,1)S(1)} %get-tuple-element.19), channel_id=1, source_target_pairs={{0,12},{4,0},{8,4},{12,8},{1,13},{5,1},{9,5},{13,9},{2,14},{6,2},{... | collective-permute-start | bytes 196616 | tf_op jit(solution)/shard_map/ppermute | solution.py:20
  99.8 2.4 %collective-permute-start.11 = (bf16[128,256]{1,0:T(8,128)(2,1)S(1)}, bf16[128,256]{1,0:T(8,128)(2,1)S(1)}, u32[]{:S(2)}, u32[]{:S(2)}) collective-permute-start(bf16[128,256]{1,0:T(8,128)(2,1)S(1)} %get-tuple-element.16), channel_id=1, source_target_pairs={{0,4},{4,8},{8,12},{12,0},{1,5},{5,9},{9,13},{13,1},{2,6},{6,10},{... | collective-permute-start | bytes 196616 | tf_op jit(solution)/shard_map/ppermute | solution.py:20
  102.2 5.0 %collective-permute-done.4 = bf16[128,768]{1,0:T(8,128)(2,1)S(1)} collective-permute-done((bf16[128,768]{1,0:T(8,128)(2,1)S(1)}, bf16[128,768]{1,0:T(8,128)(2,1)S(1)}, u32[]{:S(2)}, u32[]{:S(2)}) %collective-permute-start.4) | collective-permute-done | bytes 196640 | tf_op jit(solution)/shard_map/ppermute | solution.py:20
  107.2 0.9 slice_dynamic-update-slice_fusion.1
  108.2 0.9 constant_dynamic-slice_fusion.4.refs_0_
  109.2 0.8 slice_dynamic-update-slice_fusion.3
  110.8 2.2 %shard_map.117 = bf16[1,128,4096]{2,1,0:T(8,128)(2,1)} custom-call(bf16[4,128,768]{2,1,0:T(8,128)(2,1)} %constant_dynamic-slice_fusion.4.refs_0_, bf16[4,128,256]{2,1,0:T(8,128)(2,1)} %constant_dynamic-slice_fusion.refs_1_), custom_call_target="tpu_custom_call" | custom-call | tf_op jit(solution)/shard_map/pallas_call | solution.py:138
  (64 shorter events, 9.9 us)
Async XLA Ops:
  0.6 15.1 %copy-start = (bf16[5120,64]{0,1:T(8,128)(2,1)S(1)}, bf16[5120,64]{0,1:T(8,128)(2,1)}, u32[]{:S(2)}) copy-start(bf16[5120,64]{0,1:T(8,128)(2,1)} %param.15) | copy-start | bytes 1966084
  4.2 10.6 %copy-start.4 = (f32[1,2,5120]{2,1,0:T(2,128)S(1)}, f32[1,2,5120]{2,1,0:T(2,128)}, u32[]{:S(2)}) copy-start(f32[1,2,5120]{2,1,0:T(2,128)} %param.14) | copy-start | bytes 122884
  4.2 10.7 %copy-start.1 = (bf16[1,128,5120]{2,1,0:T(8,128)(2,1)S(1)}, bf16[1,128,5120]{2,1,0:T(8,128)(2,1)}, u32[]{:S(2)}) copy-start(bf16[1,128,5120]{2,1,0:T(8,128)(2,1)} %param.13) | copy-start | bytes 3932164
  7.1 8.6 %copy-start.7 = (f32[1,128,64]{1,2,0:T(8,128)S(1)}, f32[1,128,64]{1,2,0:T(8,128)}, u32[]{:S(2)}) copy-start(f32[1,128,64]{1,2,0:T(8,128)} %param.16) | copy-start | bytes 98308
  7.1 19.6 %collective-permute-start = (bf16[3,128,768]{2,1,0:T(8,128)(2,1)}, bf16[3,128,768]{2,1,0:T(8,128)(2,1)S(1)}, u32[]{:S(2)}, u32[]{:S(2)}) collective-permute-start(bf16[3,128,768]{2,1,0:T(8,128)(2,1)} %get-tuple-element.7), channel_id=1, source_target_pairs={{0,4},{4,8},{8,12},{12,0},{1,5},{5,9},{9,13},{13,1},{2,6},{6,10},{... | collective-permute-start | bytes 1769480 | tf_op jit(solution)/shard_map/ppermute | solution.py:20
  10.2 41.0 %collective-permute-start.1 = (bf16[3,128,768]{2,1,0:T(8,128)(2,1)}, bf16[3,128,768]{2,1,0:T(8,128)(2,1)S(1)}, u32[]{:S(2)}, u32[]{:S(2)}) collective-permute-start(bf16[3,128,768]{2,1,0:T(8,128)(2,1)} %get-tuple-element.6), channel_id=1, source_target_pairs={{0,8},{4,12},{8,0},{12,4},{1,9},{5,13},{9,1},{13,5},{2,10},{6,14},... | collective-permute-start | bytes 1769480 | tf_op jit(solution)/shard_map/ppermute | solution.py:20
  12.8 38.4 %collective-permute-start.2 = (bf16[3,128,768]{2,1,0:T(8,128)(2,1)}, bf16[3,128,768]{2,1,0:T(8,128)(2,1)S(1)}, u32[]{:S(2)}, u32[]{:S(2)}) collective-permute-start(bf16[3,128,768]{2,1,0:T(8,128)(2,1)} %get-tuple-element.5), channel_id=1, source_target_pairs={{0,12},{4,0},{8,4},{12,8},{1,13},{5,1},{9,5},{13,9},{2,14},{6,2},{... | collective-permute-start | bytes 1769480 | tf_op jit(solution)/shard_map/ppermute | solution.py:20
  15.7 0.9 copy-start.6
  15.8 1.0 copy-start.5
  16.6 6.3 %collective-permute-start.12 = (f32[1,128,64]{1,2,0:T(8,128)S(1)}, f32[1,128,64]{1,2,0:T(8,128)S(1)}, u32[]{:S(2)}, u32[]{:S(2)}) collective-permute-start(f32[1,128,64]{1,2,0:T(8,128)S(1)} %fusion.15), channel_id=1, source_target_pairs={{0,3},{1,0},{2,1},{3,2},{4,7},{5,4},{6,5},{7,6},{8,11},{9,8},{10,9... | collective-permute-start | bytes 98312 | tf_op jit(solution)/shard_map/ppermute | solution.py:20
  51.2 1.7 %copy-start.2 = (bf16[4,3,128,256]{3,2,1,0:T(8,128)(2,1)S(1)}, bf16[4,3,128,256]{3,2,1,0:T(8,128)(2,1)}, u32[]{:S(2)}) copy-start(bf16[4,3,128,256]{3,2,1,0:T(8,128)(2,1)} %shard_map.115) | copy-start | bytes 2359300
  53.7 32.8 %collective-permute-start.6 = (bf16[3,128,256]{2,1,0:T(8,128)(2,1)}, bf16[3,128,256]{2,1,0:T(8,128)(2,1)S(1)}, u32[]{:S(2)}, u32[]{:S(2)}) collective-permute-start(bf16[3,128,256]{2,1,0:T(8,128)(2,1)} %get-tuple-element.11), channel_id=1, source_target_pairs={{0,4},{4,8},{8,12},{12,0},{1,5},{5,9},{9,13},{13,1},{2,6},{6,10},{... | collective-permute-start | bytes 589832 | tf_op jit(solution)/shard_map/ppermute | solution.py:20
  66.8 20.4 %collective-permute-start.7 = (bf16[3,128,256]{2,1,0:T(8,128)(2,1)}, bf16[3,128,256]{2,1,0:T(8,128)(2,1)}, u32[]{:S(2)}, u32[]{:S(2)}) collective-permute-start(bf16[3,128,256]{2,1,0:T(8,128)(2,1)} %get-tuple-element.10), channel_id=1, source_target_pairs={{0,8},{4,12},{8,0},{12,4},{1,9},{5,13},{9,1},{13,5},{2,10},{6,14},... | collective-permute-start | bytes 589832 | tf_op jit(solution)/shard_map/ppermute | solution.py:20
  68.4 18.8 %collective-permute-start.8 = (bf16[3,128,256]{2,1,0:T(8,128)(2,1)}, bf16[3,128,256]{2,1,0:T(8,128)(2,1)}, u32[]{:S(2)}, u32[]{:S(2)}) collective-permute-start(bf16[3,128,256]{2,1,0:T(8,128)(2,1)} %get-tuple-element.9), channel_id=1, source_target_pairs={{0,12},{4,0},{8,4},{12,8},{1,13},{5,1},{9,5},{13,9},{2,14},{6,2},{... | collective-permute-start | bytes 589832 | tf_op jit(solution)/shard_map/ppermute | solution.py:20
  83.8 16.0 %collective-permute-start.3 = (bf16[128,768]{1,0:T(8,128)(2,1)}, bf16[128,768]{1,0:T(8,128)(2,1)S(1)}, u32[]{:S(2)}, u32[]{:S(2)}) collective-permute-start(bf16[128,768]{1,0:T(8,128)(2,1)} %get-tuple-element.15), channel_id=1, source_target_pairs={{0,12},{4,0},{8,4},{12,8},{1,13},{5,1},{9,5},{13,9},{2,14},{6,2},{... | collective-permute-start | bytes 589832 | tf_op jit(solution)/shard_map/ppermute | solution.py:20
  85.8 21.4 %collective-permute-start.4 = (bf16[128,768]{1,0:T(8,128)(2,1)S(1)}, bf16[128,768]{1,0:T(8,128)(2,1)S(1)}, u32[]{:S(2)}, u32[]{:S(2)}) collective-permute-start(bf16[128,768]{1,0:T(8,128)(2,1)S(1)} %get-tuple-element.14), channel_id=1, source_target_pairs={{0,8},{4,12},{8,0},{12,4},{1,9},{5,13},{9,1},{13,5},{2,10},{6,14},... | collective-permute-start | bytes 589832 | tf_op jit(solution)/shard_map/ppermute | solution.py:20
  86.5 0.7 copy-start.3
  87.2 20.0 %collective-permute-start.5 = (bf16[128,768]{1,0:T(8,128)(2,1)S(1)}, bf16[128,768]{1,0:T(8,128)(2,1)S(1)}, u32[]{:S(2)}, u32[]{:S(2)}) collective-permute-start(bf16[128,768]{1,0:T(8,128)(2,1)S(1)} %get-tuple-element.12), channel_id=1, source_target_pairs={{0,4},{4,8},{8,12},{12,0},{1,5},{5,9},{9,13},{13,1},{2,6},{6,10},{... | collective-permute-start | bytes 589832 | tf_op jit(solution)/shard_map/ppermute | solution.py:20
  95.5 13.7 %collective-permute-start.9 = (bf16[128,256]{1,0:T(8,128)(2,1)S(1)}, bf16[128,256]{1,0:T(8,128)(2,1)S(1)}, u32[]{:S(2)}, u32[]{:S(2)}) collective-permute-start(bf16[128,256]{1,0:T(8,128)(2,1)S(1)} %get-tuple-element.19), channel_id=1, source_target_pairs={{0,12},{4,0},{8,4},{12,8},{1,13},{5,1},{9,5},{13,9},{2,14},{6,2},{... | collective-permute-start | bytes 196616 | tf_op jit(solution)/shard_map/ppermute | solution.py:20
  99.3 9.9 %collective-permute-start.10 = (bf16[128,256]{1,0:T(8,128)(2,1)S(1)}, bf16[128,256]{1,0:T(8,128)(2,1)S(1)}, u32[]{:S(2)}, u32[]{:S(2)}) collective-permute-start(bf16[128,256]{1,0:T(8,128)(2,1)S(1)} %get-tuple-element.18), channel_id=1, source_target_pairs={{0,8},{4,12},{8,0},{12,4},{1,9},{5,13},{9,1},{13,5},{2,10},{6,14},... | collective-permute-start | bytes 196616 | tf_op jit(solution)/shard_map/ppermute | solution.py:20
  99.8 9.4 %collective-permute-start.11 = (bf16[128,256]{1,0:T(8,128)(2,1)S(1)}, bf16[128,256]{1,0:T(8,128)(2,1)S(1)}, u32[]{:S(2)}, u32[]{:S(2)}) collective-permute-start(bf16[128,256]{1,0:T(8,128)(2,1)S(1)} %get-tuple-element.16), channel_id=1, source_target_pairs={{0,4},{4,8},{8,12},{12,0},{1,5},{5,9},{9,13},{13,1},{2,6},{6,10},{... | collective-permute-start | bytes 196616 | tf_op jit(solution)/shard_map/ppermute | solution.py:20

commit v8 on v7

--- a/solution.py
+++ b/solution.py
@@ -143,6 +143,128 @@
     )(*backs)
 
 
+def pieces_kernel(*refs, seq, stride, offset, width, me):
+    sources, outs = refs[:3], refs[3:]
+    for step in range(seq):
+        low = ((me + step) % seq) * stride + offset
+        for kind, source in enumerate(sources):
+            outs[step][kind] = source[0, :, low:low + width]
+
+
+def pieces_of(query_rows, key_rows, value_rows, own_index, seq, stride, offset, width):
+    tokens = query_rows.shape[1]
+
+    def branch(me, *rows):
+        kernel = functools.partial(
+            pieces_kernel, seq=seq, stride=stride, offset=offset, width=width, me=me
+        )
+        return tuple(
+            pl.pallas_call(
+                kernel,
+                in_specs=[pl.BlockSpec(memory_space=pltpu.VMEM)] * 3,
+                out_specs=[pl.BlockSpec(memory_space=pltpu.VMEM)] * seq,
+                out_shape=[jax.ShapeDtypeStruct((3, tokens, width), query_rows.dtype)] * seq,
+            )(*rows)
+        )
+
+    branches = [functools.partial(branch, me) for me in range(seq)]
+    return lax.switch(own_index, branches, query_rows, key_rows, value_rows)
+
+
+def attend_pieces_kernel(lists_ref, live_ref, me_ref, *refs, block, slots, qblocks, heads, depth):
+    sources = len(refs) // 2
+    x_refs, o_refs = refs[:sources], refs[sources:]
+    tokens = x_refs[0].shape[1]
+    total = sources * tokens
+    me = me_ref[0]
+    scale = depth ** (-0.5)
+    per_source = tokens // block
+    column = lax.broadcasted_iota(jnp.int32, (1, total), 1)
+    for head in range(heads):
+        cols = slice(head * depth, (head + 1) * depth)
+        keys = jnp.concatenate([ref[1, :, cols] for ref in x_refs], axis=0)
+        values = jnp.concatenate([ref[2, :, cols] for ref in x_refs], axis=0)
+        for step in range(sources):
+            device = (me - step + sources) % sources
+            for sub in range(per_source):
+                rows = slice(sub * block, (sub + 1) * block)
+                query = x_refs[step][0, rows, cols]
+                entry = head * qblocks + device * per_source + sub
+                live = live_ref[entry]
+                active = column < 0
+                for slot in range(slots):
+                    chosen = lists_ref[entry * slots + slot]
+                    place = (me - chosen // per_source + sources) % sources
+                    low = place * tokens + (chosen % per_source) * block
+                    active = active | ((column >= low) & (column < low + block) & (slot < live))
+                scores = (
+                    lax.dot_general(
+                        query, keys, (((1,), (1,)), ((), ())), preferred_element_type=jnp.float32
+                    )
+                    * scale
+                )
+                scores = jnp.where(active, scores, -jnp.inf)
+                highest = jnp.max(scores, axis=1, keepdims=True)
+                weights = jnp.exp(scores - highest)
+                totals = jnp.sum(weights, axis=1, keepdims=True)
+                mixed = jnp.dot(
+                    weights.astype(jnp.bfloat16), values, preferred_element_type=jnp.float32
+                )
+                o_refs[step][rows, cols] = (mixed / totals).astype(o_refs[step].dtype)
+
+
+def attend_pieces(pieces, lists, live, me):
+    _, tokens, width = pieces[0].shape
+    head_total, qblocks = live.shape
+    slots = lists.shape[2]
+    depth = width // head_total
+    block = len(pieces) * tokens // qblocks
+    kernel = functools.partial(
+        attend_pieces_kernel,
+        block=block,
+        slots=slots,
+        qblocks=qblocks,
+        heads=head_total,
+        depth=depth,
+    )
+    smem = pltpu.SMEM
+    return pl.pallas_call(
+        kernel,
+        in_specs=[pl.BlockSpec(memory_space=smem)] * 3
+        + [pl.BlockSpec(memory_space=pltpu.VMEM)] * len(pieces),
+        out_specs=[pl.BlockSpec(memory_space=pltpu.VMEM)] * len(pieces),
+        out_shape=[jax.ShapeDtypeStruct((tokens, width), jnp.bfloat16)] * len(pieces),
+    )(lists.reshape(-1), live.reshape(-1), me.reshape(1), *pieces)
+
+
+def place_kernel(*refs, seq, stride, offsets, me):
+    out_ref = refs[-1]
+    for c, offset in enumerate(offsets):
+        for step in range(seq):
+            piece = refs[c * seq + step]
+            width = piece.shape[1]
+            low = ((me + step) % seq) * stride + offset
+            out_ref[0, :, low:low + width] = piece[...]
+
+
+def placed_back(backs, own_index, seq, stride, offsets):
+    tokens = backs[0].shape[0]
+
+    def branch(me, *pieces):
+        kernel = functools.partial(
+            place_kernel, seq=seq, stride=stride, offsets=tuple(offsets), me=me
+        )
+        return pl.pallas_call(
+            kernel,
+            in_specs=[pl.BlockSpec(memory_space=pltpu.VMEM)] * len(pieces),
+            out_specs=pl.BlockSpec(memory_space=pltpu.VMEM),
+            out_shape=jax.ShapeDtypeStruct((1, tokens, seq * stride), pieces[0].dtype),
+        )(*pieces)
+
+    branches = [functools.partial(branch, me) for me in range(seq)]
+    return lax.switch(own_index, branches, *backs)
+
+
 def local(
     query_rows,
     key_rows,
@@ -173,36 +295,45 @@
     previous = None
     for per_chunk, start in zip(sizes, starts):
         chunk_width = per_chunk * depth
+        first = own_index * per_device + start
+        lists = lax.dynamic_slice_in_dim(block_lists, first, per_chunk, 0)
+        live = lax.dynamic_slice_in_dim(live_counts, first, per_chunk, 0)
+        if permuted:
+            pieces = pieces_of(
+                query_rows,
+                key_rows,
+                value_rows,
+                own_index,
+                seq_count,
+                per_device * depth,
+                start * depth,
+                chunk_width,
+            )
+            if previous is not None:
+                pieces, _ = lax.optimization_barrier((pieces, previous))
+            received = [pieces[0]]
+            for step in range(1, seq_count):
+                received.append(passed_along(pieces[step], "seq", step))
+            previous = received
+            outs = attend_pieces(received, lists, live, own_index.astype(jnp.int32))
+            backs.append(outs[0])
+            for step in range(1, seq_count):
+                backs.append(passed_along(outs[step], "seq", -step))
+            continue
         send = packed_chunk(
             query_rows, key_rows, value_rows, seq_count, per_device * depth, start * depth, chunk_width
         )
         if previous is not None:
             send, _ = lax.optimization_barrier((send, previous))
-        if permuted:
-            pieces = [lax.dynamic_index_in_dim(send, own_index, 0, keepdims=False)]
-            for step in range(1, seq_count):
-                target = (own_index + step) % seq_count
-                piece = lax.dynamic_index_in_dim(send, target, 0, keepdims=False)
-                pieces.append(passed_along(piece, "seq", step))
-            packed = jnp.stack(pieces)
-            place = own_index
-        else:
-            packed = lax.all_to_all(send, "seq", 0, 0, tiled=True)
-            place = jnp.zeros((), jnp.int32)
-        first = own_index * per_device + start
-        lists = lax.dynamic_slice_in_dim(block_lists, first, per_chunk, 0)
-        live = lax.dynamic_slice_in_dim(live_counts, first, per_chunk, 0)
+        packed = lax.all_to_all(send, "seq", 0, 0, tiled=True)
         previous = packed
-        attended = attend_heads(packed, lists, live, place.astype(jnp.int32), permuted)
-        if permuted:
-            outs = [attended[0]]
-            for step in range(1, seq_count):
-                outs.append(passed_along(attended[step], "seq", -step))
-            back = jnp.roll(jnp.stack(outs), own_index, axis=0)
-        else:
-            back = lax.all_to_all(attended, "seq", 0, 0, tiled=True)
-        backs.append(back)
-    mixed_back = unpacked(backs, seq_count, per_device * depth, [s * depth for s in starts])
+        attended = attend_heads(packed, lists, live, jnp.zeros((), jnp.int32), False)
+        backs.append(lax.all_to_all(attended, "seq", 0, 0, tiled=True))
+    offsets = [s * depth for s in starts]
+    if permuted:
+        mixed_back = placed_back(backs, own_index, seq_count, per_device * depth, offsets)
+    else:
+        mixed_back = unpacked(backs, seq_count, per_device * depth, offsets)
 
     source = hidden_state[0].astype(jnp.float32)
     mean_row = jnp.mean(source, axis=1, keepdims=True)

time: 114 us -> 104 us (0.912)
  local copies, waits for them, and re-layouts: 14.9 us -> 4.99 us
  Pallas kernels: 26.4 us -> 18.7 us
  starting transfers between devices: 32 us -> 39.3 us
  waiting for transfers between devices: 33.4 us -> 37.6 us
  other arithmetic: 4.63 us -> 0.81 us
    pallas_call x5, Pallas kernels: 26.4 us -> 18.7 us  [the longest x2 12.8 us: attend_pieces(): pl.pallas_call(kernel, in_specs=[pl.BlockSpec(memory_space=smem)] * 3 + [...]
    ppermute x13, starting transfers between devices: 32 us -> 39.3 us  [passed_along(): return lax.ppermute(value, axis, pairs)]
    dynamic_slice x4 -> x0, local copies, waits for them, and re-layouts: 5.45 us -> none  [the longest x2 3.79 us: local(): pieces = [lax.dynamic_index_in_dim(send, own_index, 0, keepdims=False)]]
    ppermute x13, waiting for transfers between devices: 33.4 us -> 37.6 us  [passed_along(): return lax.ppermute(value, axis, pairs)]
    another operation x2 -> x0, other arithmetic: 3.81 us -> none  [local(): packed = jnp.stack(pieces)]
    squeeze x2 -> x0, local copies, waits for them, and re-layouts: 2.92 us -> none  [local(): outs.append(passed_along(attended[step], 'seq', -step))]
    unnamed x29 -> x23, local copies, waits for them, and re-layouts: 3.22 us -> 1.69 us
  transfers between devices with their start and end apart: 13 -> 13, of which waited for: 3 -> 4; matrix products, arithmetic and copies ran while one was open for 10% -> 5% of each run, Pallas kernels for 18% -> 15%
where the time goes in v8:
time: 104 us
  starting transfers between devices  39.3 us (38%)
  waiting for transfers between devices  37.6 us (36%)
  Pallas kernels  18.7 us (18%)
  local copies, waits for them, and re-layouts  4.99 us (5%)
  between operations  1.55 us (1%)
    ppermute x13, starting transfers between devices, passed_along(): return lax.ppermute(value, axis, pairs)  39.3 us
    ppermute x13, waiting for transfers between devices, passed_along(): return lax.ppermute(value, axis, pairs)  37.6 us
    pallas_call x2, Pallas kernels, attend_pieces(): pl.pallas_call(kernel, in_specs=[pl.BlockSpec(memory_space=smem)] * 3 + [...  12.8 us
    pallas_call x3, Pallas kernels, branch(): pl.pallas_call(kernel, in_specs=[pl.BlockSpec(memory_space=pltpu.VMEM)] *...  5.83 us
  transfers between devices with their start and end apart: 13, of which 4 were waited for; matrix products, arithmetic and copies ran while one was open for 5% of the time, Pallas kernels for 15%

profile of v8, /device:TPU:0, one launch (start us, length us, event | category | flops | bytes accessed | tf_op | source)
XLA Modules:
  0.0 103.8 jit_solution(18119524827292867645)
XLA Ops:
  0.7 3.5 %conditional.3 = ((bf16[3,128,768]{2,1,0:T(8,128)(2,1)}, bf16[3,128,768]{2,1,0:T(8,128)(2,1)}, bf16[3,128,768]{2,1,0:T(8,128)(2,1)}, bf16[3,128,768]{2,1,0:T(8,128)(2,1)})) conditional(s32[]{:T(128)} %clamp.2, (bf16[1,128,4096]{2,1,0:T(8,128)(2,1)}, bf16[1,128,4096]{2,1,0:T(8,128)(2,1)}, ...), branch_computations={%region_0.0_spmd, %region_1.0_spmd, %region_2.0_spmd, %region_3.0_... | conditional | bytes 8 | solution.py:171
  0.7 3.4 %branch_0_fun.3 = (bf16[3,128,768]{2,1,0:T(8,128)(2,1)}, bf16[3,128,768]{2,1,0:T(8,128)(2,1)}, bf16[3,128,768]{2,1,0:T(8,128)(2,1)}, bf16[3,128,768]{2,1,0:T(8,128)(2,1)}) custom-call(bf16[1,128,4096]{2,1,0:T(8,128)(2,1)} %get-tuple-element.87.refs_0_, bf16[1,128,4096]{2,1,0:T(8,128)(2,1)} %get-tuple-element.102.refs_1_, ...), custom_call_target="tpu_custom_call" | custom-call | tf_op jit(solution)/shard_map/cond/branch_0_fun/pallas_call | solution.py:162
  4.1 3.1 %collective-permute-start = (bf16[3,128,768]{2,1,0:T(8,128)(2,1)}, bf16[3,128,768]{2,1,0:T(8,128)(2,1)}, u32[]{:S(2)}, u32[]{:S(2)}) collective-permute-start(bf16[3,128,768]{2,1,0:T(8,128)(2,1)} %get-tuple-element.196), channel_id=1, source_target_pairs={{0,4},{4,8},{8,12},{12,0},{1,5},{5,9},{9,13},{13,1},{2,6},{6,10},{... | collective-permute-start | bytes 1769480 | tf_op jit(solution)/shard_map/ppermute | solution.py:20
  7.2 2.6 %collective-permute-start.1 = (bf16[3,128,768]{2,1,0:T(8,128)(2,1)}, bf16[3,128,768]{2,1,0:T(8,128)(2,1)}, u32[]{:S(2)}, u32[]{:S(2)}) collective-permute-start(bf16[3,128,768]{2,1,0:T(8,128)(2,1)} %get-tuple-element.197), channel_id=1, source_target_pairs={{0,8},{4,12},{8,0},{12,4},{1,9},{5,13},{9,1},{13,5},{2,10},{6,14},... | collective-permute-start | bytes 1769480 | tf_op jit(solution)/shard_map/ppermute | solution.py:20
  9.8 1.3 %collective-permute-start.2 = (bf16[3,128,768]{2,1,0:T(8,128)(2,1)}, bf16[3,128,768]{2,1,0:T(8,128)(2,1)}, u32[]{:S(2)}, u32[]{:S(2)}) collective-permute-start(bf16[3,128,768]{2,1,0:T(8,128)(2,1)} %get-tuple-element.198), channel_id=1, source_target_pairs={{0,12},{4,0},{8,4},{12,8},{1,13},{5,1},{9,5},{13,9},{2,14},{6,2},{... | collective-permute-start | bytes 1769480 | tf_op jit(solution)/shard_map/ppermute | solution.py:20
  12.0 2.3 %conditional.4 = ((bf16[3,128,256]{2,1,0:T(8,128)(2,1)S(1)}, bf16[3,128,256]{2,1,0:T(8,128)(2,1)S(1)}, bf16[3,128,256]{2,1,0:T(8,128)(2,1)}, bf16[3,128,256]{2,1,0:T(8,128)(2,1)})) conditional(s32[]{:T(128)} %clamp.2, (bf16[1,128,4096]{2,1,0:T(8,128)(2,1)S(1)}, bf16[1,128,4096]{2,1,0:T(8,128)(2,1)}, ...), branch_computations={%region_4.0_spmd, %region_5.0_spmd, %region_6.0_spmd, %region_7.0_... | conditional | bytes 8 | solution.py:171
  12.0 2.3 %branch_0_fun.4 = (bf16[3,128,256]{2,1,0:T(8,128)(2,1)S(1)}, bf16[3,128,256]{2,1,0:T(8,128)(2,1)S(1)}, bf16[3,128,256]{2,1,0:T(8,128)(2,1)}, bf16[3,128,256]{2,1,0:T(8,128)(2,1)}) custom-call(bf16[1,128,4096]{2,1,0:T(8,128)(2,1)S(1)} %get-tuple-element.129.refs_0_, bf16[1,128,4096]{2,1,0:T(8,128)(2,1)} %get-tuple-element.130.refs_1_, ...), custom_call_target="tpu_custom_call" | custom-call | tf_op jit(solution)/shard_map/cond/branch_0_fun/pallas_call | solution.py:162
  15.1 0.8 fusion.15
  15.9 8.0 %collective-permute-done.refs_1_ = bf16[3,128,768]{2,1,0:T(8,128)(2,1)} collective-permute-done((bf16[3,128,768]{2,1,0:T(8,128)(2,1)}, bf16[3,128,768]{2,1,0:T(8,128)(2,1)}, u32[]{:S(2)}, u32[]{:S(2)}) %collective-permute-start) | collective-permute-done | bytes 589856 | tf_op jit(solution)/shard_map/ppermute | solution.py:20
  23.9 24.4 %collective-permute-done.1.refs_2_ = bf16[3,128,768]{2,1,0:T(8,128)(2,1)} collective-permute-done((bf16[3,128,768]{2,1,0:T(8,128)(2,1)}, bf16[3,128,768]{2,1,0:T(8,128)(2,1)}, u32[]{:S(2)}, u32[]{:S(2)}) %collective-permute-start.1) | collective-permute-done | bytes 589856 | tf_op jit(solution)/shard_map/ppermute | solution.py:20
  48.3 13.1 %collective-permute-start.6 = (bf16[3,128,256]{2,1,0:T(8,128)(2,1)S(1)}, bf16[3,128,256]{2,1,0:T(8,128)(2,1)S(1)}, u32[]{:S(2)}, u32[]{:S(2)}) collective-permute-start(bf16[3,128,256]{2,1,0:T(8,128)(2,1)S(1)} %get-tuple-element.208), channel_id=1, source_target_pairs={{0,4},{4,8},{8,12},{12,0},{1,5},{5,9},{9,13},{13,1},{2,6},{6,10},{... | collective-permute-start | bytes 589832 | tf_op jit(solution)/shard_map/ppermute | solution.py:20
  62.2 1.6 %collective-permute-start.7 = (bf16[3,128,256]{2,1,0:T(8,128)(2,1)}, bf16[3,128,256]{2,1,0:T(8,128)(2,1)S(1)}, u32[]{:S(2)}, u32[]{:S(2)}) collective-permute-start(bf16[3,128,256]{2,1,0:T(8,128)(2,1)} %get-tuple-element.209), channel_id=1, source_target_pairs={{0,8},{4,12},{8,0},{12,4},{1,9},{5,13},{9,1},{13,5},{2,10},{6,14},... | collective-permute-start | bytes 589832 | tf_op jit(solution)/shard_map/ppermute | solution.py:20
  64.6 0.8 collective-permute-start.8
  65.4 8.8 %shard_map.113 = (bf16[128,768]{1,0:T(8,128)(2,1)S(1)}, bf16[128,768]{1,0:T(8,128)(2,1)}, bf16[128,768]{1,0:T(8,128)(2,1)}, bf16[128,768]{1,0:T(8,128)(2,1)}) custom-call(s32[96]{0:T(128)} %reshape.58.lists_ref, s32[24]{0:T(128)} %reshape.59.live_ref, s32[1]{0:T(128)} %bitcast.me_ref, bf16[3,128,768]{2,1,0:T(8,128)(2,1)} %get-tuple-element.195.refs_0_, ...), custom_call_target="tpu_custom_call" | custom-call | tf_op jit(solution)/shard_map/pallas_call | solution.py:231
  74.2 2.0 %collective-permute-start.3 = (bf16[128,768]{1,0:T(8,128)(2,1)}, bf16[128,768]{1,0:T(8,128)(2,1)S(1)}, u32[]{:S(2)}, u32[]{:S(2)}) collective-permute-start(bf16[128,768]{1,0:T(8,128)(2,1)} %get-tuple-element.200), channel_id=1, source_target_pairs={{0,12},{4,0},{8,4},{12,8},{1,13},{5,1},{9,5},{13,9},{2,14},{6,2},{... | collective-permute-start | bytes 589832 | tf_op jit(solution)/shard_map/ppermute | solution.py:20
  76.2 0.7 collective-permute-start.4
  77.2 0.7 reshape.61.lists_ref
  78.7 0.7 copy-done.6
  79.3 4.0 %shard_map.114 = (bf16[128,256]{1,0:T(8,128)(2,1)S(1)}, bf16[128,256]{1,0:T(8,128)(2,1)}, bf16[128,256]{1,0:T(8,128)(2,1)}, bf16[128,256]{1,0:T(8,128)(2,1)}) custom-call(s32[32]{0:T(128)} %reshape.61.lists_ref, s32[8]{0:T(128)} %reshape.62.live_ref, s32[1]{0:T(128)} %bitcast.me_ref, bf16[3,128,256]{2,1,0:T(8,128)(2,1)S(1)} %get-tuple-element.207.refs_0_, ...), custom_call_target="tpu_custom_call" | custom-call | tf_op jit(solution)/shard_map/pallas_call | solution.py:231
  83.3 2.2 %collective-permute-start.10 = (bf16[128,256]{1,0:T(8,128)(2,1)}, bf16[128,256]{1,0:T(8,128)(2,1)S(1)}, u32[]{:S(2)}, u32[]{:S(2)}) collective-permute-start(bf16[128,256]{1,0:T(8,128)(2,1)} %get-tuple-element.213), channel_id=1, source_target_pairs={{0,8},{4,12},{8,0},{12,4},{1,9},{5,13},{9,1},{13,5},{2,10},{6,14},... | collective-permute-start | bytes 196616 | tf_op jit(solution)/shard_map/ppermute | solution.py:20
  85.6 11.9 %collective-permute-start.11 = (bf16[128,256]{1,0:T(8,128)(2,1)}, bf16[128,256]{1,0:T(8,128)(2,1)S(1)}, u32[]{:S(2)}, u32[]{:S(2)}) collective-permute-start(bf16[128,256]{1,0:T(8,128)(2,1)} %get-tuple-element.214), channel_id=1, source_target_pairs={{0,4},{4,8},{8,12},{12,0},{1,5},{5,9},{9,13},{13,1},{2,6},{6,10},{... | collective-permute-start | bytes 196616 | tf_op jit(solution)/shard_map/ppermute | solution.py:20
  97.5 4.0 %collective-permute-done.11 = bf16[128,256]{1,0:T(8,128)(2,1)S(1)} collective-permute-done((bf16[128,256]{1,0:T(8,128)(2,1)}, bf16[128,256]{1,0:T(8,128)(2,1)S(1)}, u32[]{:S(2)}, u32[]{:S(2)}) %collective-permute-start.11) | collective-permute-done | bytes 65568 | tf_op jit(solution)/shard_map/ppermute | solution.py:20
  101.5 1.2 %collective-permute-done.9 = bf16[128,256]{1,0:T(8,128)(2,1)S(1)} collective-permute-done((bf16[128,256]{1,0:T(8,128)(2,1)}, bf16[128,256]{1,0:T(8,128)(2,1)S(1)}, u32[]{:S(2)}, u32[]{:S(2)}) %collective-permute-start.9) | collective-permute-done | bytes 65568 | tf_op jit(solution)/shard_map/ppermute | solution.py:20
  102.8 0.7 copy.58
  (51 shorter events, 4.0 us)
Async XLA Ops:
  0.6 14.4 %copy-start = (bf16[5120,64]{0,1:T(8,128)(2,1)S(1)}, bf16[5120,64]{0,1:T(8,128)(2,1)}, u32[]{:S(2)}) copy-start(bf16[5120,64]{0,1:T(8,128)(2,1)} %param.27) | copy-start | bytes 1966084
  0.7 10.5 %copy-start.7 = (f32[1,2,5120]{2,1,0:T(2,128)S(1)}, f32[1,2,5120]{2,1,0:T(2,128)}, u32[]{:S(2)}) copy-start(f32[1,2,5120]{2,1,0:T(2,128)} %param.26) | copy-start | bytes 122884
  0.7 10.5 %copy-start.2 = (bf16[1,128,5120]{2,1,0:T(8,128)(2,1)S(1)}, bf16[1,128,5120]{2,1,0:T(8,128)(2,1)}, u32[]{:S(2)}) copy-start(bf16[1,128,5120]{2,1,0:T(8,128)(2,1)} %param.25) | copy-start | bytes 3932164
  4.1 7.3 %copy-start.1 = (bf16[1,128,4096]{2,1,0:T(8,128)(2,1)S(1)}, bf16[1,128,4096]{2,1,0:T(8,128)(2,1)}, u32[]{:S(2)}) copy-start(bf16[1,128,4096]{2,1,0:T(8,128)(2,1)} %param.22) | copy-start | bytes 3145732
  4.1 19.7 %collective-permute-start = (bf16[3,128,768]{2,1,0:T(8,128)(2,1)}, bf16[3,128,768]{2,1,0:T(8,128)(2,1)}, u32[]{:S(2)}, u32[]{:S(2)}) collective-permute-start(bf16[3,128,768]{2,1,0:T(8,128)(2,1)} %get-tuple-element.196), channel_id=1, source_target_pairs={{0,4},{4,8},{8,12},{12,0},{1,5},{5,9},{9,13},{13,1},{2,6},{6,10},{... | collective-permute-start | bytes 1769480 | tf_op jit(solution)/shard_map/ppermute | solution.py:20
  7.2 41.1 %collective-permute-start.1 = (bf16[3,128,768]{2,1,0:T(8,128)(2,1)}, bf16[3,128,768]{2,1,0:T(8,128)(2,1)}, u32[]{:S(2)}, u32[]{:S(2)}) collective-permute-start(bf16[3,128,768]{2,1,0:T(8,128)(2,1)} %get-tuple-element.197), channel_id=1, source_target_pairs={{0,8},{4,12},{8,0},{12,4},{1,9},{5,13},{9,1},{13,5},{2,10},{6,14},... | collective-permute-start | bytes 1769480 | tf_op jit(solution)/shard_map/ppermute | solution.py:20
  9.8 38.5 %collective-permute-start.2 = (bf16[3,128,768]{2,1,0:T(8,128)(2,1)}, bf16[3,128,768]{2,1,0:T(8,128)(2,1)}, u32[]{:S(2)}, u32[]{:S(2)}) collective-permute-start(bf16[3,128,768]{2,1,0:T(8,128)(2,1)} %get-tuple-element.198), channel_id=1, source_target_pairs={{0,12},{4,0},{8,4},{12,8},{1,13},{5,1},{9,5},{13,9},{2,14},{6,2},{... | collective-permute-start | bytes 1769480 | tf_op jit(solution)/shard_map/ppermute | solution.py:20
  12.0 3.1 %copy-start.10 = (f32[1,128,64]{1,2,0:T(8,128)S(1)}, f32[1,128,64]{1,2,0:T(8,128)}, u32[]{:S(2)}) copy-start(f32[1,128,64]{1,2,0:T(8,128)} %param.28) | copy-start | bytes 98308
  15.1 46.3 %copy-start.8 = (s32[32,4,4]{0,2,1:T(4,128)S(1)}, s32[32,4,4]{0,2,1:T(4,128)}, u32[]{:S(2)}) copy-start(s32[32,4,4]{0,2,1:T(4,128)} %param.31) | copy-start | bytes 6148
  15.1 48.7 %copy-start.9 = (s32[32,4]{0,1:T(4,128)S(1)}, s32[32,4]{0,1:T(4,128)}, u32[]{:S(2)}) copy-start(s32[32,4]{0,1:T(4,128)} %param.30) | copy-start | bytes 1540
  48.3 28.6 %collective-permute-start.6 = (bf16[3,128,256]{2,1,0:T(8,128)(2,1)S(1)}, bf16[3,128,256]{2,1,0:T(8,128)(2,1)S(1)}, u32[]{:S(2)}, u32[]{:S(2)}) collective-permute-start(bf16[3,128,256]{2,1,0:T(8,128)(2,1)S(1)} %get-tuple-element.208), channel_id=1, source_target_pairs={{0,4},{4,8},{8,12},{12,0},{1,5},{5,9},{9,13},{13,1},{2,6},{6,10},{... | collective-permute-start | bytes 589832 | tf_op jit(solution)/shard_map/ppermute | solution.py:20
  62.2 14.8 %collective-permute-start.7 = (bf16[3,128,256]{2,1,0:T(8,128)(2,1)}, bf16[3,128,256]{2,1,0:T(8,128)(2,1)S(1)}, u32[]{:S(2)}, u32[]{:S(2)}) collective-permute-start(bf16[3,128,256]{2,1,0:T(8,128)(2,1)} %get-tuple-element.209), channel_id=1, source_target_pairs={{0,8},{4,12},{8,0},{12,4},{1,9},{5,13},{9,1},{13,5},{2,10},{6,14},... | collective-permute-start | bytes 589832 | tf_op jit(solution)/shard_map/ppermute | solution.py:20
  64.6 14.0 %collective-permute-start.8 = (bf16[3,128,256]{2,1,0:T(8,128)(2,1)}, bf16[3,128,256]{2,1,0:T(8,128)(2,1)S(1)}, u32[]{:S(2)}, u32[]{:S(2)}) collective-permute-start(bf16[3,128,256]{2,1,0:T(8,128)(2,1)} %get-tuple-element.210), channel_id=1, source_target_pairs={{0,12},{4,0},{8,4},{12,8},{1,13},{5,1},{9,5},{13,9},{2,14},{6,2},{... | collective-permute-start | bytes 589832 | tf_op jit(solution)/shard_map/ppermute | solution.py:20
  74.2 23.3 %collective-permute-start.3 = (bf16[128,768]{1,0:T(8,128)(2,1)}, bf16[128,768]{1,0:T(8,128)(2,1)S(1)}, u32[]{:S(2)}, u32[]{:S(2)}) collective-permute-start(bf16[128,768]{1,0:T(8,128)(2,1)} %get-tuple-element.200), channel_id=1, source_target_pairs={{0,12},{4,0},{8,4},{12,8},{1,13},{5,1},{9,5},{13,9},{2,14},{6,2},{... | collective-permute-start | bytes 589832 | tf_op jit(solution)/shard_map/ppermute | solution.py:20
  76.2 21.3 %collective-permute-start.4 = (bf16[128,768]{1,0:T(8,128)(2,1)}, bf16[128,768]{1,0:T(8,128)(2,1)S(1)}, u32[]{:S(2)}, u32[]{:S(2)}) collective-permute-start(bf16[128,768]{1,0:T(8,128)(2,1)} %get-tuple-element.201), channel_id=1, source_target_pairs={{0,8},{4,12},{8,0},{12,4},{1,9},{5,13},{9,1},{13,5},{2,10},{6,14},... | collective-permute-start | bytes 589832 | tf_op jit(solution)/shard_map/ppermute | solution.py:20
  76.9 1.7 %copy-start.4 = (bf16[3,128,256]{2,1,0:T(8,128)(2,1)}, bf16[3,128,256]{2,1,0:T(8,128)(2,1)S(1)}, u32[]{:S(2)}) copy-start(bf16[3,128,256]{2,1,0:T(8,128)(2,1)S(1)} %collective-permute-done.6.refs_1_) | copy-start | bytes 589828
  76.9 20.6 %collective-permute-start.5 = (bf16[128,768]{1,0:T(8,128)(2,1)}, bf16[128,768]{1,0:T(8,128)(2,1)S(1)}, u32[]{:S(2)}, u32[]{:S(2)}) collective-permute-start(bf16[128,768]{1,0:T(8,128)(2,1)} %get-tuple-element.202), channel_id=1, source_target_pairs={{0,4},{4,8},{8,12},{12,0},{1,5},{5,9},{9,13},{13,1},{2,6},{6,10},{... | collective-permute-start | bytes 589832 | tf_op jit(solution)/shard_map/ppermute | solution.py:20
  77.0 1.6 %copy-start.5 = (bf16[3,128,256]{2,1,0:T(8,128)(2,1)}, bf16[3,128,256]{2,1,0:T(8,128)(2,1)S(1)}, u32[]{:S(2)}) copy-start(bf16[3,128,256]{2,1,0:T(8,128)(2,1)S(1)} %collective-permute-done.7.refs_2_) | copy-start | bytes 589828
  77.0 8.6 %collective-permute-start.12 = (f32[1,128,64]{1,2,0:T(8,128)S(1)}, f32[1,128,64]{1,2,0:T(8,128)S(1)}, u32[]{:S(2)}, u32[]{:S(2)}) collective-permute-start(f32[1,128,64]{1,2,0:T(8,128)S(1)} %fusion.15), channel_id=1, source_target_pairs={{0,3},{1,0},{2,1},{3,2},{4,7},{5,4},{6,5},{7,6},{8,11},{9,8},{10,9... | collective-permute-start | bytes 98312 | tf_op jit(solution)/shard_map/ppermute | solution.py:20
  78.6 0.7 copy-start.6
  83.3 14.2 %collective-permute-start.10 = (bf16[128,256]{1,0:T(8,128)(2,1)}, bf16[128,256]{1,0:T(8,128)(2,1)S(1)}, u32[]{:S(2)}, u32[]{:S(2)}) collective-permute-start(bf16[128,256]{1,0:T(8,128)(2,1)} %get-tuple-element.213), channel_id=1, source_target_pairs={{0,8},{4,12},{8,0},{12,4},{1,9},{5,13},{9,1},{13,5},{2,10},{6,14},... | collective-permute-start | bytes 196616 | tf_op jit(solution)/shard_map/ppermute | solution.py:20
  85.6 15.9 %collective-permute-start.11 = (bf16[128,256]{1,0:T(8,128)(2,1)}, bf16[128,256]{1,0:T(8,128)(2,1)S(1)}, u32[]{:S(2)}, u32[]{:S(2)}) collective-permute-start(bf16[128,256]{1,0:T(8,128)(2,1)} %get-tuple-element.214), channel_id=1, source_target_pairs={{0,4},{4,8},{8,12},{12,0},{1,5},{5,9},{9,13},{13,1},{2,6},{6,10},{... | collective-permute-start | bytes 196616 | tf_op jit(solution)/shard_map/ppermute | solution.py:20
  97.5 5.2 %collective-permute-start.9 = (bf16[128,256]{1,0:T(8,128)(2,1)}, bf16[128,256]{1,0:T(8,128)(2,1)S(1)}, u32[]{:S(2)}, u32[]{:S(2)}) collective-permute-start(bf16[128,256]{1,0:T(8,128)(2,1)} %get-tuple-element.212), channel_id=1, source_target_pairs={{0,12},{4,0},{8,4},{12,8},{1,13},{5,1},{9,5},{13,9},{2,14},{6,2},{... | collective-permute-start | bytes 196616 | tf_op jit(solution)/shard_map/ppermute | solution.py:20
  102.8 1.0 copy-start.3

commit v9 on v8

--- a/solution.py
+++ b/solution.py
@@ -143,32 +143,28 @@
     )(*backs)
 
 
-def pieces_kernel(*refs, seq, stride, offset, width, me):
-    sources, outs = refs[:3], refs[3:]
-    for step in range(seq):
-        low = ((me + step) % seq) * stride + offset
-        for kind, source in enumerate(sources):
-            outs[step][kind] = source[0, :, low:low + width]
+def piece_kernel(query_ref, key_ref, value_ref, out_ref, *, low, width):
+    for kind, source in enumerate((query_ref, key_ref, value_ref)):
+        out_ref[kind] = source[0, :, low:low + width]
 
 
 def pieces_of(query_rows, key_rows, value_rows, own_index, seq, stride, offset, width):
     tokens = query_rows.shape[1]
 
-    def branch(me, *rows):
-        kernel = functools.partial(
-            pieces_kernel, seq=seq, stride=stride, offset=offset, width=width, me=me
-        )
-        return tuple(
-            pl.pallas_call(
-                kernel,
-                in_specs=[pl.BlockSpec(memory_space=pltpu.VMEM)] * 3,
-                out_specs=[pl.BlockSpec(memory_space=pltpu.VMEM)] * seq,
-                out_shape=[jax.ShapeDtypeStruct((3, tokens, width), query_rows.dtype)] * seq,
-            )(*rows)
-        )
-
-    branches = [functools.partial(branch, me) for me in range(seq)]
-    return lax.switch(own_index, branches, query_rows, key_rows, value_rows)
+    def branch(me, step, *rows):
+        low = ((me + step) % seq) * stride + offset
+        return pl.pallas_call(
+            functools.partial(piece_kernel, low=low, width=width),
+            in_specs=[pl.BlockSpec(memory_space=pltpu.VMEM)] * 3,
+            out_specs=pl.BlockSpec(memory_space=pltpu.VMEM),
+            out_shape=jax.ShapeDtypeStruct((3, tokens, width), query_rows.dtype),
+        )(*rows)
+
+    pieces = []
+    for step in range(seq):
+        branches = [functools.partial(branch, me, step) for me in range(seq)]
+        pieces.append(lax.switch(own_index, branches, query_rows, key_rows, value_rows))
+    return tuple(pieces)
 
 
 def attend_pieces_kernel(lists_ref, live_ref, me_ref, *refs, block, slots, qblocks, heads, depth):

time: 104 us -> 103 us (level)
  waiting for transfers between devices: 37.6 us -> 24.4 us
  Pallas kernels: 18.7 us -> 30.9 us
    pallas_call x0 -> x8, Pallas kernels: none -> 18.3 us  [branch(): pl.pallas_call(functools.partial(piece_kernel, low=low, width=width), in_...]
    ppermute x13, waiting for transfers between devices: 37.6 us -> 24.4 us  [passed_along(): return lax.ppermute(value, axis, pairs)]
    pallas_call x3 -> x1, Pallas kernels: 5.83 us -> 0.07 us  [branch(): pl.pallas_call(kernel, in_specs=[pl.BlockSpec(memory_space=pltpu.VMEM)] *...]
  transfers between devices with their start and end apart: 13 -> 13, of which waited for: 4 -> 3; matrix products, arithmetic and copies ran while one was open for 5% -> 5% of each run, Pallas kernels for 15% -> 27%
where the time goes in v9:
time: 103 us
  starting transfers between devices  39.5 us (38%)
  Pallas kernels  30.9 us (30%)
  waiting for transfers between devices  24.4 us (24%)
  local copies, waits for them, and re-layouts  4.99 us (5%)
  between operations  1.57 us (2%)
    ppermute x13, starting transfers between devices, passed_along(): return lax.ppermute(value, axis, pairs)  39.5 us
    ppermute x13, waiting for transfers between devices, passed_along(): return lax.ppermute(value, axis, pairs)  24.4 us
    pallas_call x8, Pallas kernels, branch(): pl.pallas_call(functools.partial(piece_kernel, low=low, width=width), in_...  18.3 us
    pallas_call x2, Pallas kernels, attend_pieces(): pl.pallas_call(kernel, in_specs=[pl.BlockSpec(memory_space=smem)] * 3 + [...  12.6 us
  transfers between devices with their start and end apart: 13, of which 3 were waited for; matrix products, arithmetic and copies ran while one was open for 5% of the time, Pallas kernels for 27%

profile of v9, /device:TPU:0, one launch (start us, length us, event | category | flops | bytes accessed | tf_op | source)
XLA Modules:
  0.0 103.1 jit_solution(2988554172653253742)
XLA Ops:
  0.7 2.8 %conditional.10 = (bf16[3,128,768]{2,1,0:T(8,128)(2,1)}) conditional(s32[]{:T(128)} %clamp.2, (bf16[1,128,4096]{2,1,0:T(8,128)(2,1)}, bf16[1,128,4096]{2,1,0:T(8,128)(2,1)}, bf16[1,128,4096]{2,1,0:T(8,128)(2,1)}) %tuple.117, (bf16[1,128,4096]{2,1,0:T(8,128)(2,1)}, bf16[1,128,4096]{2,1,0:T(8,128)(2,1)}, ...), branch_computations={%region_4.0_spmd, %region_5.0_spmd, %region_6.0_spmd, %region_7.0_... | conditional | bytes 8 | solution.py:166
  0.7 2.8 %branch_0_fun.10 = bf16[3,128,768]{2,1,0:T(8,128)(2,1)} custom-call(bf16[1,128,4096]{2,1,0:T(8,128)(2,1)} %get-tuple-element.295.query_ref, bf16[1,128,4096]{2,1,0:T(8,128)(2,1)} %get-tuple-element.296.key_ref, bf16[1,128,4096]{2,1,0:T(8,128)(2,1)} %get-tuple-element.297.value_ref), custom_call_target="tpu_custom_call" | custom-call | tf_op jit(solution)/shard_map/cond/branch_0_fun/pallas_call | solution.py:156
  3.5 3.1 %collective-permute-start = (bf16[3,128,768]{2,1,0:T(8,128)(2,1)}, bf16[3,128,768]{2,1,0:T(8,128)(2,1)}, u32[]{:S(2)}, u32[]{:S(2)}) collective-permute-start(bf16[3,128,768]{2,1,0:T(8,128)(2,1)} %get-tuple-element.462), channel_id=1, source_target_pairs={{0,4},{4,8},{8,12},{12,0},{1,5},{5,9},{9,13},{13,1},{2,6},{6,10},{... | collective-permute-start | bytes 1769480 | tf_op jit(solution)/shard_map/ppermute | solution.py:20
  6.5 2.7 %conditional.11 = (bf16[3,128,768]{2,1,0:T(8,128)(2,1)}) conditional(s32[]{:T(128)} %clamp.2, (bf16[1,128,4096]{2,1,0:T(8,128)(2,1)}, bf16[1,128,4096]{2,1,0:T(8,128)(2,1)}, bf16[1,128,4096]{2,1,0:T(8,128)(2,1)}) %tuple.117, (bf16[1,128,4096]{2,1,0:T(8,128)(2,1)}, bf16[1,128,4096]{2,1,0:T(8,128)(2,1)}, ...), branch_computations={%region_8.0_spmd, %region_9.0_spmd, %region_10.0_spmd, %region_11.... | conditional | bytes 8 | solution.py:166
  6.5 2.7 %branch_0_fun.11 = bf16[3,128,768]{2,1,0:T(8,128)(2,1)} custom-call(bf16[1,128,4096]{2,1,0:T(8,128)(2,1)} %get-tuple-element.316.query_ref, bf16[1,128,4096]{2,1,0:T(8,128)(2,1)} %get-tuple-element.317.key_ref, bf16[1,128,4096]{2,1,0:T(8,128)(2,1)} %get-tuple-element.318.value_ref), custom_call_target="tpu_custom_call" | custom-call | tf_op jit(solution)/shard_map/cond/branch_0_fun/pallas_call | solution.py:156
  9.2 2.6 %collective-permute-start.1 = (bf16[3,128,768]{2,1,0:T(8,128)(2,1)}, bf16[3,128,768]{2,1,0:T(8,128)(2,1)}, u32[]{:S(2)}, u32[]{:S(2)}) collective-permute-start(bf16[3,128,768]{2,1,0:T(8,128)(2,1)} %get-tuple-element.463), channel_id=1, source_target_pairs={{0,8},{4,12},{8,0},{12,4},{1,9},{5,13},{9,1},{13,5},{2,10},{6,14},... | collective-permute-start | bytes 1769480 | tf_op jit(solution)/shard_map/ppermute | solution.py:20
  11.8 2.7 %conditional.12 = (bf16[3,128,768]{2,1,0:T(8,128)(2,1)}) conditional(s32[]{:T(128)} %clamp.2, (bf16[1,128,4096]{2,1,0:T(8,128)(2,1)}, bf16[1,128,4096]{2,1,0:T(8,128)(2,1)}, bf16[1,128,4096]{2,1,0:T(8,128)(2,1)}) %tuple.117, (bf16[1,128,4096]{2,1,0:T(8,128)(2,1)}, bf16[1,128,4096]{2,1,0:T(8,128)(2,1)}, ...), branch_computations={%region_12.0_spmd, %region_13.0_spmd, %region_14.0_spmd, %region_1... | conditional | bytes 8 | solution.py:166
  11.8 2.7 %branch_0_fun.12 = bf16[3,128,768]{2,1,0:T(8,128)(2,1)} custom-call(bf16[1,128,4096]{2,1,0:T(8,128)(2,1)} %get-tuple-element.337.query_ref, bf16[1,128,4096]{2,1,0:T(8,128)(2,1)} %get-tuple-element.338.key_ref, bf16[1,128,4096]{2,1,0:T(8,128)(2,1)} %get-tuple-element.339.value_ref), custom_call_target="tpu_custom_call" | custom-call | tf_op jit(solution)/shard_map/cond/branch_0_fun/pallas_call | solution.py:156
  16.7 2.4 %conditional.9 = (bf16[3,128,768]{2,1,0:T(8,128)(2,1)}) conditional(s32[]{:T(128)} %clamp.2, (bf16[1,128,4096]{2,1,0:T(8,128)(2,1)S(1)}, bf16[1,128,4096]{2,1,0:T(8,128)(2,1)}, bf16[1,128,4096]{2,1,0:T(8,128)(2,1)}) %tuple.160, (bf16[1,128,4096]{2,1,0:T(8,128)(2,1)S(1)}, bf16[1,128,4096]{2,1,0:T(8,128)(2,1)}, ...), branch_computations={%region_0.0_spmd, %region_1.0_spmd, %region_2.0_spmd, %region_3.0_... | conditional | bytes 8 | solution.py:166
  16.7 2.4 %branch_0_fun.9 = bf16[3,128,768]{2,1,0:T(8,128)(2,1)} custom-call(bf16[1,128,4096]{2,1,0:T(8,128)(2,1)S(1)} %get-tuple-element.274.query_ref, bf16[1,128,4096]{2,1,0:T(8,128)(2,1)} %get-tuple-element.275.key_ref, bf16[1,128,4096]{2,1,0:T(8,128)(2,1)} %get-tuple-element.276.value_ref), custom_call_target="tpu_custom_call" | custom-call | tf_op jit(solution)/shard_map/cond/branch_0_fun/pallas_call | solution.py:156
  20.7 1.6 %conditional.14 = (bf16[3,128,256]{2,1,0:T(8,128)(2,1)S(1)}) conditional(s32[]{:T(128)} %clamp.2, (bf16[1,128,4096]{2,1,0:T(8,128)(2,1)S(1)}, bf16[1,128,4096]{2,1,0:T(8,128)(2,1)}, bf16[1,128,4096]{2,1,0:T(8,128)(2,1)}) %tuple.168, (bf16[1,128,4096]{2,1,0:T(8,128)(2,1)S(1)}, bf16[1,128,4096]{2,1,0:T(8,128)(2,1)}, ...), branch_computations={%region_20.0_spmd, %region_21.0_spmd, %region_22.0_spmd, %region_2... | conditional | bytes 8 | solution.py:166
  22.3 2.3 %conditional.15 = (bf16[3,128,256]{2,1,0:T(8,128)(2,1)}) conditional(s32[]{:T(128)} %clamp.2, (bf16[1,128,4096]{2,1,0:T(8,128)(2,1)S(1)}, bf16[1,128,4096]{2,1,0:T(8,128)(2,1)}, bf16[1,128,4096]{2,1,0:T(8,128)(2,1)}) %tuple.172, (bf16[1,128,4096]{2,1,0:T(8,128)(2,1)S(1)}, bf16[1,128,4096]{2,1,0:T(8,128)(2,1)}, ...), branch_computations={%region_24.0_spmd, %region_25.0_spmd, %region_26.0_spmd, %region_2... | conditional | bytes 8 | solution.py:166
  22.3 2.2 %branch_0_fun.15 = bf16[3,128,256]{2,1,0:T(8,128)(2,1)} custom-call(bf16[1,128,4096]{2,1,0:T(8,128)(2,1)S(1)} %get-tuple-element.373.query_ref, bf16[1,128,4096]{2,1,0:T(8,128)(2,1)} %get-tuple-element.374.key_ref, bf16[1,128,4096]{2,1,0:T(8,128)(2,1)} %get-tuple-element.375.value_ref), custom_call_target="tpu_custom_call" | custom-call | tf_op jit(solution)/shard_map/cond/branch_0_fun/pallas_call | solution.py:156
  24.6 2.3 %conditional.16 = (bf16[3,128,256]{2,1,0:T(8,128)(2,1)}) conditional(s32[]{:T(128)} %clamp.2, (bf16[1,128,4096]{2,1,0:T(8,128)(2,1)S(1)}, bf16[1,128,4096]{2,1,0:T(8,128)(2,1)}, bf16[1,128,4096]{2,1,0:T(8,128)(2,1)}) %tuple.176, (bf16[1,128,4096]{2,1,0:T(8,128)(2,1)S(1)}, bf16[1,128,4096]{2,1,0:T(8,128)(2,1)}, ...), branch_computations={%region_28.0_spmd, %region_29.0_spmd, %region_30.0_spmd, %region_3... | conditional | bytes 8 | solution.py:166
  24.6 2.3 %branch_0_fun.16 = bf16[3,128,256]{2,1,0:T(8,128)(2,1)} custom-call(bf16[1,128,4096]{2,1,0:T(8,128)(2,1)S(1)} %get-tuple-element.385.query_ref, bf16[1,128,4096]{2,1,0:T(8,128)(2,1)} %get-tuple-element.386.key_ref, bf16[1,128,4096]{2,1,0:T(8,128)(2,1)} %get-tuple-element.387.value_ref), custom_call_target="tpu_custom_call" | custom-call | tf_op jit(solution)/shard_map/cond/branch_0_fun/pallas_call | solution.py:156
  28.5 19.1 %collective-permute-done.1.refs_2_ = bf16[3,128,768]{2,1,0:T(8,128)(2,1)} collective-permute-done((bf16[3,128,768]{2,1,0:T(8,128)(2,1)}, bf16[3,128,768]{2,1,0:T(8,128)(2,1)}, u32[]{:S(2)}, u32[]{:S(2)}) %collective-permute-start.1) | collective-permute-done | bytes 589856 | tf_op jit(solution)/shard_map/ppermute | solution.py:20
  47.6 13.1 %collective-permute-start.6 = (bf16[3,128,256]{2,1,0:T(8,128)(2,1)S(1)}, bf16[3,128,256]{2,1,0:T(8,128)(2,1)S(1)}, u32[]{:S(2)}, u32[]{:S(2)}) collective-permute-start(bf16[3,128,256]{2,1,0:T(8,128)(2,1)S(1)} %get-tuple-element.466), channel_id=1, source_target_pairs={{0,4},{4,8},{8,12},{12,0},{1,5},{5,9},{9,13},{13,1},{2,6},{6,10},{... | collective-permute-start | bytes 589832 | tf_op jit(solution)/shard_map/ppermute | solution.py:20
  61.6 1.6 %collective-permute-start.7 = (bf16[3,128,256]{2,1,0:T(8,128)(2,1)S(1)}, bf16[3,128,256]{2,1,0:T(8,128)(2,1)S(1)}, u32[]{:S(2)}, u32[]{:S(2)}) collective-permute-start(bf16[3,128,256]{2,1,0:T(8,128)(2,1)S(1)} %copy-done.5), channel_id=1, source_target_pairs={{0,8},{4,12},{8,0},{12,4},{1,9},{5,13},{9,1},{13,5},{2,10},{6,14},... | collective-permute-start | bytes 589832 | tf_op jit(solution)/shard_map/ppermute | solution.py:20
  64.7 8.6 %shard_map.113 = (bf16[128,768]{1,0:T(8,128)(2,1)S(1)}, bf16[128,768]{1,0:T(8,128)(2,1)}, bf16[128,768]{1,0:T(8,128)(2,1)}, bf16[128,768]{1,0:T(8,128)(2,1)}) custom-call(s32[96]{0:T(128)} %reshape.58.lists_ref, s32[24]{0:T(128)} %reshape.59.live_ref, s32[1]{0:T(128)} %bitcast.me_ref, bf16[3,128,768]{2,1,0:T(8,128)(2,1)S(1)} %copy-done.3, ...), custom_call_target="tpu_custom_call" | custom-call | tf_op jit(solution)/shard_map/pallas_call | solution.py:227
  73.3 2.0 %collective-permute-start.3 = (bf16[128,768]{1,0:T(8,128)(2,1)}, bf16[128,768]{1,0:T(8,128)(2,1)S(1)}, u32[]{:S(2)}, u32[]{:S(2)}) collective-permute-start(bf16[128,768]{1,0:T(8,128)(2,1)} %get-tuple-element.444), channel_id=1, source_target_pairs={{0,12},{4,0},{8,4},{12,8},{1,13},{5,1},{9,5},{13,9},{2,14},{6,2},{... | collective-permute-start | bytes 589832 | tf_op jit(solution)/shard_map/ppermute | solution.py:20
  78.4 4.0 %shard_map.114 = (bf16[128,256]{1,0:T(8,128)(2,1)S(1)}, bf16[128,256]{1,0:T(8,128)(2,1)}, bf16[128,256]{1,0:T(8,128)(2,1)}, bf16[128,256]{1,0:T(8,128)(2,1)}) custom-call(s32[32]{0:T(128)} %reshape.61.lists_ref, s32[8]{0:T(128)} %reshape.62.live_ref, s32[1]{0:T(128)} %bitcast.me_ref, bf16[3,128,256]{2,1,0:T(8,128)(2,1)S(1)} %get-tuple-element.465.refs_0_, ...), custom_call_target="tpu_custom_call" | custom-call | tf_op jit(solution)/shard_map/pallas_call | solution.py:227
  82.4 2.2 %collective-permute-start.10 = (bf16[128,256]{1,0:T(8,128)(2,1)}, bf16[128,256]{1,0:T(8,128)(2,1)S(1)}, u32[]{:S(2)}, u32[]{:S(2)}) collective-permute-start(bf16[128,256]{1,0:T(8,128)(2,1)} %get-tuple-element.453), channel_id=1, source_target_pairs={{0,8},{4,12},{8,0},{12,4},{1,9},{5,13},{9,1},{13,5},{2,10},{6,14},... | collective-permute-start | bytes 196616 | tf_op jit(solution)/shard_map/ppermute | solution.py:20
  84.7 12.1 %collective-permute-start.11 = (bf16[128,256]{1,0:T(8,128)(2,1)}, bf16[128,256]{1,0:T(8,128)(2,1)S(1)}, u32[]{:S(2)}, u32[]{:S(2)}) collective-permute-start(bf16[128,256]{1,0:T(8,128)(2,1)} %get-tuple-element.454), channel_id=1, source_target_pairs={{0,4},{4,8},{8,12},{12,0},{1,5},{5,9},{9,13},{13,1},{2,6},{6,10},{... | collective-permute-start | bytes 196616 | tf_op jit(solution)/shard_map/ppermute | solution.py:20
  96.8 4.0 %collective-permute-done.11 = bf16[128,256]{1,0:T(8,128)(2,1)S(1)} collective-permute-done((bf16[128,256]{1,0:T(8,128)(2,1)}, bf16[128,256]{1,0:T(8,128)(2,1)S(1)}, u32[]{:S(2)}, u32[]{:S(2)}) %collective-permute-start.11) | collective-permute-done | bytes 65568 | tf_op jit(solution)/shard_map/ppermute | solution.py:20
  (67 shorter events, 15.5 us)
Async XLA Ops:
  0.6 27.0 %copy-start = (bf16[5120,64]{0,1:T(8,128)(2,1)S(1)}, bf16[5120,64]{0,1:T(8,128)(2,1)}, u32[]{:S(2)}) copy-start(bf16[5120,64]{0,1:T(8,128)(2,1)} %param.51) | copy-start | bytes 1966084
  3.5 25.0 %collective-permute-start = (bf16[3,128,768]{2,1,0:T(8,128)(2,1)}, bf16[3,128,768]{2,1,0:T(8,128)(2,1)}, u32[]{:S(2)}, u32[]{:S(2)}) collective-permute-start(bf16[3,128,768]{2,1,0:T(8,128)(2,1)} %get-tuple-element.462), channel_id=1, source_target_pairs={{0,4},{4,8},{8,12},{12,0},{1,5},{5,9},{9,13},{13,1},{2,6},{6,10},{... | collective-permute-start | bytes 1769480 | tf_op jit(solution)/shard_map/ppermute | solution.py:20
  9.2 6.7 %copy-start.9 = (f32[1,2,5120]{2,1,0:T(2,128)S(1)}, f32[1,2,5120]{2,1,0:T(2,128)}, u32[]{:S(2)}) copy-start(f32[1,2,5120]{2,1,0:T(2,128)} %param.50) | copy-start | bytes 122884
  9.2 6.7 %copy-start.2 = (bf16[1,128,5120]{2,1,0:T(8,128)(2,1)S(1)}, bf16[1,128,5120]{2,1,0:T(8,128)(2,1)}, u32[]{:S(2)}) copy-start(bf16[1,128,5120]{2,1,0:T(8,128)(2,1)} %param.49) | copy-start | bytes 3932164
  9.2 38.4 %collective-permute-start.1 = (bf16[3,128,768]{2,1,0:T(8,128)(2,1)}, bf16[3,128,768]{2,1,0:T(8,128)(2,1)}, u32[]{:S(2)}, u32[]{:S(2)}) collective-permute-start(bf16[3,128,768]{2,1,0:T(8,128)(2,1)} %get-tuple-element.463), channel_id=1, source_target_pairs={{0,8},{4,12},{8,0},{12,4},{1,9},{5,13},{9,1},{13,5},{2,10},{6,14},... | collective-permute-start | bytes 1769480 | tf_op jit(solution)/shard_map/ppermute | solution.py:20
  14.5 1.7 %copy-start.1 = (bf16[1,128,4096]{2,1,0:T(8,128)(2,1)S(1)}, bf16[1,128,4096]{2,1,0:T(8,128)(2,1)}, u32[]{:S(2)}) copy-start(bf16[1,128,4096]{2,1,0:T(8,128)(2,1)} %param.46) | copy-start | bytes 3145732
  14.5 33.1 %collective-permute-start.2 = (bf16[3,128,768]{2,1,0:T(8,128)(2,1)}, bf16[3,128,768]{2,1,0:T(8,128)(2,1)}, u32[]{:S(2)}, u32[]{:S(2)}) collective-permute-start(bf16[3,128,768]{2,1,0:T(8,128)(2,1)} %get-tuple-element.464), channel_id=1, source_target_pairs={{0,12},{4,0},{8,4},{12,8},{1,13},{5,1},{9,5},{13,9},{2,14},{6,2},{... | collective-permute-start | bytes 1769480 | tf_op jit(solution)/shard_map/ppermute | solution.py:20
  24.6 3.0 %copy-start.12 = (f32[1,128,64]{1,2,0:T(8,128)S(1)}, f32[1,128,64]{1,2,0:T(8,128)}, u32[]{:S(2)}) copy-start(f32[1,128,64]{1,2,0:T(8,128)} %param.52) | copy-start | bytes 98308
  27.6 33.1 %copy-start.10 = (s32[32,4,4]{0,2,1:T(4,128)S(1)}, s32[32,4,4]{0,2,1:T(4,128)}, u32[]{:S(2)}) copy-start(s32[32,4,4]{0,2,1:T(4,128)} %param.55) | copy-start | bytes 6148
  27.6 34.0 %copy-start.5 = (bf16[3,128,256]{2,1,0:T(8,128)(2,1)S(1)}, bf16[3,128,256]{2,1,0:T(8,128)(2,1)}, u32[]{:S(2)}) copy-start(bf16[3,128,256]{2,1,0:T(8,128)(2,1)} %get-tuple-element.467) | copy-start | bytes 589828
  27.7 35.5 %copy-start.11 = (s32[32,4]{0,1:T(4,128)S(1)}, s32[32,4]{0,1:T(4,128)}, u32[]{:S(2)}) copy-start(s32[32,4]{0,1:T(4,128)} %param.54) | copy-start | bytes 1540
  27.7 37.1 %copy-start.3 = (bf16[3,128,768]{2,1,0:T(8,128)(2,1)S(1)}, bf16[3,128,768]{2,1,0:T(8,128)(2,1)}, u32[]{:S(2)}) copy-start(bf16[3,128,768]{2,1,0:T(8,128)(2,1)} %get-tuple-element.461.refs_0_) | copy-start | bytes 1769476
  47.6 28.5 %collective-permute-start.6 = (bf16[3,128,256]{2,1,0:T(8,128)(2,1)S(1)}, bf16[3,128,256]{2,1,0:T(8,128)(2,1)S(1)}, u32[]{:S(2)}, u32[]{:S(2)}) collective-permute-start(bf16[3,128,256]{2,1,0:T(8,128)(2,1)S(1)} %get-tuple-element.466), channel_id=1, source_target_pairs={{0,4},{4,8},{8,12},{12,0},{1,5},{5,9},{9,13},{13,1},{2,6},{6,10},{... | collective-permute-start | bytes 589832 | tf_op jit(solution)/shard_map/ppermute | solution.py:20
  61.6 14.5 %collective-permute-start.7 = (bf16[3,128,256]{2,1,0:T(8,128)(2,1)S(1)}, bf16[3,128,256]{2,1,0:T(8,128)(2,1)S(1)}, u32[]{:S(2)}, u32[]{:S(2)}) collective-permute-start(bf16[3,128,256]{2,1,0:T(8,128)(2,1)S(1)} %copy-done.5), channel_id=1, source_target_pairs={{0,8},{4,12},{8,0},{12,4},{1,9},{5,13},{9,1},{13,5},{2,10},{6,14},... | collective-permute-start | bytes 589832 | tf_op jit(solution)/shard_map/ppermute | solution.py:20
  64.0 13.8 %collective-permute-start.8 = (bf16[3,128,256]{2,1,0:T(8,128)(2,1)}, bf16[3,128,256]{2,1,0:T(8,128)(2,1)S(1)}, u32[]{:S(2)}, u32[]{:S(2)}) collective-permute-start(bf16[3,128,256]{2,1,0:T(8,128)(2,1)} %get-tuple-element.468), channel_id=1, source_target_pairs={{0,12},{4,0},{8,4},{12,8},{1,13},{5,1},{9,5},{13,9},{2,14},{6,2},{... | collective-permute-start | bytes 589832 | tf_op jit(solution)/shard_map/ppermute | solution.py:20
  73.3 23.4 %collective-permute-start.3 = (bf16[128,768]{1,0:T(8,128)(2,1)}, bf16[128,768]{1,0:T(8,128)(2,1)S(1)}, u32[]{:S(2)}, u32[]{:S(2)}) collective-permute-start(bf16[128,768]{1,0:T(8,128)(2,1)} %get-tuple-element.444), channel_id=1, source_target_pairs={{0,12},{4,0},{8,4},{12,8},{1,13},{5,1},{9,5},{13,9},{2,14},{6,2},{... | collective-permute-start | bytes 589832 | tf_op jit(solution)/shard_map/ppermute | solution.py:20
  75.4 21.4 %collective-permute-start.4 = (bf16[128,768]{1,0:T(8,128)(2,1)}, bf16[128,768]{1,0:T(8,128)(2,1)S(1)}, u32[]{:S(2)}, u32[]{:S(2)}) collective-permute-start(bf16[128,768]{1,0:T(8,128)(2,1)} %get-tuple-element.445), channel_id=1, source_target_pairs={{0,8},{4,12},{8,0},{12,4},{1,9},{5,13},{9,1},{13,5},{2,10},{6,14},... | collective-permute-start | bytes 589832 | tf_op jit(solution)/shard_map/ppermute | solution.py:20
  76.1 1.7 %copy-start.6 = (bf16[3,128,256]{2,1,0:T(8,128)(2,1)}, bf16[3,128,256]{2,1,0:T(8,128)(2,1)S(1)}, u32[]{:S(2)}) copy-start(bf16[3,128,256]{2,1,0:T(8,128)(2,1)S(1)} %collective-permute-done.6.refs_1_) | copy-start | bytes 589828
  76.1 20.7 %collective-permute-start.5 = (bf16[128,768]{1,0:T(8,128)(2,1)}, bf16[128,768]{1,0:T(8,128)(2,1)S(1)}, u32[]{:S(2)}, u32[]{:S(2)}) collective-permute-start(bf16[128,768]{1,0:T(8,128)(2,1)} %get-tuple-element.446), channel_id=1, source_target_pairs={{0,4},{4,8},{8,12},{12,0},{1,5},{5,9},{9,13},{13,1},{2,6},{6,10},{... | collective-permute-start | bytes 589832 | tf_op jit(solution)/shard_map/ppermute | solution.py:20
  76.1 1.6 %copy-start.7 = (bf16[3,128,256]{2,1,0:T(8,128)(2,1)}, bf16[3,128,256]{2,1,0:T(8,128)(2,1)S(1)}, u32[]{:S(2)}) copy-start(bf16[3,128,256]{2,1,0:T(8,128)(2,1)S(1)} %collective-permute-done.7.refs_2_) | copy-start | bytes 589828
  76.1 8.5 %collective-permute-start.12 = (f32[1,128,64]{1,2,0:T(8,128)S(1)}, f32[1,128,64]{1,2,0:T(8,128)S(1)}, u32[]{:S(2)}, u32[]{:S(2)}) collective-permute-start(f32[1,128,64]{1,2,0:T(8,128)S(1)} %fusion.15), channel_id=1, source_target_pairs={{0,3},{1,0},{2,1},{3,2},{4,7},{5,4},{6,5},{7,6},{8,11},{9,8},{10,9... | collective-permute-start | bytes 98312 | tf_op jit(solution)/shard_map/ppermute | solution.py:20
  82.4 14.4 %collective-permute-start.10 = (bf16[128,256]{1,0:T(8,128)(2,1)}, bf16[128,256]{1,0:T(8,128)(2,1)S(1)}, u32[]{:S(2)}, u32[]{:S(2)}) collective-permute-start(bf16[128,256]{1,0:T(8,128)(2,1)} %get-tuple-element.453), channel_id=1, source_target_pairs={{0,8},{4,12},{8,0},{12,4},{1,9},{5,13},{9,1},{13,5},{2,10},{6,14},... | collective-permute-start | bytes 196616 | tf_op jit(solution)/shard_map/ppermute | solution.py:20
  84.7 16.1 %collective-permute-start.11 = (bf16[128,256]{1,0:T(8,128)(2,1)}, bf16[128,256]{1,0:T(8,128)(2,1)S(1)}, u32[]{:S(2)}, u32[]{:S(2)}) collective-permute-start(bf16[128,256]{1,0:T(8,128)(2,1)} %get-tuple-element.454), channel_id=1, source_target_pairs={{0,4},{4,8},{8,12},{12,0},{1,5},{5,9},{9,13},{13,1},{2,6},{6,10},{... | collective-permute-start | bytes 196616 | tf_op jit(solution)/shard_map/ppermute | solution.py:20
  96.8 5.2 %collective-permute-start.9 = (bf16[128,256]{1,0:T(8,128)(2,1)}, bf16[128,256]{1,0:T(8,128)(2,1)S(1)}, u32[]{:S(2)}, u32[]{:S(2)}) collective-permute-start(bf16[128,256]{1,0:T(8,128)(2,1)} %get-tuple-element.452), channel_id=1, source_target_pairs={{0,12},{4,0},{8,4},{12,8},{1,13},{5,1},{9,5},{13,9},{2,14},{6,2},{... | collective-permute-start | bytes 196616 | tf_op jit(solution)/shard_map/ppermute | solution.py:20
  (2 other events, 1.7 us)

commit v10 on v8

--- a/solution.py
+++ b/solution.py
@@ -281,7 +281,9 @@
     own_index = lax.axis_index("seq")
     head_count = live_counts.shape[0]
     per_device = head_count // seq_count
-    if per_device % 4 == 0:
+    if per_device % 8 == 0:
+        sizes = [per_device * 5 // 8, per_device * 2 // 8, per_device // 8]
+    elif per_device % 4 == 0:
         sizes = [per_device * 3 // 4, per_device // 4]
     else:
         sizes = [per_device]

time: 104 us -> 110 us (1.058)
  waiting for transfers between devices: 37.6 us -> 29.9 us
  starting transfers between devices: 39.3 us -> 46.2 us
  Pallas kernels: 18.7 us -> 22.8 us
  matrix products: 0.77 us -> 2.85 us
    ppermute x13 -> x19, waiting for transfers between devices: 37.6 us -> 29.9 us  [passed_along(): return lax.ppermute(value, axis, pairs)]
    ppermute x13 -> x19, starting transfers between devices: 39.3 us -> 46.2 us  [passed_along(): return lax.ppermute(value, axis, pairs)]
    pallas_call x3 -> x4, Pallas kernels: 5.83 us -> 8.2 us  [branch(): pl.pallas_call(kernel, in_specs=[pl.BlockSpec(memory_space=pltpu.VMEM)] *...]
    dot_general x1, matrix products: 0.77 us -> 2.85 us  [local(): velocity = jnp.dot(shaped, head_weight, preferred_element_type=jnp.float32)]
    pallas_call x2 -> x3, Pallas kernels: 12.8 us -> 14.6 us  [attend_pieces(): pl.pallas_call(kernel, in_specs=[pl.BlockSpec(memory_space=smem)] * 3 + [...]
  transfers between devices with their start and end apart: 13 -> 19, of which waited for: 4 -> 5; matrix products, arithmetic and copies ran while one was open for 5% -> 8% of each run, Pallas kernels for 15% -> 18%
where the time goes in v10:
time: 110 us
  starting transfers between devices  46.2 us (42%)
  waiting for transfers between devices  29.9 us (27%)
  Pallas kernels  22.8 us (21%)
  local copies, waits for them, and re-layouts  5.72 us (5%)
  matrix products  2.85 us (3%)
  between operations  1.5 us (1%)
    ppermute x19, starting transfers between devices, passed_along(): return lax.ppermute(value, axis, pairs)  46.2 us
    ppermute x19, waiting for transfers between devices, passed_along(): return lax.ppermute(value, axis, pairs)  29.9 us
    pallas_call x3, Pallas kernels, attend_pieces(): pl.pallas_call(kernel, in_specs=[pl.BlockSpec(memory_space=smem)] * 3 + [...  14.6 us
    pallas_call x4, Pallas kernels, branch(): pl.pallas_call(kernel, in_specs=[pl.BlockSpec(memory_space=pltpu.VMEM)] *...  8.2 us
    dot_general x1, matrix products, local(): velocity = jnp.dot(shaped, head_weight, preferred_element_type=jnp.float32)  2.85 us
  transfers between devices with their start and end apart: 19, of which 5 were waited for; matrix products, arithmetic and copies ran while one was open for 8% of the time, Pallas kernels for 18%

profile of v10, /device:TPU:0, one launch (start us, length us, event | category | flops | bytes accessed | tf_op | source)
XLA Modules:
  0.0 109.8 jit_solution(17412535471145574742)
XLA Ops:
  0.7 3.3 %conditional.4 = ((bf16[3,128,640]{2,1,0:T(8,128)(2,1)}, bf16[3,128,640]{2,1,0:T(8,128)(2,1)}, bf16[3,128,640]{2,1,0:T(8,128)(2,1)}, bf16[3,128,640]{2,1,0:T(8,128)(2,1)})) conditional(s32[]{:T(128)} %clamp.2, (bf16[1,128,4096]{2,1,0:T(8,128)(2,1)}, bf16[1,128,4096]{2,1,0:T(8,128)(2,1)}, ...), branch_computations={%region_0.0_spmd, %region_1.0_spmd, %region_2.0_spmd, %region_3.0_... | conditional | bytes 8 | solution.py:171
  0.7 3.2 %branch_0_fun.4 = (bf16[3,128,640]{2,1,0:T(8,128)(2,1)}, bf16[3,128,640]{2,1,0:T(8,128)(2,1)}, bf16[3,128,640]{2,1,0:T(8,128)(2,1)}, bf16[3,128,640]{2,1,0:T(8,128)(2,1)}) custom-call(bf16[1,128,4096]{2,1,0:T(8,128)(2,1)} %get-tuple-element.153.refs_0_, bf16[1,128,4096]{2,1,0:T(8,128)(2,1)} %get-tuple-element.154.refs_1_, ...), custom_call_target="tpu_custom_call" | custom-call | tf_op jit(solution)/shard_map/cond/branch_0_fun/pallas_call | solution.py:162
  3.9 3.1 %collective-permute-start = (bf16[3,128,640]{2,1,0:T(8,128)(2,1)}, bf16[3,128,640]{2,1,0:T(8,128)(2,1)S(1)}, u32[]{:S(2)}, u32[]{:S(2)}) collective-permute-start(bf16[3,128,640]{2,1,0:T(8,128)(2,1)} %get-tuple-element.292), channel_id=1, source_target_pairs={{0,4},{4,8},{8,12},{12,0},{1,5},{5,9},{9,13},{13,1},{2,6},{6,10},{... | collective-permute-start | bytes 1474568 | tf_op jit(solution)/shard_map/ppermute | solution.py:20
  7.0 2.6 %collective-permute-start.1 = (bf16[3,128,640]{2,1,0:T(8,128)(2,1)}, bf16[3,128,640]{2,1,0:T(8,128)(2,1)S(1)}, u32[]{:S(2)}, u32[]{:S(2)}) collective-permute-start(bf16[3,128,640]{2,1,0:T(8,128)(2,1)} %get-tuple-element.293), channel_id=1, source_target_pairs={{0,8},{4,12},{8,0},{12,4},{1,9},{5,13},{9,1},{13,5},{2,10},{6,14},... | collective-permute-start | bytes 1474568 | tf_op jit(solution)/shard_map/ppermute | solution.py:20
  10.9 2.8 %conditional.5 = ((bf16[3,128,256]{2,1,0:T(8,128)(2,1)}, bf16[3,128,256]{2,1,0:T(8,128)(2,1)}, bf16[3,128,256]{2,1,0:T(8,128)(2,1)}, bf16[3,128,256]{2,1,0:T(8,128)(2,1)})) conditional(s32[]{:T(128)} %clamp.2, (bf16[1,128,4096]{2,1,0:T(8,128)(2,1)}, bf16[1,128,4096]{2,1,0:T(8,128)(2,1)}, ...), branch_computations={%region_4.0_spmd, %region_5.0_spmd, %region_6.0_spmd, %region_7.0_... | conditional | bytes 8 | solution.py:171
  10.9 2.8 %branch_0_fun.5 = (bf16[3,128,256]{2,1,0:T(8,128)(2,1)}, bf16[3,128,256]{2,1,0:T(8,128)(2,1)}, bf16[3,128,256]{2,1,0:T(8,128)(2,1)}, bf16[3,128,256]{2,1,0:T(8,128)(2,1)}) custom-call(bf16[1,128,4096]{2,1,0:T(8,128)(2,1)} %get-tuple-element.185.refs_0_, bf16[1,128,4096]{2,1,0:T(8,128)(2,1)} %get-tuple-element.186.refs_1_, ...), custom_call_target="tpu_custom_call" | custom-call | tf_op jit(solution)/shard_map/cond/branch_0_fun/pallas_call | solution.py:162
  16.9 4.5 %collective-permute-done.refs_1_ = bf16[3,128,640]{2,1,0:T(8,128)(2,1)S(1)} collective-permute-done((bf16[3,128,640]{2,1,0:T(8,128)(2,1)}, bf16[3,128,640]{2,1,0:T(8,128)(2,1)S(1)}, u32[]{:S(2)}, u32[]{:S(2)}) %collective-permute-start) | collective-permute-done | bytes 491552 | tf_op jit(solution)/shard_map/ppermute | solution.py:20
  21.4 20.2 %collective-permute-done.1.refs_2_ = bf16[3,128,640]{2,1,0:T(8,128)(2,1)S(1)} collective-permute-done((bf16[3,128,640]{2,1,0:T(8,128)(2,1)}, bf16[3,128,640]{2,1,0:T(8,128)(2,1)S(1)}, u32[]{:S(2)}, u32[]{:S(2)}) %collective-permute-start.1) | collective-permute-done | bytes 491552 | tf_op jit(solution)/shard_map/ppermute | solution.py:20
  41.6 11.1 %collective-permute-start.6 = (bf16[3,128,256]{2,1,0:T(8,128)(2,1)}, bf16[3,128,256]{2,1,0:T(8,128)(2,1)S(1)}, u32[]{:S(2)}, u32[]{:S(2)}) collective-permute-start(bf16[3,128,256]{2,1,0:T(8,128)(2,1)} %get-tuple-element.304), channel_id=1, source_target_pairs={{0,4},{4,8},{8,12},{12,0},{1,5},{5,9},{9,13},{13,1},{2,6},{6,10},{... | collective-permute-start | bytes 589832 | tf_op jit(solution)/shard_map/ppermute | solution.py:20
  52.7 1.5 %collective-permute-start.7 = (bf16[3,128,256]{2,1,0:T(8,128)(2,1)}, bf16[3,128,256]{2,1,0:T(8,128)(2,1)S(1)}, u32[]{:S(2)}, u32[]{:S(2)}) collective-permute-start(bf16[3,128,256]{2,1,0:T(8,128)(2,1)} %get-tuple-element.305), channel_id=1, source_target_pairs={{0,8},{4,12},{8,0},{12,4},{1,9},{5,13},{9,1},{13,5},{2,10},{6,14},... | collective-permute-start | bytes 589832 | tf_op jit(solution)/shard_map/ppermute | solution.py:20
  55.1 7.6 %shard_map.113 = (bf16[128,640]{1,0:T(8,128)(2,1)S(1)}, bf16[128,640]{1,0:T(8,128)(2,1)}, bf16[128,640]{1,0:T(8,128)(2,1)}, bf16[128,640]{1,0:T(8,128)(2,1)}) custom-call(s32[80]{0:T(128)} %reshape.65.lists_ref, s32[20]{0:T(128)} %reshape.66.live_ref, s32[1]{0:T(128)} %bitcast.me_ref, bf16[3,128,640]{2,1,0:T(8,128)(2,1)} %get-tuple-element.291.refs_0_, ...), custom_call_target="tpu_custom_call" | custom-call | tf_op jit(solution)/shard_map/pallas_call | solution.py:231
  62.7 2.0 %collective-permute-start.3 = (bf16[128,640]{1,0:T(8,128)(2,1)}, bf16[128,640]{1,0:T(8,128)(2,1)S(1)}, u32[]{:S(2)}, u32[]{:S(2)}) collective-permute-start(bf16[128,640]{1,0:T(8,128)(2,1)} %get-tuple-element.296), channel_id=1, source_target_pairs={{0,12},{4,0},{8,4},{12,8},{1,13},{5,1},{9,5},{13,9},{2,14},{6,2},{... | collective-permute-start | bytes 491528 | tf_op jit(solution)/shard_map/ppermute | solution.py:20
  64.8 2.9 %fusion.15 = f32[1,128,64]{1,2,0:T(8,128)} fusion(bf16[5120,64]{0,1:T(8,128)(2,1)S(1)} %copy-done, bf16[1,128,5120]{2,1,0:T(8,128)(2,1)} %param.29, f32[5120]{0:T(1024)S(1)} %bitcast.33, f32[5120]{0:T(1024)S(1)} %bitcast.32, f32[128]{0:T(128)S(1)} %add_rsqrt_fusion, f32[128]{0:T(128)S(1)} %broadcast_multiply_fusion, f32[1,128,64]{1,2,0:T(8,128)} %param.32, ...), kind=kOutput, calls=%fused_computation.12 | convolution fusion | flops 87834624 | bytes 2073604 | tf_op jit(solution)/shard_map/dot_general | solution.py:346
  67.7 2.1 %conditional.6 = ((bf16[3,128,128]{2,1,0:T(8,128)(2,1)}, bf16[3,128,128]{2,1,0:T(8,128)(2,1)}, bf16[3,128,128]{2,1,0:T(8,128)(2,1)}, bf16[3,128,128]{2,1,0:T(8,128)(2,1)})) conditional(s32[]{:T(128)} %clamp.2, (bf16[1,128,4096]{2,1,0:T(8,128)(2,1)S(1)}, bf16[1,128,4096]{2,1,0:T(8,128)(2,1)S(1)}, ...), branch_computations={%region_8.0_spmd, %region_9.0_spmd, %region_10.0_spmd, %region_11.... | conditional | bytes 8 | solution.py:171
  67.7 2.1 %branch_0_fun.6 = (bf16[3,128,128]{2,1,0:T(8,128)(2,1)}, bf16[3,128,128]{2,1,0:T(8,128)(2,1)}, bf16[3,128,128]{2,1,0:T(8,128)(2,1)}, bf16[3,128,128]{2,1,0:T(8,128)(2,1)}) custom-call(bf16[1,128,4096]{2,1,0:T(8,128)(2,1)S(1)} %get-tuple-element.197.refs_0_, bf16[1,128,4096]{2,1,0:T(8,128)(2,1)S(1)} %get-tuple-element.198.refs_1_, ...), custom_call_target="tpu_custom_call" | custom-call | tf_op jit(solution)/shard_map/cond/branch_0_fun/pallas_call | solution.py:162
  71.1 6.8 %collective-permute-start.5 = (bf16[128,640]{1,0:T(8,128)(2,1)}, bf16[128,640]{1,0:T(8,128)(2,1)S(1)}, u32[]{:S(2)}, u32[]{:S(2)}) collective-permute-start(bf16[128,640]{1,0:T(8,128)(2,1)} %get-tuple-element.298), channel_id=1, source_target_pairs={{0,4},{4,8},{8,12},{12,0},{1,5},{5,9},{9,13},{13,1},{2,6},{6,10},{... | collective-permute-start | bytes 491528 | tf_op jit(solution)/shard_map/ppermute | solution.py:20
  77.9 3.5 %collective-permute-start.13 = (bf16[3,128,128]{2,1,0:T(8,128)(2,1)}, bf16[3,128,128]{2,1,0:T(8,128)(2,1)S(1)}, u32[]{:S(2)}, u32[]{:S(2)}) collective-permute-start(bf16[3,128,128]{2,1,0:T(8,128)(2,1)} %get-tuple-element.317), channel_id=1, source_target_pairs={{0,8},{4,12},{8,0},{12,4},{1,9},{5,13},{9,1},{13,5},{2,10},{6,14},... | collective-permute-start | bytes 294920 | tf_op jit(solution)/shard_map/ppermute | solution.py:20
  81.5 2.9 %collective-permute-start.14 = (bf16[3,128,128]{2,1,0:T(8,128)(2,1)}, bf16[3,128,128]{2,1,0:T(8,128)(2,1)S(1)}, u32[]{:S(2)}, u32[]{:S(2)}) collective-permute-start(bf16[3,128,128]{2,1,0:T(8,128)(2,1)} %get-tuple-element.318), channel_id=1, source_target_pairs={{0,12},{4,0},{8,4},{12,8},{1,13},{5,1},{9,5},{13,9},{2,14},{6,2},{... | collective-permute-start | bytes 294920 | tf_op jit(solution)/shard_map/ppermute | solution.py:20
  85.1 4.1 %shard_map.114 = (bf16[128,256]{1,0:T(8,128)(2,1)S(1)}, bf16[128,256]{1,0:T(8,128)(2,1)}, bf16[128,256]{1,0:T(8,128)(2,1)}, bf16[128,256]{1,0:T(8,128)(2,1)}) custom-call(s32[32]{0:T(128)} %reshape.68.lists_ref, s32[8]{0:T(128)} %reshape.69.live_ref, s32[1]{0:T(128)} %bitcast.me_ref, bf16[3,128,256]{2,1,0:T(8,128)(2,1)} %get-tuple-element.303.refs_0_, ...), custom_call_target="tpu_custom_call" | custom-call | tf_op jit(solution)/shard_map/pallas_call | solution.py:231
  89.2 4.0 %collective-permute-start.10 = (bf16[128,256]{1,0:T(8,128)(2,1)}, bf16[128,256]{1,0:T(8,128)(2,1)S(1)}, u32[]{:S(2)}, u32[]{:S(2)}) collective-permute-start(bf16[128,256]{1,0:T(8,128)(2,1)} %get-tuple-element.309), channel_id=1, source_target_pairs={{0,8},{4,12},{8,0},{12,4},{1,9},{5,13},{9,1},{13,5},{2,10},{6,14},... | collective-permute-start | bytes 196616 | tf_op jit(solution)/shard_map/ppermute | solution.py:20
  93.5 3.5 %collective-permute-start.9 = (bf16[128,256]{1,0:T(8,128)(2,1)}, bf16[128,256]{1,0:T(8,128)(2,1)S(1)}, u32[]{:S(2)}, u32[]{:S(2)}) collective-permute-start(bf16[128,256]{1,0:T(8,128)(2,1)} %get-tuple-element.308), channel_id=1, source_target_pairs={{0,12},{4,0},{8,4},{12,8},{1,13},{5,1},{9,5},{13,9},{2,14},{6,2},{... | collective-permute-start | bytes 196616 | tf_op jit(solution)/shard_map/ppermute | solution.py:20
  98.7 2.8 %shard_map.115 = (bf16[128,128]{1,0:T(8,128)(2,1)S(1)}, bf16[128,128]{1,0:T(8,128)(2,1)}, bf16[128,128]{1,0:T(8,128)(2,1)}, bf16[128,128]{1,0:T(8,128)(2,1)}) custom-call(s32[16]{0:T(128)} %reshape.70.lists_ref, s32[4]{0:T(128)} %dynamic-slice_reduce_fusion.1.live_ref, s32[1]{0:T(128)} %bitcast.me_ref, bf16[3,128,128]{2,1,0:T(8,128)(2,1)} %get-tuple-element.315.refs_0_, ...), custom_call_target="tpu_custom_call" | custom-call | tf_op jit(solution)/shard_map/pallas_call | solution.py:231
  103.6 2.4 %collective-permute-done.15 = bf16[128,128]{1,0:T(8,128)(2,1)S(1)} collective-permute-done((bf16[128,128]{1,0:T(8,128)(2,1)}, bf16[128,128]{1,0:T(8,128)(2,1)S(1)}, u32[]{:S(2)}, u32[]{:S(2)}) %collective-permute-start.15) | collective-permute-done | bytes 32800 | tf_op jit(solution)/shard_map/ppermute | solution.py:20
  106.0 1.8 %collective-permute-done.16 = bf16[128,128]{1,0:T(8,128)(2,1)S(1)} collective-permute-done((bf16[128,128]{1,0:T(8,128)(2,1)}, bf16[128,128]{1,0:T(8,128)(2,1)S(1)}, u32[]{:S(2)}, u32[]{:S(2)}) %collective-permute-start.16) | collective-permute-done | bytes 32800 | tf_op jit(solution)/shard_map/ppermute | solution.py:20
  (77 shorter events, 13.0 us)
Async XLA Ops:
  0.6 64.1 %copy-start = (bf16[5120,64]{0,1:T(8,128)(2,1)S(1)}, bf16[5120,64]{0,1:T(8,128)(2,1)}, u32[]{:S(2)}) copy-start(bf16[5120,64]{0,1:T(8,128)(2,1)} %param.31) | copy-start | bytes 1966084
  3.9 17.5 %collective-permute-start = (bf16[3,128,640]{2,1,0:T(8,128)(2,1)}, bf16[3,128,640]{2,1,0:T(8,128)(2,1)S(1)}, u32[]{:S(2)}, u32[]{:S(2)}) collective-permute-start(bf16[3,128,640]{2,1,0:T(8,128)(2,1)} %get-tuple-element.292), channel_id=1, source_target_pairs={{0,4},{4,8},{8,12},{12,0},{1,5},{5,9},{9,13},{13,1},{2,6},{6,10},{... | collective-permute-start | bytes 1474568 | tf_op jit(solution)/shard_map/ppermute | solution.py:20
  7.0 34.7 %collective-permute-start.1 = (bf16[3,128,640]{2,1,0:T(8,128)(2,1)}, bf16[3,128,640]{2,1,0:T(8,128)(2,1)S(1)}, u32[]{:S(2)}, u32[]{:S(2)}) collective-permute-start(bf16[3,128,640]{2,1,0:T(8,128)(2,1)} %get-tuple-element.293), channel_id=1, source_target_pairs={{0,8},{4,12},{8,0},{12,4},{1,9},{5,13},{9,1},{13,5},{2,10},{6,14},... | collective-permute-start | bytes 1474568 | tf_op jit(solution)/shard_map/ppermute | solution.py:20
  9.6 32.1 %collective-permute-start.2 = (bf16[3,128,640]{2,1,0:T(8,128)(2,1)}, bf16[3,128,640]{2,1,0:T(8,128)(2,1)}, u32[]{:S(2)}, u32[]{:S(2)}) collective-permute-start(bf16[3,128,640]{2,1,0:T(8,128)(2,1)} %get-tuple-element.294), channel_id=1, source_target_pairs={{0,12},{4,0},{8,4},{12,8},{1,13},{5,1},{9,5},{13,9},{2,14},{6,2},{... | collective-permute-start | bytes 1474568 | tf_op jit(solution)/shard_map/ppermute | solution.py:20
  21.4 33.7 %copy-start.5 = (bf16[3,128,640]{2,1,0:T(8,128)(2,1)}, bf16[3,128,640]{2,1,0:T(8,128)(2,1)S(1)}, u32[]{:S(2)}) copy-start(bf16[3,128,640]{2,1,0:T(8,128)(2,1)S(1)} %collective-permute-done.refs_1_) | copy-start | bytes 1474564
  41.6 13.5 %copy-start.6 = (bf16[3,128,640]{2,1,0:T(8,128)(2,1)}, bf16[3,128,640]{2,1,0:T(8,128)(2,1)S(1)}, u32[]{:S(2)}) copy-start(bf16[3,128,640]{2,1,0:T(8,128)(2,1)S(1)} %collective-permute-done.1.refs_2_) | copy-start | bytes 1474564
  41.6 28.8 %collective-permute-start.6 = (bf16[3,128,256]{2,1,0:T(8,128)(2,1)}, bf16[3,128,256]{2,1,0:T(8,128)(2,1)S(1)}, u32[]{:S(2)}, u32[]{:S(2)}) collective-permute-start(bf16[3,128,256]{2,1,0:T(8,128)(2,1)} %get-tuple-element.304), channel_id=1, source_target_pairs={{0,4},{4,8},{8,12},{12,0},{1,5},{5,9},{9,13},{13,1},{2,6},{6,10},{... | collective-permute-start | bytes 589832 | tf_op jit(solution)/shard_map/ppermute | solution.py:20
  52.7 18.3 %collective-permute-start.7 = (bf16[3,128,256]{2,1,0:T(8,128)(2,1)}, bf16[3,128,256]{2,1,0:T(8,128)(2,1)S(1)}, u32[]{:S(2)}, u32[]{:S(2)}) collective-permute-start(bf16[3,128,256]{2,1,0:T(8,128)(2,1)} %get-tuple-element.305), channel_id=1, source_target_pairs={{0,8},{4,12},{8,0},{12,4},{1,9},{5,13},{9,1},{13,5},{2,10},{6,14},... | collective-permute-start | bytes 589832 | tf_op jit(solution)/shard_map/ppermute | solution.py:20
  54.2 23.7 %collective-permute-start.8 = (bf16[3,128,256]{2,1,0:T(8,128)(2,1)}, bf16[3,128,256]{2,1,0:T(8,128)(2,1)}, u32[]{:S(2)}, u32[]{:S(2)}) collective-permute-start(bf16[3,128,256]{2,1,0:T(8,128)(2,1)} %get-tuple-element.306), channel_id=1, source_target_pairs={{0,12},{4,0},{8,4},{12,8},{1,13},{5,1},{9,5},{13,9},{2,14},{6,2},{... | collective-permute-start | bytes 589832 | tf_op jit(solution)/shard_map/ppermute | solution.py:20
  62.7 18.7 %collective-permute-start.3 = (bf16[128,640]{1,0:T(8,128)(2,1)}, bf16[128,640]{1,0:T(8,128)(2,1)S(1)}, u32[]{:S(2)}, u32[]{:S(2)}) collective-permute-start(bf16[128,640]{1,0:T(8,128)(2,1)} %get-tuple-element.296), channel_id=1, source_target_pairs={{0,12},{4,0},{8,4},{12,8},{1,13},{5,1},{9,5},{13,9},{2,14},{6,2},{... | collective-permute-start | bytes 491528 | tf_op jit(solution)/shard_map/ppermute | solution.py:20
  67.6 10.3 %collective-permute-start.18 = (f32[1,128,64]{1,2,0:T(8,128)}, f32[1,128,64]{1,2,0:T(8,128)S(1)}, u32[]{:S(2)}, u32[]{:S(2)}) collective-permute-start(f32[1,128,64]{1,2,0:T(8,128)} %fusion.15), channel_id=1, source_target_pairs={{0,3},{1,0},{2,1},{3,2},{4,7},{5,4},{6,5},{7,6},{8,11},{9,8},{10,9... | collective-permute-start | bytes 98312 | tf_op jit(solution)/shard_map/ppermute | solution.py:20
  70.5 14.6 %copy-start.7 = (bf16[3,128,256]{2,1,0:T(8,128)(2,1)}, bf16[3,128,256]{2,1,0:T(8,128)(2,1)S(1)}, u32[]{:S(2)}) copy-start(bf16[3,128,256]{2,1,0:T(8,128)(2,1)S(1)} %collective-permute-done.6.refs_1_) | copy-start | bytes 589828
  70.5 31.0 %collective-permute-start.4 = (bf16[128,640]{1,0:T(8,128)(2,1)}, bf16[128,640]{1,0:T(8,128)(2,1)S(1)}, u32[]{:S(2)}, u32[]{:S(2)}) collective-permute-start(bf16[128,640]{1,0:T(8,128)(2,1)} %get-tuple-element.297), channel_id=1, source_target_pairs={{0,8},{4,12},{8,0},{12,4},{1,9},{5,13},{9,1},{13,5},{2,10},{6,14},... | collective-permute-start | bytes 491528 | tf_op jit(solution)/shard_map/ppermute | solution.py:20
  71.1 14.0 %copy-start.8 = (bf16[3,128,256]{2,1,0:T(8,128)(2,1)}, bf16[3,128,256]{2,1,0:T(8,128)(2,1)S(1)}, u32[]{:S(2)}) copy-start(bf16[3,128,256]{2,1,0:T(8,128)(2,1)S(1)} %collective-permute-done.7.refs_2_) | copy-start | bytes 589828
  71.1 31.6 %collective-permute-start.5 = (bf16[128,640]{1,0:T(8,128)(2,1)}, bf16[128,640]{1,0:T(8,128)(2,1)S(1)}, u32[]{:S(2)}, u32[]{:S(2)}) collective-permute-start(bf16[128,640]{1,0:T(8,128)(2,1)} %get-tuple-element.298), channel_id=1, source_target_pairs={{0,4},{4,8},{8,12},{12,0},{1,5},{5,9},{9,13},{13,1},{2,6},{6,10},{... | collective-permute-start | bytes 491528 | tf_op jit(solution)/shard_map/ppermute | solution.py:20
  77.9 11.3 %collective-permute-start.12 = (bf16[3,128,128]{2,1,0:T(8,128)(2,1)}, bf16[3,128,128]{2,1,0:T(8,128)(2,1)S(1)}, u32[]{:S(2)}, u32[]{:S(2)}) collective-permute-start(bf16[3,128,128]{2,1,0:T(8,128)(2,1)} %get-tuple-element.316), channel_id=1, source_target_pairs={{0,4},{4,8},{8,12},{12,0},{1,5},{5,9},{9,13},{13,1},{2,6},{6,10},{... | collective-permute-start | bytes 294920 | tf_op jit(solution)/shard_map/ppermute | solution.py:20
  77.9 15.3 %collective-permute-start.13 = (bf16[3,128,128]{2,1,0:T(8,128)(2,1)}, bf16[3,128,128]{2,1,0:T(8,128)(2,1)S(1)}, u32[]{:S(2)}, u32[]{:S(2)}) collective-permute-start(bf16[3,128,128]{2,1,0:T(8,128)(2,1)} %get-tuple-element.317), channel_id=1, source_target_pairs={{0,8},{4,12},{8,0},{12,4},{1,9},{5,13},{9,1},{13,5},{2,10},{6,14},... | collective-permute-start | bytes 294920 | tf_op jit(solution)/shard_map/ppermute | solution.py:20
  81.5 12.0 %collective-permute-start.14 = (bf16[3,128,128]{2,1,0:T(8,128)(2,1)}, bf16[3,128,128]{2,1,0:T(8,128)(2,1)S(1)}, u32[]{:S(2)}, u32[]{:S(2)}) collective-permute-start(bf16[3,128,128]{2,1,0:T(8,128)(2,1)} %get-tuple-element.318), channel_id=1, source_target_pairs={{0,12},{4,0},{8,4},{12,8},{1,13},{5,1},{9,5},{13,9},{2,14},{6,2},{... | collective-permute-start | bytes 294920 | tf_op jit(solution)/shard_map/ppermute | solution.py:20
  89.2 13.5 %collective-permute-start.10 = (bf16[128,256]{1,0:T(8,128)(2,1)}, bf16[128,256]{1,0:T(8,128)(2,1)S(1)}, u32[]{:S(2)}, u32[]{:S(2)}) collective-permute-start(bf16[128,256]{1,0:T(8,128)(2,1)} %get-tuple-element.309), channel_id=1, source_target_pairs={{0,8},{4,12},{8,0},{12,4},{1,9},{5,13},{9,1},{13,5},{2,10},{6,14},... | collective-permute-start | bytes 196616 | tf_op jit(solution)/shard_map/ppermute | solution.py:20
  93.2 10.4 %collective-permute-start.11 = (bf16[128,256]{1,0:T(8,128)(2,1)}, bf16[128,256]{1,0:T(8,128)(2,1)S(1)}, u32[]{:S(2)}, u32[]{:S(2)}) collective-permute-start(bf16[128,256]{1,0:T(8,128)(2,1)} %get-tuple-element.310), channel_id=1, source_target_pairs={{0,4},{4,8},{8,12},{12,0},{1,5},{5,9},{9,13},{13,1},{2,6},{6,10},{... | collective-permute-start | bytes 196616 | tf_op jit(solution)/shard_map/ppermute | solution.py:20
  93.5 10.1 %collective-permute-start.9 = (bf16[128,256]{1,0:T(8,128)(2,1)}, bf16[128,256]{1,0:T(8,128)(2,1)S(1)}, u32[]{:S(2)}, u32[]{:S(2)}) collective-permute-start(bf16[128,256]{1,0:T(8,128)(2,1)} %get-tuple-element.308), channel_id=1, source_target_pairs={{0,12},{4,0},{8,4},{12,8},{1,13},{5,1},{9,5},{13,9},{2,14},{6,2},{... | collective-permute-start | bytes 196616 | tf_op jit(solution)/shard_map/ppermute | solution.py:20
  101.5 4.5 %collective-permute-start.15 = (bf16[128,128]{1,0:T(8,128)(2,1)}, bf16[128,128]{1,0:T(8,128)(2,1)S(1)}, u32[]{:S(2)}, u32[]{:S(2)}) collective-permute-start(bf16[128,128]{1,0:T(8,128)(2,1)} %get-tuple-element.320), channel_id=1, source_target_pairs={{0,12},{4,0},{8,4},{12,8},{1,13},{5,1},{9,5},{13,9},{2,14},{6,2},{... | collective-permute-start | bytes 98312 | tf_op jit(solution)/shard_map/ppermute | solution.py:20
  102.7 5.0 %collective-permute-start.16 = (bf16[128,128]{1,0:T(8,128)(2,1)}, bf16[128,128]{1,0:T(8,128)(2,1)S(1)}, u32[]{:S(2)}, u32[]{:S(2)}) collective-permute-start(bf16[128,128]{1,0:T(8,128)(2,1)} %get-tuple-element.321), channel_id=1, source_target_pairs={{0,8},{4,12},{8,0},{12,4},{1,9},{5,13},{9,1},{13,5},{2,10},{6,14},... | collective-permute-start | bytes 98312 | tf_op jit(solution)/shard_map/ppermute | solution.py:20
  102.7 6.0 %collective-permute-start.17 = (bf16[128,128]{1,0:T(8,128)(2,1)}, bf16[128,128]{1,0:T(8,128)(2,1)S(1)}, u32[]{:S(2)}, u32[]{:S(2)}) collective-permute-start(bf16[128,128]{1,0:T(8,128)(2,1)} %get-tuple-element.322), channel_id=1, source_target_pairs={{0,4},{4,8},{8,12},{12,0},{1,5},{5,9},{9,13},{13,1},{2,6},{6,10},{... | collective-permute-start | bytes 98312 | tf_op jit(solution)/shard_map/ppermute | solution.py:20
  (10 other events, 44.6 us)

commit v11 on v8

--- a/solution.py
+++ b/solution.py
@@ -182,7 +182,7 @@
     column = lax.broadcasted_iota(jnp.int32, (1, total), 1)
     for head in range(heads):
         cols = slice(head * depth, (head + 1) * depth)
-        keys = jnp.concatenate([ref[1, :, cols] for ref in x_refs], axis=0)
+        keys = jnp.concatenate([ref[1, :, cols] for ref in x_refs], axis=0).T
         values = jnp.concatenate([ref[2, :, cols] for ref in x_refs], axis=0)
         for step in range(sources):
             device = (me - step + sources) % sources
@@ -197,13 +197,10 @@
                     place = (me - chosen // per_source + sources) % sources
                     low = place * tokens + (chosen % per_source) * block
                     active = active | ((column >= low) & (column < low + block) & (slot < live))
+                bias = jnp.where(active, 0.0, -jnp.inf).astype(jnp.float32)
                 scores = (
-                    lax.dot_general(
-                        query, keys, (((1,), (1,)), ((), ())), preferred_element_type=jnp.float32
-                    )
-                    * scale
+                    jnp.dot(query, keys, preferred_element_type=jnp.float32) * scale + bias
                 )
-                scores = jnp.where(active, scores, -jnp.inf)
                 highest = jnp.max(scores, axis=1, keepdims=True)
                 weights = jnp.exp(scores - highest)
                 totals = jnp.sum(weights, axis=1, keepdims=True)

time: 104 us -> 104 us (level)
  no operation moved by 1% of the time
where the time goes in v11:
time: 104 us
  starting transfers between devices  39.3 us (38%)
  waiting for transfers between devices  37.6 us (36%)
  Pallas kernels  18.7 us (18%)
  local copies, waits for them, and re-layouts  4.98 us (5%)
  between operations  1.55 us (1%)
    ppermute x13, starting transfers between devices, passed_along(): return lax.ppermute(value, axis, pairs)  39.3 us
    ppermute x13, waiting for transfers between devices, passed_along(): return lax.ppermute(value, axis, pairs)  37.6 us
    pallas_call x2, Pallas kernels, attend_pieces(): pl.pallas_call(kernel, in_specs=[pl.BlockSpec(memory_space=smem)] * 3 + [...  12.8 us
    pallas_call x3, Pallas kernels, branch(): pl.pallas_call(kernel, in_specs=[pl.BlockSpec(memory_space=pltpu.VMEM)] *...  5.83 us
  transfers between devices with their start and end apart: 13, of which 4 were waited for; matrix products, arithmetic and copies ran while one was open for 5% of the time, Pallas kernels for 15%

profile of v11, /device:TPU:0, one launch (start us, length us, event | category | flops | bytes accessed | tf_op | source)
XLA Modules:
  0.0 103.8 jit_solution(14154928821083425252)
XLA Ops:
  0.7 3.5 %conditional.3 = ((bf16[3,128,768]{2,1,0:T(8,128)(2,1)}, bf16[3,128,768]{2,1,0:T(8,128)(2,1)}, bf16[3,128,768]{2,1,0:T(8,128)(2,1)}, bf16[3,128,768]{2,1,0:T(8,128)(2,1)})) conditional(s32[]{:T(128)} %clamp.2, (bf16[1,128,4096]{2,1,0:T(8,128)(2,1)}, bf16[1,128,4096]{2,1,0:T(8,128)(2,1)}, ...), branch_computations={%region_0.0_spmd, %region_1.0_spmd, %region_2.0_spmd, %region_3.0_... | conditional | bytes 8 | solution.py:171
  0.7 3.4 %branch_0_fun.3 = (bf16[3,128,768]{2,1,0:T(8,128)(2,1)}, bf16[3,128,768]{2,1,0:T(8,128)(2,1)}, bf16[3,128,768]{2,1,0:T(8,128)(2,1)}, bf16[3,128,768]{2,1,0:T(8,128)(2,1)}) custom-call(bf16[1,128,4096]{2,1,0:T(8,128)(2,1)} %get-tuple-element.87.refs_0_, bf16[1,128,4096]{2,1,0:T(8,128)(2,1)} %get-tuple-element.102.refs_1_, ...), custom_call_target="tpu_custom_call" | custom-call | tf_op jit(solution)/shard_map/cond/branch_0_fun/pallas_call | solution.py:162
  4.1 3.1 %collective-permute-start = (bf16[3,128,768]{2,1,0:T(8,128)(2,1)}, bf16[3,128,768]{2,1,0:T(8,128)(2,1)}, u32[]{:S(2)}, u32[]{:S(2)}) collective-permute-start(bf16[3,128,768]{2,1,0:T(8,128)(2,1)} %get-tuple-element.196), channel_id=1, source_target_pairs={{0,4},{4,8},{8,12},{12,0},{1,5},{5,9},{9,13},{13,1},{2,6},{6,10},{... | collective-permute-start | bytes 1769480 | tf_op jit(solution)/shard_map/ppermute | solution.py:20
  7.2 2.6 %collective-permute-start.1 = (bf16[3,128,768]{2,1,0:T(8,128)(2,1)}, bf16[3,128,768]{2,1,0:T(8,128)(2,1)}, u32[]{:S(2)}, u32[]{:S(2)}) collective-permute-start(bf16[3,128,768]{2,1,0:T(8,128)(2,1)} %get-tuple-element.197), channel_id=1, source_target_pairs={{0,8},{4,12},{8,0},{12,4},{1,9},{5,13},{9,1},{13,5},{2,10},{6,14},... | collective-permute-start | bytes 1769480 | tf_op jit(solution)/shard_map/ppermute | solution.py:20
  9.8 1.3 %collective-permute-start.2 = (bf16[3,128,768]{2,1,0:T(8,128)(2,1)}, bf16[3,128,768]{2,1,0:T(8,128)(2,1)}, u32[]{:S(2)}, u32[]{:S(2)}) collective-permute-start(bf16[3,128,768]{2,1,0:T(8,128)(2,1)} %get-tuple-element.198), channel_id=1, source_target_pairs={{0,12},{4,0},{8,4},{12,8},{1,13},{5,1},{9,5},{13,9},{2,14},{6,2},{... | collective-permute-start | bytes 1769480 | tf_op jit(solution)/shard_map/ppermute | solution.py:20
  12.0 2.3 %conditional.4 = ((bf16[3,128,256]{2,1,0:T(8,128)(2,1)S(1)}, bf16[3,128,256]{2,1,0:T(8,128)(2,1)S(1)}, bf16[3,128,256]{2,1,0:T(8,128)(2,1)}, bf16[3,128,256]{2,1,0:T(8,128)(2,1)})) conditional(s32[]{:T(128)} %clamp.2, (bf16[1,128,4096]{2,1,0:T(8,128)(2,1)S(1)}, bf16[1,128,4096]{2,1,0:T(8,128)(2,1)}, ...), branch_computations={%region_4.0_spmd, %region_5.0_spmd, %region_6.0_spmd, %region_7.0_... | conditional | bytes 8 | solution.py:171
  12.0 2.3 %branch_0_fun.4 = (bf16[3,128,256]{2,1,0:T(8,128)(2,1)S(1)}, bf16[3,128,256]{2,1,0:T(8,128)(2,1)S(1)}, bf16[3,128,256]{2,1,0:T(8,128)(2,1)}, bf16[3,128,256]{2,1,0:T(8,128)(2,1)}) custom-call(bf16[1,128,4096]{2,1,0:T(8,128)(2,1)S(1)} %get-tuple-element.129.refs_0_, bf16[1,128,4096]{2,1,0:T(8,128)(2,1)} %get-tuple-element.130.refs_1_, ...), custom_call_target="tpu_custom_call" | custom-call | tf_op jit(solution)/shard_map/cond/branch_0_fun/pallas_call | solution.py:162
  15.1 0.8 fusion.15
  15.9 8.0 %collective-permute-done.refs_1_ = bf16[3,128,768]{2,1,0:T(8,128)(2,1)} collective-permute-done((bf16[3,128,768]{2,1,0:T(8,128)(2,1)}, bf16[3,128,768]{2,1,0:T(8,128)(2,1)}, u32[]{:S(2)}, u32[]{:S(2)}) %collective-permute-start) | collective-permute-done | bytes 589856 | tf_op jit(solution)/shard_map/ppermute | solution.py:20
  23.9 24.4 %collective-permute-done.1.refs_2_ = bf16[3,128,768]{2,1,0:T(8,128)(2,1)} collective-permute-done((bf16[3,128,768]{2,1,0:T(8,128)(2,1)}, bf16[3,128,768]{2,1,0:T(8,128)(2,1)}, u32[]{:S(2)}, u32[]{:S(2)}) %collective-permute-start.1) | collective-permute-done | bytes 589856 | tf_op jit(solution)/shard_map/ppermute | solution.py:20
  48.3 13.1 %collective-permute-start.6 = (bf16[3,128,256]{2,1,0:T(8,128)(2,1)S(1)}, bf16[3,128,256]{2,1,0:T(8,128)(2,1)S(1)}, u32[]{:S(2)}, u32[]{:S(2)}) collective-permute-start(bf16[3,128,256]{2,1,0:T(8,128)(2,1)S(1)} %get-tuple-element.208), channel_id=1, source_target_pairs={{0,4},{4,8},{8,12},{12,0},{1,5},{5,9},{9,13},{13,1},{2,6},{6,10},{... | collective-permute-start | bytes 589832 | tf_op jit(solution)/shard_map/ppermute | solution.py:20
  62.2 1.6 %collective-permute-start.7 = (bf16[3,128,256]{2,1,0:T(8,128)(2,1)}, bf16[3,128,256]{2,1,0:T(8,128)(2,1)S(1)}, u32[]{:S(2)}, u32[]{:S(2)}) collective-permute-start(bf16[3,128,256]{2,1,0:T(8,128)(2,1)} %get-tuple-element.209), channel_id=1, source_target_pairs={{0,8},{4,12},{8,0},{12,4},{1,9},{5,13},{9,1},{13,5},{2,10},{6,14},... | collective-permute-start | bytes 589832 | tf_op jit(solution)/shard_map/ppermute | solution.py:20
  64.6 0.8 collective-permute-start.8
  65.4 8.8 %shard_map.113 = (bf16[128,768]{1,0:T(8,128)(2,1)S(1)}, bf16[128,768]{1,0:T(8,128)(2,1)}, bf16[128,768]{1,0:T(8,128)(2,1)}, bf16[128,768]{1,0:T(8,128)(2,1)}) custom-call(s32[96]{0:T(128)} %reshape.58.lists_ref, s32[24]{0:T(128)} %reshape.59.live_ref, s32[1]{0:T(128)} %bitcast.me_ref, bf16[3,128,768]{2,1,0:T(8,128)(2,1)} %get-tuple-element.195.refs_0_, ...), custom_call_target="tpu_custom_call" | custom-call | tf_op jit(solution)/shard_map/pallas_call | solution.py:228
  74.2 2.0 %collective-permute-start.3 = (bf16[128,768]{1,0:T(8,128)(2,1)}, bf16[128,768]{1,0:T(8,128)(2,1)S(1)}, u32[]{:S(2)}, u32[]{:S(2)}) collective-permute-start(bf16[128,768]{1,0:T(8,128)(2,1)} %get-tuple-element.200), channel_id=1, source_target_pairs={{0,12},{4,0},{8,4},{12,8},{1,13},{5,1},{9,5},{13,9},{2,14},{6,2},{... | collective-permute-start | bytes 589832 | tf_op jit(solution)/shard_map/ppermute | solution.py:20
  76.2 0.7 collective-permute-start.4
  77.2 0.7 reshape.61.lists_ref
  78.7 0.7 copy-done.6
  79.3 4.0 %shard_map.114 = (bf16[128,256]{1,0:T(8,128)(2,1)S(1)}, bf16[128,256]{1,0:T(8,128)(2,1)}, bf16[128,256]{1,0:T(8,128)(2,1)}, bf16[128,256]{1,0:T(8,128)(2,1)}) custom-call(s32[32]{0:T(128)} %reshape.61.lists_ref, s32[8]{0:T(128)} %reshape.62.live_ref, s32[1]{0:T(128)} %bitcast.me_ref, bf16[3,128,256]{2,1,0:T(8,128)(2,1)S(1)} %get-tuple-element.207.refs_0_, ...), custom_call_target="tpu_custom_call" | custom-call | tf_op jit(solution)/shard_map/pallas_call | solution.py:228
  83.3 2.2 %collective-permute-start.10 = (bf16[128,256]{1,0:T(8,128)(2,1)}, bf16[128,256]{1,0:T(8,128)(2,1)S(1)}, u32[]{:S(2)}, u32[]{:S(2)}) collective-permute-start(bf16[128,256]{1,0:T(8,128)(2,1)} %get-tuple-element.213), channel_id=1, source_target_pairs={{0,8},{4,12},{8,0},{12,4},{1,9},{5,13},{9,1},{13,5},{2,10},{6,14},... | collective-permute-start | bytes 196616 | tf_op jit(solution)/shard_map/ppermute | solution.py:20
  85.6 11.9 %collective-permute-start.11 = (bf16[128,256]{1,0:T(8,128)(2,1)}, bf16[128,256]{1,0:T(8,128)(2,1)S(1)}, u32[]{:S(2)}, u32[]{:S(2)}) collective-permute-start(bf16[128,256]{1,0:T(8,128)(2,1)} %get-tuple-element.214), channel_id=1, source_target_pairs={{0,4},{4,8},{8,12},{12,0},{1,5},{5,9},{9,13},{13,1},{2,6},{6,10},{... | collective-permute-start | bytes 196616 | tf_op jit(solution)/shard_map/ppermute | solution.py:20
  97.5 4.0 %collective-permute-done.11 = bf16[128,256]{1,0:T(8,128)(2,1)S(1)} collective-permute-done((bf16[128,256]{1,0:T(8,128)(2,1)}, bf16[128,256]{1,0:T(8,128)(2,1)S(1)}, u32[]{:S(2)}, u32[]{:S(2)}) %collective-permute-start.11) | collective-permute-done | bytes 65568 | tf_op jit(solution)/shard_map/ppermute | solution.py:20
  101.5 1.2 %collective-permute-done.9 = bf16[128,256]{1,0:T(8,128)(2,1)S(1)} collective-permute-done((bf16[128,256]{1,0:T(8,128)(2,1)}, bf16[128,256]{1,0:T(8,128)(2,1)S(1)}, u32[]{:S(2)}, u32[]{:S(2)}) %collective-permute-start.9) | collective-permute-done | bytes 65568 | tf_op jit(solution)/shard_map/ppermute | solution.py:20
  102.8 0.7 copy.58
  (51 shorter events, 4.0 us)
Async XLA Ops:
  0.6 14.4 %copy-start = (bf16[5120,64]{0,1:T(8,128)(2,1)S(1)}, bf16[5120,64]{0,1:T(8,128)(2,1)}, u32[]{:S(2)}) copy-start(bf16[5120,64]{0,1:T(8,128)(2,1)} %param.27) | copy-start | bytes 1966084
  0.7 10.5 %copy-start.7 = (f32[1,2,5120]{2,1,0:T(2,128)S(1)}, f32[1,2,5120]{2,1,0:T(2,128)}, u32[]{:S(2)}) copy-start(f32[1,2,5120]{2,1,0:T(2,128)} %param.26) | copy-start | bytes 122884
  0.7 10.5 %copy-start.2 = (bf16[1,128,5120]{2,1,0:T(8,128)(2,1)S(1)}, bf16[1,128,5120]{2,1,0:T(8,128)(2,1)}, u32[]{:S(2)}) copy-start(bf16[1,128,5120]{2,1,0:T(8,128)(2,1)} %param.25) | copy-start | bytes 3932164
  4.1 7.3 %copy-start.1 = (bf16[1,128,4096]{2,1,0:T(8,128)(2,1)S(1)}, bf16[1,128,4096]{2,1,0:T(8,128)(2,1)}, u32[]{:S(2)}) copy-start(bf16[1,128,4096]{2,1,0:T(8,128)(2,1)} %param.22) | copy-start | bytes 3145732
  4.1 19.7 %collective-permute-start = (bf16[3,128,768]{2,1,0:T(8,128)(2,1)}, bf16[3,128,768]{2,1,0:T(8,128)(2,1)}, u32[]{:S(2)}, u32[]{:S(2)}) collective-permute-start(bf16[3,128,768]{2,1,0:T(8,128)(2,1)} %get-tuple-element.196), channel_id=1, source_target_pairs={{0,4},{4,8},{8,12},{12,0},{1,5},{5,9},{9,13},{13,1},{2,6},{6,10},{... | collective-permute-start | bytes 1769480 | tf_op jit(solution)/shard_map/ppermute | solution.py:20
  7.2 41.1 %collective-permute-start.1 = (bf16[3,128,768]{2,1,0:T(8,128)(2,1)}, bf16[3,128,768]{2,1,0:T(8,128)(2,1)}, u32[]{:S(2)}, u32[]{:S(2)}) collective-permute-start(bf16[3,128,768]{2,1,0:T(8,128)(2,1)} %get-tuple-element.197), channel_id=1, source_target_pairs={{0,8},{4,12},{8,0},{12,4},{1,9},{5,13},{9,1},{13,5},{2,10},{6,14},... | collective-permute-start | bytes 1769480 | tf_op jit(solution)/shard_map/ppermute | solution.py:20
  9.8 38.5 %collective-permute-start.2 = (bf16[3,128,768]{2,1,0:T(8,128)(2,1)}, bf16[3,128,768]{2,1,0:T(8,128)(2,1)}, u32[]{:S(2)}, u32[]{:S(2)}) collective-permute-start(bf16[3,128,768]{2,1,0:T(8,128)(2,1)} %get-tuple-element.198), channel_id=1, source_target_pairs={{0,12},{4,0},{8,4},{12,8},{1,13},{5,1},{9,5},{13,9},{2,14},{6,2},{... | collective-permute-start | bytes 1769480 | tf_op jit(solution)/shard_map/ppermute | solution.py:20
  12.0 3.1 %copy-start.10 = (f32[1,128,64]{1,2,0:T(8,128)S(1)}, f32[1,128,64]{1,2,0:T(8,128)}, u32[]{:S(2)}) copy-start(f32[1,128,64]{1,2,0:T(8,128)} %param.28) | copy-start | bytes 98308
  15.1 46.3 %copy-start.8 = (s32[32,4,4]{0,2,1:T(4,128)S(1)}, s32[32,4,4]{0,2,1:T(4,128)}, u32[]{:S(2)}) copy-start(s32[32,4,4]{0,2,1:T(4,128)} %param.31) | copy-start | bytes 6148
  15.1 48.7 %copy-start.9 = (s32[32,4]{0,1:T(4,128)S(1)}, s32[32,4]{0,1:T(4,128)}, u32[]{:S(2)}) copy-start(s32[32,4]{0,1:T(4,128)} %param.30) | copy-start | bytes 1540
  48.3 28.6 %collective-permute-start.6 = (bf16[3,128,256]{2,1,0:T(8,128)(2,1)S(1)}, bf16[3,128,256]{2,1,0:T(8,128)(2,1)S(1)}, u32[]{:S(2)}, u32[]{:S(2)}) collective-permute-start(bf16[3,128,256]{2,1,0:T(8,128)(2,1)S(1)} %get-tuple-element.208), channel_id=1, source_target_pairs={{0,4},{4,8},{8,12},{12,0},{1,5},{5,9},{9,13},{13,1},{2,6},{6,10},{... | collective-permute-start | bytes 589832 | tf_op jit(solution)/shard_map/ppermute | solution.py:20
  62.2 14.8 %collective-permute-start.7 = (bf16[3,128,256]{2,1,0:T(8,128)(2,1)}, bf16[3,128,256]{2,1,0:T(8,128)(2,1)S(1)}, u32[]{:S(2)}, u32[]{:S(2)}) collective-permute-start(bf16[3,128,256]{2,1,0:T(8,128)(2,1)} %get-tuple-element.209), channel_id=1, source_target_pairs={{0,8},{4,12},{8,0},{12,4},{1,9},{5,13},{9,1},{13,5},{2,10},{6,14},... | collective-permute-start | bytes 589832 | tf_op jit(solution)/shard_map/ppermute | solution.py:20
  64.6 14.0 %collective-permute-start.8 = (bf16[3,128,256]{2,1,0:T(8,128)(2,1)}, bf16[3,128,256]{2,1,0:T(8,128)(2,1)S(1)}, u32[]{:S(2)}, u32[]{:S(2)}) collective-permute-start(bf16[3,128,256]{2,1,0:T(8,128)(2,1)} %get-tuple-element.210), channel_id=1, source_target_pairs={{0,12},{4,0},{8,4},{12,8},{1,13},{5,1},{9,5},{13,9},{2,14},{6,2},{... | collective-permute-start | bytes 589832 | tf_op jit(solution)/shard_map/ppermute | solution.py:20
  74.2 23.3 %collective-permute-start.3 = (bf16[128,768]{1,0:T(8,128)(2,1)}, bf16[128,768]{1,0:T(8,128)(2,1)S(1)}, u32[]{:S(2)}, u32[]{:S(2)}) collective-permute-start(bf16[128,768]{1,0:T(8,128)(2,1)} %get-tuple-element.200), channel_id=1, source_target_pairs={{0,12},{4,0},{8,4},{12,8},{1,13},{5,1},{9,5},{13,9},{2,14},{6,2},{... | collective-permute-start | bytes 589832 | tf_op jit(solution)/shard_map/ppermute | solution.py:20
  76.2 21.3 %collective-permute-start.4 = (bf16[128,768]{1,0:T(8,128)(2,1)}, bf16[128,768]{1,0:T(8,128)(2,1)S(1)}, u32[]{:S(2)}, u32[]{:S(2)}) collective-permute-start(bf16[128,768]{1,0:T(8,128)(2,1)} %get-tuple-element.201), channel_id=1, source_target_pairs={{0,8},{4,12},{8,0},{12,4},{1,9},{5,13},{9,1},{13,5},{2,10},{6,14},... | collective-permute-start | bytes 589832 | tf_op jit(solution)/shard_map/ppermute | solution.py:20
  76.9 1.7 %copy-start.4 = (bf16[3,128,256]{2,1,0:T(8,128)(2,1)}, bf16[3,128,256]{2,1,0:T(8,128)(2,1)S(1)}, u32[]{:S(2)}) copy-start(bf16[3,128,256]{2,1,0:T(8,128)(2,1)S(1)} %collective-permute-done.6.refs_1_) | copy-start | bytes 589828
  76.9 20.6 %collective-permute-start.5 = (bf16[128,768]{1,0:T(8,128)(2,1)}, bf16[128,768]{1,0:T(8,128)(2,1)S(1)}, u32[]{:S(2)}, u32[]{:S(2)}) collective-permute-start(bf16[128,768]{1,0:T(8,128)(2,1)} %get-tuple-element.202), channel_id=1, source_target_pairs={{0,4},{4,8},{8,12},{12,0},{1,5},{5,9},{9,13},{13,1},{2,6},{6,10},{... | collective-permute-start | bytes 589832 | tf_op jit(solution)/shard_map/ppermute | solution.py:20
  77.0 1.6 %copy-start.5 = (bf16[3,128,256]{2,1,0:T(8,128)(2,1)}, bf16[3,128,256]{2,1,0:T(8,128)(2,1)S(1)}, u32[]{:S(2)}) copy-start(bf16[3,128,256]{2,1,0:T(8,128)(2,1)S(1)} %collective-permute-done.7.refs_2_) | copy-start | bytes 589828
  77.0 8.6 %collective-permute-start.12 = (f32[1,128,64]{1,2,0:T(8,128)S(1)}, f32[1,128,64]{1,2,0:T(8,128)S(1)}, u32[]{:S(2)}, u32[]{:S(2)}) collective-permute-start(f32[1,128,64]{1,2,0:T(8,128)S(1)} %fusion.15), channel_id=1, source_target_pairs={{0,3},{1,0},{2,1},{3,2},{4,7},{5,4},{6,5},{7,6},{8,11},{9,8},{10,9... | collective-permute-start | bytes 98312 | tf_op jit(solution)/shard_map/ppermute | solution.py:20
  78.7 0.7 copy-start.6
  83.3 14.2 %collective-permute-start.10 = (bf16[128,256]{1,0:T(8,128)(2,1)}, bf16[128,256]{1,0:T(8,128)(2,1)S(1)}, u32[]{:S(2)}, u32[]{:S(2)}) collective-permute-start(bf16[128,256]{1,0:T(8,128)(2,1)} %get-tuple-element.213), channel_id=1, source_target_pairs={{0,8},{4,12},{8,0},{12,4},{1,9},{5,13},{9,1},{13,5},{2,10},{6,14},... | collective-permute-start | bytes 196616 | tf_op jit(solution)/shard_map/ppermute | solution.py:20
  85.6 15.9 %collective-permute-start.11 = (bf16[128,256]{1,0:T(8,128)(2,1)}, bf16[128,256]{1,0:T(8,128)(2,1)S(1)}, u32[]{:S(2)}, u32[]{:S(2)}) collective-permute-start(bf16[128,256]{1,0:T(8,128)(2,1)} %get-tuple-element.214), channel_id=1, source_target_pairs={{0,4},{4,8},{8,12},{12,0},{1,5},{5,9},{9,13},{13,1},{2,6},{6,10},{... | collective-permute-start | bytes 196616 | tf_op jit(solution)/shard_map/ppermute | solution.py:20
  97.5 5.2 %collective-permute-start.9 = (bf16[128,256]{1,0:T(8,128)(2,1)}, bf16[128,256]{1,0:T(8,128)(2,1)S(1)}, u32[]{:S(2)}, u32[]{:S(2)}) collective-permute-start(bf16[128,256]{1,0:T(8,128)(2,1)} %get-tuple-element.212), channel_id=1, source_target_pairs={{0,12},{4,0},{8,4},{12,8},{1,13},{5,1},{9,5},{13,9},{2,14},{6,2},{... | collective-permute-start | bytes 196616 | tf_op jit(solution)/shard_map/ppermute | solution.py:20
  102.8 1.0 copy-start.3

commit v12 on v10

--- a/solution.py
+++ b/solution.py
@@ -282,7 +282,7 @@
     head_count = live_counts.shape[0]
     per_device = head_count // seq_count
     if per_device % 8 == 0:
-        sizes = [per_device * 5 // 8, per_device * 2 // 8, per_device // 8]
+        sizes = [per_device * 7 // 8, per_device // 8]
     elif per_device % 4 == 0:
         sizes = [per_device * 3 // 4, per_device // 4]
     else:

time: 110 us -> 113 us (1.027)
  waiting for transfers between devices: 29.9 us -> 49.5 us
  starting transfers between devices: 46.2 us -> 34.3 us
  Pallas kernels: 22.8 us -> 19.1 us
  matrix products: 2.85 us -> 1.57 us
    ppermute x19 -> x13, waiting for transfers between devices: 29.9 us -> 49.5 us  [passed_along(): return lax.ppermute(value, axis, pairs)]
    ppermute x19 -> x13, starting transfers between devices: 46.2 us -> 34.3 us  [passed_along(): return lax.ppermute(value, axis, pairs)]
    pallas_call x4 -> x3, Pallas kernels: 8.2 us -> 6.25 us  [branch(): pl.pallas_call(kernel, in_specs=[pl.BlockSpec(memory_space=pltpu.VMEM)] *...]
    pallas_call x3 -> x2, Pallas kernels: 14.6 us -> 12.8 us  [attend_pieces(): pl.pallas_call(kernel, in_specs=[pl.BlockSpec(memory_space=smem)] * 3 + [...]
    dot_general x1, matrix products: 2.85 us -> 1.57 us  [local(): velocity = jnp.dot(shaped, head_weight, preferred_element_type=jnp.float32)]
    unnamed x31 -> x25, local copies, waits for them, and re-layouts: 1.03 us -> 2.27 us
  transfers between devices with their start and end apart: 19 -> 13, of which waited for: 5 -> 4; matrix products, arithmetic and copies ran while one was open for 8% -> 5% of each run, Pallas kernels for 18% -> 14%
where the time goes in v12:
time: 113 us
  waiting for transfers between devices  49.5 us (44%)
  starting transfers between devices  34.3 us (30%)
  Pallas kernels  19.1 us (17%)
  local copies, waits for them, and re-layouts  5.35 us (5%)
  matrix products  1.57 us (1%)
  between operations  1.5 us (1%)
  other arithmetic  1.35 us (1%)
    ppermute x13, waiting for transfers between devices, passed_along(): return lax.ppermute(value, axis, pairs)  49.5 us
    ppermute x13, starting transfers between devices, passed_along(): return lax.ppermute(value, axis, pairs)  34.3 us
    pallas_call x2, Pallas kernels, attend_pieces(): pl.pallas_call(kernel, in_specs=[pl.BlockSpec(memory_space=smem)] * 3 + [...  12.8 us
    pallas_call x3, Pallas kernels, branch(): pl.pallas_call(kernel, in_specs=[pl.BlockSpec(memory_space=pltpu.VMEM)] *...  6.25 us
    unnamed x25, local copies, waits for them, and re-layouts  2.27 us
  transfers between devices with their start and end apart: 13, of which 4 were waited for; matrix products, arithmetic and copies ran while one was open for 5% of the time, Pallas kernels for 14%

profile of v12, /device:TPU:0, one launch (start us, length us, event | category | flops | bytes accessed | tf_op | source)
XLA Modules:
  0.0 112.7 jit_solution(12727683891630790961)
XLA Ops:
  0.7 3.6 %conditional.3 = ((bf16[3,128,896]{2,1,0:T(8,128)(2,1)}, bf16[3,128,896]{2,1,0:T(8,128)(2,1)}, bf16[3,128,896]{2,1,0:T(8,128)(2,1)}, bf16[3,128,896]{2,1,0:T(8,128)(2,1)})) conditional(s32[]{:T(128)} %clamp.2, (bf16[1,128,4096]{2,1,0:T(8,128)(2,1)}, bf16[1,128,4096]{2,1,0:T(8,128)(2,1)}, ...), branch_computations={%region_0.0_spmd, %region_1.0_spmd, %region_2.0_spmd, %region_3.0_... | conditional | bytes 8 | solution.py:171
  0.7 3.5 %branch_0_fun.3 = (bf16[3,128,896]{2,1,0:T(8,128)(2,1)}, bf16[3,128,896]{2,1,0:T(8,128)(2,1)}, bf16[3,128,896]{2,1,0:T(8,128)(2,1)}, bf16[3,128,896]{2,1,0:T(8,128)(2,1)}) custom-call(bf16[1,128,4096]{2,1,0:T(8,128)(2,1)} %get-tuple-element.87.refs_0_, bf16[1,128,4096]{2,1,0:T(8,128)(2,1)} %get-tuple-element.102.refs_1_, ...), custom_call_target="tpu_custom_call" | custom-call | tf_op jit(solution)/shard_map/cond/branch_0_fun/pallas_call | solution.py:162
  4.2 3.1 %collective-permute-start = (bf16[3,128,896]{2,1,0:T(8,128)(2,1)}, bf16[3,128,896]{2,1,0:T(8,128)(2,1)S(1)}, u32[]{:S(2)}, u32[]{:S(2)}) collective-permute-start(bf16[3,128,896]{2,1,0:T(8,128)(2,1)} %get-tuple-element.196), channel_id=1, source_target_pairs={{0,4},{4,8},{8,12},{12,0},{1,5},{5,9},{9,13},{13,1},{2,6},{6,10},{... | collective-permute-start | bytes 2064392 | tf_op jit(solution)/shard_map/ppermute | solution.py:20
  7.3 2.6 %collective-permute-start.1 = (bf16[3,128,896]{2,1,0:T(8,128)(2,1)}, bf16[3,128,896]{2,1,0:T(8,128)(2,1)}, u32[]{:S(2)}, u32[]{:S(2)}) collective-permute-start(bf16[3,128,896]{2,1,0:T(8,128)(2,1)} %get-tuple-element.197), channel_id=1, source_target_pairs={{0,8},{4,12},{8,0},{12,4},{1,9},{5,13},{9,1},{13,5},{2,10},{6,14},... | collective-permute-start | bytes 2064392 | tf_op jit(solution)/shard_map/ppermute | solution.py:20
  9.9 1.3 %collective-permute-start.2 = (bf16[3,128,896]{2,1,0:T(8,128)(2,1)}, bf16[3,128,896]{2,1,0:T(8,128)(2,1)}, u32[]{:S(2)}, u32[]{:S(2)}) collective-permute-start(bf16[3,128,896]{2,1,0:T(8,128)(2,1)} %get-tuple-element.198), channel_id=1, source_target_pairs={{0,12},{4,0},{8,4},{12,8},{1,13},{5,1},{9,5},{13,9},{2,14},{6,2},{... | collective-permute-start | bytes 2064392 | tf_op jit(solution)/shard_map/ppermute | solution.py:20
  11.2 2.6 %conditional.4 = ((bf16[3,128,128]{2,1,0:T(8,128)(2,1)S(1)}, bf16[3,128,128]{2,1,0:T(8,128)(2,1)}, bf16[3,128,128]{2,1,0:T(8,128)(2,1)}, bf16[3,128,128]{2,1,0:T(8,128)(2,1)})) conditional(s32[]{:T(128)} %clamp.2, (bf16[1,128,4096]{2,1,0:T(8,128)(2,1)}, bf16[1,128,4096]{2,1,0:T(8,128)(2,1)}, ...), branch_computations={%region_4.0_spmd, %region_5.0_spmd, %region_6.0_spmd, %region_7.0_... | conditional | bytes 8 | solution.py:171
  11.2 2.6 %branch_0_fun.4 = (bf16[3,128,128]{2,1,0:T(8,128)(2,1)S(1)}, bf16[3,128,128]{2,1,0:T(8,128)(2,1)}, bf16[3,128,128]{2,1,0:T(8,128)(2,1)}, bf16[3,128,128]{2,1,0:T(8,128)(2,1)}) custom-call(bf16[1,128,4096]{2,1,0:T(8,128)(2,1)} %get-tuple-element.129.refs_0_, bf16[1,128,4096]{2,1,0:T(8,128)(2,1)} %get-tuple-element.130.refs_1_, ...), custom_call_target="tpu_custom_call" | custom-call | tf_op jit(solution)/shard_map/cond/branch_0_fun/pallas_call | solution.py:162
  16.7 9.2 %collective-permute-done.refs_1_ = bf16[3,128,896]{2,1,0:T(8,128)(2,1)S(1)} collective-permute-done((bf16[3,128,896]{2,1,0:T(8,128)(2,1)}, bf16[3,128,896]{2,1,0:T(8,128)(2,1)S(1)}, u32[]{:S(2)}, u32[]{:S(2)}) %collective-permute-start) | collective-permute-done | bytes 688160 | tf_op jit(solution)/shard_map/ppermute | solution.py:20
  25.9 28.7 %collective-permute-done.1.refs_2_ = bf16[3,128,896]{2,1,0:T(8,128)(2,1)} collective-permute-done((bf16[3,128,896]{2,1,0:T(8,128)(2,1)}, bf16[3,128,896]{2,1,0:T(8,128)(2,1)}, u32[]{:S(2)}, u32[]{:S(2)}) %collective-permute-start.1) | collective-permute-done | bytes 688160 | tf_op jit(solution)/shard_map/ppermute | solution.py:20
  54.7 15.2 %collective-permute-start.6 = (bf16[3,128,128]{2,1,0:T(8,128)(2,1)}, bf16[3,128,128]{2,1,0:T(8,128)(2,1)S(1)}, u32[]{:S(2)}, u32[]{:S(2)}) collective-permute-start(bf16[3,128,128]{2,1,0:T(8,128)(2,1)} %get-tuple-element.208), channel_id=1, source_target_pairs={{0,4},{4,8},{8,12},{12,0},{1,5},{5,9},{9,13},{13,1},{2,6},{6,10},{... | collective-permute-start | bytes 294920 | tf_op jit(solution)/shard_map/ppermute | solution.py:20
  70.8 1.6 %collective-permute-start.7 = (bf16[3,128,128]{2,1,0:T(8,128)(2,1)}, bf16[3,128,128]{2,1,0:T(8,128)(2,1)S(1)}, u32[]{:S(2)}, u32[]{:S(2)}) collective-permute-start(bf16[3,128,128]{2,1,0:T(8,128)(2,1)} %get-tuple-element.209), channel_id=1, source_target_pairs={{0,8},{4,12},{8,0},{12,4},{1,9},{5,13},{9,1},{13,5},{2,10},{6,14},... | collective-permute-start | bytes 294920 | tf_op jit(solution)/shard_map/ppermute | solution.py:20
  72.4 0.8 collective-permute-start.8
  73.2 10.0 %shard_map.113 = (bf16[128,896]{1,0:T(8,128)(2,1)S(1)}, bf16[128,896]{1,0:T(8,128)(2,1)}, bf16[128,896]{1,0:T(8,128)(2,1)}, bf16[128,896]{1,0:T(8,128)(2,1)}) custom-call(s32[112]{0:T(128)} %reshape.58.lists_ref, s32[28]{0:T(128)} %reshape.59.live_ref, s32[1]{0:T(128)} %bitcast.me_ref, bf16[3,128,896]{2,1,0:T(8,128)(2,1)} %get-tuple-element.195.refs_0_, ...), custom_call_target="tpu_custom_call" | custom-call | tf_op jit(solution)/shard_map/pallas_call | solution.py:231
  83.2 2.0 %collective-permute-start.3 = (bf16[128,896]{1,0:T(8,128)(2,1)}, bf16[128,896]{1,0:T(8,128)(2,1)S(1)}, u32[]{:S(2)}, u32[]{:S(2)}) collective-permute-start(bf16[128,896]{1,0:T(8,128)(2,1)} %get-tuple-element.200), channel_id=1, source_target_pairs={{0,12},{4,0},{8,4},{12,8},{1,13},{5,1},{9,5},{13,9},{2,14},{6,2},{... | collective-permute-start | bytes 688136 | tf_op jit(solution)/shard_map/ppermute | solution.py:20
  85.2 0.7 collective-permute-start.4
  85.9 1.6 %fusion.15 = f32[1,128,64]{1,2,0:T(8,128)S(1)} fusion(bf16[5120,64]{0,1:T(8,128)(2,1)S(1)} %copy-done, bf16[1,128,5120]{2,1,0:T(8,128)(2,1)S(1)} %copy-done.1, f32[5120]{0:T(1024)S(1)} %bitcast.33, f32[5120]{0:T(1024)S(1)} %bitcast.32, f32[128]{0:T(128)} %add_rsqrt_fusion, f32[128]{0:T(128)} %copy-done.11, f32[1,128,64]{1,2,0:T(8,128)} %param.28, f32[]{:T(128)} %bitcast.2), kind=kOutput, calls=%fused_computation.12 | convolution fusion | flops 87834624 | bytes 2073604 | tf_op jit(solution)/shard_map/dot_general | solution.py:346
  87.5 0.7 dynamic-slice_reduce_fusion.1.live_ref
  90.3 2.8 %shard_map.114 = (bf16[128,128]{1,0:T(8,128)(2,1)S(1)}, bf16[128,128]{1,0:T(8,128)(2,1)}, bf16[128,128]{1,0:T(8,128)(2,1)}, bf16[128,128]{1,0:T(8,128)(2,1)}) custom-call(s32[16]{0:T(128)} %reshape.61.lists_ref, s32[4]{0:T(128)} %dynamic-slice_reduce_fusion.1.live_ref, s32[1]{0:T(128)} %bitcast.me_ref, bf16[3,128,128]{2,1,0:T(8,128)(2,1)S(1)} %get-tuple-element.207.refs_0_, ...), custom_call_target="tpu_custom_call" | custom-call | tf_op jit(solution)/shard_map/pallas_call | solution.py:231
  93.1 2.2 %collective-permute-start.10 = (bf16[128,128]{1,0:T(8,128)(2,1)}, bf16[128,128]{1,0:T(8,128)(2,1)S(1)}, u32[]{:S(2)}, u32[]{:S(2)}) collective-permute-start(bf16[128,128]{1,0:T(8,128)(2,1)} %get-tuple-element.213), channel_id=1, source_target_pairs={{0,8},{4,12},{8,0},{12,4},{1,9},{5,13},{9,1},{13,5},{2,10},{6,14},... | collective-permute-start | bytes 98312 | tf_op jit(solution)/shard_map/ppermute | solution.py:20
  95.3 2.1 %collective-permute-start.11 = (bf16[128,128]{1,0:T(8,128)(2,1)}, bf16[128,128]{1,0:T(8,128)(2,1)S(1)}, u32[]{:S(2)}, u32[]{:S(2)}) collective-permute-start(bf16[128,128]{1,0:T(8,128)(2,1)} %get-tuple-element.214), channel_id=1, source_target_pairs={{0,4},{4,8},{8,12},{12,0},{1,5},{5,9},{9,13},{13,1},{2,6},{6,10},{... | collective-permute-start | bytes 98312 | tf_op jit(solution)/shard_map/ppermute | solution.py:20
  97.4 9.5 %collective-permute-done.10 = bf16[128,128]{1,0:T(8,128)(2,1)S(1)} collective-permute-done((bf16[128,128]{1,0:T(8,128)(2,1)}, bf16[128,128]{1,0:T(8,128)(2,1)S(1)}, u32[]{:S(2)}, u32[]{:S(2)}) %collective-permute-start.10) | collective-permute-done | bytes 32800 | tf_op jit(solution)/shard_map/ppermute | solution.py:20
  107.0 2.6 %collective-permute-start.9 = (bf16[128,128]{1,0:T(8,128)(2,1)}, bf16[128,128]{1,0:T(8,128)(2,1)S(1)}, u32[]{:S(2)}, u32[]{:S(2)}) collective-permute-start(bf16[128,128]{1,0:T(8,128)(2,1)} %get-tuple-element.212), channel_id=1, source_target_pairs={{0,12},{4,0},{8,4},{12,8},{1,13},{5,1},{9,5},{13,9},{2,14},{6,2},{... | collective-permute-start | bytes 98312 | tf_op jit(solution)/shard_map/ppermute | solution.py:20
  109.6 1.9 %collective-permute-done.9 = bf16[128,128]{1,0:T(8,128)(2,1)S(1)} collective-permute-done((bf16[128,128]{1,0:T(8,128)(2,1)}, bf16[128,128]{1,0:T(8,128)(2,1)S(1)}, u32[]{:S(2)}, u32[]{:S(2)}) %collective-permute-start.9) | collective-permute-done | bytes 32800 | tf_op jit(solution)/shard_map/ppermute | solution.py:20
  111.7 0.7 copy.54
  (50 shorter events, 5.6 us)
Async XLA Ops:
  0.6 85.3 %copy-start = (bf16[5120,64]{0,1:T(8,128)(2,1)S(1)}, bf16[5120,64]{0,1:T(8,128)(2,1)}, u32[]{:S(2)}) copy-start(bf16[5120,64]{0,1:T(8,128)(2,1)} %param.27) | copy-start | bytes 1966084
  4.2 21.7 %collective-permute-start = (bf16[3,128,896]{2,1,0:T(8,128)(2,1)}, bf16[3,128,896]{2,1,0:T(8,128)(2,1)S(1)}, u32[]{:S(2)}, u32[]{:S(2)}) collective-permute-start(bf16[3,128,896]{2,1,0:T(8,128)(2,1)} %get-tuple-element.196), channel_id=1, source_target_pairs={{0,4},{4,8},{8,12},{12,0},{1,5},{5,9},{9,13},{13,1},{2,6},{6,10},{... | collective-permute-start | bytes 2064392 | tf_op jit(solution)/shard_map/ppermute | solution.py:20
  7.3 47.4 %collective-permute-start.1 = (bf16[3,128,896]{2,1,0:T(8,128)(2,1)}, bf16[3,128,896]{2,1,0:T(8,128)(2,1)}, u32[]{:S(2)}, u32[]{:S(2)}) collective-permute-start(bf16[3,128,896]{2,1,0:T(8,128)(2,1)} %get-tuple-element.197), channel_id=1, source_target_pairs={{0,8},{4,12},{8,0},{12,4},{1,9},{5,13},{9,1},{13,5},{2,10},{6,14},... | collective-permute-start | bytes 2064392 | tf_op jit(solution)/shard_map/ppermute | solution.py:20
  9.9 4.6 %copy-start.8 = (s32[32,4,4]{0,2,1:T(4,128)S(1)}, s32[32,4,4]{0,2,1:T(4,128)}, u32[]{:S(2)}) copy-start(s32[32,4,4]{0,2,1:T(4,128)} %param.31) | copy-start | bytes 6148
  9.9 5.4 %copy-start.1 = (bf16[1,128,5120]{2,1,0:T(8,128)(2,1)S(1)}, bf16[1,128,5120]{2,1,0:T(8,128)(2,1)}, u32[]{:S(2)}) copy-start(bf16[1,128,5120]{2,1,0:T(8,128)(2,1)} %param.25) | copy-start | bytes 3932164
  9.9 44.8 %collective-permute-start.2 = (bf16[3,128,896]{2,1,0:T(8,128)(2,1)}, bf16[3,128,896]{2,1,0:T(8,128)(2,1)}, u32[]{:S(2)}, u32[]{:S(2)}) collective-permute-start(bf16[3,128,896]{2,1,0:T(8,128)(2,1)} %get-tuple-element.198), channel_id=1, source_target_pairs={{0,12},{4,0},{8,4},{12,8},{1,13},{5,1},{9,5},{13,9},{2,14},{6,2},{... | collective-permute-start | bytes 2064392 | tf_op jit(solution)/shard_map/ppermute | solution.py:20
  15.3 1.3 %copy-start.7 = (f32[1,2,5120]{2,1,0:T(2,128)S(1)}, f32[1,2,5120]{2,1,0:T(2,128)}, u32[]{:S(2)}) copy-start(f32[1,2,5120]{2,1,0:T(2,128)} %param.26) | copy-start | bytes 122884
  15.3 54.6 %copy-start.9 = (s32[32,4]{0,1:T(4,128)S(1)}, s32[32,4]{0,1:T(4,128)}, u32[]{:S(2)}) copy-start(s32[32,4]{0,1:T(4,128)} %param.30) | copy-start | bytes 1540
  25.9 47.3 %copy-start.3 = (bf16[3,128,896]{2,1,0:T(8,128)(2,1)}, bf16[3,128,896]{2,1,0:T(8,128)(2,1)S(1)}, u32[]{:S(2)}) copy-start(bf16[3,128,896]{2,1,0:T(8,128)(2,1)S(1)} %collective-permute-done.refs_1_) | copy-start | bytes 2064388
  54.7 31.2 %collective-permute-start.6 = (bf16[3,128,128]{2,1,0:T(8,128)(2,1)}, bf16[3,128,128]{2,1,0:T(8,128)(2,1)S(1)}, u32[]{:S(2)}, u32[]{:S(2)}) collective-permute-start(bf16[3,128,128]{2,1,0:T(8,128)(2,1)} %get-tuple-element.208), channel_id=1, source_target_pairs={{0,4},{4,8},{8,12},{12,0},{1,5},{5,9},{9,13},{13,1},{2,6},{6,10},{... | collective-permute-start | bytes 294920 | tf_op jit(solution)/shard_map/ppermute | solution.py:20
  70.8 18.3 %collective-permute-start.7 = (bf16[3,128,128]{2,1,0:T(8,128)(2,1)}, bf16[3,128,128]{2,1,0:T(8,128)(2,1)S(1)}, u32[]{:S(2)}, u32[]{:S(2)}) collective-permute-start(bf16[3,128,128]{2,1,0:T(8,128)(2,1)} %get-tuple-element.209), channel_id=1, source_target_pairs={{0,8},{4,12},{8,0},{12,4},{1,9},{5,13},{9,1},{13,5},{2,10},{6,14},... | collective-permute-start | bytes 294920 | tf_op jit(solution)/shard_map/ppermute | solution.py:20
  72.4 16.6 %collective-permute-start.8 = (bf16[3,128,128]{2,1,0:T(8,128)(2,1)}, bf16[3,128,128]{2,1,0:T(8,128)(2,1)S(1)}, u32[]{:S(2)}, u32[]{:S(2)}) collective-permute-start(bf16[3,128,128]{2,1,0:T(8,128)(2,1)} %get-tuple-element.210), channel_id=1, source_target_pairs={{0,12},{4,0},{8,4},{12,8},{1,13},{5,1},{9,5},{13,9},{2,14},{6,2},{... | collective-permute-start | bytes 294920 | tf_op jit(solution)/shard_map/ppermute | solution.py:20
  83.2 28.3 %collective-permute-start.3 = (bf16[128,896]{1,0:T(8,128)(2,1)}, bf16[128,896]{1,0:T(8,128)(2,1)S(1)}, u32[]{:S(2)}, u32[]{:S(2)}) collective-permute-start(bf16[128,896]{1,0:T(8,128)(2,1)} %get-tuple-element.200), channel_id=1, source_target_pairs={{0,12},{4,0},{8,4},{12,8},{1,13},{5,1},{9,5},{13,9},{2,14},{6,2},{... | collective-permute-start | bytes 688136 | tf_op jit(solution)/shard_map/ppermute | solution.py:20
  85.2 26.3 %collective-permute-start.4 = (bf16[128,896]{1,0:T(8,128)(2,1)}, bf16[128,896]{1,0:T(8,128)(2,1)S(1)}, u32[]{:S(2)}, u32[]{:S(2)}) collective-permute-start(bf16[128,896]{1,0:T(8,128)(2,1)} %get-tuple-element.201), channel_id=1, source_target_pairs={{0,8},{4,12},{8,0},{12,4},{1,9},{5,13},{9,1},{13,5},{2,10},{6,14},... | collective-permute-start | bytes 688136 | tf_op jit(solution)/shard_map/ppermute | solution.py:20
  85.9 1.6 %copy-start.4 = (bf16[3,128,128]{2,1,0:T(8,128)(2,1)}, bf16[3,128,128]{2,1,0:T(8,128)(2,1)S(1)}, u32[]{:S(2)}) copy-start(bf16[3,128,128]{2,1,0:T(8,128)(2,1)S(1)} %collective-permute-done.6.refs_1_) | copy-start | bytes 294916
  85.9 25.6 %collective-permute-start.5 = (bf16[128,896]{1,0:T(8,128)(2,1)}, bf16[128,896]{1,0:T(8,128)(2,1)S(1)}, u32[]{:S(2)}, u32[]{:S(2)}) collective-permute-start(bf16[128,896]{1,0:T(8,128)(2,1)} %get-tuple-element.202), channel_id=1, source_target_pairs={{0,4},{4,8},{8,12},{12,0},{1,5},{5,9},{9,13},{13,1},{2,6},{6,10},{... | collective-permute-start | bytes 688136 | tf_op jit(solution)/shard_map/ppermute | solution.py:20
  85.9 1.6 %copy-start.10 = (s32[32,4]{0,1:T(4,128)S(1)}, s32[32,4]{0,1:T(4,128)}, u32[]{:S(2)}) copy-start(s32[32,4]{0,1:T(4,128)} %param.30) | copy-start | bytes 1540
  89.0 0.6 copy-start.5
  89.0 6.3 %collective-permute-start.12 = (f32[1,128,64]{1,2,0:T(8,128)S(1)}, f32[1,128,64]{1,2,0:T(8,128)S(1)}, u32[]{:S(2)}, u32[]{:S(2)}) collective-permute-start(f32[1,128,64]{1,2,0:T(8,128)S(1)} %fusion.15), channel_id=1, source_target_pairs={{0,3},{1,0},{2,1},{3,2},{4,7},{5,4},{6,5},{7,6},{8,11},{9,8},{10,9... | collective-permute-start | bytes 98312 | tf_op jit(solution)/shard_map/ppermute | solution.py:20
  89.7 0.6 copy-start.6
  93.1 13.9 %collective-permute-start.10 = (bf16[128,128]{1,0:T(8,128)(2,1)}, bf16[128,128]{1,0:T(8,128)(2,1)S(1)}, u32[]{:S(2)}, u32[]{:S(2)}) collective-permute-start(bf16[128,128]{1,0:T(8,128)(2,1)} %get-tuple-element.213), channel_id=1, source_target_pairs={{0,8},{4,12},{8,0},{12,4},{1,9},{5,13},{9,1},{13,5},{2,10},{6,14},... | collective-permute-start | bytes 98312 | tf_op jit(solution)/shard_map/ppermute | solution.py:20
  95.3 14.3 %collective-permute-start.11 = (bf16[128,128]{1,0:T(8,128)(2,1)}, bf16[128,128]{1,0:T(8,128)(2,1)S(1)}, u32[]{:S(2)}, u32[]{:S(2)}) collective-permute-start(bf16[128,128]{1,0:T(8,128)(2,1)} %get-tuple-element.214), channel_id=1, source_target_pairs={{0,4},{4,8},{8,12},{12,0},{1,5},{5,9},{9,13},{13,1},{2,6},{6,10},{... | collective-permute-start | bytes 98312 | tf_op jit(solution)/shard_map/ppermute | solution.py:20
  107.0 4.6 %collective-permute-start.9 = (bf16[128,128]{1,0:T(8,128)(2,1)}, bf16[128,128]{1,0:T(8,128)(2,1)S(1)}, u32[]{:S(2)}, u32[]{:S(2)}) collective-permute-start(bf16[128,128]{1,0:T(8,128)(2,1)} %get-tuple-element.212), channel_id=1, source_target_pairs={{0,12},{4,0},{8,4},{12,8},{1,13},{5,1},{9,5},{13,9},{2,14},{6,2},{... | collective-permute-start | bytes 98312 | tf_op jit(solution)/shard_map/ppermute | solution.py:20
  111.7 1.0 copy-start.2
  (1 other events, 0.5 us)

commit v13 on v8

--- a/solution.py
+++ b/solution.py
@@ -6,6 +6,7 @@
 from jax.experimental import pallas as pl
 from jax.experimental.pallas import tpu as pltpu
 from jax.sharding import PartitionSpec as P
+
 
 STEPS = 8
 
@@ -265,7 +266,7 @@
     return lax.switch(own_index, branches, *backs)
 
 
-def local(
+def local_body(
     query_rows,
     key_rows,
     value_rows,
@@ -286,13 +287,19 @@
     else:
         sizes = [per_device]
     starts = [sum(sizes[:c]) for c in range(len(sizes))]
-    tokens = query_rows.shape[1]
     width = query_rows.shape[2]
     depth = width // head_count
     permuted = seq_count <= 8
 
     backs = []
     previous = None
+    pending = None
+
+    def send_back(outs):
+        backs.append(outs[0])
+        for step in range(1, seq_count):
+            backs.append(passed_along(outs[step], "seq", -step))
+
     for per_chunk, start in zip(sizes, starts):
         chunk_width = per_chunk * depth
         first = own_index * per_device + start
@@ -314,11 +321,13 @@
             received = [pieces[0]]
             for step in range(1, seq_count):
                 received.append(passed_along(pieces[step], "seq", step))
+            if pending is not None:
+                held, _ = lax.optimization_barrier((pending, received))
+                send_back(held)
+                pending = attend_pieces(received, lists, live, own_index.astype(jnp.int32))
+            else:
+                pending = attend_pieces(received, lists, live, own_index.astype(jnp.int32))
             previous = received
-            outs = attend_pieces(received, lists, live, own_index.astype(jnp.int32))
-            backs.append(outs[0])
-            for step in range(1, seq_count):
-                backs.append(passed_along(outs[step], "seq", -step))
             continue
         send = packed_chunk(
             query_rows, key_rows, value_rows, seq_count, per_device * depth, start * depth, chunk_width
@@ -329,6 +338,8 @@
         previous = packed
         attended = attend_heads(packed, lists, live, jnp.zeros((), jnp.int32), False)
         backs.append(lax.all_to_all(attended, "seq", 0, 0, tiled=True))
+    if pending is not None:
+        send_back(pending)
     offsets = [s * depth for s in starts]
     if permuted:
         mixed_back = placed_back(backs, own_index, seq_count, per_device * depth, offsets)
@@ -362,7 +373,7 @@
         P(),
     )
     return jax.shard_map(
-        local,
+        local_body,
         mesh=mesh,
         in_specs=placed,
         out_specs=(P(("groups", "queue"), "seq", None), P(("groups", "queue"), "seq", None)),

time: 104 us -> 109 us (1.048)
  waiting for transfers between devices: 37.6 us -> 40 us
  starting transfers between devices: 39.3 us -> 40.6 us
    ppermute x13, waiting for transfers between devices: 37.6 us -> 40 us  [passed_along(): return lax.ppermute(value, axis, pairs)]
    ppermute x13, starting transfers between devices: 39.3 us -> 40.6 us  [passed_along(): return lax.ppermute(value, axis, pairs)]
  transfers between devices with their start and end apart: 13 -> 13, of which waited for: 4 -> 7; matrix products, arithmetic and copies ran while one was open for 5% -> 6% of each run, Pallas kernels for 15% -> 11%
where the time goes in v13:
time: 109 us
  starting transfers between devices  40.6 us (37%)
  waiting for transfers between devices  40 us (37%)
  Pallas kernels  19.1 us (18%)
  local copies, waits for them, and re-layouts  4.23 us (4%)
  matrix products  1.59 us (1%)
  between operations  1.48 us (1%)
  other arithmetic  1.43 us (1%)
    ppermute x13, starting transfers between devices, passed_along(): return lax.ppermute(value, axis, pairs)  40.6 us
    ppermute x13, waiting for transfers between devices, passed_along(): return lax.ppermute(value, axis, pairs)  40 us
    pallas_call x2, Pallas kernels, attend_pieces(): pl.pallas_call(kernel, in_specs=[pl.BlockSpec(memory_space=smem)] * 3 + [...  12.9 us
    pallas_call x3, Pallas kernels, branch(): pl.pallas_call(kernel, in_specs=[pl.BlockSpec(memory_space=pltpu.VMEM)] *...  6.2 us
  transfers between devices with their start and end apart: 13, of which 7 were waited for; matrix products, arithmetic and copies ran while one was open for 6% of the time, Pallas kernels for 11%

profile of v13, /device:TPU:0, one launch (start us, length us, event | category | flops | bytes accessed | tf_op | source)
XLA Modules:
  0.0 108.6 jit_solution(1096572403493577803)
XLA Ops:
  0.7 3.4 %conditional.3 = ((bf16[3,128,768]{2,1,0:T(8,128)(2,1)}, bf16[3,128,768]{2,1,0:T(8,128)(2,1)}, bf16[3,128,768]{2,1,0:T(8,128)(2,1)}, bf16[3,128,768]{2,1,0:T(8,128)(2,1)})) conditional(s32[]{:T(128)} %clamp.2, (bf16[1,128,4096]{2,1,0:T(8,128)(2,1)}, bf16[1,128,4096]{2,1,0:T(8,128)(2,1)}, ...), branch_computations={%region_0.0_spmd, %region_1.0_spmd, %region_2.0_spmd, %region_3.0_... | conditional | bytes 8 | solution.py:172
  0.7 3.4 %branch_0_fun.3 = (bf16[3,128,768]{2,1,0:T(8,128)(2,1)}, bf16[3,128,768]{2,1,0:T(8,128)(2,1)}, bf16[3,128,768]{2,1,0:T(8,128)(2,1)}, bf16[3,128,768]{2,1,0:T(8,128)(2,1)}) custom-call(bf16[1,128,4096]{2,1,0:T(8,128)(2,1)} %get-tuple-element.87.refs_0_, bf16[1,128,4096]{2,1,0:T(8,128)(2,1)} %get-tuple-element.102.refs_1_, ...), custom_call_target="tpu_custom_call" | custom-call | tf_op jit(solution)/shard_map/cond/branch_0_fun/pallas_call | solution.py:163
  4.0 3.1 %collective-permute-start = (bf16[3,128,768]{2,1,0:T(8,128)(2,1)}, bf16[3,128,768]{2,1,0:T(8,128)(2,1)S(1)}, u32[]{:S(2)}, u32[]{:S(2)}) collective-permute-start(bf16[3,128,768]{2,1,0:T(8,128)(2,1)} %get-tuple-element.200), channel_id=1, source_target_pairs={{0,4},{4,8},{8,12},{12,0},{1,5},{5,9},{9,13},{13,1},{2,6},{6,10},{... | collective-permute-start | bytes 1769480 | tf_op jit(solution)/shard_map/ppermute | solution.py:21
  7.1 2.6 %collective-permute-start.1 = (bf16[3,128,768]{2,1,0:T(8,128)(2,1)}, bf16[3,128,768]{2,1,0:T(8,128)(2,1)S(1)}, u32[]{:S(2)}, u32[]{:S(2)}) collective-permute-start(bf16[3,128,768]{2,1,0:T(8,128)(2,1)} %get-tuple-element.201), channel_id=1, source_target_pairs={{0,8},{4,12},{8,0},{12,4},{1,9},{5,13},{9,1},{13,5},{2,10},{6,14},... | collective-permute-start | bytes 1769480 | tf_op jit(solution)/shard_map/ppermute | solution.py:21
  9.7 1.4 %collective-permute-start.2 = (bf16[3,128,768]{2,1,0:T(8,128)(2,1)}, bf16[3,128,768]{2,1,0:T(8,128)(2,1)}, u32[]{:S(2)}, u32[]{:S(2)}) collective-permute-start(bf16[3,128,768]{2,1,0:T(8,128)(2,1)} %get-tuple-element.202), channel_id=1, source_target_pairs={{0,12},{4,0},{8,4},{12,8},{1,13},{5,1},{9,5},{13,9},{2,14},{6,2},{... | collective-permute-start | bytes 1769480 | tf_op jit(solution)/shard_map/ppermute | solution.py:21
  11.1 2.8 %conditional.4 = ((bf16[3,128,256]{2,1,0:T(8,128)(2,1)}, bf16[3,128,256]{2,1,0:T(8,128)(2,1)}, bf16[3,128,256]{2,1,0:T(8,128)(2,1)}, bf16[3,128,256]{2,1,0:T(8,128)(2,1)})) conditional(s32[]{:T(128)} %clamp.2, (bf16[1,128,4096]{2,1,0:T(8,128)(2,1)}, bf16[1,128,4096]{2,1,0:T(8,128)(2,1)}, ...), branch_computations={%region_4.0_spmd, %region_5.0_spmd, %region_6.0_spmd, %region_7.0_... | conditional | bytes 8 | solution.py:172
  11.1 2.8 %branch_0_fun.4 = (bf16[3,128,256]{2,1,0:T(8,128)(2,1)}, bf16[3,128,256]{2,1,0:T(8,128)(2,1)}, bf16[3,128,256]{2,1,0:T(8,128)(2,1)}, bf16[3,128,256]{2,1,0:T(8,128)(2,1)}) custom-call(bf16[1,128,4096]{2,1,0:T(8,128)(2,1)} %get-tuple-element.129.refs_0_, bf16[1,128,4096]{2,1,0:T(8,128)(2,1)} %get-tuple-element.130.refs_1_, ...), custom_call_target="tpu_custom_call" | custom-call | tf_op jit(solution)/shard_map/cond/branch_0_fun/pallas_call | solution.py:163
  19.3 4.4 %collective-permute-done.refs_1_ = bf16[3,128,768]{2,1,0:T(8,128)(2,1)S(1)} collective-permute-done((bf16[3,128,768]{2,1,0:T(8,128)(2,1)}, bf16[3,128,768]{2,1,0:T(8,128)(2,1)S(1)}, u32[]{:S(2)}, u32[]{:S(2)}) %collective-permute-start) | collective-permute-done | bytes 589856 | tf_op jit(solution)/shard_map/ppermute | solution.py:21
  23.7 24.4 %collective-permute-done.1.refs_2_ = bf16[3,128,768]{2,1,0:T(8,128)(2,1)S(1)} collective-permute-done((bf16[3,128,768]{2,1,0:T(8,128)(2,1)}, bf16[3,128,768]{2,1,0:T(8,128)(2,1)S(1)}, u32[]{:S(2)}, u32[]{:S(2)}) %collective-permute-start.1) | collective-permute-done | bytes 589856 | tf_op jit(solution)/shard_map/ppermute | solution.py:21
  48.1 13.2 %collective-permute-start.3 = (bf16[3,128,256]{2,1,0:T(8,128)(2,1)}, bf16[3,128,256]{2,1,0:T(8,128)(2,1)S(1)}, u32[]{:S(2)}, u32[]{:S(2)}) collective-permute-start(bf16[3,128,256]{2,1,0:T(8,128)(2,1)} %get-tuple-element.212), channel_id=1, source_target_pairs={{0,4},{4,8},{8,12},{12,0},{1,5},{5,9},{9,13},{13,1},{2,6},{6,10},{... | collective-permute-start | bytes 589832 | tf_op jit(solution)/shard_map/ppermute | solution.py:21
  61.3 1.5 %collective-permute-start.4 = (bf16[3,128,256]{2,1,0:T(8,128)(2,1)}, bf16[3,128,256]{2,1,0:T(8,128)(2,1)}, u32[]{:S(2)}, u32[]{:S(2)}) collective-permute-start(bf16[3,128,256]{2,1,0:T(8,128)(2,1)} %get-tuple-element.213), channel_id=1, source_target_pairs={{0,8},{4,12},{8,0},{12,4},{1,9},{5,13},{9,1},{13,5},{2,10},{6,14},... | collective-permute-start | bytes 589832 | tf_op jit(solution)/shard_map/ppermute | solution.py:21
  62.8 0.9 collective-permute-start.5
  63.7 8.8 %shard_map.113 = (bf16[128,768]{1,0:T(8,128)(2,1)S(1)}, bf16[128,768]{1,0:T(8,128)(2,1)}, bf16[128,768]{1,0:T(8,128)(2,1)}, bf16[128,768]{1,0:T(8,128)(2,1)}) custom-call(s32[96]{0:T(128)} %reshape.58.lists_ref, s32[24]{0:T(128)} %reshape.59.live_ref, s32[1]{0:T(128)} %bitcast.me_ref, bf16[3,128,768]{2,1,0:T(8,128)(2,1)} %get-tuple-element.199.refs_0_, ...), custom_call_target="tpu_custom_call" | custom-call | tf_op jit(solution)/shard_map/pallas_call | solution.py:232
  72.5 2.6 %collective-permute-done.4.refs_2_ = bf16[3,128,256]{2,1,0:T(8,128)(2,1)} collective-permute-done((bf16[3,128,256]{2,1,0:T(8,128)(2,1)}, bf16[3,128,256]{2,1,0:T(8,128)(2,1)}, u32[]{:S(2)}, u32[]{:S(2)}) %collective-permute-start.4) | collective-permute-done | bytes 196640 | tf_op jit(solution)/shard_map/ppermute | solution.py:21
  75.1 4.1 %shard_map.114 = (bf16[128,256]{1,0:T(8,128)(2,1)S(1)}, bf16[128,256]{1,0:T(8,128)(2,1)}, bf16[128,256]{1,0:T(8,128)(2,1)}, bf16[128,256]{1,0:T(8,128)(2,1)}) custom-call(s32[32]{0:T(128)} %reshape.61.lists_ref, s32[8]{0:T(128)} %reshape.62.live_ref, s32[1]{0:T(128)} %bitcast.me_ref, bf16[3,128,256]{2,1,0:T(8,128)(2,1)} %get-tuple-element.211.refs_0_, ...), custom_call_target="tpu_custom_call" | custom-call | tf_op jit(solution)/shard_map/pallas_call | solution.py:232
  79.2 3.7 %collective-permute-start.10 = (bf16[128,256]{1,0:T(8,128)(2,1)}, bf16[128,256]{1,0:T(8,128)(2,1)S(1)}, u32[]{:S(2)}, u32[]{:S(2)}) collective-permute-start(bf16[128,256]{1,0:T(8,128)(2,1)} %get-tuple-element.221), channel_id=1, source_target_pairs={{0,8},{4,12},{8,0},{12,4},{1,9},{5,13},{9,1},{13,5},{2,10},{6,14},... | collective-permute-start | bytes 196616 | tf_op jit(solution)/shard_map/ppermute | solution.py:21
  82.9 3.4 %collective-permute-start.6 = (bf16[128,768]{1,0:T(8,128)(2,1)}, bf16[128,768]{1,0:T(8,128)(2,1)S(1)}, u32[]{:S(2)}, u32[]{:S(2)}) collective-permute-start(bf16[128,768]{1,0:T(8,128)(2,1)} %get-tuple-element.216), channel_id=1, source_target_pairs={{0,12},{4,0},{8,4},{12,8},{1,13},{5,1},{9,5},{13,9},{2,14},{6,2},{... | collective-permute-start | bytes 589832 | tf_op jit(solution)/shard_map/ppermute | solution.py:21
  86.3 1.6 %collective-permute-start.7 = (bf16[128,768]{1,0:T(8,128)(2,1)}, bf16[128,768]{1,0:T(8,128)(2,1)S(1)}, u32[]{:S(2)}, u32[]{:S(2)}) collective-permute-start(bf16[128,768]{1,0:T(8,128)(2,1)} %get-tuple-element.217), channel_id=1, source_target_pairs={{0,8},{4,12},{8,0},{12,4},{1,9},{5,13},{9,1},{13,5},{2,10},{6,14},... | collective-permute-start | bytes 589832 | tf_op jit(solution)/shard_map/ppermute | solution.py:21
  87.9 1.6 %fusion.15 = f32[1,128,64]{1,2,0:T(8,128)S(1)} fusion(bf16[5120,64]{0,1:T(8,128)(2,1)S(1)} %copy-done, bf16[1,128,5120]{2,1,0:T(8,128)(2,1)S(1)} %copy-done.1, f32[5120]{0:T(1024)} %bitcast.33, f32[5120]{0:T(1024)} %bitcast.32, f32[128]{0:T(128)S(1)} %add_rsqrt_fusion, f32[128]{0:T(128)S(1)} %broadcast_multiply_fusion, f32[1,128,64]{1,2,0:T(8,128)} %param.28, ...), kind=kOutput, calls=%fused_computation.12 | convolution fusion | flops 87834624 | bytes 2073604 | tf_op jit(solution)/shard_map/dot_general | solution.py:355
  89.5 1.6 %collective-permute-done.12 = f32[1,128,64]{1,2,0:T(8,128)S(1)} collective-permute-done((f32[1,128,64]{1,2,0:T(8,128)S(1)}, f32[1,128,64]{1,2,0:T(8,128)S(1)}, u32[]{:S(2)}, u32[]{:S(2)}) %collective-permute-start.12) | collective-permute-done | bytes 32800 | tf_op jit(solution)/shard_map/ppermute | solution.py:21
  91.1 1.9 %collective-permute-start.11 = (bf16[128,256]{1,0:T(8,128)(2,1)S(1)}, bf16[128,256]{1,0:T(8,128)(2,1)S(1)}, u32[]{:S(2)}, u32[]{:S(2)}) collective-permute-start(bf16[128,256]{1,0:T(8,128)(2,1)S(1)} %copy-done.10), channel_id=1, source_target_pairs={{0,4},{4,8},{8,12},{12,0},{1,5},{5,9},{9,13},{13,1},{2,6},{6,10},{... | collective-permute-start | bytes 196616 | tf_op jit(solution)/shard_map/ppermute | solution.py:21
  93.0 7.4 %collective-permute-start.9 = (bf16[128,256]{1,0:T(8,128)(2,1)S(1)}, bf16[128,256]{1,0:T(8,128)(2,1)S(1)}, u32[]{:S(2)}, u32[]{:S(2)}) collective-permute-start(bf16[128,256]{1,0:T(8,128)(2,1)S(1)} %copy-done.9), channel_id=1, source_target_pairs={{0,12},{4,0},{8,4},{12,8},{1,13},{5,1},{9,5},{13,9},{2,14},{6,2},{... | collective-permute-start | bytes 196616 | tf_op jit(solution)/shard_map/ppermute | solution.py:21
  100.5 2.8 %collective-permute-done.11 = bf16[128,256]{1,0:T(8,128)(2,1)S(1)} collective-permute-done((bf16[128,256]{1,0:T(8,128)(2,1)S(1)}, bf16[128,256]{1,0:T(8,128)(2,1)S(1)}, u32[]{:S(2)}, u32[]{:S(2)}) %collective-permute-start.11) | collective-permute-done | bytes 65568 | tf_op jit(solution)/shard_map/ppermute | solution.py:21
  103.3 3.4 %collective-permute-done.9 = bf16[128,256]{1,0:T(8,128)(2,1)S(1)} collective-permute-done((bf16[128,256]{1,0:T(8,128)(2,1)S(1)}, bf16[128,256]{1,0:T(8,128)(2,1)S(1)}, u32[]{:S(2)}, u32[]{:S(2)}) %collective-permute-start.9) | collective-permute-done | bytes 65568 | tf_op jit(solution)/shard_map/ppermute | solution.py:21
  (51 shorter events, 6.7 us)
Async XLA Ops:
  0.6 87.2 %copy-start = (bf16[5120,64]{0,1:T(8,128)(2,1)S(1)}, bf16[5120,64]{0,1:T(8,128)(2,1)}, u32[]{:S(2)}) copy-start(bf16[5120,64]{0,1:T(8,128)(2,1)} %param.27) | copy-start | bytes 1966084
  4.0 19.6 %collective-permute-start = (bf16[3,128,768]{2,1,0:T(8,128)(2,1)}, bf16[3,128,768]{2,1,0:T(8,128)(2,1)S(1)}, u32[]{:S(2)}, u32[]{:S(2)}) collective-permute-start(bf16[3,128,768]{2,1,0:T(8,128)(2,1)} %get-tuple-element.200), channel_id=1, source_target_pairs={{0,4},{4,8},{8,12},{12,0},{1,5},{5,9},{9,13},{13,1},{2,6},{6,10},{... | collective-permute-start | bytes 1769480 | tf_op jit(solution)/shard_map/ppermute | solution.py:21
  7.1 41.0 %collective-permute-start.1 = (bf16[3,128,768]{2,1,0:T(8,128)(2,1)}, bf16[3,128,768]{2,1,0:T(8,128)(2,1)S(1)}, u32[]{:S(2)}, u32[]{:S(2)}) collective-permute-start(bf16[3,128,768]{2,1,0:T(8,128)(2,1)} %get-tuple-element.201), channel_id=1, source_target_pairs={{0,8},{4,12},{8,0},{12,4},{1,9},{5,13},{9,1},{13,5},{2,10},{6,14},... | collective-permute-start | bytes 1769480 | tf_op jit(solution)/shard_map/ppermute | solution.py:21
  9.7 4.2 %copy-start.7 = (s32[32,4,4]{0,2,1:T(4,128)S(1)}, s32[32,4,4]{0,2,1:T(4,128)}, u32[]{:S(2)}) copy-start(s32[32,4,4]{0,2,1:T(4,128)} %param.31) | copy-start | bytes 6148
  9.7 4.2 %copy-start.8 = (s32[32,4]{0,1:T(4,128)S(1)}, s32[32,4]{0,1:T(4,128)}, u32[]{:S(2)}) copy-start(s32[32,4]{0,1:T(4,128)} %param.30) | copy-start | bytes 1540
  9.7 8.1 %copy-start.6 = (f32[1,2,5120]{2,1,0:T(2,128)S(1)}, f32[1,2,5120]{2,1,0:T(2,128)}, u32[]{:S(2)}) copy-start(f32[1,2,5120]{2,1,0:T(2,128)} %param.26) | copy-start | bytes 122884
  9.7 8.8 %copy-start.1 = (bf16[1,128,5120]{2,1,0:T(8,128)(2,1)S(1)}, bf16[1,128,5120]{2,1,0:T(8,128)(2,1)}, u32[]{:S(2)}) copy-start(bf16[1,128,5120]{2,1,0:T(8,128)(2,1)} %param.25) | copy-start | bytes 3932164
  9.7 38.4 %collective-permute-start.2 = (bf16[3,128,768]{2,1,0:T(8,128)(2,1)}, bf16[3,128,768]{2,1,0:T(8,128)(2,1)}, u32[]{:S(2)}, u32[]{:S(2)}) collective-permute-start(bf16[3,128,768]{2,1,0:T(8,128)(2,1)} %get-tuple-element.202), channel_id=1, source_target_pairs={{0,12},{4,0},{8,4},{12,8},{1,13},{5,1},{9,5},{13,9},{2,14},{6,2},{... | collective-permute-start | bytes 1769480 | tf_op jit(solution)/shard_map/ppermute | solution.py:21
  23.7 40.0 %copy-start.3 = (bf16[3,128,768]{2,1,0:T(8,128)(2,1)}, bf16[3,128,768]{2,1,0:T(8,128)(2,1)S(1)}, u32[]{:S(2)}) copy-start(bf16[3,128,768]{2,1,0:T(8,128)(2,1)S(1)} %collective-permute-done.refs_1_) | copy-start | bytes 1769476
  48.1 15.6 %copy-start.4 = (bf16[3,128,768]{2,1,0:T(8,128)(2,1)}, bf16[3,128,768]{2,1,0:T(8,128)(2,1)S(1)}, u32[]{:S(2)}) copy-start(bf16[3,128,768]{2,1,0:T(8,128)(2,1)S(1)} %collective-permute-done.1.refs_2_) | copy-start | bytes 1769476
  48.1 24.4 %collective-permute-start.3 = (bf16[3,128,256]{2,1,0:T(8,128)(2,1)}, bf16[3,128,256]{2,1,0:T(8,128)(2,1)S(1)}, u32[]{:S(2)}, u32[]{:S(2)}) collective-permute-start(bf16[3,128,256]{2,1,0:T(8,128)(2,1)} %get-tuple-element.212), channel_id=1, source_target_pairs={{0,4},{4,8},{8,12},{12,0},{1,5},{5,9},{9,13},{13,1},{2,6},{6,10},{... | collective-permute-start | bytes 589832 | tf_op jit(solution)/shard_map/ppermute | solution.py:21
  61.3 13.8 %collective-permute-start.4 = (bf16[3,128,256]{2,1,0:T(8,128)(2,1)}, bf16[3,128,256]{2,1,0:T(8,128)(2,1)}, u32[]{:S(2)}, u32[]{:S(2)}) collective-permute-start(bf16[3,128,256]{2,1,0:T(8,128)(2,1)} %get-tuple-element.213), channel_id=1, source_target_pairs={{0,8},{4,12},{8,0},{12,4},{1,9},{5,13},{9,1},{13,5},{2,10},{6,14},... | collective-permute-start | bytes 589832 | tf_op jit(solution)/shard_map/ppermute | solution.py:21
  62.8 12.3 %collective-permute-start.5 = (bf16[3,128,256]{2,1,0:T(8,128)(2,1)}, bf16[3,128,256]{2,1,0:T(8,128)(2,1)}, u32[]{:S(2)}, u32[]{:S(2)}) collective-permute-start(bf16[3,128,256]{2,1,0:T(8,128)(2,1)} %get-tuple-element.214), channel_id=1, source_target_pairs={{0,12},{4,0},{8,4},{12,8},{1,13},{5,1},{9,5},{13,9},{2,14},{6,2},{... | collective-permute-start | bytes 589832 | tf_op jit(solution)/shard_map/ppermute | solution.py:21
  72.5 2.6 %copy-start.5 = (bf16[3,128,256]{2,1,0:T(8,128)(2,1)}, bf16[3,128,256]{2,1,0:T(8,128)(2,1)S(1)}, u32[]{:S(2)}) copy-start(bf16[3,128,256]{2,1,0:T(8,128)(2,1)S(1)} %collective-permute-done.3.refs_1_) | copy-start | bytes 589828
  79.2 13.8 %collective-permute-start.10 = (bf16[128,256]{1,0:T(8,128)(2,1)}, bf16[128,256]{1,0:T(8,128)(2,1)S(1)}, u32[]{:S(2)}, u32[]{:S(2)}) collective-permute-start(bf16[128,256]{1,0:T(8,128)(2,1)} %get-tuple-element.221), channel_id=1, source_target_pairs={{0,8},{4,12},{8,0},{12,4},{1,9},{5,13},{9,1},{13,5},{2,10},{6,14},... | collective-permute-start | bytes 196616 | tf_op jit(solution)/shard_map/ppermute | solution.py:21
  82.9 23.8 %collective-permute-start.6 = (bf16[128,768]{1,0:T(8,128)(2,1)}, bf16[128,768]{1,0:T(8,128)(2,1)S(1)}, u32[]{:S(2)}, u32[]{:S(2)}) collective-permute-start(bf16[128,768]{1,0:T(8,128)(2,1)} %get-tuple-element.216), channel_id=1, source_target_pairs={{0,12},{4,0},{8,4},{12,8},{1,13},{5,1},{9,5},{13,9},{2,14},{6,2},{... | collective-permute-start | bytes 589832 | tf_op jit(solution)/shard_map/ppermute | solution.py:21
  86.3 21.2 %collective-permute-start.7 = (bf16[128,768]{1,0:T(8,128)(2,1)}, bf16[128,768]{1,0:T(8,128)(2,1)S(1)}, u32[]{:S(2)}, u32[]{:S(2)}) collective-permute-start(bf16[128,768]{1,0:T(8,128)(2,1)} %get-tuple-element.217), channel_id=1, source_target_pairs={{0,8},{4,12},{8,0},{12,4},{1,9},{5,13},{9,1},{13,5},{2,10},{6,14},... | collective-permute-start | bytes 589832 | tf_op jit(solution)/shard_map/ppermute | solution.py:21
  87.8 19.6 %collective-permute-start.8 = (bf16[128,768]{1,0:T(8,128)(2,1)}, bf16[128,768]{1,0:T(8,128)(2,1)S(1)}, u32[]{:S(2)}, u32[]{:S(2)}) collective-permute-start(bf16[128,768]{1,0:T(8,128)(2,1)} %get-tuple-element.218), channel_id=1, source_target_pairs={{0,4},{4,8},{8,12},{12,0},{1,5},{5,9},{9,13},{13,1},{2,6},{6,10},{... | collective-permute-start | bytes 589832 | tf_op jit(solution)/shard_map/ppermute | solution.py:21
  87.8 3.3 %copy-start.10 = (bf16[128,256]{1,0:T(8,128)(2,1)S(1)}, bf16[128,256]{1,0:T(8,128)(2,1)}, u32[]{:S(2)}) copy-start(bf16[128,256]{1,0:T(8,128)(2,1)} %get-tuple-element.222) | copy-start | bytes 196612
  87.9 5.2 %copy-start.9 = (bf16[128,256]{1,0:T(8,128)(2,1)S(1)}, bf16[128,256]{1,0:T(8,128)(2,1)}, u32[]{:S(2)}) copy-start(bf16[128,256]{1,0:T(8,128)(2,1)} %get-tuple-element.220) | copy-start | bytes 196612
  89.5 1.7 %collective-permute-start.12 = (f32[1,128,64]{1,2,0:T(8,128)S(1)}, f32[1,128,64]{1,2,0:T(8,128)S(1)}, u32[]{:S(2)}, u32[]{:S(2)}) collective-permute-start(f32[1,128,64]{1,2,0:T(8,128)S(1)} %fusion.15), channel_id=1, source_target_pairs={{0,3},{1,0},{2,1},{3,2},{4,7},{5,4},{6,5},{7,6},{8,11},{9,8},{10,9... | collective-permute-start | bytes 98312 | tf_op jit(solution)/shard_map/ppermute | solution.py:21
  91.1 12.2 %collective-permute-start.11 = (bf16[128,256]{1,0:T(8,128)(2,1)S(1)}, bf16[128,256]{1,0:T(8,128)(2,1)S(1)}, u32[]{:S(2)}, u32[]{:S(2)}) collective-permute-start(bf16[128,256]{1,0:T(8,128)(2,1)S(1)} %copy-done.10), channel_id=1, source_target_pairs={{0,4},{4,8},{8,12},{12,0},{1,5},{5,9},{9,13},{13,1},{2,6},{6,10},{... | collective-permute-start | bytes 196616 | tf_op jit(solution)/shard_map/ppermute | solution.py:21
  93.0 13.6 %collective-permute-start.9 = (bf16[128,256]{1,0:T(8,128)(2,1)S(1)}, bf16[128,256]{1,0:T(8,128)(2,1)S(1)}, u32[]{:S(2)}, u32[]{:S(2)}) collective-permute-start(bf16[128,256]{1,0:T(8,128)(2,1)S(1)} %copy-done.9), channel_id=1, source_target_pairs={{0,12},{4,0},{8,4},{12,8},{1,13},{5,1},{9,5},{13,9},{2,14},{6,2},{... | collective-permute-start | bytes 196616 | tf_op jit(solution)/shard_map/ppermute | solution.py:21
  107.6 1.0 copy-start.2

commit v14 on v12

--- a/solution.py
+++ b/solution.py
@@ -282,7 +282,7 @@
     head_count = live_counts.shape[0]
     per_device = head_count // seq_count
     if per_device % 8 == 0:
-        sizes = [per_device * 7 // 8, per_device // 8]
+        sizes = [per_device * 5 // 8, per_device * 3 // 8]
     elif per_device % 4 == 0:
         sizes = [per_device * 3 // 4, per_device // 4]
     else:

time: 113 us -> 106 us (0.938)
  waiting for transfers between devices: 49.5 us -> 33.8 us
  starting transfers between devices: 34.3 us -> 43.8 us
    ppermute x13, waiting for transfers between devices: 49.5 us -> 33.8 us  [passed_along(): return lax.ppermute(value, axis, pairs)]
    ppermute x13, starting transfers between devices: 34.3 us -> 43.8 us  [passed_along(): return lax.ppermute(value, axis, pairs)]
    unnamed x25 -> x29, local copies, waits for them, and re-layouts: 2.27 us -> 2.7 us
  transfers between devices with their start and end apart: 13 -> 13, of which waited for: 4 -> 6; matrix products, arithmetic and copies ran while one was open for 5% -> 5% of each run, Pallas kernels for 14% -> 14%
where the time goes in v14:
time: 106 us
  starting transfers between devices  43.8 us (41%)
  waiting for transfers between devices  33.8 us (32%)
  Pallas kernels  18.3 us (17%)
  local copies, waits for them, and re-layouts  5.92 us (6%)
  between operations  1.53 us (1%)
  matrix products  1.39 us (1%)
    ppermute x13, starting transfers between devices, passed_along(): return lax.ppermute(value, axis, pairs)  43.8 us
    ppermute x13, waiting for transfers between devices, passed_along(): return lax.ppermute(value, axis, pairs)  33.8 us
    pallas_call x2, Pallas kernels, attend_pieces(): pl.pallas_call(kernel, in_specs=[pl.BlockSpec(memory_space=smem)] * 3 + [...  12.7 us
    pallas_call x3, Pallas kernels, branch(): pl.pallas_call(kernel, in_specs=[pl.BlockSpec(memory_space=pltpu.VMEM)] *...  5.6 us
    unnamed x29, local copies, waits for them, and re-layouts  2.7 us
  transfers between devices with their start and end apart: 13, of which 6 were waited for; matrix products, arithmetic and copies ran while one was open for 5% of the time, Pallas kernels for 14%

profile of v14, /device:TPU:0, one launch (start us, length us, event | category | flops | bytes accessed | tf_op | source)
XLA Modules:
  0.0 105.6 jit_solution(15119946126863584339)
XLA Ops:
  0.7 3.3 %conditional.3 = ((bf16[3,128,640]{2,1,0:T(8,128)(2,1)}, bf16[3,128,640]{2,1,0:T(8,128)(2,1)}, bf16[3,128,640]{2,1,0:T(8,128)(2,1)}, bf16[3,128,640]{2,1,0:T(8,128)(2,1)})) conditional(s32[]{:T(128)} %clamp.2, (bf16[1,128,4096]{2,1,0:T(8,128)(2,1)}, bf16[1,128,4096]{2,1,0:T(8,128)(2,1)}, ...), branch_computations={%region_0.0_spmd, %region_1.0_spmd, %region_2.0_spmd, %region_3.0_... | conditional | bytes 8 | solution.py:171
  0.7 3.3 %branch_0_fun.3 = (bf16[3,128,640]{2,1,0:T(8,128)(2,1)}, bf16[3,128,640]{2,1,0:T(8,128)(2,1)}, bf16[3,128,640]{2,1,0:T(8,128)(2,1)}, bf16[3,128,640]{2,1,0:T(8,128)(2,1)}) custom-call(bf16[1,128,4096]{2,1,0:T(8,128)(2,1)} %get-tuple-element.87.refs_0_, bf16[1,128,4096]{2,1,0:T(8,128)(2,1)} %get-tuple-element.102.refs_1_, ...), custom_call_target="tpu_custom_call" | custom-call | tf_op jit(solution)/shard_map/cond/branch_0_fun/pallas_call | solution.py:162
  4.0 3.1 %collective-permute-start = (bf16[3,128,640]{2,1,0:T(8,128)(2,1)}, bf16[3,128,640]{2,1,0:T(8,128)(2,1)S(1)}, u32[]{:S(2)}, u32[]{:S(2)}) collective-permute-start(bf16[3,128,640]{2,1,0:T(8,128)(2,1)} %get-tuple-element.196), channel_id=1, source_target_pairs={{0,4},{4,8},{8,12},{12,0},{1,5},{5,9},{9,13},{13,1},{2,6},{6,10},{... | collective-permute-start | bytes 1474568 | tf_op jit(solution)/shard_map/ppermute | solution.py:20
  7.1 2.6 %collective-permute-start.1 = (bf16[3,128,640]{2,1,0:T(8,128)(2,1)}, bf16[3,128,640]{2,1,0:T(8,128)(2,1)}, u32[]{:S(2)}, u32[]{:S(2)}) collective-permute-start(bf16[3,128,640]{2,1,0:T(8,128)(2,1)} %get-tuple-element.197), channel_id=1, source_target_pairs={{0,8},{4,12},{8,0},{12,4},{1,9},{5,13},{9,1},{13,5},{2,10},{6,14},... | collective-permute-start | bytes 1474568 | tf_op jit(solution)/shard_map/ppermute | solution.py:20
  9.7 1.3 %collective-permute-start.2 = (bf16[3,128,640]{2,1,0:T(8,128)(2,1)}, bf16[3,128,640]{2,1,0:T(8,128)(2,1)}, u32[]{:S(2)}, u32[]{:S(2)}) collective-permute-start(bf16[3,128,640]{2,1,0:T(8,128)(2,1)} %get-tuple-element.198), channel_id=1, source_target_pairs={{0,12},{4,0},{8,4},{12,8},{1,13},{5,1},{9,5},{13,9},{2,14},{6,2},{... | collective-permute-start | bytes 1474568 | tf_op jit(solution)/shard_map/ppermute | solution.py:20
  13.0 1.4 %fusion.15 = f32[1,128,64]{1,2,0:T(8,128)} fusion(bf16[5120,64]{0,1:T(8,128)(2,1)S(1)} %copy-done, bf16[1,128,5120]{2,1,0:T(8,128)(2,1)S(1)} %copy-done.4, f32[5120]{0:T(1024)S(1)} %bitcast.33, f32[5120]{0:T(1024)S(1)} %bitcast.32, f32[128]{0:T(128)S(1)} %add_rsqrt_fusion, f32[128]{0:T(128)S(1)} %broadcast_multiply_fusion, ...), kind=kOutput, calls=%fused_computation.12 | convolution fusion | flops 87834624 | bytes 2073604 | tf_op jit(solution)/shard_map/dot_general | solution.py:346
  14.7 2.2 %conditional.4 = ((bf16[3,128,384]{2,1,0:T(8,128)(2,1)S(1)}, bf16[3,128,384]{2,1,0:T(8,128)(2,1)}, bf16[3,128,384]{2,1,0:T(8,128)(2,1)}, bf16[3,128,384]{2,1,0:T(8,128)(2,1)})) conditional(s32[]{:T(128)} %clamp.2, (bf16[1,128,4096]{2,1,0:T(8,128)(2,1)S(1)}, bf16[1,128,4096]{2,1,0:T(8,128)(2,1)S(1)}, ...), branch_computations={%region_4.0_spmd, %region_5.0_spmd, %region_6.0_spmd, %region_7.0_... | conditional | bytes 8 | solution.py:171
  14.7 2.2 %branch_0_fun.4 = (bf16[3,128,384]{2,1,0:T(8,128)(2,1)S(1)}, bf16[3,128,384]{2,1,0:T(8,128)(2,1)}, bf16[3,128,384]{2,1,0:T(8,128)(2,1)}, bf16[3,128,384]{2,1,0:T(8,128)(2,1)}) custom-call(bf16[1,128,4096]{2,1,0:T(8,128)(2,1)S(1)} %get-tuple-element.129.refs_0_, bf16[1,128,4096]{2,1,0:T(8,128)(2,1)S(1)} %get-tuple-element.130.refs_1_, ...), custom_call_target="tpu_custom_call" | custom-call | tf_op jit(solution)/shard_map/cond/branch_0_fun/pallas_call | solution.py:162
  16.9 4.6 %collective-permute-done.refs_1_ = bf16[3,128,640]{2,1,0:T(8,128)(2,1)S(1)} collective-permute-done((bf16[3,128,640]{2,1,0:T(8,128)(2,1)}, bf16[3,128,640]{2,1,0:T(8,128)(2,1)S(1)}, u32[]{:S(2)}, u32[]{:S(2)}) %collective-permute-start) | collective-permute-done | bytes 491552 | tf_op jit(solution)/shard_map/ppermute | solution.py:20
  21.5 20.3 %collective-permute-done.1.refs_2_ = bf16[3,128,640]{2,1,0:T(8,128)(2,1)} collective-permute-done((bf16[3,128,640]{2,1,0:T(8,128)(2,1)}, bf16[3,128,640]{2,1,0:T(8,128)(2,1)}, u32[]{:S(2)}, u32[]{:S(2)}) %collective-permute-start.1) | collective-permute-done | bytes 491552 | tf_op jit(solution)/shard_map/ppermute | solution.py:20
  41.8 11.0 %collective-permute-start.6 = (bf16[3,128,384]{2,1,0:T(8,128)(2,1)}, bf16[3,128,384]{2,1,0:T(8,128)(2,1)S(1)}, u32[]{:S(2)}, u32[]{:S(2)}) collective-permute-start(bf16[3,128,384]{2,1,0:T(8,128)(2,1)} %get-tuple-element.208), channel_id=1, source_target_pairs={{0,4},{4,8},{8,12},{12,0},{1,5},{5,9},{9,13},{13,1},{2,6},{6,10},{... | collective-permute-start | bytes 884744 | tf_op jit(solution)/shard_map/ppermute | solution.py:20
  52.8 1.6 %collective-permute-start.7 = (bf16[3,128,384]{2,1,0:T(8,128)(2,1)}, bf16[3,128,384]{2,1,0:T(8,128)(2,1)S(1)}, u32[]{:S(2)}, u32[]{:S(2)}) collective-permute-start(bf16[3,128,384]{2,1,0:T(8,128)(2,1)} %get-tuple-element.209), channel_id=1, source_target_pairs={{0,8},{4,12},{8,0},{12,4},{1,9},{5,13},{9,1},{13,5},{2,10},{6,14},... | collective-permute-start | bytes 884744 | tf_op jit(solution)/shard_map/ppermute | solution.py:20
  55.3 0.8 collective-permute-start.8
  56.8 7.6 %shard_map.113 = (bf16[128,640]{1,0:T(8,128)(2,1)S(1)}, bf16[128,640]{1,0:T(8,128)(2,1)}, bf16[128,640]{1,0:T(8,128)(2,1)}, bf16[128,640]{1,0:T(8,128)(2,1)}) custom-call(s32[80]{0:T(128)} %reshape.58.lists_ref, s32[20]{0:T(128)} %reshape.59.live_ref, s32[1]{0:T(128)} %bitcast.me_ref, bf16[3,128,640]{2,1,0:T(8,128)(2,1)} %get-tuple-element.195.refs_0_, ...), custom_call_target="tpu_custom_call" | custom-call | tf_op jit(solution)/shard_map/pallas_call | solution.py:231
  64.4 2.0 %collective-permute-start.3 = (bf16[128,640]{1,0:T(8,128)(2,1)}, bf16[128,640]{1,0:T(8,128)(2,1)S(1)}, u32[]{:S(2)}, u32[]{:S(2)}) collective-permute-start(bf16[128,640]{1,0:T(8,128)(2,1)} %get-tuple-element.200), channel_id=1, source_target_pairs={{0,12},{4,0},{8,4},{12,8},{1,13},{5,1},{9,5},{13,9},{2,14},{6,2},{... | collective-permute-start | bytes 491528 | tf_op jit(solution)/shard_map/ppermute | solution.py:20
  67.2 5.8 %collective-permute-done.7.refs_2_ = bf16[3,128,384]{2,1,0:T(8,128)(2,1)S(1)} collective-permute-done((bf16[3,128,384]{2,1,0:T(8,128)(2,1)}, bf16[3,128,384]{2,1,0:T(8,128)(2,1)S(1)}, u32[]{:S(2)}, u32[]{:S(2)}) %collective-permute-start.7) | collective-permute-done | bytes 294944 | tf_op jit(solution)/shard_map/ppermute | solution.py:20
  73.0 13.5 %collective-permute-start.5 = (bf16[128,640]{1,0:T(8,128)(2,1)}, bf16[128,640]{1,0:T(8,128)(2,1)S(1)}, u32[]{:S(2)}, u32[]{:S(2)}) collective-permute-start(bf16[128,640]{1,0:T(8,128)(2,1)} %get-tuple-element.202), channel_id=1, source_target_pairs={{0,4},{4,8},{8,12},{12,0},{1,5},{5,9},{9,13},{13,1},{2,6},{6,10},{... | collective-permute-start | bytes 491528 | tf_op jit(solution)/shard_map/ppermute | solution.py:20
  88.1 0.7 copy-done.9
  88.8 5.1 %shard_map.114 = (bf16[128,384]{1,0:T(8,128)(2,1)S(1)}, bf16[128,384]{1,0:T(8,128)(2,1)}, bf16[128,384]{1,0:T(8,128)(2,1)}, bf16[128,384]{1,0:T(8,128)(2,1)}) custom-call(s32[48]{0:T(128)} %reshape.61.lists_ref, s32[12]{0:T(128)} %reshape.62.live_ref, s32[1]{0:T(128)} %bitcast.me_ref, bf16[3,128,384]{2,1,0:T(8,128)(2,1)S(1)} %get-tuple-element.207.refs_0_, ...), custom_call_target="tpu_custom_call" | custom-call | tf_op jit(solution)/shard_map/pallas_call | solution.py:231
  93.9 3.3 %collective-permute-start.10 = (bf16[128,384]{1,0:T(8,128)(2,1)}, bf16[128,384]{1,0:T(8,128)(2,1)S(1)}, u32[]{:S(2)}, u32[]{:S(2)}) collective-permute-start(bf16[128,384]{1,0:T(8,128)(2,1)} %get-tuple-element.213), channel_id=1, source_target_pairs={{0,8},{4,12},{8,0},{12,4},{1,9},{5,13},{9,1},{13,5},{2,10},{6,14},... | collective-permute-start | bytes 294920 | tf_op jit(solution)/shard_map/ppermute | solution.py:20
  97.2 3.8 %collective-permute-start.9 = (bf16[128,384]{1,0:T(8,128)(2,1)}, bf16[128,384]{1,0:T(8,128)(2,1)S(1)}, u32[]{:S(2)}, u32[]{:S(2)}) collective-permute-start(bf16[128,384]{1,0:T(8,128)(2,1)} %get-tuple-element.212), channel_id=1, source_target_pairs={{0,12},{4,0},{8,4},{12,8},{1,13},{5,1},{9,5},{13,9},{2,14},{6,2},{... | collective-permute-start | bytes 294920 | tf_op jit(solution)/shard_map/ppermute | solution.py:20
  101.0 1.7 %collective-permute-done.10 = bf16[128,384]{1,0:T(8,128)(2,1)S(1)} collective-permute-done((bf16[128,384]{1,0:T(8,128)(2,1)}, bf16[128,384]{1,0:T(8,128)(2,1)S(1)}, u32[]{:S(2)}, u32[]{:S(2)}) %collective-permute-start.10) | collective-permute-done | bytes 98336 | tf_op jit(solution)/shard_map/ppermute | solution.py:20
  102.7 1.2 %collective-permute-done.11 = bf16[128,384]{1,0:T(8,128)(2,1)S(1)} collective-permute-done((bf16[128,384]{1,0:T(8,128)(2,1)}, bf16[128,384]{1,0:T(8,128)(2,1)S(1)}, u32[]{:S(2)}, u32[]{:S(2)}) %collective-permute-start.11) | collective-permute-done | bytes 98336 | tf_op jit(solution)/shard_map/ppermute | solution.py:20
  104.2 1.4 %copy.58 = f32[1,128,64]{1,2,0:T(8,128)} copy(f32[1,128,64]{1,2,0:T(8,128)} %collective-permute-done.12) | data formatting | bytes 65536
  (57 shorter events, 5.7 us)
Async XLA Ops:
  0.6 12.0 %copy-start = (bf16[5120,64]{0,1:T(8,128)(2,1)S(1)}, bf16[5120,64]{0,1:T(8,128)(2,1)}, u32[]{:S(2)}) copy-start(bf16[5120,64]{0,1:T(8,128)(2,1)} %param.27) | copy-start | bytes 1966084
  0.7 11.0 %copy-start.10 = (f32[1,2,5120]{2,1,0:T(2,128)S(1)}, f32[1,2,5120]{2,1,0:T(2,128)}, u32[]{:S(2)}) copy-start(f32[1,2,5120]{2,1,0:T(2,128)} %param.26) | copy-start | bytes 122884
  0.7 11.1 %copy-start.3 = (bf16[1,128,5120]{2,1,0:T(8,128)(2,1)S(1)}, bf16[1,128,5120]{2,1,0:T(8,128)(2,1)}, u32[]{:S(2)}) copy-start(bf16[1,128,5120]{2,1,0:T(8,128)(2,1)} %param.25) | copy-start | bytes 3932164
  4.0 17.5 %collective-permute-start = (bf16[3,128,640]{2,1,0:T(8,128)(2,1)}, bf16[3,128,640]{2,1,0:T(8,128)(2,1)S(1)}, u32[]{:S(2)}, u32[]{:S(2)}) collective-permute-start(bf16[3,128,640]{2,1,0:T(8,128)(2,1)} %get-tuple-element.196), channel_id=1, source_target_pairs={{0,4},{4,8},{8,12},{12,0},{1,5},{5,9},{9,13},{13,1},{2,6},{6,10},{... | collective-permute-start | bytes 1474568 | tf_op jit(solution)/shard_map/ppermute | solution.py:20
  7.1 34.8 %collective-permute-start.1 = (bf16[3,128,640]{2,1,0:T(8,128)(2,1)}, bf16[3,128,640]{2,1,0:T(8,128)(2,1)}, u32[]{:S(2)}, u32[]{:S(2)}) collective-permute-start(bf16[3,128,640]{2,1,0:T(8,128)(2,1)} %get-tuple-element.197), channel_id=1, source_target_pairs={{0,8},{4,12},{8,0},{12,4},{1,9},{5,13},{9,1},{13,5},{2,10},{6,14},... | collective-permute-start | bytes 1474568 | tf_op jit(solution)/shard_map/ppermute | solution.py:20
  9.7 32.2 %collective-permute-start.2 = (bf16[3,128,640]{2,1,0:T(8,128)(2,1)}, bf16[3,128,640]{2,1,0:T(8,128)(2,1)}, u32[]{:S(2)}, u32[]{:S(2)}) collective-permute-start(bf16[3,128,640]{2,1,0:T(8,128)(2,1)} %get-tuple-element.198), channel_id=1, source_target_pairs={{0,12},{4,0},{8,4},{12,8},{1,13},{5,1},{9,5},{13,9},{2,14},{6,2},{... | collective-permute-start | bytes 1474568 | tf_op jit(solution)/shard_map/ppermute | solution.py:20
  13.0 1.4 %copy-start.1 = (bf16[1,128,4096]{2,1,0:T(8,128)(2,1)S(1)}, bf16[1,128,4096]{2,1,0:T(8,128)(2,1)}, u32[]{:S(2)}) copy-start(bf16[1,128,4096]{2,1,0:T(8,128)(2,1)} %param.22) | copy-start | bytes 3145732
  13.0 1.5 %copy-start.2 = (bf16[1,128,4096]{2,1,0:T(8,128)(2,1)S(1)}, bf16[1,128,4096]{2,1,0:T(8,128)(2,1)}, u32[]{:S(2)}) copy-start(bf16[1,128,4096]{2,1,0:T(8,128)(2,1)} %param.23) | copy-start | bytes 3145732
  14.6 39.8 %copy-start.11 = (s32[32,4,4]{0,2,1:T(4,128)S(1)}, s32[32,4,4]{0,2,1:T(4,128)}, u32[]{:S(2)}) copy-start(s32[32,4,4]{0,2,1:T(4,128)} %param.31) | copy-start | bytes 6148
  14.6 41.5 %copy-start.12 = (s32[32,4]{0,1:T(4,128)S(1)}, s32[32,4]{0,1:T(4,128)}, u32[]{:S(2)}) copy-start(s32[32,4]{0,1:T(4,128)} %param.30) | copy-start | bytes 1540
  14.6 82.6 %collective-permute-start.12 = (f32[1,128,64]{1,2,0:T(8,128)}, f32[1,128,64]{1,2,0:T(8,128)}, u32[]{:S(2)}, u32[]{:S(2)}) collective-permute-start(f32[1,128,64]{1,2,0:T(8,128)} %fusion.15), channel_id=1, source_target_pairs={{0,3},{1,0},{2,1},{3,2},{4,7},{5,4},{6,5},{7,6},{8,11},{9,8},{10,9... | collective-permute-start | bytes 98312 | tf_op jit(solution)/shard_map/ppermute | solution.py:20
  21.5 35.3 %copy-start.6 = (bf16[3,128,640]{2,1,0:T(8,128)(2,1)}, bf16[3,128,640]{2,1,0:T(8,128)(2,1)S(1)}, u32[]{:S(2)}) copy-start(bf16[3,128,640]{2,1,0:T(8,128)(2,1)S(1)} %collective-permute-done.refs_1_) | copy-start | bytes 1474564
  41.8 24.7 %collective-permute-start.6 = (bf16[3,128,384]{2,1,0:T(8,128)(2,1)}, bf16[3,128,384]{2,1,0:T(8,128)(2,1)S(1)}, u32[]{:S(2)}, u32[]{:S(2)}) collective-permute-start(bf16[3,128,384]{2,1,0:T(8,128)(2,1)} %get-tuple-element.208), channel_id=1, source_target_pairs={{0,4},{4,8},{8,12},{12,0},{1,5},{5,9},{9,13},{13,1},{2,6},{6,10},{... | collective-permute-start | bytes 884744 | tf_op jit(solution)/shard_map/ppermute | solution.py:20
  52.8 20.2 %collective-permute-start.7 = (bf16[3,128,384]{2,1,0:T(8,128)(2,1)}, bf16[3,128,384]{2,1,0:T(8,128)(2,1)S(1)}, u32[]{:S(2)}, u32[]{:S(2)}) collective-permute-start(bf16[3,128,384]{2,1,0:T(8,128)(2,1)} %get-tuple-element.209), channel_id=1, source_target_pairs={{0,8},{4,12},{8,0},{12,4},{1,9},{5,13},{9,1},{13,5},{2,10},{6,14},... | collective-permute-start | bytes 884744 | tf_op jit(solution)/shard_map/ppermute | solution.py:20
  55.3 32.8 %collective-permute-start.8 = (bf16[3,128,384]{2,1,0:T(8,128)(2,1)}, bf16[3,128,384]{2,1,0:T(8,128)(2,1)S(1)}, u32[]{:S(2)}, u32[]{:S(2)}) collective-permute-start(bf16[3,128,384]{2,1,0:T(8,128)(2,1)} %get-tuple-element.210), channel_id=1, source_target_pairs={{0,12},{4,0},{8,4},{12,8},{1,13},{5,1},{9,5},{13,9},{2,14},{6,2},{... | collective-permute-start | bytes 884744 | tf_op jit(solution)/shard_map/ppermute | solution.py:20
  64.4 32.8 %collective-permute-start.3 = (bf16[128,640]{1,0:T(8,128)(2,1)}, bf16[128,640]{1,0:T(8,128)(2,1)S(1)}, u32[]{:S(2)}, u32[]{:S(2)}) collective-permute-start(bf16[128,640]{1,0:T(8,128)(2,1)} %get-tuple-element.200), channel_id=1, source_target_pairs={{0,12},{4,0},{8,4},{12,8},{1,13},{5,1},{9,5},{13,9},{2,14},{6,2},{... | collective-permute-start | bytes 491528 | tf_op jit(solution)/shard_map/ppermute | solution.py:20
  66.5 21.6 %copy-start.7 = (bf16[3,128,384]{2,1,0:T(8,128)(2,1)}, bf16[3,128,384]{2,1,0:T(8,128)(2,1)S(1)}, u32[]{:S(2)}) copy-start(bf16[3,128,384]{2,1,0:T(8,128)(2,1)S(1)} %collective-permute-done.6.refs_1_) | copy-start | bytes 884740
  66.5 34.5 %collective-permute-start.4 = (bf16[128,640]{1,0:T(8,128)(2,1)}, bf16[128,640]{1,0:T(8,128)(2,1)S(1)}, u32[]{:S(2)}, u32[]{:S(2)}) collective-permute-start(bf16[128,640]{1,0:T(8,128)(2,1)} %get-tuple-element.201), channel_id=1, source_target_pairs={{0,8},{4,12},{8,0},{12,4},{1,9},{5,13},{9,1},{13,5},{2,10},{6,14},... | collective-permute-start | bytes 491528 | tf_op jit(solution)/shard_map/ppermute | solution.py:20
  73.0 15.1 %copy-start.8 = (bf16[3,128,384]{2,1,0:T(8,128)(2,1)}, bf16[3,128,384]{2,1,0:T(8,128)(2,1)S(1)}, u32[]{:S(2)}) copy-start(bf16[3,128,384]{2,1,0:T(8,128)(2,1)S(1)} %collective-permute-done.7.refs_2_) | copy-start | bytes 884740
  73.0 28.0 %collective-permute-start.5 = (bf16[128,640]{1,0:T(8,128)(2,1)}, bf16[128,640]{1,0:T(8,128)(2,1)S(1)}, u32[]{:S(2)}, u32[]{:S(2)}) collective-permute-start(bf16[128,640]{1,0:T(8,128)(2,1)} %get-tuple-element.202), channel_id=1, source_target_pairs={{0,4},{4,8},{8,12},{12,0},{1,5},{5,9},{9,13},{13,1},{2,6},{6,10},{... | collective-permute-start | bytes 491528 | tf_op jit(solution)/shard_map/ppermute | solution.py:20
  93.9 8.8 %collective-permute-start.10 = (bf16[128,384]{1,0:T(8,128)(2,1)}, bf16[128,384]{1,0:T(8,128)(2,1)S(1)}, u32[]{:S(2)}, u32[]{:S(2)}) collective-permute-start(bf16[128,384]{1,0:T(8,128)(2,1)} %get-tuple-element.213), channel_id=1, source_target_pairs={{0,8},{4,12},{8,0},{12,4},{1,9},{5,13},{9,1},{13,5},{2,10},{6,14},... | collective-permute-start | bytes 294920 | tf_op jit(solution)/shard_map/ppermute | solution.py:20
  97.2 6.7 %collective-permute-start.11 = (bf16[128,384]{1,0:T(8,128)(2,1)}, bf16[128,384]{1,0:T(8,128)(2,1)S(1)}, u32[]{:S(2)}, u32[]{:S(2)}) collective-permute-start(bf16[128,384]{1,0:T(8,128)(2,1)} %get-tuple-element.214), channel_id=1, source_target_pairs={{0,4},{4,8},{8,12},{12,0},{1,5},{5,9},{9,13},{13,1},{2,6},{6,10},{... | collective-permute-start | bytes 294920 | tf_op jit(solution)/shard_map/ppermute | solution.py:20
  97.2 6.8 %collective-permute-start.9 = (bf16[128,384]{1,0:T(8,128)(2,1)}, bf16[128,384]{1,0:T(8,128)(2,1)S(1)}, u32[]{:S(2)}, u32[]{:S(2)}) collective-permute-start(bf16[128,384]{1,0:T(8,128)(2,1)} %get-tuple-element.212), channel_id=1, source_target_pairs={{0,12},{4,0},{8,4},{12,8},{1,13},{5,1},{9,5},{13,9},{2,14},{6,2},{... | collective-permute-start | bytes 294920 | tf_op jit(solution)/shard_map/ppermute | solution.py:20
  104.2 1.4 %copy-start.5 = (bf16[1,128,4096]{2,1,0:T(8,128)(2,1)}, bf16[1,128,4096]{2,1,0:T(8,128)(2,1)S(1)}, u32[]{:S(2)}) copy-start(bf16[1,128,4096]{2,1,0:T(8,128)(2,1)S(1)} %get-tuple-element.255) | copy-start | bytes 3145732
  (3 other events, 3.3 us)

commit v15 on v8

--- a/solution.py
+++ b/solution.py
@@ -171,9 +171,12 @@
     return lax.switch(own_index, branches, query_rows, key_rows, value_rows)
 
 
-def attend_pieces_kernel(lists_ref, live_ref, me_ref, *refs, block, slots, qblocks, heads, depth):
-    sources = len(refs) // 2
-    x_refs, o_refs = refs[:sources], refs[sources:]
+def attend_pieces_kernel(
+    lists_ref, live_ref, me_ref, *refs, block, slots, qblocks, heads, depth, steps
+):
+    sources = len(refs) - len(steps)
+    x_refs, outs = refs[:sources], refs[sources:]
+    o_refs = dict(zip(steps, outs))
     tokens = x_refs[0].shape[1]
     total = sources * tokens
     me = me_ref[0]
@@ -184,7 +187,7 @@
         cols = slice(head * depth, (head + 1) * depth)
         keys = jnp.concatenate([ref[1, :, cols] for ref in x_refs], axis=0)
         values = jnp.concatenate([ref[2, :, cols] for ref in x_refs], axis=0)
-        for step in range(sources):
+        for step in steps:
             device = (me - step + sources) % sources
             for sub in range(per_source):
                 rows = slice(sub * block, (sub + 1) * block)
@@ -213,7 +216,8 @@
                 o_refs[step][rows, cols] = (mixed / totals).astype(o_refs[step].dtype)
 
 
-def attend_pieces(pieces, lists, live, me):
+def attend_pieces(pieces, lists, live, me, steps=None):
+    steps = tuple(range(len(pieces))) if steps is None else tuple(steps)
     _, tokens, width = pieces[0].shape
     head_total, qblocks = live.shape
     slots = lists.shape[2]
@@ -226,14 +230,15 @@
         qblocks=qblocks,
         heads=head_total,
         depth=depth,
+        steps=steps,
     )
     smem = pltpu.SMEM
     return pl.pallas_call(
         kernel,
         in_specs=[pl.BlockSpec(memory_space=smem)] * 3
         + [pl.BlockSpec(memory_space=pltpu.VMEM)] * len(pieces),
-        out_specs=[pl.BlockSpec(memory_space=pltpu.VMEM)] * len(pieces),
-        out_shape=[jax.ShapeDtypeStruct((tokens, width), jnp.bfloat16)] * len(pieces),
+        out_specs=[pl.BlockSpec(memory_space=pltpu.VMEM)] * len(steps),
+        out_shape=[jax.ShapeDtypeStruct((tokens, width), jnp.bfloat16)] * len(steps),
     )(lists.reshape(-1), live.reshape(-1), me.reshape(1), *pieces)
 
 
@@ -315,10 +320,19 @@
             for step in range(1, seq_count):
                 received.append(passed_along(pieces[step], "seq", step))
             previous = received
-            outs = attend_pieces(received, lists, live, own_index.astype(jnp.int32))
-            backs.append(outs[0])
-            for step in range(1, seq_count):
-                backs.append(passed_along(outs[step], "seq", -step))
+            if start + per_chunk < per_device:
+                outs = attend_pieces(received, lists, live, own_index.astype(jnp.int32))
+                backs.append(outs[0])
+                for step in range(1, seq_count):
+                    backs.append(passed_along(outs[step], "seq", -step))
+                continue
+            returned = {}
+            for step in list(range(1, seq_count)) + [0]:
+                (piece,) = attend_pieces(
+                    received, lists, live, own_index.astype(jnp.int32), steps=(step,)
+                )
+                returned[step] = passed_along(piece, "seq", -step) if step else piece
+            backs.extend(returned[step] for step in range(seq_count))
             continue
         send = packed_chunk(
             query_rows, key_rows, value_rows, seq_count, per_device * depth, start * depth, chunk_width

time: 104 us -> 107 us (1.029)
  Pallas kernels: 18.7 us -> 23.7 us
  waiting for transfers between devices: 37.6 us -> 35.8 us
    pallas_call x2 -> x5, Pallas kernels: 12.8 us -> 17.9 us  [attend_pieces(): pl.pallas_call(kernel, in_specs=[pl.BlockSpec(memory_space=smem)] * 3 + [...]
    ppermute x13, waiting for transfers between devices: 37.6 us -> 35.8 us  [passed_along(): return lax.ppermute(value, axis, pairs)]
  transfers between devices with their start and end apart: 13 -> 13, of which waited for: 4 -> 4; matrix products, arithmetic and copies ran while one was open for 5% -> 5% of each run, Pallas kernels for 15% -> 19%
where the time goes in v15:
time: 107 us
  starting transfers between devices  39.3 us (37%)
  waiting for transfers between devices  35.8 us (33%)
  Pallas kernels  23.7 us (22%)
  local copies, waits for them, and re-layouts  4.97 us (5%)
  between operations  1.58 us (1%)
    ppermute x13, starting transfers between devices, passed_along(): return lax.ppermute(value, axis, pairs)  39.3 us
    ppermute x13, waiting for transfers between devices, passed_along(): return lax.ppermute(value, axis, pairs)  35.8 us
    pallas_call x5, Pallas kernels, attend_pieces(): pl.pallas_call(kernel, in_specs=[pl.BlockSpec(memory_space=smem)] * 3 + [...  17.9 us
    pallas_call x3, Pallas kernels, branch(): pl.pallas_call(kernel, in_specs=[pl.BlockSpec(memory_space=pltpu.VMEM)] *...  5.81 us
  transfers between devices with their start and end apart: 13, of which 4 were waited for; matrix products, arithmetic and copies ran while one was open for 5% of the time, Pallas kernels for 19%

profile of v15, /device:TPU:0, one launch (start us, length us, event | category | flops | bytes accessed | tf_op | source)
XLA Modules:
  0.0 107.0 jit_solution(5588396536747504286)
XLA Ops:
  0.7 3.4 %conditional.3 = ((bf16[3,128,768]{2,1,0:T(8,128)(2,1)}, bf16[3,128,768]{2,1,0:T(8,128)(2,1)}, bf16[3,128,768]{2,1,0:T(8,128)(2,1)}, bf16[3,128,768]{2,1,0:T(8,128)(2,1)})) conditional(s32[]{:T(128)} %clamp.2, (bf16[1,128,4096]{2,1,0:T(8,128)(2,1)}, bf16[1,128,4096]{2,1,0:T(8,128)(2,1)}, ...), branch_computations={%region_0.0_spmd, %region_1.0_spmd, %region_2.0_spmd, %region_3.0_... | conditional | bytes 8 | solution.py:171
  0.7 3.4 %branch_0_fun.3 = (bf16[3,128,768]{2,1,0:T(8,128)(2,1)}, bf16[3,128,768]{2,1,0:T(8,128)(2,1)}, bf16[3,128,768]{2,1,0:T(8,128)(2,1)}, bf16[3,128,768]{2,1,0:T(8,128)(2,1)}) custom-call(bf16[1,128,4096]{2,1,0:T(8,128)(2,1)} %get-tuple-element.87.refs_0_, bf16[1,128,4096]{2,1,0:T(8,128)(2,1)} %get-tuple-element.102.refs_1_, ...), custom_call_target="tpu_custom_call" | custom-call | tf_op jit(solution)/shard_map/cond/branch_0_fun/pallas_call | solution.py:162
  4.1 3.1 %collective-permute-start = (bf16[3,128,768]{2,1,0:T(8,128)(2,1)}, bf16[3,128,768]{2,1,0:T(8,128)(2,1)}, u32[]{:S(2)}, u32[]{:S(2)}) collective-permute-start(bf16[3,128,768]{2,1,0:T(8,128)(2,1)} %get-tuple-element.192), channel_id=1, source_target_pairs={{0,4},{4,8},{8,12},{12,0},{1,5},{5,9},{9,13},{13,1},{2,6},{6,10},{... | collective-permute-start | bytes 1769480 | tf_op jit(solution)/shard_map/ppermute | solution.py:20
  7.2 2.6 %collective-permute-start.1 = (bf16[3,128,768]{2,1,0:T(8,128)(2,1)}, bf16[3,128,768]{2,1,0:T(8,128)(2,1)}, u32[]{:S(2)}, u32[]{:S(2)}) collective-permute-start(bf16[3,128,768]{2,1,0:T(8,128)(2,1)} %get-tuple-element.193), channel_id=1, source_target_pairs={{0,8},{4,12},{8,0},{12,4},{1,9},{5,13},{9,1},{13,5},{2,10},{6,14},... | collective-permute-start | bytes 1769480 | tf_op jit(solution)/shard_map/ppermute | solution.py:20
  9.8 1.3 %collective-permute-start.2 = (bf16[3,128,768]{2,1,0:T(8,128)(2,1)}, bf16[3,128,768]{2,1,0:T(8,128)(2,1)}, u32[]{:S(2)}, u32[]{:S(2)}) collective-permute-start(bf16[3,128,768]{2,1,0:T(8,128)(2,1)} %get-tuple-element.194), channel_id=1, source_target_pairs={{0,12},{4,0},{8,4},{12,8},{1,13},{5,1},{9,5},{13,9},{2,14},{6,2},{... | collective-permute-start | bytes 1769480 | tf_op jit(solution)/shard_map/ppermute | solution.py:20
  11.9 2.3 %conditional.4 = ((bf16[3,128,256]{2,1,0:T(8,128)(2,1)S(1)}, bf16[3,128,256]{2,1,0:T(8,128)(2,1)S(1)}, bf16[3,128,256]{2,1,0:T(8,128)(2,1)}, bf16[3,128,256]{2,1,0:T(8,128)(2,1)})) conditional(s32[]{:T(128)} %clamp.2, (bf16[1,128,4096]{2,1,0:T(8,128)(2,1)S(1)}, bf16[1,128,4096]{2,1,0:T(8,128)(2,1)}, ...), branch_computations={%region_4.0_spmd, %region_5.0_spmd, %region_6.0_spmd, %region_7.0_... | conditional | bytes 8 | solution.py:171
  12.0 2.3 %branch_0_fun.4 = (bf16[3,128,256]{2,1,0:T(8,128)(2,1)S(1)}, bf16[3,128,256]{2,1,0:T(8,128)(2,1)S(1)}, bf16[3,128,256]{2,1,0:T(8,128)(2,1)}, bf16[3,128,256]{2,1,0:T(8,128)(2,1)}) custom-call(bf16[1,128,4096]{2,1,0:T(8,128)(2,1)S(1)} %get-tuple-element.129.refs_0_, bf16[1,128,4096]{2,1,0:T(8,128)(2,1)} %get-tuple-element.130.refs_1_, ...), custom_call_target="tpu_custom_call" | custom-call | tf_op jit(solution)/shard_map/cond/branch_0_fun/pallas_call | solution.py:162
  15.1 0.8 fusion.15
  15.9 8.0 %collective-permute-done.refs_1_ = bf16[3,128,768]{2,1,0:T(8,128)(2,1)} collective-permute-done((bf16[3,128,768]{2,1,0:T(8,128)(2,1)}, bf16[3,128,768]{2,1,0:T(8,128)(2,1)}, u32[]{:S(2)}, u32[]{:S(2)}) %collective-permute-start) | collective-permute-done | bytes 589856 | tf_op jit(solution)/shard_map/ppermute | solution.py:20
  23.8 24.4 %collective-permute-done.1.refs_2_ = bf16[3,128,768]{2,1,0:T(8,128)(2,1)} collective-permute-done((bf16[3,128,768]{2,1,0:T(8,128)(2,1)}, bf16[3,128,768]{2,1,0:T(8,128)(2,1)}, u32[]{:S(2)}, u32[]{:S(2)}) %collective-permute-start.1) | collective-permute-done | bytes 589856 | tf_op jit(solution)/shard_map/ppermute | solution.py:20
  48.3 13.1 %collective-permute-start.6 = (bf16[3,128,256]{2,1,0:T(8,128)(2,1)S(1)}, bf16[3,128,256]{2,1,0:T(8,128)(2,1)S(1)}, u32[]{:S(2)}, u32[]{:S(2)}) collective-permute-start(bf16[3,128,256]{2,1,0:T(8,128)(2,1)S(1)} %get-tuple-element.204), channel_id=1, source_target_pairs={{0,4},{4,8},{8,12},{12,0},{1,5},{5,9},{9,13},{13,1},{2,6},{6,10},{... | collective-permute-start | bytes 589832 | tf_op jit(solution)/shard_map/ppermute | solution.py:20
  62.2 1.6 %collective-permute-start.7 = (bf16[3,128,256]{2,1,0:T(8,128)(2,1)S(1)}, bf16[3,128,256]{2,1,0:T(8,128)(2,1)S(1)}, u32[]{:S(2)}, u32[]{:S(2)}) collective-permute-start(bf16[3,128,256]{2,1,0:T(8,128)(2,1)S(1)} %copy-done.10), channel_id=1, source_target_pairs={{0,8},{4,12},{8,0},{12,4},{1,9},{5,13},{9,1},{13,5},{2,10},{6,14},... | collective-permute-start | bytes 589832 | tf_op jit(solution)/shard_map/ppermute | solution.py:20
  64.6 0.8 collective-permute-start.8
  65.4 8.8 %shard_map.113 = (bf16[128,768]{1,0:T(8,128)(2,1)S(1)}, bf16[128,768]{1,0:T(8,128)(2,1)}, bf16[128,768]{1,0:T(8,128)(2,1)}, bf16[128,768]{1,0:T(8,128)(2,1)}) custom-call(s32[96]{0:T(128)} %reshape.67.lists_ref, s32[24]{0:T(128)} %reshape.68.live_ref, s32[1]{0:T(128)} %bitcast.me_ref, bf16[3,128,768]{2,1,0:T(8,128)(2,1)} %get-tuple-element.191.refs_0_, ...), custom_call_target="tpu_custom_call" | custom-call | tf_op jit(solution)/shard_map/pallas_call | solution.py:236
  74.2 2.0 %collective-permute-start.3 = (bf16[128,768]{1,0:T(8,128)(2,1)}, bf16[128,768]{1,0:T(8,128)(2,1)S(1)}, u32[]{:S(2)}, u32[]{:S(2)}) collective-permute-start(bf16[128,768]{1,0:T(8,128)(2,1)} %get-tuple-element.196), channel_id=1, source_target_pairs={{0,12},{4,0},{8,4},{12,8},{1,13},{5,1},{9,5},{13,9},{2,14},{6,2},{... | collective-permute-start | bytes 589832 | tf_op jit(solution)/shard_map/ppermute | solution.py:20
  76.2 0.7 collective-permute-start.4
  79.3 2.4 %shard_map.117 = bf16[128,256]{1,0:T(8,128)(2,1)} custom-call(s32[32]{0:T(128)} %reshape.70.lists_ref, s32[8]{0:T(128)} %reshape.71.live_ref, s32[1]{0:T(128)} %bitcast.me_ref, bf16[3,128,256]{2,1,0:T(8,128)(2,1)S(1)} %get-tuple-element.203.refs_0_, bf16[3,128,256]{2,1,0:T(8,128)(2,1)} %copy-done.3, bf16[3,128,256]{2,1,0:T(8,128)(2,1)} %copy-done.4, ...), custom_call_target="tpu_custom_call" | custom-call | tf_op jit(solution)/shard_map/pallas_call | solution.py:236
  81.7 10.6 %collective-permute-start.11 = (bf16[128,256]{1,0:T(8,128)(2,1)}, bf16[128,256]{1,0:T(8,128)(2,1)S(1)}, u32[]{:S(2)}, u32[]{:S(2)}) collective-permute-start(bf16[128,256]{1,0:T(8,128)(2,1)} %shard_map.117), channel_id=1, source_target_pairs={{0,4},{4,8},{8,12},{12,0},{1,5},{5,9},{9,13},{13,1},{2,6},{6,10},{... | collective-permute-start | bytes 196616 | tf_op jit(solution)/shard_map/ppermute | solution.py:20
  92.3 2.4 %shard_map.116 = bf16[128,256]{1,0:T(8,128)(2,1)} custom-call(s32[32]{0:T(128)} %reshape.70.lists_ref, s32[8]{0:T(128)} %reshape.71.live_ref, s32[1]{0:T(128)} %bitcast.me_ref, bf16[3,128,256]{2,1,0:T(8,128)(2,1)S(1)} %get-tuple-element.203.refs_0_, bf16[3,128,256]{2,1,0:T(8,128)(2,1)} %copy-done.3, bf16[3,128,256]{2,1,0:T(8,128)(2,1)} %copy-done.4, ...), custom_call_target="tpu_custom_call" | custom-call | tf_op jit(solution)/shard_map/pallas_call | solution.py:236
  94.7 2.4 %shard_map.115 = bf16[128,256]{1,0:T(8,128)(2,1)} custom-call(s32[32]{0:T(128)} %reshape.70.lists_ref, s32[8]{0:T(128)} %reshape.71.live_ref, s32[1]{0:T(128)} %bitcast.me_ref, bf16[3,128,256]{2,1,0:T(8,128)(2,1)S(1)} %get-tuple-element.203.refs_0_, bf16[3,128,256]{2,1,0:T(8,128)(2,1)} %copy-done.3, bf16[3,128,256]{2,1,0:T(8,128)(2,1)} %copy-done.4, ...), custom_call_target="tpu_custom_call" | custom-call | tf_op jit(solution)/shard_map/pallas_call | solution.py:236
  97.1 3.6 %collective-permute-start.10 = (bf16[128,256]{1,0:T(8,128)(2,1)}, bf16[128,256]{1,0:T(8,128)(2,1)S(1)}, u32[]{:S(2)}, u32[]{:S(2)}) collective-permute-start(bf16[128,256]{1,0:T(8,128)(2,1)} %shard_map.116), channel_id=1, source_target_pairs={{0,8},{4,12},{8,0},{12,4},{1,9},{5,13},{9,1},{13,5},{2,10},{6,14},... | collective-permute-start | bytes 196616 | tf_op jit(solution)/shard_map/ppermute | solution.py:20
  100.7 1.8 %shard_map.114 = bf16[128,256]{1,0:T(8,128)(2,1)S(1)} custom-call(s32[32]{0:T(128)} %reshape.70.lists_ref, s32[8]{0:T(128)} %reshape.71.live_ref, s32[1]{0:T(128)} %bitcast.me_ref, bf16[3,128,256]{2,1,0:T(8,128)(2,1)S(1)} %get-tuple-element.203.refs_0_, bf16[3,128,256]{2,1,0:T(8,128)(2,1)} %copy-done.3, bf16[3,128,256]{2,1,0:T(8,128)(2,1)} %copy-done.4, ...), custom_call_target="tpu_custom_call" | custom-call | tf_op jit(solution)/shard_map/pallas_call | solution.py:236
  102.5 2.1 %collective-permute-done.10 = bf16[128,256]{1,0:T(8,128)(2,1)S(1)} collective-permute-done((bf16[128,256]{1,0:T(8,128)(2,1)}, bf16[128,256]{1,0:T(8,128)(2,1)S(1)}, u32[]{:S(2)}, u32[]{:S(2)}) %collective-permute-start.10) | collective-permute-done | bytes 65568 | tf_op jit(solution)/shard_map/ppermute | solution.py:20
  104.6 1.3 %collective-permute-done.9 = bf16[128,256]{1,0:T(8,128)(2,1)S(1)} collective-permute-done((bf16[128,256]{1,0:T(8,128)(2,1)}, bf16[128,256]{1,0:T(8,128)(2,1)S(1)}, u32[]{:S(2)}, u32[]{:S(2)}) %collective-permute-start.9) | collective-permute-done | bytes 65568 | tf_op jit(solution)/shard_map/ppermute | solution.py:20
  (58 shorter events, 6.0 us)
Async XLA Ops:
  0.6 14.4 %copy-start = (bf16[5120,64]{0,1:T(8,128)(2,1)S(1)}, bf16[5120,64]{0,1:T(8,128)(2,1)}, u32[]{:S(2)}) copy-start(bf16[5120,64]{0,1:T(8,128)(2,1)} %param.27) | copy-start | bytes 1966084
  0.7 10.5 %copy-start.7 = (f32[1,2,5120]{2,1,0:T(2,128)S(1)}, f32[1,2,5120]{2,1,0:T(2,128)}, u32[]{:S(2)}) copy-start(f32[1,2,5120]{2,1,0:T(2,128)} %param.26) | copy-start | bytes 122884
  0.7 10.5 %copy-start.2 = (bf16[1,128,5120]{2,1,0:T(8,128)(2,1)S(1)}, bf16[1,128,5120]{2,1,0:T(8,128)(2,1)}, u32[]{:S(2)}) copy-start(bf16[1,128,5120]{2,1,0:T(8,128)(2,1)} %param.25) | copy-start | bytes 3932164
  4.1 7.3 %copy-start.1 = (bf16[1,128,4096]{2,1,0:T(8,128)(2,1)S(1)}, bf16[1,128,4096]{2,1,0:T(8,128)(2,1)}, u32[]{:S(2)}) copy-start(bf16[1,128,4096]{2,1,0:T(8,128)(2,1)} %param.22) | copy-start | bytes 3145732
  4.1 19.7 %collective-permute-start = (bf16[3,128,768]{2,1,0:T(8,128)(2,1)}, bf16[3,128,768]{2,1,0:T(8,128)(2,1)}, u32[]{:S(2)}, u32[]{:S(2)}) collective-permute-start(bf16[3,128,768]{2,1,0:T(8,128)(2,1)} %get-tuple-element.192), channel_id=1, source_target_pairs={{0,4},{4,8},{8,12},{12,0},{1,5},{5,9},{9,13},{13,1},{2,6},{6,10},{... | collective-permute-start | bytes 1769480 | tf_op jit(solution)/shard_map/ppermute | solution.py:20
  7.2 41.1 %collective-permute-start.1 = (bf16[3,128,768]{2,1,0:T(8,128)(2,1)}, bf16[3,128,768]{2,1,0:T(8,128)(2,1)}, u32[]{:S(2)}, u32[]{:S(2)}) collective-permute-start(bf16[3,128,768]{2,1,0:T(8,128)(2,1)} %get-tuple-element.193), channel_id=1, source_target_pairs={{0,8},{4,12},{8,0},{12,4},{1,9},{5,13},{9,1},{13,5},{2,10},{6,14},... | collective-permute-start | bytes 1769480 | tf_op jit(solution)/shard_map/ppermute | solution.py:20
  9.8 38.5 %collective-permute-start.2 = (bf16[3,128,768]{2,1,0:T(8,128)(2,1)}, bf16[3,128,768]{2,1,0:T(8,128)(2,1)}, u32[]{:S(2)}, u32[]{:S(2)}) collective-permute-start(bf16[3,128,768]{2,1,0:T(8,128)(2,1)} %get-tuple-element.194), channel_id=1, source_target_pairs={{0,12},{4,0},{8,4},{12,8},{1,13},{5,1},{9,5},{13,9},{2,14},{6,2},{... | collective-permute-start | bytes 1769480 | tf_op jit(solution)/shard_map/ppermute | solution.py:20
  11.9 3.1 %copy-start.12 = (f32[1,128,64]{1,2,0:T(8,128)S(1)}, f32[1,128,64]{1,2,0:T(8,128)}, u32[]{:S(2)}) copy-start(f32[1,128,64]{1,2,0:T(8,128)} %param.28) | copy-start | bytes 98308
  15.1 46.3 %copy-start.8 = (s32[32,4,4]{0,2,1:T(4,128)S(1)}, s32[32,4,4]{0,2,1:T(4,128)}, u32[]{:S(2)}) copy-start(s32[32,4,4]{0,2,1:T(4,128)} %param.31) | copy-start | bytes 6148
  15.1 47.2 %copy-start.10 = (bf16[3,128,256]{2,1,0:T(8,128)(2,1)S(1)}, bf16[3,128,256]{2,1,0:T(8,128)(2,1)}, u32[]{:S(2)}) copy-start(bf16[3,128,256]{2,1,0:T(8,128)(2,1)} %get-tuple-element.205) | copy-start | bytes 589828
  15.1 48.7 %copy-start.9 = (s32[32,4]{0,1:T(4,128)S(1)}, s32[32,4]{0,1:T(4,128)}, u32[]{:S(2)}) copy-start(s32[32,4]{0,1:T(4,128)} %param.30) | copy-start | bytes 1540
  15.1 49.5 %copy-start.11 = (bf16[3,128,256]{2,1,0:T(8,128)(2,1)S(1)}, bf16[3,128,256]{2,1,0:T(8,128)(2,1)}, u32[]{:S(2)}) copy-start(bf16[3,128,256]{2,1,0:T(8,128)(2,1)} %get-tuple-element.206) | copy-start | bytes 589828
  48.3 28.7 %collective-permute-start.6 = (bf16[3,128,256]{2,1,0:T(8,128)(2,1)S(1)}, bf16[3,128,256]{2,1,0:T(8,128)(2,1)S(1)}, u32[]{:S(2)}, u32[]{:S(2)}) collective-permute-start(bf16[3,128,256]{2,1,0:T(8,128)(2,1)S(1)} %get-tuple-element.204), channel_id=1, source_target_pairs={{0,4},{4,8},{8,12},{12,0},{1,5},{5,9},{9,13},{13,1},{2,6},{6,10},{... | collective-permute-start | bytes 589832 | tf_op jit(solution)/shard_map/ppermute | solution.py:20
  62.2 14.8 %collective-permute-start.7 = (bf16[3,128,256]{2,1,0:T(8,128)(2,1)S(1)}, bf16[3,128,256]{2,1,0:T(8,128)(2,1)S(1)}, u32[]{:S(2)}, u32[]{:S(2)}) collective-permute-start(bf16[3,128,256]{2,1,0:T(8,128)(2,1)S(1)} %copy-done.10), channel_id=1, source_target_pairs={{0,8},{4,12},{8,0},{12,4},{1,9},{5,13},{9,1},{13,5},{2,10},{6,14},... | collective-permute-start | bytes 589832 | tf_op jit(solution)/shard_map/ppermute | solution.py:20
  64.6 14.0 %collective-permute-start.8 = (bf16[3,128,256]{2,1,0:T(8,128)(2,1)S(1)}, bf16[3,128,256]{2,1,0:T(8,128)(2,1)S(1)}, u32[]{:S(2)}, u32[]{:S(2)}) collective-permute-start(bf16[3,128,256]{2,1,0:T(8,128)(2,1)S(1)} %copy-done.11), channel_id=1, source_target_pairs={{0,12},{4,0},{8,4},{12,8},{1,13},{5,1},{9,5},{13,9},{2,14},{6,2},{... | collective-permute-start | bytes 589832 | tf_op jit(solution)/shard_map/ppermute | solution.py:20
  74.2 26.5 %collective-permute-start.3 = (bf16[128,768]{1,0:T(8,128)(2,1)}, bf16[128,768]{1,0:T(8,128)(2,1)S(1)}, u32[]{:S(2)}, u32[]{:S(2)}) collective-permute-start(bf16[128,768]{1,0:T(8,128)(2,1)} %get-tuple-element.196), channel_id=1, source_target_pairs={{0,12},{4,0},{8,4},{12,8},{1,13},{5,1},{9,5},{13,9},{2,14},{6,2},{... | collective-permute-start | bytes 589832 | tf_op jit(solution)/shard_map/ppermute | solution.py:20
  76.2 26.3 %collective-permute-start.4 = (bf16[128,768]{1,0:T(8,128)(2,1)}, bf16[128,768]{1,0:T(8,128)(2,1)S(1)}, u32[]{:S(2)}, u32[]{:S(2)}) collective-permute-start(bf16[128,768]{1,0:T(8,128)(2,1)} %get-tuple-element.197), channel_id=1, source_target_pairs={{0,8},{4,12},{8,0},{12,4},{1,9},{5,13},{9,1},{13,5},{2,10},{6,14},... | collective-permute-start | bytes 589832 | tf_op jit(solution)/shard_map/ppermute | solution.py:20
  76.9 1.7 %copy-start.3 = (bf16[3,128,256]{2,1,0:T(8,128)(2,1)}, bf16[3,128,256]{2,1,0:T(8,128)(2,1)S(1)}, u32[]{:S(2)}) copy-start(bf16[3,128,256]{2,1,0:T(8,128)(2,1)S(1)} %collective-permute-done.6.refs_1_) | copy-start | bytes 589828
  76.9 25.6 %collective-permute-start.5 = (bf16[128,768]{1,0:T(8,128)(2,1)}, bf16[128,768]{1,0:T(8,128)(2,1)S(1)}, u32[]{:S(2)}, u32[]{:S(2)}) collective-permute-start(bf16[128,768]{1,0:T(8,128)(2,1)} %get-tuple-element.198), channel_id=1, source_target_pairs={{0,4},{4,8},{8,12},{12,0},{1,5},{5,9},{9,13},{13,1},{2,6},{6,10},{... | collective-permute-start | bytes 589832 | tf_op jit(solution)/shard_map/ppermute | solution.py:20
  77.0 1.6 %copy-start.4 = (bf16[3,128,256]{2,1,0:T(8,128)(2,1)}, bf16[3,128,256]{2,1,0:T(8,128)(2,1)S(1)}, u32[]{:S(2)}) copy-start(bf16[3,128,256]{2,1,0:T(8,128)(2,1)S(1)} %collective-permute-done.7.refs_2_) | copy-start | bytes 589828
  77.0 20.1 %collective-permute-start.12 = (f32[1,128,64]{1,2,0:T(8,128)S(1)}, f32[1,128,64]{1,2,0:T(8,128)S(1)}, u32[]{:S(2)}, u32[]{:S(2)}) collective-permute-start(f32[1,128,64]{1,2,0:T(8,128)S(1)} %fusion.15), channel_id=1, source_target_pairs={{0,3},{1,0},{2,1},{3,2},{4,7},{5,4},{6,5},{7,6},{8,11},{9,8},{10,9... | collective-permute-start | bytes 98312 | tf_op jit(solution)/shard_map/ppermute | solution.py:20
  81.7 20.8 %collective-permute-start.11 = (bf16[128,256]{1,0:T(8,128)(2,1)}, bf16[128,256]{1,0:T(8,128)(2,1)S(1)}, u32[]{:S(2)}, u32[]{:S(2)}) collective-permute-start(bf16[128,256]{1,0:T(8,128)(2,1)} %shard_map.117), channel_id=1, source_target_pairs={{0,4},{4,8},{8,12},{12,0},{1,5},{5,9},{9,13},{13,1},{2,6},{6,10},{... | collective-permute-start | bytes 196616 | tf_op jit(solution)/shard_map/ppermute | solution.py:20
  97.1 7.5 %collective-permute-start.10 = (bf16[128,256]{1,0:T(8,128)(2,1)}, bf16[128,256]{1,0:T(8,128)(2,1)S(1)}, u32[]{:S(2)}, u32[]{:S(2)}) collective-permute-start(bf16[128,256]{1,0:T(8,128)(2,1)} %shard_map.116), channel_id=1, source_target_pairs={{0,8},{4,12},{8,0},{12,4},{1,9},{5,13},{9,1},{13,5},{2,10},{6,14},... | collective-permute-start | bytes 196616 | tf_op jit(solution)/shard_map/ppermute | solution.py:20
  100.7 5.2 %collective-permute-start.9 = (bf16[128,256]{1,0:T(8,128)(2,1)}, bf16[128,256]{1,0:T(8,128)(2,1)S(1)}, u32[]{:S(2)}, u32[]{:S(2)}) collective-permute-start(bf16[128,256]{1,0:T(8,128)(2,1)} %shard_map.115), channel_id=1, source_target_pairs={{0,12},{4,0},{8,4},{12,8},{1,13},{5,1},{9,5},{13,9},{2,14},{6,2},{... | collective-permute-start | bytes 196616 | tf_op jit(solution)/shard_map/ppermute | solution.py:20
  (2 other events, 1.7 us)
